TPU v7x, 32 devices: a whole 2x2x4 slice. The times are simulated.
32 devices in a mesh: dp: 8 (over z, core), leaf: 4 (over y, x).
Axes of the slice: x: 2, y: 2, z: 4, core: 2. Of those that a mesh axis runs over, the one named last changes fastest.
Arguments:
- features: bfloat16 [51200, 384], P(('dp', 'leaf')), may hold values from -6 to 6
- head_weight: bfloat16 [384, 1536], replicated, may hold values from -0.3125 to 0.3125
- gain: float32 [1536], replicated, may hold values from 0.5 to 1.5
- shift: float32 [1536], replicated, may hold values from -3 to 3
- node_weights: bfloat16 [4096, 1536], P('leaf'), may hold values from -0.15625 to 0.15625
- subtree_map: int32 [64], replicated, may hold values from 0 to 63, each once
- node_ids: int32 [512, 64], P('dp'), may hold values from -1 to 4095, as said below
Outputs:
- head_grad: float32 [384, 1536], P(None, 'dp')
- gain_grad: float32 [1536], P('dp')
- shift_grad: float32 [1536], P('dp')
- node_grad: float32 [4096, 1536], P('leaf', 'dp')
Inputs may be any that keep to these rules, and one draw needn't show every extreme that they name: `node_ids`: each image has 1 to 16 positive ids, all in one subtree, in its first columns, then -1; and 1 to 48 hard-negative ids in another subtree from column 16 on, then -1. Ids of one image are distinct. The first image has full counts.
All inputs are finite; a program needn't handle non-finite values.
Results may differ from a plain program's by a relative error of at most 0.0036.
Values may be sent and summed in bfloat16 or wider, within the bound.
No kernel may reach another device: no remote copies, remote signals or barrier semaphores. Data moves between devices by JAX's collectives and lax.ppermute only.
A program may use at most 128 MiB of HBM per device.

v0:
```python
import jax
import jax.numpy as jnp
from jax import lax
from jax.sharding import PartitionSpec as P

P_SIZE = 100
SUB_SIZE = 64
KPOS = 16


def slot_table(slot_rows, owned_rows, values_rows, slots_dev):
    column = jnp.arange(slots_dev, dtype=jnp.int32)[None, None, :]
    match = (slot_rows[:, :, None] == column) & owned_rows[:, :, None]
    return jnp.sum(jnp.where(match, values_rows[:, :, None], 0.0), axis=1)


def shards(features, head_weight, gain, shift, node_weights, subtree_map, node_ids):
    images_here = features.shape[0] // P_SIZE
    width = head_weight.shape[1]
    linear_scores = jnp.dot(features, head_weight, preferred_element_type=jnp.float32)
    shifted = gain * linear_scores + shift
    sig = jax.nn.sigmoid(shifted)
    active = shifted * sig
    embedded = jnp.mean(active.reshape(images_here, P_SIZE, width), axis=1).astype(jnp.bfloat16)
    grouped = lax.all_gather(embedded, "leaf", axis=0, tiled=True)
    slots_dev = node_weights.shape[0]
    valid_pair = node_ids >= 0
    safe_ids = jnp.where(valid_pair, node_ids, 0)
    subtree = safe_ids // SUB_SIZE
    matches = (
        subtree[:, :, None] == jnp.arange(subtree_map.shape[0], dtype=jnp.int32)[None, None, :]
    )
    placed = jnp.sum(jnp.where(matches, subtree_map[None, None, :], 0), axis=2)
    slot_row = placed * SUB_SIZE + safe_ids % SUB_SIZE
    owned = valid_pair & (slot_row // slots_dev == lax.axis_index("leaf"))
    local_slot = jnp.where(owned, slot_row % slots_dev, 0)
    scores = lax.dot_general(
        grouped, node_weights, (((1,), (1,)), ((), ())), preferred_element_type=jnp.float32
    )
    target = (jnp.arange(node_ids.shape[1]) < KPOS).astype(jnp.float32)
    hit_count = slot_table(local_slot, owned, jnp.ones(local_slot.shape, jnp.float32), slots_dev)
    positive = slot_table(
        local_slot, owned, jnp.broadcast_to(target[None, :], local_slot.shape), slots_dev
    )
    table = jnp.where(hit_count > 0.5, jax.nn.sigmoid(scores) - positive, 0.0).astype(jnp.bfloat16)
    grad_part = jnp.dot(table, node_weights, preferred_element_type=jnp.float32)
    emb_grad = lax.psum_scatter(grad_part, "leaf", scatter_dimension=0, tiled=True)
    column_ids = jnp.arange(slots_dev, dtype=jnp.int32)[None, None, :]
    pick = (local_slot[:, :, None] == column_ids) & owned[:, :, None]
    coef = jnp.sum(jnp.where(pick, table.astype(jnp.float32)[:, None, :], 0.0), axis=2).astype(
        jnp.bfloat16
    )
    columns = lax.all_to_all(grouped, "dp", split_axis=1, concat_axis=0, tiled=True)
    all_coef = lax.all_gather(coef, "dp", axis=0, tiled=True)
    all_slot = lax.all_gather(local_slot, "dp", axis=0, tiled=True)
    every_pair = jnp.ones(all_slot.shape, jnp.bool_)
    all_table = slot_table(all_slot, every_pair, all_coef.astype(jnp.float32), slots_dev).astype(
        jnp.bfloat16
    )
    node_grad = lax.dot_general(
        all_table, columns, (((0,), (0,)), ((), ())), preferred_element_type=jnp.float32
    )
    slope = (sig * (1.0 + shifted * (1.0 - sig))).reshape(images_here, P_SIZE, width)
    pixel_gradient = ((emb_grad / P_SIZE)[:, None, :] * slope).reshape(images_here * P_SIZE, width)
    lin_grad = (pixel_gradient * gain).astype(jnp.bfloat16)
    head_term = lax.dot_general(
        features, lin_grad, (((0,), (0,)), ((), ())), preferred_element_type=jnp.float32
    )
    gain_term = jnp.sum(pixel_gradient * linear_scores, axis=0)
    shift_term = jnp.sum(pixel_gradient, axis=0)
    split_sums = (
        lax.psum_scatter(head_term, "dp", scatter_dimension=1, tiled=True),
        lax.psum_scatter(gain_term, "dp", scatter_dimension=0, tiled=True),
        lax.psum_scatter(shift_term, "dp", scatter_dimension=0, tiled=True),
    )
    head_grad, gain_grad, shift_grad = lax.psum(
        (split_sums[0], split_sums[1], split_sums[2]), "leaf"
    )
    return (head_grad, gain_grad, shift_grad, node_grad)


def solution(mesh):
    in_specs = (P(("dp", "leaf"), None), P(), P(), P(), P("leaf", None), P(), P("dp", None))
    out_specs = (P(None, "dp"), P("dp"), P("dp"), P("leaf", "dp"))
    return jax.shard_map(shards, mesh=mesh, in_specs=in_specs, out_specs=out_specs, check_vma=False)
```

profile of v0, /device:TPU:0, one launch (start us, length us, event | category | flops | bytes accessed | tf_op | source)
XLA Modules:
  0.0 237.6 jit_solution(990321862324019750)
XLA Ops:
  7.2 0.0 reduce-scatter.3.cloned.1.call-start
  7.2 0.9 add_select_fusion.3
  8.2 11.9 %fusion.1 = (f32[1600,1536]{1,0:T(8,128)}, f32[1600,1536]{1,0:T(8,128)}) fusion(f32[1536]{0:T(1024)} %param.10, f32[1536]{0:T(1024)} %param.9, bf16[1600,384]{1,0:T(8,128)(2,1)} %param.7, bf16[384,1536]{1,0:T(8,128)(2,1)} %param.8), kind=kOutput, calls=%fused_computation.11 | convolution fusion | flops 1902182400 | bytes 22081536 | tf_op jit(solution)/shard_map/dot_general | solution.py:20
  20.1 10.0 %reshape.27 = f32[16,100,1536]{2,1,0:T(8,128)} reshape(f32[1600,1536]{1,0:T(8,128)} %get-tuple-element.15) | data formatting | bytes 19660800 | tf_op jit(solution)/shard_map/reshape | solution.py:24
  30.1 5.3 %reduce_sum.74 = f32[16,1536]{1,0:T(8,128)S(1)} reduce(f32[16,100,1536]{2,1,0:T(8,128)} %reshape.27, f32[]{:T(128)} %constant.65.clone.1), dimensions={1}, to_apply=%region_2.3 | reduce | flops 2433024 | bytes 9928708 | tf_op jit(solution)/shard_map/reduce_sum | solution.py:24
  35.5 10.2 %all_gather.9 = bf16[64,1536]{1,0:T(8,128)(2,1)S(1)} all-gather(bf16[16,1536]{1,0:T(8,128)(2,1)S(1)} %multiply_convert_fusion.4), channel_id=1, replica_groups=mesh['dp'=8,'leaf'=4] {'leaf'}, dimensions={0}, use_global_device_ids=true | all-gather | bytes 245760 | tf_op jit(solution)/shard_map/all_gather | solution.py:25
  45.6 1.8 select_reduce_fusion.4
  47.5 0.1 fusion.15
  47.6 9.4 %select_reduce_fusion.3 = (f32[64,1024]{1,0:T(8,128)S(1)}, f32[64,1024]{1,0:T(8,128)S(1)}) fusion(s32[64,64]{1,0:T(8,128)S(1)} %get-tuple-element.13, pred[64,64]{1,0:T(8,128)(4,1)S(1)} %get-tuple-element.14, f32[64]{0:T(128)S(1)} %compare_convert_fusion), kind=kLoop, calls=%fused_computation.4 | loop fusion | flops 25034752 | bytes 545024 | tf_op jit(solution)/shard_map/reduce_sum | solution.py:14
  56.9 1.8 fusion.21
  58.7 1.4 fusion.22
  60.2 0.2 reduce-scatter.5.cloned.1.call-start
  60.4 24.7 %reduce-scatter.3.cloned.1.call-done = f32[16,1536]{1,0:T(8,128)} async-done(((f32[64,1536]{1,0:T(8,128)}), f32[16,1536]{1,0:T(8,128)}) %reduce-scatter.3.cloned.1.call-update) | async-done | bytes 98320 | tf_op jit(solution)/shard_map/reduce_scatter | solution.py:47
  85.1 0.9 broadcast_multiply_fusion
  86.0 5.2 %mul.45 = f32[16,100,1536]{2,1,0:T(8,128)} broadcast(f32[16,1536]{1,0:T(8,128)S(1)} %broadcast_multiply_fusion), dimensions={0,2} | broadcast | bytes 9928704 | tf_op jit(solution)/shard_map/mul | solution.py:64
  91.2 10.0 %mul.46 = f32[1600,1536]{1,0:T(8,128)} reshape(f32[16,100,1536]{2,1,0:T(8,128)} %mul.45) | data formatting | bytes 19660800 | tf_op jit(solution)/shard_map/mul | solution.py:64
  101.2 9.0 %fusion.20 = (f32[1536]{0:T(1024)S(1)}, f32[1536]{0:T(1024)S(1)}, f32[1600,1536]{1,0:T(8,128)S(1)}) fusion(f32[1600,1536]{1,0:T(8,128)} %get-tuple-element.16, f32[1600,1536]{1,0:T(8,128)} %mul.46, f32[1536]{0:T(1024)S(1)} %copy-done.2, f32[1536]{0:T(1024)S(1)} %copy-done.3), kind=kLoop, calls=%fused_computation.52 | loop fusion | flops 31945728 | bytes 29515776 | tf_op jit(solution)/shard_map/reduce_sum | solution.py:70
  110.3 4.5 %fusion.4 = f32[384,1536]{0,1:T(8,128)} fusion(bf16[1600,384]{1,0:T(8,128)(2,1)S(1)} %copy-done.5, f32[1600,1536]{1,0:T(8,128)S(1)} %get-tuple-element.12, f32[1536]{0:T(1024)S(1)} %copy-done.3), kind=kOutput, calls=%fused_computation.15 | convolution fusion | flops 1892352000 | bytes 13424640 | tf_op jit(solution)/shard_map/dot_general | solution.py:66
  114.8 0.9 all_to_all.14
  115.7 1.7 copy.13
  117.4 4.6 %all-to-all-start = ((bf16[64,8,192]{2,0,1:T(8,128)(2,1)}), bf16[64,8,192]{2,0,1:T(8,128)(2,1)}, u32[]{:S(2)}, u32[]{:S(2)}) async-start(bf16[64,8,192]{2,0,1:T(8,128)(2,1)} %copy.13), calls=%async_computation.2 | async-start | bytes 524288 | tf_op jit(solution)/shard_map/all_to_all | solution.py:53
  122.1 5.3 %select_reduce_fusion.1 = bf16[64,64]{1,0:T(8,128)(2,1)S(1)} fusion(f32[64,1024]{1,0:T(8,128)} %get-tuple-element.17, s32[64,64]{1,0:T(8,128)S(1)} %get-tuple-element.13, pred[64,64]{1,0:T(8,128)(4,1)S(1)} %get-tuple-element.14), kind=kLoop, calls=%fused_computation.2 | loop fusion | flops 16773120 | bytes 290816 | tf_op jit(solution)/shard_map/reduce_sum | solution.py:50
  127.4 16.8 %all_gather.11 = bf16[512,64]{1,0:T(8,128)(2,1)S(1)} all-gather(bf16[64,64]{1,0:T(8,128)(2,1)S(1)} %select_reduce_fusion.1), channel_id=1, replica_groups=mesh['dp'=8,'leaf'=4] {'dp'}, dimensions={0}, use_global_device_ids=true | all-gather | bytes 73728 | tf_op jit(solution)/shard_map/all_gather | solution.py:54
  144.3 15.8 %all_gather.10 = s32[512,64]{1,0:T(8,128)} all-gather(s32[64,64]{1,0:T(8,128)S(1)} %get-tuple-element.13), channel_id=1, replica_groups=mesh['dp'=8,'leaf'=4] {'dp'}, dimensions={0}, use_global_device_ids=true | all-gather | bytes 147456 | tf_op jit(solution)/shard_map/all_gather | solution.py:55
  160.1 28.2 %select_reduce_fusion = bf16[512,1024]{1,0:T(8,128)(2,1)} fusion(f32[512,64]{1,0:T(8,128)S(1)} %convert_element_type.30, s32[512,64]{1,0:T(8,128)} %all_gather.10), kind=kLoop, calls=%fused_computation | loop fusion | flops 100139008 | bytes 1310720 | tf_op jit(solution)/shard_map/reduce_sum | solution.py:14
  188.3 0.6 dynamic-slice
  189.6 2.6 %fusion.23 = f32[1024,192]{0,1:T(8,128)} fusion(bf16[512,1024]{1,0:T(8,128)(2,1)} %select_reduce_fusion, bf16[512,192]{1,0:T(8,128)(2,1)} %bitcast.2), kind=kOutput, calls=%fused_computation.55 | convolution fusion | flops 201326592 | bytes 2031616 | tf_op jit(solution)/shard_map/dot_general | solution.py:60
  192.1 27.6 %all-reduce.2 = (f32[1536]{0:T(1024)S(1)}, f32[1536]{0:T(1024)S(1)}) all-reduce(f32[1536]{0:T(1024)S(1)} %get-tuple-element.5, f32[1536]{0:T(1024)S(1)} %get-tuple-element.4), channel_id=4, replica_groups=mesh['dp'=8,'leaf'=4] {'dp'}, use_global_device_ids=true, to_apply=%region_8.9.clone | all-reduce | flops 3072 | bytes 24576
  219.8 0.1 dynamic-slice.1
  219.8 0.1 dynamic-slice.3
  219.9 9.4 %all-reduce.3 = (f32[192]{0:T(256)}, f32[192]{0:T(256)}) all-reduce(f32[192]{0:T(256)S(1)} %dynamic-slice.1, f32[192]{0:T(256)S(1)} %dynamic-slice.3), channel_id=1, replica_groups=mesh['dp'=8,'leaf'=4] {'leaf'}, use_global_device_ids=true, to_apply=%region_9.10 | all-reduce | flops 384 | bytes 3072 | tf_op jit(solution)/shard_map/psum | solution.py:76
  229.4 1.7 copy.15
  (24 shorter events, 0.2 us)
Async XLA Ops:
  7.2 49.8 %copy-start = (bf16[1024,1536]{1,0:T(8,128)(2,1)S(1)}, bf16[1024,1536]{1,0:T(8,128)(2,1)}, u32[]{:S(2)}) copy-start(bf16[1024,1536]{1,0:T(8,128)(2,1)} %param.11) | copy-start | bytes 9437188
  7.2 77.9 %reduce-scatter.3.cloned.1.call-start = ((), (), s32[]{:S(2)}) async-start(), calls=%async_computation.3 | async-start | bytes 491520 | tf_op jit(solution)/shard_map/reduce_scatter | solution.py:47
  30.1 15.5 %copy-start.4 = (s32[64]{0:T(128)S(1)}, s32[64]{0:T(128)}, u32[]{:S(2)}) copy-start(s32[64]{0:T(128)} %param.12) | copy-start | bytes 772
  30.1 17.3 %copy-start.1 = (s32[64,64]{1,0:T(8,128)S(1)}, s32[64,64]{1,0:T(8,128)}, u32[]{:S(2)}) copy-start(s32[64,64]{1,0:T(8,128)} %param.13) | copy-start | bytes 49156
  60.2 99.9 %reduce-scatter.5.cloned.1.call-start = ((), (), s32[]{:S(2)}) async-start(), calls=%async_computation.4 | async-start | bytes 2654208 | tf_op jit(solution)/shard_map/reduce_scatter | solution.py:72
  91.1 10.1 %copy-start.2 = (f32[1536]{0:T(1024)S(1)}, f32[1536]{0:T(1024)}, u32[]{:S(2)}) copy-start(f32[1536]{0:T(1024)} %param.10) | copy-start | bytes 18436
  91.2 10.1 %copy-start.3 = (f32[1536]{0:T(1024)S(1)}, f32[1536]{0:T(1024)}, u32[]{:S(2)}) copy-start(f32[1536]{0:T(1024)} %param.9) | copy-start | bytes 18436
  101.2 9.0 %copy-start.5 = (bf16[1600,384]{1,0:T(8,128)(2,1)S(1)}, bf16[1600,384]{1,0:T(8,128)(2,1)}, u32[]{:S(2)}) copy-start(bf16[1600,384]{1,0:T(8,128)(2,1)} %param.7) | copy-start | bytes 3686404
  110.3 78.1 %copy-start.6 = (u32[32]{0:T(128)S(1)}, u32[32]{0:T(128)}, u32[]{:S(2)}) copy-start(u32[32]{0:T(128)} %constant.71) | copy-start | bytes 388
  117.4 72.2 %all-to-all-start = ((bf16[64,8,192]{2,0,1:T(8,128)(2,1)}), bf16[64,8,192]{2,0,1:T(8,128)(2,1)}, u32[]{:S(2)}, u32[]{:S(2)}) async-start(bf16[64,8,192]{2,0,1:T(8,128)(2,1)} %copy.13), calls=%async_computation.2 | async-start | bytes 524288 | tf_op jit(solution)/shard_map/all_to_all | solution.py:53
  122.0 107.4 %all-reduce.6.cloned.1.call-start = ((), (), s32[]{:S(2)}) async-start(), calls=%async_computation.5 | async-start | bytes 589824 | tf_op jit(solution)/shard_map/psum | solution.py:76
Sparse Core Ops, SparseCore 0:
  60.3 24.7 reduce-scatter.2
  114.9 41.0 reduce-scatter.4
  160.2 41.8 all-reduce.5
where the time goes:
time: 239 us; the launch traced here: 238 us
  blocking collectives  79.9 us (33%)
  other arithmetic  61 us (26%)
  local copies, waits for them, and re-layouts  30.4 us (13%)
  waiting for transfers between devices  24.7 us (10%)
  matrix products  22.2 us (9%)
  between operations  14.5 us (6%)
  starting transfers between devices  4.89 us (2%)
    reduce_sum x2, other arithmetic, slot_table(): return jnp.sum(jnp.where(match, values_rows[:, :, None], 0.0), axis=1)  37.6 us
    unnamed x1, blocking collectives  27.6 us
    reduce_scatter x1, waiting for transfers between devices, shards(): lax.psum_scatter(grad_part, 'leaf', scatter_dimension=0, tiled=True)  24.7 us
    all_gather x1, blocking collectives, shards(): all_coef = lax.all_gather(coef, 'dp', axis=0, tiled=True)  16.8 us
    all_gather x1, blocking collectives, shards(): all_slot = lax.all_gather(local_slot, 'dp', axis=0, tiled=True)  15.8 us
    mul x2, local copies, waits for them, and re-layouts, shards(): (emb_grad / P_SIZE)[:, None, :] * slope  15.2 us
    dot_general x1, matrix products, shards(): jnp.dot(features, head_weight, preferred_element_type=jnp.float32)  11.9 us
    all_gather x1, blocking collectives, shards(): grouped = lax.all_gather(embedded, 'leaf', axis=0, tiled=True)  10.2 us
  transfers between devices with their start and end apart: 4, of which 1 were waited for; matrix products, arithmetic and copies ran while one was open for 16% of the time, Pallas kernels for 0%

commit v1 on v0

v1 whole, which is shorter than its diff:
```python
import jax
import jax.numpy as jnp
from jax import lax
from jax.sharding import PartitionSpec as P

P_SIZE = 100
SUB_SIZE = 64
KPOS = 16
HIGHEST = lax.Precision.HIGHEST


def block_table(pos_vec, pos_blk, neg_vec, neg_blk, blocks):
    lane_block = jnp.arange(blocks * SUB_SIZE, dtype=jnp.int32)[None, :] // SUB_SIZE
    pos_wide = jnp.tile(pos_vec, (1, blocks))
    neg_wide = jnp.tile(neg_vec, (1, blocks))
    pos_part = jnp.where(lane_block == pos_blk[:, None], pos_wide, 0.0)
    neg_part = jnp.where(lane_block == neg_blk[:, None], neg_wide, 0.0)
    return pos_part + neg_part


def pick_block(values, blk, blocks):
    rows = values.shape[0]
    split = values.reshape(rows, blocks, SUB_SIZE)
    hit = jnp.arange(blocks, dtype=jnp.int32)[None, :, None] == blk[:, None, None]
    return jnp.sum(jnp.where(hit, split, 0.0), axis=1)


def lane_mask(ids, valid):
    column = jnp.arange(SUB_SIZE, dtype=jnp.int32)[None, None, :]
    hit = ((ids % SUB_SIZE)[:, :, None] == column) & valid[:, :, None]
    return jnp.any(hit, axis=1)


def shards(features, head_weight, gain, shift, node_weights, subtree_map, node_ids):
    rows = features.shape[0]
    images_here = rows // P_SIZE
    width = head_weight.shape[1]
    slots_dev = node_weights.shape[0]
    blocks = slots_dev // SUB_SIZE
    n_dp = lax.axis_size("dp")
    leaf = lax.axis_index("leaf")

    select = (
        jnp.arange(rows, dtype=jnp.int32)[None, :] // P_SIZE
        == jnp.arange(images_here, dtype=jnp.int32)[:, None]
    ).astype(jnp.float32)

    linear_scores = jnp.dot(features, head_weight, preferred_element_type=jnp.float32)
    shifted = gain * linear_scores + shift
    sig = jax.nn.sigmoid(shifted)
    active = shifted * sig
    image_sum = jnp.dot(select, active, precision=HIGHEST, preferred_element_type=jnp.float32)
    embedded = (image_sum / P_SIZE).astype(jnp.bfloat16)
    grouped = lax.all_gather(embedded, "leaf", axis=0, tiled=True)
    group = grouped.shape[0]

    valid = node_ids >= 0
    safe_ids = jnp.where(valid, node_ids, 0)
    block_of = subtree_map[safe_ids // SUB_SIZE]
    pos_block = block_of[:, 0]
    neg_block = block_of[:, KPOS]
    pos_here = jnp.where(pos_block // blocks == leaf, pos_block % blocks, -1)
    neg_here = jnp.where(neg_block // blocks == leaf, neg_block % blocks, -1)
    pos_mask = lane_mask(safe_ids[:, :KPOS], valid[:, :KPOS])
    neg_mask = lane_mask(safe_ids[:, KPOS:], valid[:, KPOS:])

    scores = lax.dot_general(
        grouped, node_weights, (((1,), (1,)), ((), ())), preferred_element_type=jnp.float32
    )
    pos_logit = pick_block(scores, pos_here, blocks)
    neg_logit = pick_block(scores, neg_here, blocks)
    pos_coef = jnp.where(pos_mask & (pos_here >= 0)[:, None], jax.nn.sigmoid(pos_logit) - 1.0, 0.0)
    neg_coef = jnp.where(neg_mask & (neg_here >= 0)[:, None], jax.nn.sigmoid(neg_logit), 0.0)
    pos_coef = pos_coef.astype(jnp.bfloat16)
    neg_coef = neg_coef.astype(jnp.bfloat16)
    table = block_table(pos_coef, pos_here, neg_coef, neg_here, blocks).astype(jnp.bfloat16)
    grad_part = jnp.dot(table, node_weights, preferred_element_type=jnp.float32)
    emb_grad = lax.psum_scatter(grad_part, "leaf", scatter_dimension=0, tiled=True)

    col_width = width // n_dp
    column_chunks = grouped.reshape(group, n_dp, col_width).transpose(1, 0, 2)
    compact = jnp.concatenate(
        [
            pos_coef,
            neg_coef,
            pos_here[:, None].astype(jnp.bfloat16),
            neg_here[:, None].astype(jnp.bfloat16),
        ],
        axis=1,
    )
    send = jnp.concatenate(
        [column_chunks, jnp.broadcast_to(compact[None], (n_dp,) + compact.shape)], axis=2
    )
    recv = lax.all_to_all(send, "dp", split_axis=0, concat_axis=0, tiled=True)
    columns = recv[:, :, :col_width].reshape(n_dp * group, col_width)
    info = recv[:, :, col_width:].reshape(n_dp * group, compact.shape[1])
    all_pos = info[:, :SUB_SIZE]
    all_neg = info[:, SUB_SIZE : 2 * SUB_SIZE]
    all_pos_blk = info[:, 2 * SUB_SIZE].astype(jnp.int32)
    all_neg_blk = info[:, 2 * SUB_SIZE + 1].astype(jnp.int32)
    all_table = block_table(all_pos, all_pos_blk, all_neg, all_neg_blk, blocks).astype(jnp.bfloat16)
    node_grad = lax.dot_general(
        all_table, columns, (((0,), (0,)), ((), ())), preferred_element_type=jnp.float32
    )

    spread = jnp.dot(select.T, emb_grad / P_SIZE, precision=HIGHEST, preferred_element_type=jnp.float32)
    pixel_gradient = spread * (sig * (1.0 + shifted * (1.0 - sig)))
    lin_grad = (pixel_gradient * gain).astype(jnp.bfloat16)
    head_term = lax.dot_general(
        features, lin_grad, (((0,), (0,)), ((), ())), preferred_element_type=jnp.float32
    )
    gain_term = jnp.sum(pixel_gradient * linear_scores, axis=0)
    shift_term = jnp.sum(pixel_gradient, axis=0)
    stacked = jnp.concatenate([head_term, gain_term[None], shift_term[None]], axis=0)
    reduced = lax.psum(lax.psum_scatter(stacked, "dp", scatter_dimension=1, tiled=True), "leaf")
    e_size = head_term.shape[0]
    return (reduced[:e_size], reduced[e_size], reduced[e_size + 1], node_grad)


def solution(mesh):
    in_specs = (P(("dp", "leaf"), None), P(), P(), P(), P("leaf", None), P(), P("dp", None))
    out_specs = (P(None, "dp"), P("dp"), P("dp"), P("leaf", "dp"))
    return jax.shard_map(shards, mesh=mesh, in_specs=in_specs, out_specs=out_specs, check_vma=False)
```

time: 239 us -> 222 us (0.929)
  waiting for transfers between devices: 24.7 us -> 100 us
  blocking collectives: 79.9 us -> 10.2 us
  other arithmetic: 61 us -> 14.8 us
  local copies, waits for them, and re-layouts: 30.4 us -> 47.8 us
  matrix products: 22.2 us -> 28.8 us
    reduce_sum x6 -> x1, other arithmetic: 59.1 us -> 1.45 us  [pick_block(): return jnp.sum(jnp.where(hit, split, 0.0), axis=1)]
    psum x1, waiting for transfers between devices: 0.01 us -> 42.4 us  [shards(): lax.psum(lax.psum_scatter(stacked, 'dp', scatter_dimension=1, tiled=True)...]
    all_gather x2 -> x0, blocking collectives: 32.6 us -> none  [the longest x1 16.8 us: shards(): all_coef = lax.all_gather(coef, 'dp', axis=0, tiled=True)]
    unnamed x1 -> x0, blocking collectives: 27.6 us -> none
    gather x0 -> x2, local copies, waits for them, and re-layouts: none -> 24.8 us  [shards(): block_of = subtree_map[safe_ids // SUB_SIZE]]
    all_to_all x1, waiting for transfers between devices: 0.01 us -> 19.1 us  [shards(): recv = lax.all_to_all(send, 'dp', split_axis=0, concat_axis=0, tiled=True)]
    dot_general x0 -> x2, matrix products: none -> 16.5 us  [the longest x1 10.8 us: shards(): jnp.dot(select.T, emb_grad / P_SIZE, precision=HIGHEST, preferred_element...]
    mul x2 -> x0, local copies, waits for them, and re-layouts: 15.2 us -> none  [shards(): (emb_grad / P_SIZE)[:, None, :] * slope]
  transfers between devices with their start and end apart: 4 -> 4, of which waited for: 1 -> 4; matrix products, arithmetic and copies ran while one was open for 16% -> 5% of each run, Pallas kernels for 0% -> 0%
where the time goes in v1:
time: 222 us; the launch traced here: 221 us
  waiting for transfers between devices  100 us (45%)
  local copies, waits for them, and re-layouts  47.8 us (22%)
  matrix products  28.8 us (13%)
  other arithmetic  14.8 us (7%)
  between operations  14 us (6%)
  blocking collectives  10.2 us (5%)
  starting transfers between devices  4.89 us (2%)
    psum x1, waiting for transfers between devices, shards(): lax.psum(lax.psum_scatter(stacked, 'dp', scatter_dimension=1, tiled=True)...  42.4 us
    gather x2, local copies, waits for them, and re-layouts, shards(): block_of = subtree_map[safe_ids // SUB_SIZE]  24.8 us
    reduce_scatter x1, waiting for transfers between devices, shards(): lax.psum_scatter(grad_part, 'leaf', scatter_dimension=0, tiled=True)  24.6 us
    all_to_all x1, waiting for transfers between devices, shards(): recv = lax.all_to_all(send, 'dp', split_axis=0, concat_axis=0, tiled=True)  19.1 us
    unnamed x4, waiting for transfers between devices  14.2 us
    dot_general x1, matrix products, shards(): jnp.dot(select.T, emb_grad / P_SIZE, precision=HIGHEST, preferred_element...  10.8 us
    all_gather x1, blocking collectives, shards(): grouped = lax.all_gather(embedded, 'leaf', axis=0, tiled=True)  10.2 us
    unnamed x25, local copies, waits for them, and re-layouts  9.45 us
  transfers between devices with their start and end apart: 4, of which 4 were waited for; matrix products, arithmetic and copies ran while one was open for 5% of the time, Pallas kernels for 0%

profile of v1, /device:TPU:0, one launch (start us, length us, event | category | flops | bytes accessed | tf_op | source)
XLA Modules:
  0.0 220.9 jit_solution(9904976137338489691)
XLA Ops:
  7.3 0.9 broadcast_select_fusion
  10.4 24.7 %gather_fusion = s32[4096]{0:T(1024)S(1)} fusion(s32[64]{0:T(128)S(1)} %copy-done.1, s32[4096]{0:T(1024)S(1)} %broadcast_clamp_fusion), kind=kCustom, calls=%fused_computation | custom fusion | bytes 49152 | tf_op jit(solution)/shard_map/gather | solution.py:59
  37.8 4.4 %fusion.58 = f32[1600,1536]{1,0:T(8,128)S(1)} fusion(bf16[1600,384]{1,0:T(8,128)(2,1)} %param.7, bf16[384,1536]{1,0:T(8,128)(2,1)} %param.8), kind=kOutput, calls=%fused_computation.131 | convolution fusion | flops 1887436800 | bytes 12238848 | tf_op jit(solution)/shard_map/dot_general | solution.py:48
  42.2 5.6 %fusion.11 = bf16[16,1536]{1,0:T(8,128)(2,1)S(1)} fusion(f32[1600,1536]{1,0:T(8,128)S(1)} %fusion.58, f32[1536]{0:T(1024)S(1)} %copy-done.6, f32[1536]{0:T(1024)S(1)} %copy-done.7, s32[1600]{0:T(1024)S(1)} %add_select_fusion.8), kind=kOutput, calls=%fused_computation.16 | convolution fusion | flops 486679552 | bytes 9898240 | tf_op jit(solution)/shard_map/dot_general | solution.py:52
  47.9 10.2 %all_gather.3 = bf16[64,1536]{1,0:T(8,128)(2,1)S(1)} all-gather(bf16[16,1536]{1,0:T(8,128)(2,1)S(1)} %fusion.11), channel_id=1, replica_groups=mesh['dp'=8,'leaf'=4] {'leaf'}, dimensions={0}, use_global_device_ids=true | all-gather | bytes 245760 | tf_op jit(solution)/shard_map/all_gather | solution.py:54
  58.0 1.8 fusion.59
  59.8 1.9 reshape.411
  62.3 1.5 select_reduce_fusion
  64.6 1.1 tile.13
  65.7 2.3 %fusion.15 = pred[64,64]{1,0:T(8,128)(4,1)S(1)} fusion(s32[64,48]{1,0:T(8,128)} %add_select_fusion, pred[64,48]{1,0:T(8,128)(4,1)S(1)} %slice.67), kind=kLoop, calls=%fused_computation.21 | loop fusion | flops 585728 | bytes 19456 | tf_op jit(solution)/shard_map/reduce_or | solution.py:31
  69.5 1.8 tile.15
  71.3 2.4 %fusion.20 = f32[64,1536]{1,0:T(8,128)} fusion(bf16[1024,1536]{1,0:T(8,128)(2,1)S(1)} %copy-done, bf16[64,1024]{1,0:T(8,128)(2,1)S(1)} %tile.13, bf16[64,1024]{1,0:T(8,128)(2,1)} %tile.15, s32[1024]{0:T(1024)} %add_select_fusion.9, s32[64]{0:T(128)} %reduce.3, s32[64]{0:T(128)} %reduce), kind=kOutput, calls=%fused_computation.33 | convolution fusion | flops 201654272 | bytes 3805696 | tf_op jit(solution)/shard_map/dot_general | solution.py:77
  73.9 24.6 %reduce-scatter.5.cloned.1.call-done = f32[16,1536]{1,0:T(8,128)} async-done(((f32[64,1536]{1,0:T(8,128)}), f32[16,1536]{1,0:T(8,128)}) %reduce-scatter.5.cloned.1.call-update) | async-done | bytes 98320 | tf_op jit(solution)/shard_map/reduce_scatter | solution.py:78
  98.6 10.8 %multiply_reduce_fusion = (f32[1536]{0:T(1024)S(1)}, f32[1536]{0:T(1024)S(1)}, f32[1600,1536]{1,0:T(8,128)S(1)}) fusion(f32[1600,1536]{1,0:T(8,128)} %copy-done.2, f32[1536]{0:T(1024)} %param.10, f32[1536]{0:T(1024)} %param.9, f32[16,1536]{1,0:T(8,128)} %reduce-scatter.5.cloned.1.call-done, s32[1600]{0:T(1024)} %copy-done.5), kind=kOutput, calls=%fused_computation.1 | convolution fusion | flops 503855104 | bytes 19790080 | tf_op jit(solution)/shard_map/dot_general | solution.py:106
  109.5 2.4 %fusion.7 = f32[384,1536]{1,0:T(8,128)S(1)} fusion(bf16[1600,384]{1,0:T(8,128)(2,1)S(1)} %copy-done.3, f32[1600,1536]{1,0:T(8,128)S(1)} %get-tuple-element.46, f32[1536]{0:T(1024)S(1)} %copy-done.8), kind=kOutput, calls=%fused_computation.13 | convolution fusion | flops 1892352000 | bytes 13424640 | tf_op jit(solution)/shard_map/dot_general | solution.py:109
  111.9 1.6 pad_maximum_fusion
  113.6 3.4 %copy.27 = f32[386,1536]{0,1:T(8,128)} copy(f32[386,1536]{1,0:T(8,128)} %pad_maximum_fusion) | data formatting | bytes 4743168
  117.0 0.9 reshape.412
  117.9 1.0 copy.36
  120.0 4.6 %all-to-all-start = ((bf16[8,64,322]{2,1,0:T(8,128)(2,1)}), bf16[8,64,322]{2,1,0:T(8,128)(2,1)}, u32[]{:S(2)}, u32[]{:S(2)}) async-start(bf16[8,64,322]{2,1,0:T(8,128)(2,1)} %pad_maximum_fusion.1), calls=%async_computation.1 | async-start | bytes 786432 | tf_op jit(solution)/shard_map/all_to_all | solution.py:94
  124.6 19.1 %all-to-all-done = bf16[8,64,322]{2,1,0:T(8,128)(2,1)} async-done(((bf16[8,64,322]{2,1,0:T(8,128)(2,1)}), bf16[8,64,322]{2,1,0:T(8,128)(2,1)}, u32[]{:S(2)}, u32[]{:S(2)}) %all-to-all-start) | async-done | bytes 329760 | tf_op jit(solution)/shard_map/all_to_all | solution.py:94
  143.7 1.1 slice.71
  145.7 1.1 copy.34
  146.7 1.1 copy.33
  148.6 1.0 copy.32
  149.7 14.1 %reduce-scatter.7.cloned.1.call-done = f32[192,386]{1,0:T(8,128)} async-done(((f32[1536,386]{1,0:T(8,128)}), f32[192,386]{1,0:T(8,128)}) %reduce-scatter.7.cloned.1.call-update) | async-done | bytes 296464
  163.8 1.9 copy.28
  166.3 1.0 slice.76
  167.3 1.4 fusion.60
  168.7 42.4 %all-reduce.2.cloned.1.call-done = f32[386,192]{1,0:T(8,128)} async-done(((f32[386,192]{1,0:T(8,128)}), f32[386,192]{1,0:T(8,128)}) %all-reduce.2.cloned.1.call-update) | async-done | bytes 296464 | tf_op jit(solution)/shard_map/psum | solution.py:115
  211.1 1.0 slice.68
  213.0 1.3 fusion.56
  (56 shorter events, 12.4 us)
Async XLA Ops:
  7.2 50.9 %copy-start = (bf16[1024,1536]{1,0:T(8,128)(2,1)S(1)}, bf16[1024,1536]{1,0:T(8,128)(2,1)}, u32[]{:S(2)}) copy-start(bf16[1024,1536]{1,0:T(8,128)(2,1)} %param.11) | copy-start | bytes 9437188
  7.2 3.2 %copy-start.1 = (s32[64]{0:T(128)S(1)}, s32[64]{0:T(128)}, u32[]{:S(2)}) copy-start(s32[64]{0:T(128)} %param.12) | copy-start | bytes 772
  7.2 91.4 %reduce-scatter.5.cloned.1.call-start = ((), (), s32[]{:S(2)}) async-start(), calls=%async_computation.3 | async-start | bytes 491520 | tf_op jit(solution)/shard_map/reduce_scatter | solution.py:78
  7.3 34.9 %copy-start.5 = (s32[1600]{0:T(1024)}, s32[1600]{0:T(1024)S(1)}, u32[]{:S(2)}) copy-start(s32[1600]{0:T(1024)S(1)} %add_select_fusion.8) | copy-start | bytes 19204
  35.1 7.1 %copy-start.6 = (f32[1536]{0:T(1024)S(1)}, f32[1536]{0:T(1024)}, u32[]{:S(2)}) copy-start(f32[1536]{0:T(1024)} %param.10) | copy-start | bytes 18436
  35.1 7.1 %copy-start.7 = (f32[1536]{0:T(1024)S(1)}, f32[1536]{0:T(1024)}, u32[]{:S(2)}) copy-start(f32[1536]{0:T(1024)} %param.9) | copy-start | bytes 18436
  42.2 5.7 %copy-start.2 = (f32[1600,1536]{1,0:T(8,128)}, f32[1600,1536]{1,0:T(8,128)S(1)}, u32[]{:S(2)}) copy-start(f32[1600,1536]{1,0:T(8,128)S(1)} %fusion.58) | copy-start | bytes 29491204
  73.7 35.8 %copy-start.8 = (f32[1536]{0:T(1024)S(1)}, f32[1536]{0:T(1024)}, u32[]{:S(2)}) copy-start(f32[1536]{0:T(1024)} %param.9) | copy-start | bytes 18436
  73.7 90.1 %reduce-scatter.7.cloned.1.call-start = ((), (), s32[]{:S(2)}) async-start(), calls=%async_computation.5 | async-start | bytes 3538944
  98.6 10.9 %copy-start.3 = (bf16[1600,384]{1,0:T(8,128)(2,1)S(1)}, bf16[1600,384]{1,0:T(8,128)(2,1)}, u32[]{:S(2)}) copy-start(bf16[1600,384]{1,0:T(8,128)(2,1)} %param.7) | copy-start | bytes 3686404
  111.9 7.0 %copy-start.4 = (bf16[64,1]{1,0:T(8,128)(2,1)S(1)}, bf16[64,1]{1,0:T(8,128)(2,1)}, u32[]{:S(2)}) copy-start(bf16[64,1]{1,0:T(8,128)(2,1)} %get-tuple-element.42) | copy-start | bytes 388
  120.0 23.8 %all-to-all-start = ((bf16[8,64,322]{2,1,0:T(8,128)(2,1)}), bf16[8,64,322]{2,1,0:T(8,128)(2,1)}, u32[]{:S(2)}, u32[]{:S(2)}) async-start(bf16[8,64,322]{2,1,0:T(8,128)(2,1)} %pad_maximum_fusion.1), calls=%async_computation.1 | async-start | bytes 786432 | tf_op jit(solution)/shard_map/all_to_all | solution.py:94
  124.6 86.6 %all-reduce.2.cloned.1.call-start = ((), (), s32[]{:S(2)}) async-start(), calls=%async_computation.4 | async-start | bytes 802816 | tf_op jit(solution)/shard_map/psum | solution.py:115
Sparse Core Ops, SparseCore 0:
  73.8 24.7 reduce-scatter.4
  117.1 46.6 reduce-scatter.6
  166.8 44.2 all-reduce.1

commit v2 on v1

--- a/solution.py
+++ b/solution.py
@@ -31,6 +31,50 @@
     return jnp.any(hit, axis=1)
 
 
+def partners(size, bit):
+    return [(i, i ^ (1 << bit)) for i in range(size)]
+
+
+def doubling_gather(x, name):
+    size = lax.axis_size(name)
+    idx = lax.axis_index(name)
+    cur = x[None]
+    bit = 0
+    while (1 << bit) < size:
+        other = lax.ppermute(cur, name, partners(size, bit))
+        low = (idx // (1 << bit)) % 2 == 0
+        cur = jnp.where(low, jnp.concatenate([cur, other], 0), jnp.concatenate([other, cur], 0))
+        bit += 1
+    return cur.reshape((size * x.shape[0],) + x.shape[1:])
+
+
+def halving_scatter(parts, name):
+    size = lax.axis_size(name)
+    idx = lax.axis_index(name)
+    cur = [p.reshape((size, p.shape[0] // size) + p.shape[1:]) for p in parts]
+    bit = 0
+    while (1 << bit) < size:
+        mine = (idx // (1 << bit)) % 2
+        pairs = [c.reshape((c.shape[0] // 2, 2) + c.shape[1:]) for c in cur]
+        keep = [lax.dynamic_index_in_dim(p, mine, axis=1, keepdims=False) for p in pairs]
+        give = [lax.dynamic_index_in_dim(p, 1 - mine, axis=1, keepdims=False) for p in pairs]
+        got = lax.ppermute(tuple(give), name, partners(size, bit))
+        cur = [k + g for k, g in zip(keep, got)]
+        bit += 1
+    return [c.reshape(c.shape[1:]) for c in cur]
+
+
+def butterfly_sum(parts, name):
+    size = lax.axis_size(name)
+    cur = tuple(parts)
+    bit = 0
+    while (1 << bit) < size:
+        got = lax.ppermute(cur, name, partners(size, bit))
+        cur = tuple(c + g for c, g in zip(cur, got))
+        bit += 1
+    return cur
+
+
 def shards(features, head_weight, gain, shift, node_weights, subtree_map, node_ids):
     rows = features.shape[0]
     images_here = rows // P_SIZE
@@ -51,14 +95,15 @@
     active = shifted * sig
     image_sum = jnp.dot(select, active, precision=HIGHEST, preferred_element_type=jnp.float32)
     embedded = (image_sum / P_SIZE).astype(jnp.bfloat16)
-    grouped = lax.all_gather(embedded, "leaf", axis=0, tiled=True)
+    grouped = doubling_gather(embedded, "leaf")
     group = grouped.shape[0]
 
     valid = node_ids >= 0
     safe_ids = jnp.where(valid, node_ids, 0)
-    block_of = subtree_map[safe_ids // SUB_SIZE]
-    pos_block = block_of[:, 0]
-    neg_block = block_of[:, KPOS]
+    subtree_ids = jnp.arange(subtree_map.shape[0], dtype=jnp.int32)[None, :]
+    lead_sub = safe_ids[:, jnp.array([0, KPOS])] // SUB_SIZE
+    pos_block = jnp.sum(jnp.where(lead_sub[:, :1] == subtree_ids, subtree_map[None, :], 0), axis=1)
+    neg_block = jnp.sum(jnp.where(lead_sub[:, 1:] == subtree_ids, subtree_map[None, :], 0), axis=1)
     pos_here = jnp.where(pos_block // blocks == leaf, pos_block % blocks, -1)
     neg_here = jnp.where(neg_block // blocks == leaf, neg_block % blocks, -1)
     pos_mask = lane_mask(safe_ids[:, :KPOS], valid[:, :KPOS])
@@ -75,7 +120,7 @@
     neg_coef = neg_coef.astype(jnp.bfloat16)
     table = block_table(pos_coef, pos_here, neg_coef, neg_here, blocks).astype(jnp.bfloat16)
     grad_part = jnp.dot(table, node_weights, preferred_element_type=jnp.float32)
-    emb_grad = lax.psum_scatter(grad_part, "leaf", scatter_dimension=0, tiled=True)
+    (emb_grad,) = halving_scatter([grad_part], "leaf")
 
     col_width = width // n_dp
     column_chunks = grouped.reshape(group, n_dp, col_width).transpose(1, 0, 2)
@@ -107,14 +152,14 @@
     pixel_gradient = spread * (sig * (1.0 + shifted * (1.0 - sig)))
     lin_grad = (pixel_gradient * gain).astype(jnp.bfloat16)
     head_term = lax.dot_general(
-        features, lin_grad, (((0,), (0,)), ((), ())), preferred_element_type=jnp.float32
+        lin_grad, features, (((0,), (0,)), ((), ())), preferred_element_type=jnp.float32
     )
     gain_term = jnp.sum(pixel_gradient * linear_scores, axis=0)
     shift_term = jnp.sum(pixel_gradient, axis=0)
-    stacked = jnp.concatenate([head_term, gain_term[None], shift_term[None]], axis=0)
-    reduced = lax.psum(lax.psum_scatter(stacked, "dp", scatter_dimension=1, tiled=True), "leaf")
-    e_size = head_term.shape[0]
-    return (reduced[:e_size], reduced[e_size], reduced[e_size + 1], node_grad)
+    side_terms = jnp.stack([gain_term, shift_term], axis=1)
+    head_part, side_part = halving_scatter([head_term, side_terms], "dp")
+    head_sum, side_sum = butterfly_sum([head_part, side_part], "leaf")
+    return (head_sum.T, side_sum[:, 0], side_sum[:, 1], node_grad)
 
 
 def solution(mesh):

time: 222 us -> 132 us (0.59)
  waiting for transfers between devices: 100 us -> 44.1 us
  local copies, waits for them, and re-layouts: 47.8 us -> 18.9 us
  starting transfers between devices: 4.89 us -> 25.5 us
  between operations: 14 us -> 1.28 us
  blocking collectives: 10.2 us -> 0 us
    psum x1 -> x0, waiting for transfers between devices: 42.4 us -> none  [shards(): lax.psum(lax.psum_scatter(stacked, 'dp', scatter_dimension=1, tiled=True)...]
    ppermute x0 -> x14, waiting for transfers between devices: none -> 32.7 us  [the longest x8 24.4 us: halving_scatter(): got = lax.ppermute(tuple(give), name, partners(size, bit))]
    reduce_scatter x1 -> x0, waiting for transfers between devices: 24.6 us -> none  [shards(): lax.psum_scatter(grad_part, 'leaf', scatter_dimension=0, tiled=True)]
    gather x2 -> x1, local copies, waits for them, and re-layouts: 24.8 us -> 0.56 us  [shards(): lead_sub = safe_ids[:, jnp.array([0, KPOS])] // SUB_SIZE]
    ppermute x0 -> x14, starting transfers between devices: none -> 19.8 us  [the longest x8 9.96 us: halving_scatter(): got = lax.ppermute(tuple(give), name, partners(size, bit))]
    unnamed x4 -> x0, waiting for transfers between devices: 14.2 us -> none
    all_gather x1 -> x0, blocking collectives: 10.2 us -> none  [shards(): grouped = lax.all_gather(embedded, 'leaf', axis=0, tiled=True)]
    all_to_all x1, waiting for transfers between devices: 19.1 us -> 11.5 us  [shards(): recv = lax.all_to_all(send, 'dp', split_axis=0, concat_axis=0, tiled=True)]
  transfers between devices with their start and end apart: 4 -> 15, of which waited for: 4 -> 9; matrix products, arithmetic and copies ran while one was open for 5% -> 16% of each run, Pallas kernels for 0% -> 0%
where the time goes in v2:
time: 132 us
  waiting for transfers between devices  44.1 us (33%)
  matrix products  28.9 us (22%)
  starting transfers between devices  25.5 us (19%)
  local copies, waits for them, and re-layouts  18.9 us (14%)
  other arithmetic  13.2 us (10%)
    ppermute x8, waiting for transfers between devices, halving_scatter(): got = lax.ppermute(tuple(give), name, partners(size, bit))  24.4 us
    all_to_all x1, waiting for transfers between devices, shards(): recv = lax.all_to_all(send, 'dp', split_axis=0, concat_axis=0, tiled=True)  11.5 us
    dot_general x1, matrix products, shards(): jnp.dot(select.T, emb_grad / P_SIZE, precision=HIGHEST, preferred_element...  10.9 us
    ppermute x8, starting transfers between devices, halving_scatter(): got = lax.ppermute(tuple(give), name, partners(size, bit))  9.96 us
    unnamed x47, local copies, waits for them, and re-layouts  7.58 us
    all_to_all x1, starting transfers between devices, shards(): recv = lax.all_to_all(send, 'dp', split_axis=0, concat_axis=0, tiled=True)  5.74 us
    ppermute x4, waiting for transfers between devices, butterfly_sum(): got = lax.ppermute(cur, name, partners(size, bit))  5.71 us
    dot_general x1, matrix products, shards(): jnp.dot(select, active, precision=HIGHEST, preferred_element_type=jnp.flo...  5.63 us
  transfers between devices with their start and end apart: 15, of which 9 were waited for; matrix products, arithmetic and copies ran while one was open for 16% of the time, Pallas kernels for 0%

profile of v2, /device:TPU:0, one launch (start us, length us, event | category | flops | bytes accessed | tf_op | source)
XLA Modules:
  0.0 132.0 jit_solution(7917601474077474394)
XLA Ops:
  0.7 4.5 %fusion.64 = f32[1600,1536]{1,0:T(8,128)S(1)} fusion(bf16[1600,384]{1,0:T(8,128)(2,1)} %param.8, bf16[384,1536]{1,0:T(8,128)(2,1)} %param.9), kind=kOutput, calls=%fused_computation.174 | convolution fusion | flops 1887436800 | bytes 12238848 | tf_op jit(solution)/shard_map/dot_general | solution.py:92
  5.3 5.6 %fusion.15 = bf16[1,16,1536]{2,1,0:T(8,128)(2,1)S(1)} fusion(f32[1600,1536]{1,0:T(8,128)S(1)} %fusion.64, f32[1536]{0:T(1024)S(1)} %copy-done.17, f32[1536]{0:T(1024)S(1)} %copy-done.18, s32[1600]{0:T(1024)S(1)} %add_select_fusion.7), kind=kOutput, calls=%fused_computation.17 | convolution fusion | flops 486679552 | bytes 9898240 | tf_op jit(solution)/shard_map/dot_general | solution.py:96
  10.9 3.0 %collective-permute-start = (bf16[1,16,1536]{2,1,0:T(8,128)(2,1)S(1)}, bf16[1,16,1536]{2,1,0:T(8,128)(2,1)S(1)}, u32[]{:S(2)}, u32[]{:S(2)}) collective-permute-start(bf16[1,16,1536]{2,1,0:T(8,128)(2,1)S(1)} %fusion.15), channel_id=1, source_target_pairs={{0,1},{1,0},{2,3},{3,2},{4,5},{5,4},{6,7},{7,6},{8,9},{9,8},{10,11... | collective-permute-start | bytes 147464 | tf_op jit(solution)/shard_map/ppermute | solution.py:44
  15.7 1.1 fusion.19
  17.9 1.6 %collective-permute-start.1 = (bf16[2,16,1536]{2,1,0:T(8,128)(2,1)S(1)}, bf16[2,16,1536]{2,1,0:T(8,128)(2,1)S(1)}, u32[]{:S(2)}, u32[]{:S(2)}) collective-permute-start(bf16[2,16,1536]{2,1,0:T(8,128)(2,1)S(1)} %maximum_select_fusion.1), channel_id=1, source_target_pairs={{0,2},{1,3},{2,0},{3,1},{4,6},{5,7},{6,4},{7,5},{8,10},{9,11},{10,... | collective-permute-start | bytes 294920 | tf_op jit(solution)/shard_map/ppermute | solution.py:44
  20.1 2.5 %collective-permute-done.1 = bf16[2,16,1536]{2,1,0:T(8,128)(2,1)S(1)} collective-permute-done((bf16[2,16,1536]{2,1,0:T(8,128)(2,1)S(1)}, bf16[2,16,1536]{2,1,0:T(8,128)(2,1)S(1)}, u32[]{:S(2)}, u32[]{:S(2)}) %collective-permute-start.1) | collective-permute-done | bytes 98336 | tf_op jit(solution)/shard_map/ppermute | solution.py:44
  22.6 1.8 %select_reduce_fusion = (f32[64,64]{1,0:T(8,128)S(1)}, f32[64,64]{1,0:T(8,128)S(1)}) fusion(pred[64,16]{0,1:T(8,128)(4,1)S(1)} %iota_compare_fusion.7, pred[64,16]{0,1:T(8,128)(4,1)S(1)} %iota_compare_fusion.8, bf16[64,1536,1]{1,0,2:T(8,128)(2,1)S(1)} %bitcast.87, bf16[16,64,1536]{2,1,0:T(8,128)(2,1)S(1)} %bitcast.77), kind=kOutput, calls=%fused_computation.28 | convolution fusion | flops 201580544 | bytes 3377152 | tf_op jit(solution)/shard_map/dot_general | solution.py:112
  26.4 1.7 %fusion.7 = f32[2,2,16,1536]{3,2,1,0:T(8,128)S(1)} fusion(bf16[1024,1536]{1,0:T(8,128)(2,1)S(1)} %copy-done, bf16[2,2,16,1024]{3,2,1,0:T(8,128)(2,1)} %tile.13, bf16[2,2,16,1024]{3,2,1,0:T(8,128)(2,1)} %tile.15, s32[2,2,16]{2,1,0:T(2,128)} %get-tuple-element.25, s32[2,2,16]{2,1,0:T(2,128)} %get-tuple-element.26, s32[1024]{0:T(1024)} %add_select_fusion.8), kind=kOutput, calls=%fused_computation.13 | convolution fusion | flops 201654272 | bytes 3805696 | tf_op jit(solution)/shard_map/dot_general | solution.py:122
  28.9 5.8 %collective-permute-done.2 = f32[2,16,1536]{2,1,0:T(8,128)} collective-permute-done((f32[2,16,1536]{2,1,0:T(8,128)}, f32[2,16,1536]{2,1,0:T(8,128)}, u32[]{:S(2)}, u32[]{:S(2)}) %collective-permute-start.2) | collective-permute-done | bytes 196640 | tf_op jit(solution)/shard_map/ppermute | solution.py:61
  36.4 1.6 %collective-permute-start.3 = (f32[1,16,1536]{2,1,0:T(8,128)S(1)}, f32[1,16,1536]{2,1,0:T(8,128)S(1)}, u32[]{:S(2)}, u32[]{:S(2)}) collective-permute-start(f32[1,16,1536]{2,1,0:T(8,128)S(1)} %constant_dynamic-slice_fusion.5), channel_id=1, source_target_pairs={{0,2},{1,3},{2,0},{3,1},{4,6},{5,7},{6,4},{7,5},{8,10},{9,11},{10,... | collective-permute-start | bytes 294920 | tf_op jit(solution)/shard_map/ppermute | solution.py:61
  38.0 3.1 %collective-permute-done.3 = f32[1,16,1536]{2,1,0:T(8,128)S(1)} collective-permute-done((f32[1,16,1536]{2,1,0:T(8,128)S(1)}, f32[1,16,1536]{2,1,0:T(8,128)S(1)}, u32[]{:S(2)}, u32[]{:S(2)}) %collective-permute-start.3) | collective-permute-done | bytes 98336 | tf_op jit(solution)/shard_map/ppermute | solution.py:61
  41.1 10.9 %fusion.61 = (f32[1536]{0:T(1024)S(1)}, f32[1536]{0:T(1024)S(1)}, f32[1600,1536]{1,0:T(8,128)S(1)}) fusion(f32[1600,1536]{1,0:T(8,128)} %copy-done.1, f32[1536]{0:T(1024)} %param.11, f32[1536]{0:T(1024)} %param.10, f32[1,16,1536]{2,1,0:T(8,128)S(1)} %collective-permute-done.3, f32[2,16,1536]{2,1,0:T(8,128)} %copy-done.7, s32[]{:T(128)S(6)} %select_n.420, ...), kind=kOutput, calls=%fused_computation.171 | convolution fusion | flops 503879680 | bytes 19894276 | tf_op jit(solution)/shard_map/dot_general | solution.py:151
  52.0 3.1 %fusion.2 = f32[1536,384]{1,0:T(8,128)S(1)} fusion(bf16[1600,384]{1,0:T(8,128)(2,1)S(1)} %copy-done.5, f32[1600,1536]{1,0:T(8,128)S(1)} %get-tuple-element.24, f32[1536]{0:T(1024)S(1)} %copy-done.19), kind=kOutput, calls=%fused_computation.8 | convolution fusion | flops 1892352000 | bytes 13424640 | tf_op jit(solution)/shard_map/dot_general | solution.py:154
  55.1 1.4 %copy-done.3 = f32[1536,384]{1,0:T(8,128)} copy-done((f32[1536,384]{1,0:T(8,128)}, f32[1536,384]{1,0:T(8,128)S(1)}, u32[]{:S(2)}) %copy-start.3) | copy-done | bytes 2359320
  58.8 1.7 %collective-permute-done.9 = f32[4,192,2]{1,0,2:T(4,128)S(1)} collective-permute-done((f32[4,192,2]{1,0,2:T(4,128)S(1)}, f32[4,192,2]{1,0,2:T(4,128)S(1)}, u32[]{:S(2)}, u32[]{:S(2)}) %collective-permute-start.9) | collective-permute-done | bytes 6176 | tf_op jit(solution)/shard_map/ppermute | solution.py:61
  60.5 1.7 %collective-permute-start.10 = (f32[2,192,2]{1,2,0:T(2,128)S(1)}, f32[2,192,2]{1,2,0:T(2,128)S(1)}, u32[]{:S(2)}, u32[]{:S(2)}) collective-permute-start(f32[2,192,2]{1,2,0:T(2,128)S(1)} %dynamic-slice_bitcast_fusion.3), channel_id=1, source_target_pairs={{0,8},{4,12},{8,0},{12,4},{16,24},{20,28},{24,16},{28,20},{1,9},{5... | collective-permute-start | bytes 9224 | tf_op jit(solution)/shard_map/ppermute | solution.py:61
  62.2 1.7 %bitcast_add_fusion = f32[4,192,384]{2,1,0:T(8,128)S(1)} fusion(f32[4,192,384]{2,1,0:T(8,128)} %collective-permute-done.4, f32[4,2,192,384]{3,2,1,0:T(8,128)} %bitcast.84, s32[]{:T(128)S(6)} %select_n.423), kind=kLoop, calls=%fused_computation.23 | loop fusion | flops 294912 | bytes 3538948 | tf_op jit(solution)/shard_map/add | solution.py:62
  66.3 2.7 %collective-permute-start.11 = (f32[1,192,2]{1,2,0:T(2,128)S(1)}, f32[1,192,2]{1,2,0:T(2,128)S(1)}, u32[]{:S(2)}, u32[]{:S(2)}) collective-permute-start(f32[1,192,2]{1,2,0:T(2,128)S(1)} %constant_dynamic-slice_fusion), channel_id=1, source_target_pairs={{0,16},{4,20},{8,24},{12,28},{16,0},{20,4},{24,8},{28,12},{1,17},{... | collective-permute-start | bytes 4616 | tf_op jit(solution)/shard_map/ppermute | solution.py:61
  69.0 1.2 select_n.434
  70.3 9.0 %collective-permute-done.11 = f32[1,192,2]{1,2,0:T(2,128)S(1)} collective-permute-done((f32[1,192,2]{1,2,0:T(2,128)S(1)}, f32[1,192,2]{1,2,0:T(2,128)S(1)}, u32[]{:S(2)}, u32[]{:S(2)}) %collective-permute-start.11) | collective-permute-done | bytes 1568 | tf_op jit(solution)/shard_map/ppermute | solution.py:61
  80.7 5.7 %all-to-all-start = ((bf16[8,64,322]{2,1,0:T(8,128)(2,1)}), bf16[8,64,322]{2,1,0:T(8,128)(2,1)}, u32[]{:S(2)}, u32[]{:S(2)}) async-start(bf16[8,64,322]{2,1,0:T(8,128)(2,1)} %pad_maximum_fusion), calls=%async_computation | async-start | bytes 786432 | tf_op jit(solution)/shard_map/all_to_all | solution.py:139
  86.5 1.6 %collective-permute-start.13 = (f32[192,2]{0,1:T(2,128)S(1)}, f32[192,2]{0,1:T(2,128)S(1)}, u32[]{:S(2)}, u32[]{:S(2)}) collective-permute-start(f32[192,2]{0,1:T(2,128)S(1)} %add.318), channel_id=1, source_target_pairs={{0,2},{1,3},{2,0},{3,1},{4,6},{5,7},{6,4},{7,5},{8,10},{9,11},{10,... | collective-permute-start | bytes 4616 | tf_op jit(solution)/shard_map/ppermute | solution.py:72
  88.1 1.3 bitcast_add_fusion.1
  90.9 2.9 %collective-permute-start.6 = (f32[1,192,384]{2,1,0:T(8,128)}, f32[1,192,384]{2,1,0:T(8,128)}, u32[]{:S(2)}, u32[]{:S(2)}) collective-permute-start(f32[1,192,384]{2,1,0:T(8,128)} %constant_dynamic-slice_fusion.4), channel_id=1, source_target_pairs={{0,16},{4,20},{8,24},{12,28},{16,0},{20,4},{24,8},{28,12},{1,17},{... | collective-permute-start | bytes 884744 | tf_op jit(solution)/shard_map/ppermute | solution.py:61
  94.5 11.5 %all-to-all-done = bf16[8,64,322]{2,1,0:T(8,128)(2,1)} async-done(((bf16[8,64,322]{2,1,0:T(8,128)(2,1)}), bf16[8,64,322]{2,1,0:T(8,128)(2,1)}, u32[]{:S(2)}, u32[]{:S(2)}) %all-to-all-start) | async-done | bytes 329760 | tf_op jit(solution)/shard_map/all_to_all | solution.py:139
  107.0 4.8 %collective-permute-done.6 = f32[1,192,384]{2,1,0:T(8,128)} collective-permute-done((f32[1,192,384]{2,1,0:T(8,128)}, f32[1,192,384]{2,1,0:T(8,128)}, u32[]{:S(2)}, u32[]{:S(2)}) %collective-permute-start.6) | collective-permute-done | bytes 294944 | tf_op jit(solution)/shard_map/ppermute | solution.py:61
  111.8 1.8 %add_bitcast_fusion.1 = f32[192,384]{1,0:T(8,128)} fusion(f32[1,192,384]{2,1,0:T(8,128)} %collective-permute-done.6, f32[2,192,384]{2,1,0:T(8,128)} %copy-done.4, s32[]{:T(128)S(6)} %select_n.431), kind=kLoop, calls=%fused_computation.35 | loop fusion | flops 73728 | bytes 884740 | tf_op jit(solution)/shard_map/reshape | solution.py:64
  113.6 1.5 %collective-permute-start.7 = (f32[192,384]{1,0:T(8,128)}, f32[192,384]{1,0:T(8,128)}, u32[]{:S(2)}, u32[]{:S(2)}) collective-permute-start(f32[192,384]{1,0:T(8,128)} %add_bitcast_fusion.1), channel_id=1, source_target_pairs={{0,1},{1,0},{2,3},{3,2},{4,5},{5,4},{6,7},{7,6},{8,9},{9,8},{10,11... | collective-permute-start | bytes 884744 | tf_op jit(solution)/shard_map/ppermute | solution.py:72
  119.9 2.5 %collective-permute-done.7 = f32[192,384]{1,0:T(8,128)} collective-permute-done((f32[192,384]{1,0:T(8,128)}, f32[192,384]{1,0:T(8,128)}, u32[]{:S(2)}, u32[]{:S(2)}) %collective-permute-start.7) | collective-permute-done | bytes 294944 | tf_op jit(solution)/shard_map/ppermute | solution.py:72
  123.5 1.6 %collective-permute-start.8 = (f32[192,384]{1,0:T(8,128)S(1)}, f32[192,384]{1,0:T(8,128)S(1)}, u32[]{:S(2)}, u32[]{:S(2)}) collective-permute-start(f32[192,384]{1,0:T(8,128)S(1)} %add.313), channel_id=1, source_target_pairs={{0,2},{1,3},{2,0},{3,1},{4,6},{5,7},{6,4},{7,5},{8,10},{9,11},{10,... | collective-permute-start | bytes 884744 | tf_op jit(solution)/shard_map/ppermute | solution.py:72
  126.7 1.4 %fusion.65 = f32[1024,192]{0,1:T(8,128)} fusion(bf16[512,1024]{0,1:T(8,128)(2,1)S(1)} %bitcast.80, bf16[512,192]{1,0:T(8,128)(2,1)S(1)} %bitcast.86), kind=kOutput, calls=%fused_computation.175 | convolution fusion | flops 201326592 | bytes 2031616 | tf_op jit(solution)/shard_map/dot_general | solution.py:147
  128.0 3.2 %collective-permute-done.8 = f32[192,384]{1,0:T(8,128)S(1)} collective-permute-done((f32[192,384]{1,0:T(8,128)S(1)}, f32[192,384]{1,0:T(8,128)S(1)}, u32[]{:S(2)}, u32[]{:S(2)}) %collective-permute-start.8) | collective-permute-done | bytes 294944 | tf_op jit(solution)/shard_map/ppermute | solution.py:72
  (124 shorter events, 25.3 us)
Async XLA Ops:
  0.6 22.0 %copy-start = (bf16[1024,1536]{1,0:T(8,128)(2,1)S(1)}, bf16[1024,1536]{1,0:T(8,128)(2,1)}, u32[]{:S(2)}) copy-start(bf16[1024,1536]{1,0:T(8,128)(2,1)} %param.12) | copy-start | bytes 9437188
  0.7 4.5 %copy-start.15 = (s32[1600]{0:T(1024)}, s32[1600]{0:T(1024)S(1)}, u32[]{:S(2)}) copy-start(s32[1600]{0:T(1024)S(1)} %add_select_fusion.7) | copy-start | bytes 19204
  0.7 4.5 %copy-start.17 = (f32[1536]{0:T(1024)S(1)}, f32[1536]{0:T(1024)}, u32[]{:S(2)}) copy-start(f32[1536]{0:T(1024)} %param.11) | copy-start | bytes 18436
  0.7 4.5 %copy-start.18 = (f32[1536]{0:T(1024)S(1)}, f32[1536]{0:T(1024)}, u32[]{:S(2)}) copy-start(f32[1536]{0:T(1024)} %param.10) | copy-start | bytes 18436
  5.2 5.7 %copy-start.1 = (f32[1600,1536]{1,0:T(8,128)}, f32[1600,1536]{1,0:T(8,128)S(1)}, u32[]{:S(2)}) copy-start(f32[1600,1536]{1,0:T(8,128)S(1)} %fusion.64) | copy-start | bytes 29491204
  5.2 8.7 %copy-start.10 = (s32[64,64]{1,0:T(8,128)S(1)}, s32[64,64]{1,0:T(8,128)}, u32[]{:S(2)}) copy-start(s32[64,64]{1,0:T(8,128)} %param.14) | copy-start | bytes 49156
  5.3 9.4 %copy-start.16 = (s32[64]{0:T(128)S(1)}, s32[64]{0:T(128)}, u32[]{:S(2)}) copy-start(s32[64]{0:T(128)} %param.13) | copy-start | bytes 772
  10.9 6.9 %collective-permute-start = (bf16[1,16,1536]{2,1,0:T(8,128)(2,1)S(1)}, bf16[1,16,1536]{2,1,0:T(8,128)(2,1)S(1)}, u32[]{:S(2)}, u32[]{:S(2)}) collective-permute-start(bf16[1,16,1536]{2,1,0:T(8,128)(2,1)S(1)} %fusion.15), channel_id=1, source_target_pairs={{0,1},{1,0},{2,3},{3,2},{4,5},{5,4},{6,7},{7,6},{8,9},{9,8},{10,11... | collective-permute-start | bytes 147464 | tf_op jit(solution)/shard_map/ppermute | solution.py:44
  17.9 4.7 %collective-permute-start.1 = (bf16[2,16,1536]{2,1,0:T(8,128)(2,1)S(1)}, bf16[2,16,1536]{2,1,0:T(8,128)(2,1)S(1)}, u32[]{:S(2)}, u32[]{:S(2)}) collective-permute-start(bf16[2,16,1536]{2,1,0:T(8,128)(2,1)S(1)} %maximum_select_fusion.1), channel_id=1, source_target_pairs={{0,2},{1,3},{2,0},{3,1},{4,6},{5,7},{6,4},{7,5},{8,10},{9,11},{10,... | collective-permute-start | bytes 294920 | tf_op jit(solution)/shard_map/ppermute | solution.py:44
  22.6 1.8 %copy-start.6 = (bf16[4,16,1536]{2,1,0:T(8,128)(2,1)}, bf16[4,16,1536]{2,1,0:T(8,128)(2,1)S(1)}, u32[]{:S(2)}) copy-start(bf16[4,16,1536]{2,1,0:T(8,128)(2,1)S(1)} %maximum_select_fusion) | copy-start | bytes 589828
  25.5 0.9 copy-start.8
  28.8 6.0 %collective-permute-start.2 = (f32[2,16,1536]{2,1,0:T(8,128)}, f32[2,16,1536]{2,1,0:T(8,128)}, u32[]{:S(2)}, u32[]{:S(2)}) collective-permute-start(f32[2,16,1536]{2,1,0:T(8,128)} %dynamic-slice_bitcast_fusion.2), channel_id=1, source_target_pairs={{0,1},{1,0},{2,3},{3,2},{4,5},{5,4},{6,7},{7,6},{8,9},{9,8},{10,11... | collective-permute-start | bytes 589832 | tf_op jit(solution)/shard_map/ppermute | solution.py:61
  36.4 4.7 %collective-permute-start.3 = (f32[1,16,1536]{2,1,0:T(8,128)S(1)}, f32[1,16,1536]{2,1,0:T(8,128)S(1)}, u32[]{:S(2)}, u32[]{:S(2)}) collective-permute-start(f32[1,16,1536]{2,1,0:T(8,128)S(1)} %constant_dynamic-slice_fusion.5), channel_id=1, source_target_pairs={{0,2},{1,3},{2,0},{3,1},{4,6},{5,7},{6,4},{7,5},{8,10},{9,11},{10,... | collective-permute-start | bytes 294920 | tf_op jit(solution)/shard_map/ppermute | solution.py:61
  38.0 14.0 %copy-start.5 = (bf16[1600,384]{1,0:T(8,128)(2,1)S(1)}, bf16[1600,384]{1,0:T(8,128)(2,1)}, u32[]{:S(2)}) copy-start(bf16[1600,384]{1,0:T(8,128)(2,1)} %param.8) | copy-start | bytes 3686404
  38.0 14.0 %copy-start.19 = (f32[1536]{0:T(1024)S(1)}, f32[1536]{0:T(1024)}, u32[]{:S(2)}) copy-start(f32[1536]{0:T(1024)} %param.10) | copy-start | bytes 18436
  52.0 5.7 %copy-start.14 = (s32[64]{0:T(128)S(1)}, s32[64]{0:T(128)}, u32[]{:S(2)}) copy-start(s32[64]{0:T(128)} %copy-done.13) | copy-start | bytes 772
  52.0 5.7 %copy-start.12 = (s32[64]{0:T(128)S(1)}, s32[64]{0:T(128)}, u32[]{:S(2)}) copy-start(s32[64]{0:T(128)} %copy-done.11) | copy-start | bytes 772
  55.1 1.4 %copy-start.3 = (f32[1536,384]{1,0:T(8,128)}, f32[1536,384]{1,0:T(8,128)S(1)}, u32[]{:S(2)}) copy-start(f32[1536,384]{1,0:T(8,128)S(1)} %fusion.2) | copy-start | bytes 7077892
  55.1 13.9 %copy-start.9 = (bf16[64,64]{1,0:T(8,128)(2,1)S(1)}, bf16[64,64]{1,0:T(8,128)(2,1)}, u32[]{:S(2)}) copy-start(bf16[64,64]{1,0:T(8,128)(2,1)} %copy-done.8) | copy-start | bytes 24580
  57.6 4.5 %collective-permute-start.4 = (f32[4,192,384]{2,1,0:T(8,128)}, f32[4,192,384]{2,1,0:T(8,128)}, u32[]{:S(2)}, u32[]{:S(2)}) collective-permute-start(f32[4,192,384]{2,1,0:T(8,128)} %dynamic-slice_bitcast_fusion), channel_id=1, source_target_pairs={{0,4},{4,0},{8,12},{12,8},{16,20},{20,16},{24,28},{28,24},{1,5},{5... | collective-permute-start | bytes 3538952 | tf_op jit(solution)/shard_map/ppermute | solution.py:61
  58.0 2.5 %collective-permute-start.9 = (f32[4,192,2]{1,0,2:T(4,128)S(1)}, f32[4,192,2]{1,0,2:T(4,128)S(1)}, u32[]{:S(2)}, u32[]{:S(2)}) collective-permute-start(f32[4,192,2]{1,0,2:T(4,128)S(1)} %bitcast.94), channel_id=1, source_target_pairs={{0,4},{4,0},{8,12},{12,8},{16,20},{20,16},{24,28},{28,24},{1,5},{5... | collective-permute-start | bytes 18440 | tf_op jit(solution)/shard_map/ppermute | solution.py:61
  60.5 5.7 %collective-permute-start.10 = (f32[2,192,2]{1,2,0:T(2,128)S(1)}, f32[2,192,2]{1,2,0:T(2,128)S(1)}, u32[]{:S(2)}, u32[]{:S(2)}) collective-permute-start(f32[2,192,2]{1,2,0:T(2,128)S(1)} %dynamic-slice_bitcast_fusion.3), channel_id=1, source_target_pairs={{0,8},{4,12},{8,0},{12,4},{16,24},{20,28},{24,16},{28,20},{1,9},{5... | collective-permute-start | bytes 9224 | tf_op jit(solution)/shard_map/ppermute | solution.py:61
  63.9 1.0 copy-start.2
  65.8 22.3 %collective-permute-start.5 = (f32[2,192,384]{2,1,0:T(8,128)}, f32[2,192,384]{2,1,0:T(8,128)}, u32[]{:S(2)}, u32[]{:S(2)}) collective-permute-start(f32[2,192,384]{2,1,0:T(8,128)} %dynamic-slice_bitcast_fusion.1), channel_id=1, source_target_pairs={{0,8},{4,12},{8,0},{12,4},{16,24},{20,28},{24,16},{28,20},{1,9},{5... | collective-permute-start | bytes 1769480 | tf_op jit(solution)/shard_map/ppermute | solution.py:61
  66.3 13.0 %collective-permute-start.11 = (f32[1,192,2]{1,2,0:T(2,128)S(1)}, f32[1,192,2]{1,2,0:T(2,128)S(1)}, u32[]{:S(2)}, u32[]{:S(2)}) collective-permute-start(f32[1,192,2]{1,2,0:T(2,128)S(1)} %constant_dynamic-slice_fusion), channel_id=1, source_target_pairs={{0,16},{4,20},{8,24},{12,28},{16,0},{20,4},{24,8},{28,12},{1,17},{... | collective-permute-start | bytes 4616 | tf_op jit(solution)/shard_map/ppermute | solution.py:61
  79.3 7.2 %collective-permute-start.12 = (f32[192,2]{0,1:T(2,128)S(1)}, f32[192,2]{0,1:T(2,128)S(1)}, u32[]{:S(2)}, u32[]{:S(2)}) collective-permute-start(f32[192,2]{0,1:T(2,128)S(1)} %fusion.57), channel_id=1, source_target_pairs={{0,1},{1,0},{2,3},{3,2},{4,5},{5,4},{6,7},{7,6},{8,9},{9,8},{10,11... | collective-permute-start | bytes 4616 | tf_op jit(solution)/shard_map/ppermute | solution.py:72
  80.7 25.2 %all-to-all-start = ((bf16[8,64,322]{2,1,0:T(8,128)(2,1)}), bf16[8,64,322]{2,1,0:T(8,128)(2,1)}, u32[]{:S(2)}, u32[]{:S(2)}) async-start(bf16[8,64,322]{2,1,0:T(8,128)(2,1)} %pad_maximum_fusion), calls=%async_computation | async-start | bytes 786432 | tf_op jit(solution)/shard_map/all_to_all | solution.py:139
  86.5 7.4 %collective-permute-start.13 = (f32[192,2]{0,1:T(2,128)S(1)}, f32[192,2]{0,1:T(2,128)S(1)}, u32[]{:S(2)}, u32[]{:S(2)}) collective-permute-start(f32[192,2]{0,1:T(2,128)S(1)} %add.318), channel_id=1, source_target_pairs={{0,2},{1,3},{2,0},{3,1},{4,6},{5,7},{6,4},{7,5},{8,10},{9,11},{10,... | collective-permute-start | bytes 4616 | tf_op jit(solution)/shard_map/ppermute | solution.py:72
  89.4 0.8 copy-start.4
  90.9 20.8 %collective-permute-start.6 = (f32[1,192,384]{2,1,0:T(8,128)}, f32[1,192,384]{2,1,0:T(8,128)}, u32[]{:S(2)}, u32[]{:S(2)}) collective-permute-start(f32[1,192,384]{2,1,0:T(8,128)} %constant_dynamic-slice_fusion.4), channel_id=1, source_target_pairs={{0,16},{4,20},{8,24},{12,28},{16,0},{20,4},{24,8},{28,12},{1,17},{... | collective-permute-start | bytes 884744 | tf_op jit(solution)/shard_map/ppermute | solution.py:61
  113.6 8.9 %collective-permute-start.7 = (f32[192,384]{1,0:T(8,128)}, f32[192,384]{1,0:T(8,128)}, u32[]{:S(2)}, u32[]{:S(2)}) collective-permute-start(f32[192,384]{1,0:T(8,128)} %add_bitcast_fusion.1), channel_id=1, source_target_pairs={{0,1},{1,0},{2,3},{3,2},{4,5},{5,4},{6,7},{7,6},{8,9},{9,8},{10,11... | collective-permute-start | bytes 884744 | tf_op jit(solution)/shard_map/ppermute | solution.py:72
  123.5 7.7 %collective-permute-start.8 = (f32[192,384]{1,0:T(8,128)S(1)}, f32[192,384]{1,0:T(8,128)S(1)}, u32[]{:S(2)}, u32[]{:S(2)}) collective-permute-start(f32[192,384]{1,0:T(8,128)S(1)} %add.313), channel_id=1, source_target_pairs={{0,2},{1,3},{2,0},{3,1},{4,6},{5,7},{6,4},{7,5},{8,10},{9,11},{10,... | collective-permute-start | bytes 884744 | tf_op jit(solution)/shard_map/ppermute | solution.py:72
  (3 other events, 1.7 us)

commit v3 on v2

--- a/solution.py
+++ b/solution.py
@@ -6,7 +6,6 @@
 P_SIZE = 100
 SUB_SIZE = 64
 KPOS = 16
-HIGHEST = lax.Precision.HIGHEST
 
 
 def block_table(pos_vec, pos_blk, neg_vec, neg_blk, blocks):
@@ -29,6 +28,14 @@
     column = jnp.arange(SUB_SIZE, dtype=jnp.int32)[None, None, :]
     hit = ((ids % SUB_SIZE)[:, :, None] == column) & valid[:, :, None]
     return jnp.any(hit, axis=1)
+
+
+def split3(x):
+    hi = x.astype(jnp.bfloat16)
+    rest = x - hi.astype(jnp.float32)
+    mid = rest.astype(jnp.bfloat16)
+    lo = (rest - mid.astype(jnp.float32)).astype(jnp.bfloat16)
+    return hi, mid, lo
 
 
 def partners(size, bit):
@@ -87,13 +94,17 @@
     select = (
         jnp.arange(rows, dtype=jnp.int32)[None, :] // P_SIZE
         == jnp.arange(images_here, dtype=jnp.int32)[:, None]
-    ).astype(jnp.float32)
+    ).astype(jnp.bfloat16)
 
     linear_scores = jnp.dot(features, head_weight, preferred_element_type=jnp.float32)
     shifted = gain * linear_scores + shift
     sig = jax.nn.sigmoid(shifted)
     active = shifted * sig
-    image_sum = jnp.dot(select, active, precision=HIGHEST, preferred_element_type=jnp.float32)
+    image_sum = jnp.dot(
+        jnp.concatenate([select] * 3, axis=1),
+        jnp.concatenate(split3(active), axis=0),
+        preferred_element_type=jnp.float32,
+    )
     embedded = (image_sum / P_SIZE).astype(jnp.bfloat16)
     grouped = doubling_gather(embedded, "leaf")
     group = grouped.shape[0]
@@ -137,6 +148,7 @@
         [column_chunks, jnp.broadcast_to(compact[None], (n_dp,) + compact.shape)], axis=2
     )
     recv = lax.all_to_all(send, "dp", split_axis=0, concat_axis=0, tiled=True)
+    recv, emb_grad = lax.optimization_barrier((recv, emb_grad))
     columns = recv[:, :, :col_width].reshape(n_dp * group, col_width)
     info = recv[:, :, col_width:].reshape(n_dp * group, compact.shape[1])
     all_pos = info[:, :SUB_SIZE]
@@ -148,7 +160,11 @@
         all_table, columns, (((0,), (0,)), ((), ())), preferred_element_type=jnp.float32
     )
 
-    spread = jnp.dot(select.T, emb_grad / P_SIZE, precision=HIGHEST, preferred_element_type=jnp.float32)
+    spread = jnp.dot(
+        jnp.concatenate([select.T] * 3, axis=1),
+        jnp.concatenate(split3(emb_grad / P_SIZE), axis=0),
+        preferred_element_type=jnp.float32,
+    )
     pixel_gradient = spread * (sig * (1.0 + shifted * (1.0 - sig)))
     lin_grad = (pixel_gradient * gain).astype(jnp.bfloat16)
     head_term = lax.dot_general(

time: 132 us -> 134 us (1.015)
  other arithmetic: 13.2 us -> 18.3 us
  starting transfers between devices: 25.5 us -> 20.8 us
  local copies, waits for them, and re-layouts: 18.9 us -> 22.9 us
  waiting for transfers between devices: 44.1 us -> 40.7 us
    all_to_all x1, waiting for transfers between devices: 11.5 us -> 3.06 us  [shards(): recv = lax.all_to_all(send, 'dp', split_axis=0, concat_axis=0, tiled=True)]
    ppermute x4, waiting for transfers between devices: 5.71 us -> 10.6 us  [butterfly_sum(): got = lax.ppermute(cur, name, partners(size, bit))]
    dot_general x2, matrix products: 16.5 us -> 11.7 us  [the longest x1 9.02 us: shards(): jnp.dot(jnp.concatenate([select.T] * 3, axis=1), jnp.concatenate(split3(e...]
    dot_general x1, matrix products: 4.5 us -> 8.63 us  [shards(): jnp.dot(features, head_weight, preferred_element_type=jnp.float32)]
    ppermute x8, starting transfers between devices: 9.96 us -> 6.7 us  [halving_scatter(): got = lax.ppermute(tuple(give), name, partners(size, bit))]
    another operation x2, local copies, waits for them, and re-layouts: 0.9 us -> 2.54 us  [block_table(): neg_wide = jnp.tile(neg_vec, (1, blocks))]
    dot_general x1, matrix products: 1.81 us -> 3.35 us  [shards(): lax.dot_general(grouped, node_weights, (((1,), (1,)), ((), ())), preferre...]
    unnamed x47 -> x39, local copies, waits for them, and re-layouts: 7.58 us -> 9.01 us
  transfers between devices with their start and end apart: 15 -> 15, of which waited for: 9 -> 9; matrix products, arithmetic and copies ran while one was open for 16% -> 18% of each run, Pallas kernels for 0% -> 0%
where the time goes in v3:
time: 134 us
  waiting for transfers between devices  40.7 us (30%)
  matrix products  29.8 us (22%)
  local copies, waits for them, and re-layouts  22.9 us (17%)
  starting transfers between devices  20.8 us (16%)
  other arithmetic  18.3 us (14%)
    ppermute x8, waiting for transfers between devices, halving_scatter(): got = lax.ppermute(tuple(give), name, partners(size, bit))  24.5 us
    ppermute x4, waiting for transfers between devices, butterfly_sum(): got = lax.ppermute(cur, name, partners(size, bit))  10.6 us
    dot_general x1, matrix products, shards(): jnp.dot(jnp.concatenate([select.T] * 3, axis=1), jnp.concatenate(split3(e...  9.02 us
    unnamed x39, local copies, waits for them, and re-layouts  9.01 us
    dot_general x1, matrix products, shards(): jnp.dot(features, head_weight, preferred_element_type=jnp.float32)  8.63 us
    ppermute x8, starting transfers between devices, halving_scatter(): got = lax.ppermute(tuple(give), name, partners(size, bit))  6.7 us
    all_to_all x1, starting transfers between devices, shards(): recv = lax.all_to_all(send, 'dp', split_axis=0, concat_axis=0, tiled=True)  5.38 us
    add x5, other arithmetic, halving_scatter(): cur = [k + g for k, g in zip(keep, got)]  4.81 us
  transfers between devices with their start and end apart: 15, of which 9 were waited for; matrix products, arithmetic and copies ran while one was open for 18% of the time, Pallas kernels for 0%

profile of v3, /device:TPU:0, one launch (start us, length us, event | category | flops | bytes accessed | tf_op | source)
XLA Modules:
  0.0 133.6 jit_solution(12485708680702086132)
XLA Ops:
  1.4 8.6 %fusion.68 = (bf16[1600,1536]{1,0:T(8,128)(2,1)S(1)}, bf16[1600,1536]{1,0:T(8,128)(2,1)S(1)}, bf16[1600,1536]{1,0:T(8,128)(2,1)S(1)}, f32[1600,1536]{1,0:T(8,128)}) fusion(f32[1536]{0:T(1024)} %param.11, f32[1536]{0:T(1024)} %param.10, bf16[1600,384]{1,0:T(8,128)(2,1)} %param.8, bf16[384,1536]{1,0:T(8,128)(2,1)} %param.9), kind=kOutput, calls=%fused_computation.185 | convolution fusion | flops 1919385600 | bytes 26996736 | tf_op jit(solution)/shard_map/dot_general | solution.py:99
  10.0 2.7 %fusion.18 = bf16[1,16,1536]{2,1,0:T(8,128)(2,1)S(1)} fusion(pred[16,4800]{1,0:T(8,128)(4,1)S(1)} %concatenate.39, bf16[1600,1536]{1,0:T(8,128)(2,1)S(1)} %get-tuple-element.20, bf16[1600,1536]{1,0:T(8,128)(2,1)S(1)} %get-tuple-element.19, bf16[1600,1536]{1,0:T(8,128)(2,1)S(1)} %get-tuple-element.18), kind=kOutput, calls=%fused_computation.22 | convolution fusion | flops 280215552 | bytes 14871552 | tf_op jit(solution)/shard_map/dot_general | solution.py:103
  12.7 3.0 %collective-permute-start = (bf16[1,16,1536]{2,1,0:T(8,128)(2,1)S(1)}, bf16[1,16,1536]{2,1,0:T(8,128)(2,1)S(1)}, u32[]{:S(2)}, u32[]{:S(2)}) collective-permute-start(bf16[1,16,1536]{2,1,0:T(8,128)(2,1)S(1)} %fusion.18), channel_id=1, source_target_pairs={{0,1},{1,0},{2,3},{3,2},{4,5},{5,4},{6,7},{7,6},{8,9},{9,8},{10,11... | collective-permute-start | bytes 147464 | tf_op jit(solution)/shard_map/ppermute | solution.py:51
  17.9 1.7 %fusion.22 = pred[64,64]{1,0:T(8,128)(4,1)} fusion(s32[64,48]{1,0:T(8,128)S(1)} %copy.67, pred[64,48]{1,0:T(8,128)(4,1)S(1)} %copy.68), kind=kLoop, calls=%fused_computation.27 | loop fusion | flops 585728 | bytes 19456 | tf_op jit(solution)/shard_map/reduce_or | solution.py:30
  21.3 1.6 %collective-permute-start.1 = (bf16[2,16,1536]{2,1,0:T(8,128)(2,1)S(1)}, bf16[2,16,1536]{2,1,0:T(8,128)(2,1)S(1)}, u32[]{:S(2)}, u32[]{:S(2)}) collective-permute-start(bf16[2,16,1536]{2,1,0:T(8,128)(2,1)S(1)} %maximum_select_fusion.1), channel_id=1, source_target_pairs={{0,2},{1,3},{2,0},{3,1},{4,6},{5,7},{6,4},{7,5},{8,10},{9,11},{10,... | collective-permute-start | bytes 294920 | tf_op jit(solution)/shard_map/ppermute | solution.py:51
  23.5 2.5 %collective-permute-done.1 = bf16[2,16,1536]{2,1,0:T(8,128)(2,1)S(1)} collective-permute-done((bf16[2,16,1536]{2,1,0:T(8,128)(2,1)S(1)}, bf16[2,16,1536]{2,1,0:T(8,128)(2,1)S(1)}, u32[]{:S(2)}, u32[]{:S(2)}) %collective-permute-start.1) | collective-permute-done | bytes 98336 | tf_op jit(solution)/shard_map/ppermute | solution.py:51
  26.7 1.2 select_n.399
  27.9 3.4 %select_reduce_fusion.1 = (f32[64,64]{1,0:T(8,128)S(1)}, f32[64,64]{1,0:T(8,128)}) fusion(pred[64,16]{0,1:T(8,128)(4,1)S(1)} %iota_compare_fusion.7, pred[64,16]{0,1:T(8,128)(4,1)S(1)} %iota_compare_fusion.6, bf16[64,1536,1]{1,0,2:T(8,128)(2,1)} %bitcast.85, bf16[16,64,1536]{2,1,0:T(8,128)(2,1)S(1)} %bitcast.75), kind=kOutput, calls=%fused_computation.34 | convolution fusion | flops 201580544 | bytes 3377152 | tf_op jit(solution)/shard_map/dot_general | solution.py:123
  32.1 1.1 tile.13
  35.4 1.8 %tile.15 = bf16[2,2,16,1024]{3,2,1,0:T(8,128)(2,1)} reshape(bf16[64,16,64]{2,1,0:T(8,128)(2,1)} %tile.14) | data formatting | bytes 262144 | tf_op jit(solution)/shard_map/tile | solution.py:14
  37.2 1.6 %fusion.10 = f32[2,2,16,1536]{3,2,1,0:T(8,128)S(1)} fusion(bf16[1024,1536]{1,0:T(8,128)(2,1)S(1)} %copy-done, bf16[2,2,16,1024]{3,2,1,0:T(8,128)(2,1)S(1)} %tile.13, bf16[2,2,16,1024]{3,2,1,0:T(8,128)(2,1)} %tile.15, s32[2,2,16]{2,1,0:T(2,128)} %get-tuple-element.36, s32[2,2,16]{2,1,0:T(2,128)} %get-tuple-element.37, s32[1024]{0:T(1024)} %add_select_fusion.8), kind=kOutput, calls=%fused_computation.18 | convolution fusion | flops 201654272 | bytes 3805696 | tf_op jit(solution)/shard_map/dot_general | solution.py:133
  41.4 5.4 %all-to-all-start = ((bf16[8,64,322]{2,1,0:T(8,128)(2,1)}), bf16[8,64,322]{2,1,0:T(8,128)(2,1)S(1)}, u32[]{:S(2)}, u32[]{:S(2)}) async-start(bf16[8,64,322]{2,1,0:T(8,128)(2,1)} %pad_maximum_fusion), calls=%async_computation | async-start | bytes 786432 | tf_op jit(solution)/shard_map/all_to_all | solution.py:150
  49.2 1.5 %collective-permute-start.3 = (f32[1,16,1536]{2,1,0:T(8,128)}, f32[1,16,1536]{2,1,0:T(8,128)}, u32[]{:S(2)}, u32[]{:S(2)}) collective-permute-start(f32[1,16,1536]{2,1,0:T(8,128)} %constant_dynamic-slice_fusion.5), channel_id=1, source_target_pairs={{0,2},{1,3},{2,0},{3,1},{4,6},{5,7},{6,4},{7,5},{8,10},{9,11},{10,... | collective-permute-start | bytes 294920 | tf_op jit(solution)/shard_map/ppermute | solution.py:68
  50.7 1.3 iota_compare_fusion.3
  52.0 2.7 %collective-permute-done.3 = f32[1,16,1536]{2,1,0:T(8,128)} collective-permute-done((f32[1,16,1536]{2,1,0:T(8,128)}, f32[1,16,1536]{2,1,0:T(8,128)}, u32[]{:S(2)}, u32[]{:S(2)}) %collective-permute-start.3) | collective-permute-done | bytes 98336 | tf_op jit(solution)/shard_map/ppermute | solution.py:68
  54.7 1.6 %add_bitcast_fusion.2 = f32[16,1536]{1,0:T(8,128)} fusion(f32[1,16,1536]{2,1,0:T(8,128)} %collective-permute-done.3, f32[2,16,1536]{2,1,0:T(8,128)} %copy-done.5, s32[]{:T(128)S(6)} %select_n.435), kind=kLoop, calls=%fused_computation.68 | loop fusion | flops 24576 | bytes 294916 | tf_op jit(solution)/shard_map/reshape | solution.py:71
  56.3 3.1 %all-to-all-done = bf16[8,64,322]{2,1,0:T(8,128)(2,1)S(1)} async-done(((bf16[8,64,322]{2,1,0:T(8,128)(2,1)}), bf16[8,64,322]{2,1,0:T(8,128)(2,1)S(1)}, u32[]{:S(2)}, u32[]{:S(2)}) %all-to-all-start) | async-done | bytes 329760 | tf_op jit(solution)/shard_map/all_to_all | solution.py:150
  60.4 9.0 %fusion.69 = (f32[1536]{0:T(1024)S(1)}, f32[1536]{0:T(1024)}, f32[1600,1536]{1,0:T(8,128)S(1)}) fusion(f32[1600,1536]{1,0:T(8,128)} %get-tuple-element.34, f32[1536]{0:T(1024)} %param.11, f32[1536]{0:T(1024)} %param.10, bf16[16,1536]{1,0:T(8,128)(2,1)S(1)} %get-tuple-element.26, bf16[16,1536]{1,0:T(8,128)(2,1)S(1)} %get-tuple-element.27, ...), kind=kOutput, calls=%fused_computation.186 | convolution fusion | flops 268471296 | bytes 19858432 | tf_op jit(solution)/shard_map/dot_general | solution.py:163
  69.4 3.1 %fusion.8 = f32[1536,384]{1,0:T(8,128)S(1)} fusion(bf16[1600,384]{1,0:T(8,128)(2,1)S(1)} %copy-done.14, f32[1600,1536]{1,0:T(8,128)S(1)} %get-tuple-element.35, f32[1536]{0:T(1024)S(1)} %copy-done.15), kind=kOutput, calls=%fused_computation.16 | convolution fusion | flops 1892352000 | bytes 13424640 | tf_op jit(solution)/shard_map/dot_general | solution.py:170
  72.5 1.4 %copy-done.2 = f32[1536,384]{1,0:T(8,128)} copy-done((f32[1536,384]{1,0:T(8,128)}, f32[1536,384]{1,0:T(8,128)S(1)}, u32[]{:S(2)}) %copy-start.2) | copy-done | bytes 2359320
  73.9 1.1 dynamic-slice_bitcast_fusion
  78.2 1.7 %bitcast_add_fusion = f32[4,192,384]{2,1,0:T(8,128)S(1)} fusion(f32[4,192,384]{2,1,0:T(8,128)} %collective-permute-done.4, f32[4,2,192,384]{3,2,1,0:T(8,128)} %bitcast.82, s32[]{:T(128)S(6)} %select_n.438), kind=kLoop, calls=%fused_computation.28 | loop fusion | flops 294912 | bytes 3538948 | tf_op jit(solution)/shard_map/add | solution.py:69
  87.3 2.0 %collective-permute-start.10 = (f32[2,192,2]{1,2,0:T(2,128)S(1)}, f32[2,192,2]{1,2,0:T(2,128)S(1)}, u32[]{:S(2)}, u32[]{:S(2)}) collective-permute-start(f32[2,192,2]{1,2,0:T(2,128)S(1)} %dynamic-slice_bitcast_fusion.3), channel_id=1, source_target_pairs={{0,8},{4,12},{8,0},{12,4},{16,24},{20,28},{24,16},{28,20},{1,9},{5... | collective-permute-start | bytes 9224 | tf_op jit(solution)/shard_map/ppermute | solution.py:68
  89.2 8.4 %collective-permute-done.5 = f32[2,192,384]{2,1,0:T(8,128)} collective-permute-done((f32[2,192,384]{2,1,0:T(8,128)}, f32[2,192,384]{2,1,0:T(8,128)}, u32[]{:S(2)}, u32[]{:S(2)}) %collective-permute-start.5) | collective-permute-done | bytes 589856 | tf_op jit(solution)/shard_map/ppermute | solution.py:68
  97.6 1.3 bitcast_add_fusion.1
  99.1 2.9 %collective-permute-start.11 = (f32[1,192,2]{1,2,0:T(2,128)S(1)}, f32[1,192,2]{1,2,0:T(2,128)S(1)}, u32[]{:S(2)}, u32[]{:S(2)}) collective-permute-start(f32[1,192,2]{1,2,0:T(2,128)S(1)} %constant_dynamic-slice_fusion), channel_id=1, source_target_pairs={{0,16},{4,20},{8,24},{12,28},{16,0},{20,4},{24,8},{28,12},{1,17},{... | collective-permute-start | bytes 4616 | tf_op jit(solution)/shard_map/ppermute | solution.py:68
  102.0 12.5 %collective-permute-done.6 = f32[1,192,384]{2,1,0:T(8,128)S(1)} collective-permute-done((f32[1,192,384]{2,1,0:T(8,128)S(1)}, f32[1,192,384]{2,1,0:T(8,128)S(1)}, u32[]{:S(2)}, u32[]{:S(2)}) %collective-permute-start.6) | collective-permute-done | bytes 294944 | tf_op jit(solution)/shard_map/ppermute | solution.py:68
  114.5 1.6 %collective-permute-start.7 = (f32[192,384]{1,0:T(8,128)S(1)}, f32[192,384]{1,0:T(8,128)S(1)}, u32[]{:S(2)}, u32[]{:S(2)}) collective-permute-start(f32[192,384]{1,0:T(8,128)S(1)} %add_bitcast_fusion.1), channel_id=1, source_target_pairs={{0,1},{1,0},{2,3},{3,2},{4,5},{5,4},{6,7},{7,6},{8,9},{9,8},{10,11... | collective-permute-start | bytes 884744 | tf_op jit(solution)/shard_map/ppermute | solution.py:79
  118.1 5.3 %collective-permute-done.12 = f32[192,2]{0,1:T(2,128)S(1)} collective-permute-done((f32[192,2]{0,1:T(2,128)S(1)}, f32[192,2]{0,1:T(2,128)S(1)}, u32[]{:S(2)}, u32[]{:S(2)}) %collective-permute-start.12) | collective-permute-done | bytes 1568 | tf_op jit(solution)/shard_map/ppermute | solution.py:79
  123.5 1.5 %collective-permute-start.13 = (f32[192,2]{0,1:T(2,128)S(1)}, f32[192,2]{0,1:T(2,128)S(1)}, u32[]{:S(2)}, u32[]{:S(2)}) collective-permute-start(f32[192,2]{0,1:T(2,128)S(1)} %add.320), channel_id=1, source_target_pairs={{0,2},{1,3},{2,0},{3,1},{4,6},{5,7},{6,4},{7,5},{8,10},{9,11},{10,... | collective-permute-start | bytes 4616 | tf_op jit(solution)/shard_map/ppermute | solution.py:79
  125.6 1.4 %fusion.72 = f32[1024,192]{0,1:T(8,128)} fusion(bf16[512,1024]{0,1:T(8,128)(2,1)S(1)} %bitcast.78, bf16[512,192]{1,0:T(8,128)(2,1)S(1)} %bitcast.84), kind=kOutput, calls=%fused_computation.189 | convolution fusion | flops 201326592 | bytes 2031616 | tf_op jit(solution)/shard_map/dot_general | solution.py:159
  127.6 5.2 %collective-permute-done.8 = f32[192,384]{1,0:T(8,128)S(1)} collective-permute-done((f32[192,384]{1,0:T(8,128)S(1)}, f32[192,384]{1,0:T(8,128)S(1)}, u32[]{:S(2)}, u32[]{:S(2)}) %collective-permute-start.8) | collective-permute-done | bytes 294944 | tf_op jit(solution)/shard_map/ppermute | solution.py:79
  (121 shorter events, 29.4 us)
Async XLA Ops:
  0.6 27.2 %copy-start = (bf16[1024,1536]{1,0:T(8,128)(2,1)S(1)}, bf16[1024,1536]{1,0:T(8,128)(2,1)}, u32[]{:S(2)}) copy-start(bf16[1024,1536]{1,0:T(8,128)(2,1)} %param.12) | copy-start | bytes 9437188
  0.7 0.6 copy-start.8
  10.0 5.7 %copy-start.11 = (s32[64,64]{1,0:T(8,128)S(1)}, s32[64,64]{1,0:T(8,128)}, u32[]{:S(2)}) copy-start(s32[64,64]{1,0:T(8,128)} %param.14) | copy-start | bytes 49156
  10.0 6.4 %copy-start.13 = (s32[64]{0:T(128)S(1)}, s32[64]{0:T(128)}, u32[]{:S(2)}) copy-start(s32[64]{0:T(128)} %param.13) | copy-start | bytes 772
  12.7 8.6 %collective-permute-start = (bf16[1,16,1536]{2,1,0:T(8,128)(2,1)S(1)}, bf16[1,16,1536]{2,1,0:T(8,128)(2,1)S(1)}, u32[]{:S(2)}, u32[]{:S(2)}) collective-permute-start(bf16[1,16,1536]{2,1,0:T(8,128)(2,1)S(1)} %fusion.18), channel_id=1, source_target_pairs={{0,1},{1,0},{2,3},{3,2},{4,5},{5,4},{6,7},{7,6},{8,9},{9,8},{10,11... | collective-permute-start | bytes 147464 | tf_op jit(solution)/shard_map/ppermute | solution.py:51
  21.3 4.7 %collective-permute-start.1 = (bf16[2,16,1536]{2,1,0:T(8,128)(2,1)S(1)}, bf16[2,16,1536]{2,1,0:T(8,128)(2,1)S(1)}, u32[]{:S(2)}, u32[]{:S(2)}) collective-permute-start(bf16[2,16,1536]{2,1,0:T(8,128)(2,1)S(1)} %maximum_select_fusion.1), channel_id=1, source_target_pairs={{0,2},{1,3},{2,0},{3,1},{4,6},{5,7},{6,4},{7,5},{8,10},{9,11},{10,... | collective-permute-start | bytes 294920 | tf_op jit(solution)/shard_map/ppermute | solution.py:51
  34.1 0.6 copy-start.6
  37.2 3.2 %copy-start.7 = (bf16[64,64]{1,0:T(8,128)(2,1)S(1)}, bf16[64,64]{1,0:T(8,128)(2,1)}, u32[]{:S(2)}) copy-start(bf16[64,64]{1,0:T(8,128)(2,1)} %copy-done.6) | copy-start | bytes 24580
  37.2 3.2 %copy-start.9 = (bf16[64,1]{1,0:T(8,128)(2,1)S(1)}, bf16[64,1]{1,0:T(8,128)(2,1)}, u32[]{:S(2)}) copy-start(bf16[64,1]{1,0:T(8,128)(2,1)} %get-tuple-element.40) | copy-start | bytes 388
  37.2 3.2 %copy-start.10 = (bf16[64,1]{1,0:T(8,128)(2,1)S(1)}, bf16[64,1]{1,0:T(8,128)(2,1)}, u32[]{:S(2)}) copy-start(bf16[64,1]{1,0:T(8,128)(2,1)} %get-tuple-element.41) | copy-start | bytes 388
  38.9 0.8 copy-start.4
  40.3 6.5 %collective-permute-start.2 = (f32[2,16,1536]{2,1,0:T(8,128)}, f32[2,16,1536]{2,1,0:T(8,128)}, u32[]{:S(2)}, u32[]{:S(2)}) collective-permute-start(f32[2,16,1536]{2,1,0:T(8,128)} %dynamic-slice_bitcast_fusion.2), channel_id=1, source_target_pairs={{0,1},{1,0},{2,3},{3,2},{4,5},{5,4},{6,7},{7,6},{8,9},{9,8},{10,11... | collective-permute-start | bytes 589832 | tf_op jit(solution)/shard_map/ppermute | solution.py:68
  41.4 17.9 %all-to-all-start = ((bf16[8,64,322]{2,1,0:T(8,128)(2,1)}), bf16[8,64,322]{2,1,0:T(8,128)(2,1)S(1)}, u32[]{:S(2)}, u32[]{:S(2)}) async-start(bf16[8,64,322]{2,1,0:T(8,128)(2,1)} %pad_maximum_fusion), calls=%async_computation | async-start | bytes 786432 | tf_op jit(solution)/shard_map/all_to_all | solution.py:150
  47.9 0.7 copy-start.5
  49.2 5.5 %collective-permute-start.3 = (f32[1,16,1536]{2,1,0:T(8,128)}, f32[1,16,1536]{2,1,0:T(8,128)}, u32[]{:S(2)}, u32[]{:S(2)}) collective-permute-start(f32[1,16,1536]{2,1,0:T(8,128)} %constant_dynamic-slice_fusion.5), channel_id=1, source_target_pairs={{0,2},{1,3},{2,0},{3,1},{4,6},{5,7},{6,4},{7,5},{8,10},{9,11},{10,... | collective-permute-start | bytes 294920 | tf_op jit(solution)/shard_map/ppermute | solution.py:68
  59.4 10.0 %copy-start.3 = (bf16[8,64,322]{2,1,0:T(8,128)(2,1)}, bf16[8,64,322]{2,1,0:T(8,128)(2,1)S(1)}, u32[]{:S(2)}) copy-start(bf16[8,64,322]{2,1,0:T(8,128)(2,1)S(1)} %all-to-all-done) | copy-start | bytes 989188
  60.4 9.0 %copy-start.14 = (bf16[1600,384]{1,0:T(8,128)(2,1)S(1)}, bf16[1600,384]{1,0:T(8,128)(2,1)}, u32[]{:S(2)}) copy-start(bf16[1600,384]{1,0:T(8,128)(2,1)} %param.8) | copy-start | bytes 3686404
  60.4 9.0 %copy-start.15 = (f32[1536]{0:T(1024)S(1)}, f32[1536]{0:T(1024)}, u32[]{:S(2)}) copy-start(f32[1536]{0:T(1024)} %param.10) | copy-start | bytes 18436
  69.4 6.7 %copy-start.12 = (f32[1536]{0:T(1024)S(1)}, f32[1536]{0:T(1024)}, u32[]{:S(2)}) copy-start(f32[1536]{0:T(1024)} %get-tuple-element.9) | copy-start | bytes 18436
  72.5 1.4 %copy-start.2 = (f32[1536,384]{1,0:T(8,128)}, f32[1536,384]{1,0:T(8,128)S(1)}, u32[]{:S(2)}) copy-start(f32[1536,384]{1,0:T(8,128)S(1)} %fusion.8) | copy-start | bytes 7077892
  75.0 3.2 %collective-permute-start.4 = (f32[4,192,384]{2,1,0:T(8,128)}, f32[4,192,384]{2,1,0:T(8,128)}, u32[]{:S(2)}, u32[]{:S(2)}) collective-permute-start(f32[4,192,384]{2,1,0:T(8,128)} %dynamic-slice_bitcast_fusion), channel_id=1, source_target_pairs={{0,4},{4,0},{8,12},{12,8},{16,20},{20,16},{24,28},{28,24},{1,5},{5... | collective-permute-start | bytes 3538952 | tf_op jit(solution)/shard_map/ppermute | solution.py:68
  80.0 1.0 copy-start.1
  81.8 15.7 %collective-permute-start.5 = (f32[2,192,384]{2,1,0:T(8,128)}, f32[2,192,384]{2,1,0:T(8,128)}, u32[]{:S(2)}, u32[]{:S(2)}) collective-permute-start(f32[2,192,384]{2,1,0:T(8,128)} %dynamic-slice_bitcast_fusion.1), channel_id=1, source_target_pairs={{0,8},{4,12},{8,0},{12,4},{16,24},{20,28},{24,16},{28,20},{1,9},{5... | collective-permute-start | bytes 1769480 | tf_op jit(solution)/shard_map/ppermute | solution.py:68
  82.5 4.1 %collective-permute-start.9 = (f32[4,192,2]{1,0,2:T(4,128)}, f32[4,192,2]{1,0,2:T(4,128)}, u32[]{:S(2)}, u32[]{:S(2)}) collective-permute-start(f32[4,192,2]{1,0,2:T(4,128)} %bitcast.74), channel_id=1, source_target_pairs={{0,4},{4,0},{8,12},{12,8},{16,20},{20,16},{24,28},{28,24},{1,5},{5... | collective-permute-start | bytes 18440 | tf_op jit(solution)/shard_map/ppermute | solution.py:68
  87.3 11.8 %collective-permute-start.10 = (f32[2,192,2]{1,2,0:T(2,128)S(1)}, f32[2,192,2]{1,2,0:T(2,128)S(1)}, u32[]{:S(2)}, u32[]{:S(2)}) collective-permute-start(f32[2,192,2]{1,2,0:T(2,128)S(1)} %dynamic-slice_bitcast_fusion.3), channel_id=1, source_target_pairs={{0,8},{4,12},{8,0},{12,4},{16,24},{20,28},{24,16},{28,20},{1,9},{5... | collective-permute-start | bytes 9224 | tf_op jit(solution)/shard_map/ppermute | solution.py:68
  98.9 15.5 %collective-permute-start.6 = (f32[1,192,384]{2,1,0:T(8,128)S(1)}, f32[1,192,384]{2,1,0:T(8,128)S(1)}, u32[]{:S(2)}, u32[]{:S(2)}) collective-permute-start(f32[1,192,384]{2,1,0:T(8,128)S(1)} %constant_dynamic-slice_fusion.4), channel_id=1, source_target_pairs={{0,16},{4,20},{8,24},{12,28},{16,0},{20,4},{24,8},{28,12},{1,17},{... | collective-permute-start | bytes 884744 | tf_op jit(solution)/shard_map/ppermute | solution.py:68
  99.1 17.0 %collective-permute-start.11 = (f32[1,192,2]{1,2,0:T(2,128)S(1)}, f32[1,192,2]{1,2,0:T(2,128)S(1)}, u32[]{:S(2)}, u32[]{:S(2)}) collective-permute-start(f32[1,192,2]{1,2,0:T(2,128)S(1)} %constant_dynamic-slice_fusion), channel_id=1, source_target_pairs={{0,16},{4,20},{8,24},{12,28},{16,0},{20,4},{24,8},{28,12},{1,17},{... | collective-permute-start | bytes 4616 | tf_op jit(solution)/shard_map/ppermute | solution.py:68
  114.5 10.5 %collective-permute-start.7 = (f32[192,384]{1,0:T(8,128)S(1)}, f32[192,384]{1,0:T(8,128)S(1)}, u32[]{:S(2)}, u32[]{:S(2)}) collective-permute-start(f32[192,384]{1,0:T(8,128)S(1)} %add_bitcast_fusion.1), channel_id=1, source_target_pairs={{0,1},{1,0},{2,3},{3,2},{4,5},{5,4},{6,7},{7,6},{8,9},{9,8},{10,11... | collective-permute-start | bytes 884744 | tf_op jit(solution)/shard_map/ppermute | solution.py:79
  116.1 7.4 %collective-permute-start.12 = (f32[192,2]{0,1:T(2,128)S(1)}, f32[192,2]{0,1:T(2,128)S(1)}, u32[]{:S(2)}, u32[]{:S(2)}) collective-permute-start(f32[192,2]{0,1:T(2,128)S(1)} %fusion.63), channel_id=1, source_target_pairs={{0,1},{1,0},{2,3},{3,2},{4,5},{5,4},{6,7},{7,6},{8,9},{9,8},{10,11... | collective-permute-start | bytes 4616 | tf_op jit(solution)/shard_map/ppermute | solution.py:79
  123.5 3.6 %collective-permute-start.13 = (f32[192,2]{0,1:T(2,128)S(1)}, f32[192,2]{0,1:T(2,128)S(1)}, u32[]{:S(2)}, u32[]{:S(2)}) collective-permute-start(f32[192,2]{0,1:T(2,128)S(1)} %add.320), channel_id=1, source_target_pairs={{0,2},{1,3},{2,0},{3,1},{4,6},{5,7},{6,4},{7,5},{8,10},{9,11},{10,... | collective-permute-start | bytes 4616 | tf_op jit(solution)/shard_map/ppermute | solution.py:79
  125.0 7.8 %collective-permute-start.8 = (f32[192,384]{1,0:T(8,128)S(1)}, f32[192,384]{1,0:T(8,128)S(1)}, u32[]{:S(2)}, u32[]{:S(2)}) collective-permute-start(f32[192,384]{1,0:T(8,128)S(1)} %add.315), channel_id=1, source_target_pairs={{0,2},{1,3},{2,0},{3,1},{4,6},{5,7},{6,4},{7,5},{8,10},{9,11},{10,... | collective-permute-start | bytes 884744 | tf_op jit(solution)/shard_map/ppermute | solution.py:79

commit v4 on v3

--- a/solution.py
+++ b/solution.py
@@ -31,11 +31,11 @@
 
 
 def split3(x):
-    hi = x.astype(jnp.bfloat16)
-    rest = x - hi.astype(jnp.float32)
-    mid = rest.astype(jnp.bfloat16)
-    lo = (rest - mid.astype(jnp.float32)).astype(jnp.bfloat16)
-    return hi, mid, lo
+    hi = lax.reduce_precision(x, exponent_bits=8, mantissa_bits=7)
+    rest = x - hi
+    mid = lax.reduce_precision(rest, exponent_bits=8, mantissa_bits=7)
+    lo = rest - mid
+    return hi.astype(jnp.bfloat16), mid.astype(jnp.bfloat16), lo.astype(jnp.bfloat16)
 
 
 def partners(size, bit):

time: 134 us -> 135 us (level)
  no operation moved by 1% of the time
where the time goes in v4:
time: 135 us; the launch traced here: 134 us
  waiting for transfers between devices  40.7 us (30%)
  matrix products  30.4 us (23%)
  local copies, waits for them, and re-layouts  22.9 us (17%)
  starting transfers between devices  20.8 us (15%)
  other arithmetic  18.3 us (14%)
    ppermute x8, waiting for transfers between devices, halving_scatter(): got = lax.ppermute(tuple(give), name, partners(size, bit))  24.5 us
    ppermute x4, waiting for transfers between devices, butterfly_sum(): got = lax.ppermute(cur, name, partners(size, bit))  10.6 us
    dot_general x1, matrix products, shards(): jnp.dot(features, head_weight, preferred_element_type=jnp.float32)  9.24 us
    dot_general x1, matrix products, shards(): jnp.dot(jnp.concatenate([select.T] * 3, axis=1), jnp.concatenate(split3(e...  9.02 us
    unnamed x39, local copies, waits for them, and re-layouts  9.01 us
    ppermute x8, starting transfers between devices, halving_scatter(): got = lax.ppermute(tuple(give), name, partners(size, bit))  6.7 us
    all_to_all x1, starting transfers between devices, shards(): recv = lax.all_to_all(send, 'dp', split_axis=0, concat_axis=0, tiled=True)  5.37 us
    add x5, other arithmetic, halving_scatter(): cur = [k + g for k, g in zip(keep, got)]  4.81 us
  transfers between devices with their start and end apart: 15, of which 9 were waited for; matrix products, arithmetic and copies ran while one was open for 18% of the time, Pallas kernels for 0%

profile of v4, /device:TPU:0, one launch (start us, length us, event | category | flops | bytes accessed | tf_op | source)
XLA Modules:
  0.0 134.2 jit_solution(2552419605642384441)
XLA Ops:
  1.4 9.2 %reduce-precision_convert_fusion.1 = (bf16[1600,1536]{1,0:T(8,128)(2,1)S(1)}, bf16[1600,1536]{1,0:T(8,128)(2,1)S(1)}, bf16[1600,1536]{1,0:T(8,128)(2,1)S(1)}, f32[1600,1536]{1,0:T(8,128)}) fusion(f32[1536]{0:T(1024)} %param.11, f32[1536]{0:T(1024)} %param.10, bf16[1600,384]{1,0:T(8,128)(2,1)} %param.8, bf16[384,1536]{1,0:T(8,128)(2,1)} %param.9), kind=kOutput, calls=%fused_computation.10 | convolution fusion | flops 1919385600 | bytes 26996736 | tf_op jit(solution)/shard_map/dot_general | solution.py:99
  10.7 2.7 %fusion.18 = bf16[1,16,1536]{2,1,0:T(8,128)(2,1)S(1)} fusion(pred[16,4800]{1,0:T(8,128)(4,1)S(1)} %concatenate.39, bf16[1600,1536]{1,0:T(8,128)(2,1)S(1)} %get-tuple-element.20, bf16[1600,1536]{1,0:T(8,128)(2,1)S(1)} %get-tuple-element.19, bf16[1600,1536]{1,0:T(8,128)(2,1)S(1)} %get-tuple-element.18), kind=kOutput, calls=%fused_computation.24 | convolution fusion | flops 280215552 | bytes 14871552 | tf_op jit(solution)/shard_map/dot_general | solution.py:103
  13.3 3.0 %collective-permute-start = (bf16[1,16,1536]{2,1,0:T(8,128)(2,1)S(1)}, bf16[1,16,1536]{2,1,0:T(8,128)(2,1)S(1)}, u32[]{:S(2)}, u32[]{:S(2)}) collective-permute-start(bf16[1,16,1536]{2,1,0:T(8,128)(2,1)S(1)} %fusion.18), channel_id=1, source_target_pairs={{0,1},{1,0},{2,3},{3,2},{4,5},{5,4},{6,7},{7,6},{8,9},{9,8},{10,11... | collective-permute-start | bytes 147464 | tf_op jit(solution)/shard_map/ppermute | solution.py:51
  18.5 1.7 %fusion.22 = pred[64,64]{1,0:T(8,128)(4,1)} fusion(s32[64,48]{1,0:T(8,128)S(1)} %copy.67, pred[64,48]{1,0:T(8,128)(4,1)S(1)} %copy.68), kind=kLoop, calls=%fused_computation.29 | loop fusion | flops 585728 | bytes 19456 | tf_op jit(solution)/shard_map/reduce_or | solution.py:30
  21.9 1.6 %collective-permute-start.1 = (bf16[2,16,1536]{2,1,0:T(8,128)(2,1)S(1)}, bf16[2,16,1536]{2,1,0:T(8,128)(2,1)S(1)}, u32[]{:S(2)}, u32[]{:S(2)}) collective-permute-start(bf16[2,16,1536]{2,1,0:T(8,128)(2,1)S(1)} %maximum_select_fusion.1), channel_id=1, source_target_pairs={{0,2},{1,3},{2,0},{3,1},{4,6},{5,7},{6,4},{7,5},{8,10},{9,11},{10,... | collective-permute-start | bytes 294920 | tf_op jit(solution)/shard_map/ppermute | solution.py:51
  24.1 2.5 %collective-permute-done.1 = bf16[2,16,1536]{2,1,0:T(8,128)(2,1)S(1)} collective-permute-done((bf16[2,16,1536]{2,1,0:T(8,128)(2,1)S(1)}, bf16[2,16,1536]{2,1,0:T(8,128)(2,1)S(1)}, u32[]{:S(2)}, u32[]{:S(2)}) %collective-permute-start.1) | collective-permute-done | bytes 98336 | tf_op jit(solution)/shard_map/ppermute | solution.py:51
  27.3 1.2 select_n.399
  28.5 3.4 %select_reduce_fusion.1 = (f32[64,64]{1,0:T(8,128)S(1)}, f32[64,64]{1,0:T(8,128)}) fusion(pred[64,16]{0,1:T(8,128)(4,1)S(1)} %iota_compare_fusion.7, pred[64,16]{0,1:T(8,128)(4,1)S(1)} %iota_compare_fusion.6, bf16[64,1536,1]{1,0,2:T(8,128)(2,1)} %bitcast.85, bf16[16,64,1536]{2,1,0:T(8,128)(2,1)S(1)} %bitcast.75), kind=kOutput, calls=%fused_computation.36 | convolution fusion | flops 201580544 | bytes 3377152 | tf_op jit(solution)/shard_map/dot_general | solution.py:123
  32.7 1.1 tile.13
  36.0 1.8 %tile.15 = bf16[2,2,16,1024]{3,2,1,0:T(8,128)(2,1)} reshape(bf16[64,16,64]{2,1,0:T(8,128)(2,1)} %tile.14) | data formatting | bytes 262144 | tf_op jit(solution)/shard_map/tile | solution.py:14
  37.8 1.6 %fusion.10 = f32[2,2,16,1536]{3,2,1,0:T(8,128)S(1)} fusion(bf16[1024,1536]{1,0:T(8,128)(2,1)S(1)} %copy-done, bf16[2,2,16,1024]{3,2,1,0:T(8,128)(2,1)S(1)} %tile.13, bf16[2,2,16,1024]{3,2,1,0:T(8,128)(2,1)} %tile.15, s32[2,2,16]{2,1,0:T(2,128)} %get-tuple-element.36, s32[2,2,16]{2,1,0:T(2,128)} %get-tuple-element.37, s32[1024]{0:T(1024)} %add_select_fusion.8), kind=kOutput, calls=%fused_computation.20 | convolution fusion | flops 201654272 | bytes 3805696 | tf_op jit(solution)/shard_map/dot_general | solution.py:133
  42.0 5.4 %all-to-all-start = ((bf16[8,64,322]{2,1,0:T(8,128)(2,1)}), bf16[8,64,322]{2,1,0:T(8,128)(2,1)S(1)}, u32[]{:S(2)}, u32[]{:S(2)}) async-start(bf16[8,64,322]{2,1,0:T(8,128)(2,1)} %pad_maximum_fusion), calls=%async_computation | async-start | bytes 786432 | tf_op jit(solution)/shard_map/all_to_all | solution.py:150
  49.8 1.5 %collective-permute-start.3 = (f32[1,16,1536]{2,1,0:T(8,128)}, f32[1,16,1536]{2,1,0:T(8,128)}, u32[]{:S(2)}, u32[]{:S(2)}) collective-permute-start(f32[1,16,1536]{2,1,0:T(8,128)} %constant_dynamic-slice_fusion.5), channel_id=1, source_target_pairs={{0,2},{1,3},{2,0},{3,1},{4,6},{5,7},{6,4},{7,5},{8,10},{9,11},{10,... | collective-permute-start | bytes 294920 | tf_op jit(solution)/shard_map/ppermute | solution.py:68
  51.3 1.3 iota_compare_fusion.3
  52.6 2.7 %collective-permute-done.3 = f32[1,16,1536]{2,1,0:T(8,128)} collective-permute-done((f32[1,16,1536]{2,1,0:T(8,128)}, f32[1,16,1536]{2,1,0:T(8,128)}, u32[]{:S(2)}, u32[]{:S(2)}) %collective-permute-start.3) | collective-permute-done | bytes 98336 | tf_op jit(solution)/shard_map/ppermute | solution.py:68
  55.3 1.6 %add_bitcast_fusion.2 = f32[16,1536]{1,0:T(8,128)} fusion(f32[1,16,1536]{2,1,0:T(8,128)} %collective-permute-done.3, f32[2,16,1536]{2,1,0:T(8,128)} %copy-done.5, s32[]{:T(128)S(6)} %select_n.435), kind=kLoop, calls=%fused_computation.73 | loop fusion | flops 24576 | bytes 294916 | tf_op jit(solution)/shard_map/reshape | solution.py:71
  56.9 3.1 %all-to-all-done = bf16[8,64,322]{2,1,0:T(8,128)(2,1)S(1)} async-done(((bf16[8,64,322]{2,1,0:T(8,128)(2,1)}), bf16[8,64,322]{2,1,0:T(8,128)(2,1)S(1)}, u32[]{:S(2)}, u32[]{:S(2)}) %all-to-all-start) | async-done | bytes 329760 | tf_op jit(solution)/shard_map/all_to_all | solution.py:150
  61.0 9.0 %fusion.68 = (f32[1536]{0:T(1024)S(1)}, f32[1536]{0:T(1024)}, f32[1600,1536]{1,0:T(8,128)S(1)}) fusion(f32[1600,1536]{1,0:T(8,128)} %get-tuple-element.34, f32[1536]{0:T(1024)} %param.11, f32[1536]{0:T(1024)} %param.10, bf16[16,1536]{1,0:T(8,128)(2,1)S(1)} %get-tuple-element.26, bf16[16,1536]{1,0:T(8,128)(2,1)S(1)} %get-tuple-element.27, ...), kind=kOutput, calls=%fused_computation.188 | convolution fusion | flops 268471296 | bytes 19858432 | tf_op jit(solution)/shard_map/dot_general | solution.py:163
  70.0 3.1 %fusion.8 = f32[1536,384]{1,0:T(8,128)S(1)} fusion(bf16[1600,384]{1,0:T(8,128)(2,1)S(1)} %copy-done.14, f32[1600,1536]{1,0:T(8,128)S(1)} %get-tuple-element.35, f32[1536]{0:T(1024)S(1)} %copy-done.15), kind=kOutput, calls=%fused_computation.18 | convolution fusion | flops 1892352000 | bytes 13424640 | tf_op jit(solution)/shard_map/dot_general | solution.py:170
  73.1 1.4 %copy-done.2 = f32[1536,384]{1,0:T(8,128)} copy-done((f32[1536,384]{1,0:T(8,128)}, f32[1536,384]{1,0:T(8,128)S(1)}, u32[]{:S(2)}) %copy-start.2) | copy-done | bytes 2359320
  74.5 1.1 dynamic-slice_bitcast_fusion
  78.8 1.7 %bitcast_add_fusion = f32[4,192,384]{2,1,0:T(8,128)S(1)} fusion(f32[4,192,384]{2,1,0:T(8,128)} %collective-permute-done.4, f32[4,2,192,384]{3,2,1,0:T(8,128)} %bitcast.82, s32[]{:T(128)S(6)} %select_n.438), kind=kLoop, calls=%fused_computation.30 | loop fusion | flops 294912 | bytes 3538948 | tf_op jit(solution)/shard_map/add | solution.py:69
  87.9 2.0 %collective-permute-start.10 = (f32[2,192,2]{1,2,0:T(2,128)S(1)}, f32[2,192,2]{1,2,0:T(2,128)S(1)}, u32[]{:S(2)}, u32[]{:S(2)}) collective-permute-start(f32[2,192,2]{1,2,0:T(2,128)S(1)} %dynamic-slice_bitcast_fusion.3), channel_id=1, source_target_pairs={{0,8},{4,12},{8,0},{12,4},{16,24},{20,28},{24,16},{28,20},{1,9},{5... | collective-permute-start | bytes 9224 | tf_op jit(solution)/shard_map/ppermute | solution.py:68
  89.8 8.4 %collective-permute-done.5 = f32[2,192,384]{2,1,0:T(8,128)} collective-permute-done((f32[2,192,384]{2,1,0:T(8,128)}, f32[2,192,384]{2,1,0:T(8,128)}, u32[]{:S(2)}, u32[]{:S(2)}) %collective-permute-start.5) | collective-permute-done | bytes 589856 | tf_op jit(solution)/shard_map/ppermute | solution.py:68
  98.2 1.3 bitcast_add_fusion.1
  99.7 2.9 %collective-permute-start.11 = (f32[1,192,2]{1,2,0:T(2,128)S(1)}, f32[1,192,2]{1,2,0:T(2,128)S(1)}, u32[]{:S(2)}, u32[]{:S(2)}) collective-permute-start(f32[1,192,2]{1,2,0:T(2,128)S(1)} %constant_dynamic-slice_fusion), channel_id=1, source_target_pairs={{0,16},{4,20},{8,24},{12,28},{16,0},{20,4},{24,8},{28,12},{1,17},{... | collective-permute-start | bytes 4616 | tf_op jit(solution)/shard_map/ppermute | solution.py:68
  102.6 12.5 %collective-permute-done.6 = f32[1,192,384]{2,1,0:T(8,128)S(1)} collective-permute-done((f32[1,192,384]{2,1,0:T(8,128)S(1)}, f32[1,192,384]{2,1,0:T(8,128)S(1)}, u32[]{:S(2)}, u32[]{:S(2)}) %collective-permute-start.6) | collective-permute-done | bytes 294944 | tf_op jit(solution)/shard_map/ppermute | solution.py:68
  115.1 1.6 %collective-permute-start.7 = (f32[192,384]{1,0:T(8,128)S(1)}, f32[192,384]{1,0:T(8,128)S(1)}, u32[]{:S(2)}, u32[]{:S(2)}) collective-permute-start(f32[192,384]{1,0:T(8,128)S(1)} %add_bitcast_fusion.1), channel_id=1, source_target_pairs={{0,1},{1,0},{2,3},{3,2},{4,5},{5,4},{6,7},{7,6},{8,9},{9,8},{10,11... | collective-permute-start | bytes 884744 | tf_op jit(solution)/shard_map/ppermute | solution.py:79
  118.8 5.3 %collective-permute-done.12 = f32[192,2]{0,1:T(2,128)S(1)} collective-permute-done((f32[192,2]{0,1:T(2,128)S(1)}, f32[192,2]{0,1:T(2,128)S(1)}, u32[]{:S(2)}, u32[]{:S(2)}) %collective-permute-start.12) | collective-permute-done | bytes 1568 | tf_op jit(solution)/shard_map/ppermute | solution.py:79
  124.1 1.5 %collective-permute-start.13 = (f32[192,2]{0,1:T(2,128)S(1)}, f32[192,2]{0,1:T(2,128)S(1)}, u32[]{:S(2)}, u32[]{:S(2)}) collective-permute-start(f32[192,2]{0,1:T(2,128)S(1)} %add.320), channel_id=1, source_target_pairs={{0,2},{1,3},{2,0},{3,1},{4,6},{5,7},{6,4},{7,5},{8,10},{9,11},{10,... | collective-permute-start | bytes 4616 | tf_op jit(solution)/shard_map/ppermute | solution.py:79
  126.2 1.4 %fusion.71 = f32[1024,192]{0,1:T(8,128)} fusion(bf16[512,1024]{0,1:T(8,128)(2,1)S(1)} %bitcast.78, bf16[512,192]{1,0:T(8,128)(2,1)S(1)} %bitcast.84), kind=kOutput, calls=%fused_computation.191 | convolution fusion | flops 201326592 | bytes 2031616 | tf_op jit(solution)/shard_map/dot_general | solution.py:159
  128.3 5.2 %collective-permute-done.8 = f32[192,384]{1,0:T(8,128)S(1)} collective-permute-done((f32[192,384]{1,0:T(8,128)S(1)}, f32[192,384]{1,0:T(8,128)S(1)}, u32[]{:S(2)}, u32[]{:S(2)}) %collective-permute-start.8) | collective-permute-done | bytes 294944 | tf_op jit(solution)/shard_map/ppermute | solution.py:79
  (121 shorter events, 29.4 us)
Async XLA Ops:
  0.6 27.9 %copy-start = (bf16[1024,1536]{1,0:T(8,128)(2,1)S(1)}, bf16[1024,1536]{1,0:T(8,128)(2,1)}, u32[]{:S(2)}) copy-start(bf16[1024,1536]{1,0:T(8,128)(2,1)} %param.12) | copy-start | bytes 9437188
  0.7 0.6 copy-start.8
  10.7 5.7 %copy-start.11 = (s32[64,64]{1,0:T(8,128)S(1)}, s32[64,64]{1,0:T(8,128)}, u32[]{:S(2)}) copy-start(s32[64,64]{1,0:T(8,128)} %param.14) | copy-start | bytes 49156
  10.7 6.4 %copy-start.13 = (s32[64]{0:T(128)S(1)}, s32[64]{0:T(128)}, u32[]{:S(2)}) copy-start(s32[64]{0:T(128)} %param.13) | copy-start | bytes 772
  13.3 8.6 %collective-permute-start = (bf16[1,16,1536]{2,1,0:T(8,128)(2,1)S(1)}, bf16[1,16,1536]{2,1,0:T(8,128)(2,1)S(1)}, u32[]{:S(2)}, u32[]{:S(2)}) collective-permute-start(bf16[1,16,1536]{2,1,0:T(8,128)(2,1)S(1)} %fusion.18), channel_id=1, source_target_pairs={{0,1},{1,0},{2,3},{3,2},{4,5},{5,4},{6,7},{7,6},{8,9},{9,8},{10,11... | collective-permute-start | bytes 147464 | tf_op jit(solution)/shard_map/ppermute | solution.py:51
  21.9 4.7 %collective-permute-start.1 = (bf16[2,16,1536]{2,1,0:T(8,128)(2,1)S(1)}, bf16[2,16,1536]{2,1,0:T(8,128)(2,1)S(1)}, u32[]{:S(2)}, u32[]{:S(2)}) collective-permute-start(bf16[2,16,1536]{2,1,0:T(8,128)(2,1)S(1)} %maximum_select_fusion.1), channel_id=1, source_target_pairs={{0,2},{1,3},{2,0},{3,1},{4,6},{5,7},{6,4},{7,5},{8,10},{9,11},{10,... | collective-permute-start | bytes 294920 | tf_op jit(solution)/shard_map/ppermute | solution.py:51
  34.7 0.6 copy-start.6
  37.8 3.2 %copy-start.7 = (bf16[64,64]{1,0:T(8,128)(2,1)S(1)}, bf16[64,64]{1,0:T(8,128)(2,1)}, u32[]{:S(2)}) copy-start(bf16[64,64]{1,0:T(8,128)(2,1)} %copy-done.6) | copy-start | bytes 24580
  37.8 3.2 %copy-start.9 = (bf16[64,1]{1,0:T(8,128)(2,1)S(1)}, bf16[64,1]{1,0:T(8,128)(2,1)}, u32[]{:S(2)}) copy-start(bf16[64,1]{1,0:T(8,128)(2,1)} %get-tuple-element.40) | copy-start | bytes 388
  37.8 3.2 %copy-start.10 = (bf16[64,1]{1,0:T(8,128)(2,1)S(1)}, bf16[64,1]{1,0:T(8,128)(2,1)}, u32[]{:S(2)}) copy-start(bf16[64,1]{1,0:T(8,128)(2,1)} %get-tuple-element.41) | copy-start | bytes 388
  39.5 0.8 copy-start.4
  40.9 6.5 %collective-permute-start.2 = (f32[2,16,1536]{2,1,0:T(8,128)}, f32[2,16,1536]{2,1,0:T(8,128)}, u32[]{:S(2)}, u32[]{:S(2)}) collective-permute-start(f32[2,16,1536]{2,1,0:T(8,128)} %dynamic-slice_bitcast_fusion.2), channel_id=1, source_target_pairs={{0,1},{1,0},{2,3},{3,2},{4,5},{5,4},{6,7},{7,6},{8,9},{9,8},{10,11... | collective-permute-start | bytes 589832 | tf_op jit(solution)/shard_map/ppermute | solution.py:68
  42.0 17.9 %all-to-all-start = ((bf16[8,64,322]{2,1,0:T(8,128)(2,1)}), bf16[8,64,322]{2,1,0:T(8,128)(2,1)S(1)}, u32[]{:S(2)}, u32[]{:S(2)}) async-start(bf16[8,64,322]{2,1,0:T(8,128)(2,1)} %pad_maximum_fusion), calls=%async_computation | async-start | bytes 786432 | tf_op jit(solution)/shard_map/all_to_all | solution.py:150
  48.5 0.7 copy-start.5
  49.8 5.5 %collective-permute-start.3 = (f32[1,16,1536]{2,1,0:T(8,128)}, f32[1,16,1536]{2,1,0:T(8,128)}, u32[]{:S(2)}, u32[]{:S(2)}) collective-permute-start(f32[1,16,1536]{2,1,0:T(8,128)} %constant_dynamic-slice_fusion.5), channel_id=1, source_target_pairs={{0,2},{1,3},{2,0},{3,1},{4,6},{5,7},{6,4},{7,5},{8,10},{9,11},{10,... | collective-permute-start | bytes 294920 | tf_op jit(solution)/shard_map/ppermute | solution.py:68
  60.0 10.0 %copy-start.3 = (bf16[8,64,322]{2,1,0:T(8,128)(2,1)}, bf16[8,64,322]{2,1,0:T(8,128)(2,1)S(1)}, u32[]{:S(2)}) copy-start(bf16[8,64,322]{2,1,0:T(8,128)(2,1)S(1)} %all-to-all-done) | copy-start | bytes 989188
  61.0 9.1 %copy-start.14 = (bf16[1600,384]{1,0:T(8,128)(2,1)S(1)}, bf16[1600,384]{1,0:T(8,128)(2,1)}, u32[]{:S(2)}) copy-start(bf16[1600,384]{1,0:T(8,128)(2,1)} %param.8) | copy-start | bytes 3686404
  61.0 9.0 %copy-start.15 = (f32[1536]{0:T(1024)S(1)}, f32[1536]{0:T(1024)}, u32[]{:S(2)}) copy-start(f32[1536]{0:T(1024)} %param.10) | copy-start | bytes 18436
  70.0 6.7 %copy-start.12 = (f32[1536]{0:T(1024)S(1)}, f32[1536]{0:T(1024)}, u32[]{:S(2)}) copy-start(f32[1536]{0:T(1024)} %get-tuple-element.9) | copy-start | bytes 18436
  73.1 1.4 %copy-start.2 = (f32[1536,384]{1,0:T(8,128)}, f32[1536,384]{1,0:T(8,128)S(1)}, u32[]{:S(2)}) copy-start(f32[1536,384]{1,0:T(8,128)S(1)} %fusion.8) | copy-start | bytes 7077892
  75.6 3.2 %collective-permute-start.4 = (f32[4,192,384]{2,1,0:T(8,128)}, f32[4,192,384]{2,1,0:T(8,128)}, u32[]{:S(2)}, u32[]{:S(2)}) collective-permute-start(f32[4,192,384]{2,1,0:T(8,128)} %dynamic-slice_bitcast_fusion), channel_id=1, source_target_pairs={{0,4},{4,0},{8,12},{12,8},{16,20},{20,16},{24,28},{28,24},{1,5},{5... | collective-permute-start | bytes 3538952 | tf_op jit(solution)/shard_map/ppermute | solution.py:68
  80.6 1.0 copy-start.1
  82.5 15.7 %collective-permute-start.5 = (f32[2,192,384]{2,1,0:T(8,128)}, f32[2,192,384]{2,1,0:T(8,128)}, u32[]{:S(2)}, u32[]{:S(2)}) collective-permute-start(f32[2,192,384]{2,1,0:T(8,128)} %dynamic-slice_bitcast_fusion.1), channel_id=1, source_target_pairs={{0,8},{4,12},{8,0},{12,4},{16,24},{20,28},{24,16},{28,20},{1,9},{5... | collective-permute-start | bytes 1769480 | tf_op jit(solution)/shard_map/ppermute | solution.py:68
  83.1 4.1 %collective-permute-start.9 = (f32[4,192,2]{1,0,2:T(4,128)}, f32[4,192,2]{1,0,2:T(4,128)}, u32[]{:S(2)}, u32[]{:S(2)}) collective-permute-start(f32[4,192,2]{1,0,2:T(4,128)} %bitcast.74), channel_id=1, source_target_pairs={{0,4},{4,0},{8,12},{12,8},{16,20},{20,16},{24,28},{28,24},{1,5},{5... | collective-permute-start | bytes 18440 | tf_op jit(solution)/shard_map/ppermute | solution.py:68
  87.9 11.8 %collective-permute-start.10 = (f32[2,192,2]{1,2,0:T(2,128)S(1)}, f32[2,192,2]{1,2,0:T(2,128)S(1)}, u32[]{:S(2)}, u32[]{:S(2)}) collective-permute-start(f32[2,192,2]{1,2,0:T(2,128)S(1)} %dynamic-slice_bitcast_fusion.3), channel_id=1, source_target_pairs={{0,8},{4,12},{8,0},{12,4},{16,24},{20,28},{24,16},{28,20},{1,9},{5... | collective-permute-start | bytes 9224 | tf_op jit(solution)/shard_map/ppermute | solution.py:68
  99.5 15.5 %collective-permute-start.6 = (f32[1,192,384]{2,1,0:T(8,128)S(1)}, f32[1,192,384]{2,1,0:T(8,128)S(1)}, u32[]{:S(2)}, u32[]{:S(2)}) collective-permute-start(f32[1,192,384]{2,1,0:T(8,128)S(1)} %constant_dynamic-slice_fusion.4), channel_id=1, source_target_pairs={{0,16},{4,20},{8,24},{12,28},{16,0},{20,4},{24,8},{28,12},{1,17},{... | collective-permute-start | bytes 884744 | tf_op jit(solution)/shard_map/ppermute | solution.py:68
  99.7 17.0 %collective-permute-start.11 = (f32[1,192,2]{1,2,0:T(2,128)S(1)}, f32[1,192,2]{1,2,0:T(2,128)S(1)}, u32[]{:S(2)}, u32[]{:S(2)}) collective-permute-start(f32[1,192,2]{1,2,0:T(2,128)S(1)} %constant_dynamic-slice_fusion), channel_id=1, source_target_pairs={{0,16},{4,20},{8,24},{12,28},{16,0},{20,4},{24,8},{28,12},{1,17},{... | collective-permute-start | bytes 4616 | tf_op jit(solution)/shard_map/ppermute | solution.py:68
  115.1 10.5 %collective-permute-start.7 = (f32[192,384]{1,0:T(8,128)S(1)}, f32[192,384]{1,0:T(8,128)S(1)}, u32[]{:S(2)}, u32[]{:S(2)}) collective-permute-start(f32[192,384]{1,0:T(8,128)S(1)} %add_bitcast_fusion.1), channel_id=1, source_target_pairs={{0,1},{1,0},{2,3},{3,2},{4,5},{5,4},{6,7},{7,6},{8,9},{9,8},{10,11... | collective-permute-start | bytes 884744 | tf_op jit(solution)/shard_map/ppermute | solution.py:79
  116.7 7.4 %collective-permute-start.12 = (f32[192,2]{0,1:T(2,128)S(1)}, f32[192,2]{0,1:T(2,128)S(1)}, u32[]{:S(2)}, u32[]{:S(2)}) collective-permute-start(f32[192,2]{0,1:T(2,128)S(1)} %fusion.63), channel_id=1, source_target_pairs={{0,1},{1,0},{2,3},{3,2},{4,5},{5,4},{6,7},{7,6},{8,9},{9,8},{10,11... | collective-permute-start | bytes 4616 | tf_op jit(solution)/shard_map/ppermute | solution.py:79
  124.1 3.6 %collective-permute-start.13 = (f32[192,2]{0,1:T(2,128)S(1)}, f32[192,2]{0,1:T(2,128)S(1)}, u32[]{:S(2)}, u32[]{:S(2)}) collective-permute-start(f32[192,2]{0,1:T(2,128)S(1)} %add.320), channel_id=1, source_target_pairs={{0,2},{1,3},{2,0},{3,1},{4,6},{5,7},{6,4},{7,5},{8,10},{9,11},{10,... | collective-permute-start | bytes 4616 | tf_op jit(solution)/shard_map/ppermute | solution.py:79
  125.6 7.8 %collective-permute-start.8 = (f32[192,384]{1,0:T(8,128)S(1)}, f32[192,384]{1,0:T(8,128)S(1)}, u32[]{:S(2)}, u32[]{:S(2)}) collective-permute-start(f32[192,384]{1,0:T(8,128)S(1)} %add.315), channel_id=1, source_target_pairs={{0,2},{1,3},{2,0},{3,1},{4,6},{5,7},{6,4},{7,5},{8,10},{9,11},{10,... | collective-permute-start | bytes 884744 | tf_op jit(solution)/shard_map/ppermute | solution.py:79

commit v5 on v4

--- a/solution.py
+++ b/solution.py
@@ -80,6 +80,58 @@
         cur = tuple(c + g for c, g in zip(cur, got))
         bit += 1
     return cur
+
+
+def halve_steps(x, name, axis, bits):
+    idx = lax.axis_index(name)
+    size = lax.axis_size(name)
+    for bit in bits:
+        n = x.shape[axis]
+        pairs = x.reshape(x.shape[:axis] + (n // 2, 2) + x.shape[axis + 1 :])
+        mine = (idx // (1 << bit)) % 2
+        keep = lax.dynamic_index_in_dim(pairs, mine, axis + 1, keepdims=False)
+        give = lax.dynamic_index_in_dim(pairs, 1 - mine, axis + 1, keepdims=False)
+        x = keep + lax.ppermute(give, name, partners(size, bit))
+    return x
+
+
+def double_steps(x, name, axis, bits):
+    idx = lax.axis_index(name)
+    size = lax.axis_size(name)
+    for bit in bits:
+        other = lax.ppermute(x, name, partners(size, bit))
+        low = (idx // (1 << bit)) % 2 == 0
+        x = jnp.where(low, jnp.concatenate([x, other], axis), jnp.concatenate([other, x], axis))
+    return x
+
+
+def axis_bits(name):
+    size = lax.axis_size(name)
+    bit = 0
+    while (1 << bit) < size:
+        bit += 1
+    return list(range(bit))
+
+
+def reduce_head(head, side):
+    n_dp = lax.axis_size("dp")
+    n_leaf = lax.axis_size("leaf")
+    rows, cols = head.shape
+    w = rows // n_dp
+    dbits = axis_bits("dp")
+    lbits = axis_bits("leaf")
+    h = halve_steps(head.reshape(n_dp, w, cols), "dp", 0, dbits[:1])
+    s = halve_steps(side.reshape(n_dp, w, side.shape[1]), "dp", 0, dbits[:1])
+    half = cols // 2
+    first = halve_steps(h[:, :, :half], "dp", 0, dbits[1:])
+    s = halve_steps(s, "dp", 0, dbits[1:])
+    second = h[:, :, half:].reshape(h.shape[:2] + (n_leaf, half // n_leaf))
+    second = halve_steps(second, "leaf", 2, lbits)
+    second = halve_steps(second, "dp", 0, dbits[1:])
+    first, s = butterfly_sum((first, s), "leaf")
+    second = double_steps(second, "leaf", 2, lbits)
+    head_sum = jnp.concatenate([first.reshape(w, half), second.reshape(w, half)], axis=1)
+    return head_sum, s.reshape(w, side.shape[1])
 
 
 def shards(features, head_weight, gain, shift, node_weights, subtree_map, node_ids):
@@ -173,8 +225,7 @@
     gain_term = jnp.sum(pixel_gradient * linear_scores, axis=0)
     shift_term = jnp.sum(pixel_gradient, axis=0)
     side_terms = jnp.stack([gain_term, shift_term], axis=1)
-    head_part, side_part = halving_scatter([head_term, side_terms], "dp")
-    head_sum, side_sum = butterfly_sum([head_part, side_part], "leaf")
+    head_sum, side_sum = reduce_head(head_term, side_terms)
     return (head_sum.T, side_sum[:, 0], side_sum[:, 1], node_grad)
 
 

time: 135 us -> 137 us (1.015)
  starting transfers between devices: 20.8 us -> 30 us
  waiting for transfers between devices: 40.7 us -> 34.3 us
  matrix products: 30.4 us -> 34.8 us
  other arithmetic: 18.3 us -> 15.8 us
  local copies, waits for them, and re-layouts: 22.9 us -> 20.6 us
    ppermute x8 -> x2, waiting for transfers between devices: 24.5 us -> 3.68 us  [halving_scatter(): got = lax.ppermute(tuple(give), name, partners(size, bit))]
    ppermute x0 -> x12, waiting for transfers between devices: none -> 18.2 us  [the longest x10 12.8 us: halve_steps(): x = keep + lax.ppermute(give, name, partners(size, bit))]
    ppermute x0 -> x12, starting transfers between devices: none -> 14.3 us  [the longest x10 11.6 us: halve_steps(): x = keep + lax.ppermute(give, name, partners(size, bit))]
    ppermute x4, waiting for transfers between devices: 10.6 us -> 3.46 us  [butterfly_sum(): got = lax.ppermute(cur, name, partners(size, bit))]
    unnamed x39 -> x23, local copies, waits for them, and re-layouts: 9.01 us -> 3.34 us
    ppermute x8 -> x2, starting transfers between devices: 6.7 us -> 1.61 us  [halving_scatter(): got = lax.ppermute(tuple(give), name, partners(size, bit))]
    squeeze x0 -> x9, local copies, waits for them, and re-layouts: none -> 3.98 us  [halve_steps(): give = lax.dynamic_index_in_dim(pairs, 1 - mine, axis + 1, keepdims=False)]
    add x5 -> x1, other arithmetic: 4.81 us -> 0.96 us  [halving_scatter(): cur = [k + g for k, g in zip(keep, got)]]
  transfers between devices with their start and end apart: 15 -> 21, of which waited for: 9 -> 13; matrix products, arithmetic and copies ran while one was open for 18% -> 27% of each run, Pallas kernels for 0% -> 0%
where the time goes in v5:
time: 137 us
  matrix products  34.8 us (25%)
  waiting for transfers between devices  34.3 us (25%)
  starting transfers between devices  30 us (22%)
  local copies, waits for them, and re-layouts  20.6 us (15%)
  other arithmetic  15.8 us (12%)
    ppermute x10, waiting for transfers between devices, halve_steps(): x = keep + lax.ppermute(give, name, partners(size, bit))  12.8 us
    ppermute x10, starting transfers between devices, halve_steps(): x = keep + lax.ppermute(give, name, partners(size, bit))  11.6 us
    dot_general x1, matrix products, shards(): jnp.dot(jnp.concatenate([select.T] * 3, axis=1), jnp.concatenate(split3(e...  10.9 us
    dot_general x1, matrix products, shards(): jnp.dot(features, head_weight, preferred_element_type=jnp.float32)  9.17 us
    all_to_all x1, waiting for transfers between devices, shards(): recv = lax.all_to_all(send, 'dp', split_axis=0, concat_axis=0, tiled=True)  6.39 us
    dot_general x1, matrix products, shards(): lax.dot_general(lin_grad, features, (((0,), (0,)), ((), ())), preferred_e...  6.01 us
    ppermute x2, waiting for transfers between devices, double_steps(): other = lax.ppermute(x, name, partners(size, bit))  5.4 us
    all_to_all x1, starting transfers between devices, shards(): recv = lax.all_to_all(send, 'dp', split_axis=0, concat_axis=0, tiled=True)  5.37 us
  transfers between devices with their start and end apart: 21, of which 13 were waited for; matrix products, arithmetic and copies ran while one was open for 27% of the time, Pallas kernels for 0%

profile of v5, /device:TPU:0, one launch (start us, length us, event | category | flops | bytes accessed | tf_op | source)
XLA Modules:
  0.0 136.6 jit_solution(2565835041119863820)
XLA Ops:
  0.8 9.2 %reduce-precision_convert_fusion.1 = (bf16[1600,1536]{1,0:T(8,128)(2,1)S(1)}, bf16[1600,1536]{1,0:T(8,128)(2,1)S(1)}, bf16[1600,1536]{1,0:T(8,128)(2,1)S(1)}, f32[1600,1536]{1,0:T(8,128)}) fusion(f32[1536]{0:T(1024)} %param.11, f32[1536]{0:T(1024)} %param.10, bf16[1600,384]{1,0:T(8,128)(2,1)} %param.8, bf16[384,1536]{1,0:T(8,128)(2,1)} %param.9), kind=kOutput, calls=%fused_computation.10 | convolution fusion | flops 1919385600 | bytes 26996736 | tf_op jit(solution)/shard_map/dot_general | solution.py:151
  10.0 2.7 %fusion.18 = bf16[1,16,1536]{2,1,0:T(8,128)(2,1)S(1)} fusion(pred[16,4800]{1,0:T(8,128)(4,1)S(1)} %concatenate.80, bf16[1600,1536]{1,0:T(8,128)(2,1)S(1)} %get-tuple-element.24, bf16[1600,1536]{1,0:T(8,128)(2,1)S(1)} %get-tuple-element.23, bf16[1600,1536]{1,0:T(8,128)(2,1)S(1)} %get-tuple-element.22), kind=kOutput, calls=%fused_computation.24 | convolution fusion | flops 280215552 | bytes 14871552 | tf_op jit(solution)/shard_map/dot_general | solution.py:155
  12.7 3.0 %collective-permute-start = (bf16[1,16,1536]{2,1,0:T(8,128)(2,1)S(1)}, bf16[1,16,1536]{2,1,0:T(8,128)(2,1)S(1)}, u32[]{:S(2)}, u32[]{:S(2)}) collective-permute-start(bf16[1,16,1536]{2,1,0:T(8,128)(2,1)S(1)} %fusion.18), channel_id=1, source_target_pairs={{0,1},{1,0},{2,3},{3,2},{4,5},{5,4},{6,7},{7,6},{8,9},{9,8},{10,11... | collective-permute-start | bytes 147464 | tf_op jit(solution)/shard_map/ppermute | solution.py:51
  20.9 1.6 %collective-permute-start.1 = (bf16[2,16,1536]{2,1,0:T(8,128)(2,1)S(1)}, bf16[2,16,1536]{2,1,0:T(8,128)(2,1)S(1)}, u32[]{:S(2)}, u32[]{:S(2)}) collective-permute-start(bf16[2,16,1536]{2,1,0:T(8,128)(2,1)S(1)} %maximum_select_fusion.2), channel_id=1, source_target_pairs={{0,2},{1,3},{2,0},{3,1},{4,6},{5,7},{6,4},{7,5},{8,10},{9,11},{10,... | collective-permute-start | bytes 294920 | tf_op jit(solution)/shard_map/ppermute | solution.py:51
  23.1 2.5 %collective-permute-done.1 = bf16[2,16,1536]{2,1,0:T(8,128)(2,1)S(1)} collective-permute-done((bf16[2,16,1536]{2,1,0:T(8,128)(2,1)S(1)}, bf16[2,16,1536]{2,1,0:T(8,128)(2,1)S(1)}, u32[]{:S(2)}, u32[]{:S(2)}) %collective-permute-start.1) | collective-permute-done | bytes 98336 | tf_op jit(solution)/shard_map/ppermute | solution.py:51
  26.5 1.8 %select_reduce_fusion.1 = (f32[64,64]{1,0:T(8,128)S(1)}, f32[64,64]{1,0:T(8,128)S(1)}) fusion(pred[64,16]{0,1:T(8,128)(4,1)S(1)} %iota_compare_fusion.7, pred[64,16]{0,1:T(8,128)(4,1)S(1)} %iota_compare_fusion.6, bf16[64,1536,1]{1,0,2:T(8,128)(2,1)S(1)} %bitcast.100, bf16[16,64,1536]{2,1,0:T(8,128)(2,1)S(1)} %bitcast.88), kind=kOutput, calls=%fused_computation.34 | convolution fusion | flops 201580544 | bytes 3377152 | tf_op jit(solution)/shard_map/dot_general | solution.py:175
  30.3 1.7 %fusion.10 = f32[2,2,16,1536]{3,2,1,0:T(8,128)S(1)} fusion(bf16[1024,1536]{1,0:T(8,128)(2,1)S(1)} %copy-done, bf16[2,2,16,1024]{3,2,1,0:T(8,128)(2,1)} %tile.13, bf16[2,2,16,1024]{3,2,1,0:T(8,128)(2,1)} %tile.15, s32[2,2,16]{2,1,0:T(2,128)} %get-tuple-element.42, s32[2,2,16]{2,1,0:T(2,128)} %get-tuple-element.43, s32[1024]{0:T(1024)} %add_select_fusion.8), kind=kOutput, calls=%fused_computation.20 | convolution fusion | flops 201654272 | bytes 3805696 | tf_op jit(solution)/shard_map/dot_general | solution.py:185
  35.5 5.4 %all-to-all-start = ((bf16[8,64,322]{2,1,0:T(8,128)(2,1)}), bf16[8,64,322]{2,1,0:T(8,128)(2,1)}, u32[]{:S(2)}, u32[]{:S(2)}) async-start(bf16[8,64,322]{2,1,0:T(8,128)(2,1)} %pad_maximum_fusion), calls=%async_computation | async-start | bytes 786432 | tf_op jit(solution)/shard_map/all_to_all | solution.py:202
  41.8 1.6 %collective-permute-start.3 = (f32[1,16,1536]{2,1,0:T(8,128)S(1)}, f32[1,16,1536]{2,1,0:T(8,128)S(1)}, u32[]{:S(2)}, u32[]{:S(2)}) collective-permute-start(f32[1,16,1536]{2,1,0:T(8,128)S(1)} %constant_dynamic-slice_fusion.9), channel_id=1, source_target_pairs={{0,2},{1,3},{2,0},{3,1},{4,6},{5,7},{6,4},{7,5},{8,10},{9,11},{10,... | collective-permute-start | bytes 294920 | tf_op jit(solution)/shard_map/ppermute | solution.py:68
  43.4 3.7 %collective-permute-done.3 = f32[1,16,1536]{2,1,0:T(8,128)S(1)} collective-permute-done((f32[1,16,1536]{2,1,0:T(8,128)S(1)}, f32[1,16,1536]{2,1,0:T(8,128)S(1)}, u32[]{:S(2)}, u32[]{:S(2)}) %collective-permute-start.3) | collective-permute-done | bytes 98336 | tf_op jit(solution)/shard_map/ppermute | solution.py:68
  47.1 6.4 %all-to-all-done = bf16[8,64,322]{2,1,0:T(8,128)(2,1)} async-done(((bf16[8,64,322]{2,1,0:T(8,128)(2,1)}), bf16[8,64,322]{2,1,0:T(8,128)(2,1)}, u32[]{:S(2)}, u32[]{:S(2)}) %all-to-all-start) | async-done | bytes 329760 | tf_op jit(solution)/shard_map/all_to_all | solution.py:202
  55.5 10.9 %fusion.70 = (f32[1536]{0:T(1024)S(1)}, f32[1536]{0:T(1024)S(1)}, f32[1600,1536]{1,0:T(8,128)}) fusion(f32[1600,1536]{1,0:T(8,128)} %get-tuple-element.40, f32[1536]{0:T(1024)} %param.11, f32[1536]{0:T(1024)} %param.10, bf16[16,1536]{1,0:T(8,128)(2,1)S(1)} %get-tuple-element.32, bf16[16,1536]{1,0:T(8,128)(2,1)S(1)} %get-tuple-element.33, ...), kind=kOutput, calls=%fused_computation.202 | convolution fusion | flops 268471296 | bytes 19858432 | tf_op jit(solution)/shard_map/dot_general | solution.py:215
  66.7 6.0 %fusion.8 = f32[1536,384]{1,0:T(8,128)S(1)} fusion(bf16[1600,384]{1,0:T(8,128)(2,1)} %param.8, f32[1600,1536]{1,0:T(8,128)} %get-tuple-element.41, f32[1536]{0:T(1024)S(1)} %copy-done.7), kind=kOutput, calls=%fused_computation.18 | convolution fusion | flops 1892352000 | bytes 13424640 | tf_op jit(solution)/shard_map/dot_general | solution.py:222
  79.7 1.8 %collective-permute-start.17 = (f32[1,192,2]{1,2,0:T(2,128)S(1)}, f32[1,192,2]{1,2,0:T(2,128)S(1)}, u32[]{:S(2)}, u32[]{:S(2)}) collective-permute-start(f32[1,192,2]{1,2,0:T(2,128)S(1)} %constant_dynamic-slice_fusion), channel_id=1, source_target_pairs={{0,16},{4,20},{8,24},{12,28},{16,0},{20,4},{24,8},{28,12},{1,17},{... | collective-permute-start | bytes 4616 | tf_op jit(solution)/shard_map/ppermute | solution.py:94
  81.5 1.6 %fusion.23 = bf16[512,16,64]{0,2,1:T(8,128)(2,1)} fusion(s32[512]{0:T(512)S(1)} %bitcast.107, s32[512]{0:T(512)S(1)} %bitcast.106, s32[16,64]{1,0:T(8,128)S(1)} %add_select_fusion.5, bf16[512,64]{0,1:T(8,128)(2,1)S(1)} %copy.96, bf16[512,64]{0,1:T(8,128)(2,1)S(1)} %copy.94), kind=kLoop, calls=%fused_computation.32 | loop fusion | flops 2621440 | bytes 1187840 | tf_op jit(solution)/shard_map/add | solution.py:17
  84.1 1.5 %collective-permute-start.18 = (f32[1,192,2]{1,2,0:T(2,128)S(1)}, f32[1,192,2]{1,2,0:T(2,128)S(1)}, u32[]{:S(2)}, u32[]{:S(2)}) collective-permute-start(f32[1,192,2]{1,2,0:T(2,128)S(1)} %fusion.65), channel_id=1, source_target_pairs={{0,1},{1,0},{2,3},{3,2},{4,5},{5,4},{6,7},{7,6},{8,9},{9,8},{10,11... | collective-permute-start | bytes 4616 | tf_op jit(solution)/shard_map/ppermute | solution.py:79
  85.6 1.7 %bitcast_add_fusion = f32[4,192,384]{2,1,0:T(8,128)S(1)} fusion(f32[4,192,384]{2,1,0:T(8,128)} %collective-permute-done.4, f32[4,2,192,384]{3,2,1,0:T(8,128)} %bitcast.97, s32[]{:T(128)S(6)} %select_n.510), kind=kLoop, calls=%fused_computation.30 | loop fusion | flops 294912 | bytes 3538948 | tf_op jit(solution)/shard_map/add | solution.py:94
  88.8 2.4 %copy.85 = f32[4,192,192]{1,2,0:T(8,128)} copy(f32[4,192,192]{2,1,0:T(8,128)} %get-tuple-element.26) | data formatting | bytes 1179648 | tf_op jit(solution)/shard_map/slice | solution.py:128
  92.8 2.6 %fusion.74 = f32[1024,192]{0,1:T(8,128)} fusion(bf16[512,1024]{0,1:T(8,128)(2,1)} %bitcast.89, bf16[512,192]{1,0:T(8,128)(2,1)S(1)} %bitcast.99), kind=kOutput, calls=%fused_computation.206 | convolution fusion | flops 201326592 | bytes 2031616 | tf_op jit(solution)/shard_map/dot_general | solution.py:211
  95.5 1.5 %collective-permute-start.19 = (f32[1,192,2]{1,2,0:T(2,128)S(1)}, f32[1,192,2]{1,2,0:T(2,128)S(1)}, u32[]{:S(2)}, u32[]{:S(2)}) collective-permute-start(f32[1,192,2]{1,2,0:T(2,128)S(1)} %add.357), channel_id=1, source_target_pairs={{0,2},{1,3},{2,0},{3,1},{4,6},{5,7},{6,4},{7,5},{8,10},{9,11},{10,... | collective-permute-start | bytes 4616 | tf_op jit(solution)/shard_map/ppermute | solution.py:79
  98.0 2.1 %collective-permute-start.5 = (f32[2,192,192]{2,1,0:T(8,128)S(1)}, f32[2,192,192]{2,1,0:T(8,128)S(1)}, u32[]{:S(2)}, u32[]{:S(2)}) collective-permute-start(f32[2,192,192]{2,1,0:T(8,128)S(1)} %dynamic-slice_bitcast_fusion.2), channel_id=1, source_target_pairs={{0,8},{4,12},{8,0},{12,4},{16,24},{20,28},{24,16},{28,20},{1,9},{5... | collective-permute-start | bytes 884744 | tf_op jit(solution)/shard_map/ppermute | solution.py:94
  100.1 2.4 %collective-permute-done.9 = f32[4,192,2,48]{1,3,2,0:T(8,128)S(1)} collective-permute-done((f32[4,192,2,48]{1,3,2,0:T(8,128)S(1)}, f32[4,192,2,48]{1,3,2,0:T(8,128)S(1)}, u32[]{:S(2)}, u32[]{:S(2)}) %collective-permute-start.9) | collective-permute-done | bytes 294944 | tf_op jit(solution)/shard_map/ppermute | solution.py:94
  103.6 1.6 %collective-permute-start.10 = (f32[4,192,1,48]{1,3,2,0:T(8,128)S(1)}, f32[4,192,1,48]{1,3,2,0:T(8,128)S(1)}, u32[]{:S(2)}, u32[]{:S(2)}) collective-permute-start(f32[4,192,1,48]{1,3,2,0:T(8,128)S(1)} %constant_dynamic-slice_fusion.7), channel_id=1, source_target_pairs={{0,2},{1,3},{2,0},{3,1},{4,6},{5,7},{6,4},{7,5},{8,10},{9,11},{10,... | collective-permute-start | bytes 442376 | tf_op jit(solution)/shard_map/ppermute | solution.py:94
  105.2 2.5 %collective-permute-done.5 = f32[2,192,192]{2,1,0:T(8,128)S(1)} collective-permute-done((f32[2,192,192]{2,1,0:T(8,128)S(1)}, f32[2,192,192]{2,1,0:T(8,128)S(1)}, u32[]{:S(2)}, u32[]{:S(2)}) %collective-permute-start.5) | collective-permute-done | bytes 294944 | tf_op jit(solution)/shard_map/ppermute | solution.py:94
  107.8 1.6 %collective-permute-done.10 = f32[4,192,1,48]{1,3,2,0:T(8,128)S(1)} collective-permute-done((f32[4,192,1,48]{1,3,2,0:T(8,128)S(1)}, f32[4,192,1,48]{1,3,2,0:T(8,128)S(1)}, u32[]{:S(2)}, u32[]{:S(2)}) %collective-permute-start.10) | collective-permute-done | bytes 147488 | tf_op jit(solution)/shard_map/ppermute | solution.py:94
  110.6 2.0 %collective-permute-start.6 = (f32[1,192,192]{2,1,0:T(8,128)S(1)}, f32[1,192,192]{2,1,0:T(8,128)S(1)}, u32[]{:S(2)}, u32[]{:S(2)}) collective-permute-start(f32[1,192,192]{2,1,0:T(8,128)S(1)} %constant_dynamic-slice_fusion.8), channel_id=1, source_target_pairs={{0,16},{4,20},{8,24},{12,28},{16,0},{20,4},{24,8},{28,12},{1,17},{... | collective-permute-start | bytes 442376 | tf_op jit(solution)/shard_map/ppermute | solution.py:94
  112.7 1.7 %collective-permute-done.11 = f32[2,192,1,48]{1,3,2,0:T(8,128)S(1)} collective-permute-done((f32[2,192,1,48]{1,3,2,0:T(8,128)S(1)}, f32[2,192,1,48]{1,3,2,0:T(8,128)S(1)}, u32[]{:S(2)}, u32[]{:S(2)}) %collective-permute-start.11) | collective-permute-done | bytes 73760 | tf_op jit(solution)/shard_map/ppermute | solution.py:94
  114.4 1.7 %collective-permute-start.12 = (f32[1,192,1,48]{1,3,2,0:T(8,128)S(1)}, f32[1,192,1,48]{1,3,2,0:T(8,128)S(1)}, u32[]{:S(2)}, u32[]{:S(2)}) collective-permute-start(f32[1,192,1,48]{1,3,2,0:T(8,128)S(1)} %constant_dynamic-slice_fusion.6), channel_id=1, source_target_pairs={{0,16},{4,20},{8,24},{12,28},{16,0},{20,4},{24,8},{28,12},{1,17},{... | collective-permute-start | bytes 110600 | tf_op jit(solution)/shard_map/ppermute | solution.py:94
  116.1 4.1 %collective-permute-done.6 = f32[1,192,192]{2,1,0:T(8,128)S(1)} collective-permute-done((f32[1,192,192]{2,1,0:T(8,128)S(1)}, f32[1,192,192]{2,1,0:T(8,128)S(1)}, u32[]{:S(2)}, u32[]{:S(2)}) %collective-permute-start.6) | collective-permute-done | bytes 147488 | tf_op jit(solution)/shard_map/ppermute | solution.py:94
  122.4 4.1 %collective-permute-done.13 = f32[1,192,1,48]{1,3,2,0:T(8,128)S(1)} collective-permute-done((f32[1,192,1,48]{1,3,2,0:T(8,128)S(1)}, f32[1,192,1,48]{1,3,2,0:T(8,128)S(1)}, u32[]{:S(2)}, u32[]{:S(2)}) %collective-permute-start.13) | collective-permute-done | bytes 36896 | tf_op jit(solution)/shard_map/ppermute | solution.py:102
  126.5 1.6 %collective-permute-start.14 = (f32[1,192,2,48]{1,3,2,0:T(8,128)S(1)}, f32[1,192,2,48]{1,3,2,0:T(8,128)S(1)}, u32[]{:S(2)}, u32[]{:S(2)}) collective-permute-start(f32[1,192,2,48]{1,3,2,0:T(8,128)S(1)} %maximum_select_fusion.3), channel_id=1, source_target_pairs={{0,2},{1,3},{2,0},{3,1},{4,6},{5,7},{6,4},{7,5},{8,10},{9,11},{10,... | collective-permute-start | bytes 221192 | tf_op jit(solution)/shard_map/ppermute | solution.py:102
  131.3 3.5 %collective-permute-done.8 = f32[1,192,192]{2,1,0:T(8,128)} collective-permute-done((f32[1,192,192]{2,1,0:T(8,128)}, f32[1,192,192]{2,1,0:T(8,128)}, u32[]{:S(2)}, u32[]{:S(2)}) %collective-permute-start.8) | collective-permute-done | bytes 147488 | tf_op jit(solution)/shard_map/ppermute | solution.py:79
  (131 shorter events, 37.2 us)
Async XLA Ops:
  0.6 25.9 %copy-start = (bf16[1024,1536]{1,0:T(8,128)(2,1)S(1)}, bf16[1024,1536]{1,0:T(8,128)(2,1)}, u32[]{:S(2)}) copy-start(bf16[1024,1536]{1,0:T(8,128)(2,1)} %param.12) | copy-start | bytes 9437188
  10.0 5.7 %copy-start.5 = (s32[64,64]{1,0:T(8,128)S(1)}, s32[64,64]{1,0:T(8,128)}, u32[]{:S(2)}) copy-start(s32[64,64]{1,0:T(8,128)} %param.14) | copy-start | bytes 49156
  10.0 7.0 %copy-start.6 = (s32[64]{0:T(128)S(1)}, s32[64]{0:T(128)}, u32[]{:S(2)}) copy-start(s32[64]{0:T(128)} %param.13) | copy-start | bytes 772
  12.7 8.2 %collective-permute-start = (bf16[1,16,1536]{2,1,0:T(8,128)(2,1)S(1)}, bf16[1,16,1536]{2,1,0:T(8,128)(2,1)S(1)}, u32[]{:S(2)}, u32[]{:S(2)}) collective-permute-start(bf16[1,16,1536]{2,1,0:T(8,128)(2,1)S(1)} %fusion.18), channel_id=1, source_target_pairs={{0,1},{1,0},{2,3},{3,2},{4,5},{5,4},{6,7},{7,6},{8,9},{9,8},{10,11... | collective-permute-start | bytes 147464 | tf_op jit(solution)/shard_map/ppermute | solution.py:51
  20.9 4.7 %collective-permute-start.1 = (bf16[2,16,1536]{2,1,0:T(8,128)(2,1)S(1)}, bf16[2,16,1536]{2,1,0:T(8,128)(2,1)S(1)}, u32[]{:S(2)}, u32[]{:S(2)}) collective-permute-start(bf16[2,16,1536]{2,1,0:T(8,128)(2,1)S(1)} %maximum_select_fusion.2), channel_id=1, source_target_pairs={{0,2},{1,3},{2,0},{3,1},{4,6},{5,7},{6,4},{7,5},{8,10},{9,11},{10,... | collective-permute-start | bytes 294920 | tf_op jit(solution)/shard_map/ppermute | solution.py:51
  29.4 0.9 copy-start.3
  30.3 3.4 %copy-start.4 = (bf16[64,64]{1,0:T(8,128)(2,1)S(1)}, bf16[64,64]{1,0:T(8,128)(2,1)}, u32[]{:S(2)}) copy-start(bf16[64,64]{1,0:T(8,128)(2,1)} %copy-done.3) | copy-start | bytes 24580
  32.7 8.2 %collective-permute-start.2 = (f32[2,16,1536]{2,1,0:T(8,128)}, f32[2,16,1536]{2,1,0:T(8,128)}, u32[]{:S(2)}, u32[]{:S(2)}) collective-permute-start(f32[2,16,1536]{2,1,0:T(8,128)} %dynamic-slice_bitcast_fusion.3), channel_id=1, source_target_pairs={{0,1},{1,0},{2,3},{3,2},{4,5},{5,4},{6,7},{7,6},{8,9},{9,8},{10,11... | collective-permute-start | bytes 589832 | tf_op jit(solution)/shard_map/ppermute | solution.py:68
  35.5 18.0 %all-to-all-start = ((bf16[8,64,322]{2,1,0:T(8,128)(2,1)}), bf16[8,64,322]{2,1,0:T(8,128)(2,1)}, u32[]{:S(2)}, u32[]{:S(2)}) async-start(bf16[8,64,322]{2,1,0:T(8,128)(2,1)} %pad_maximum_fusion), calls=%async_computation | async-start | bytes 786432 | tf_op jit(solution)/shard_map/all_to_all | solution.py:202
  41.8 5.3 %collective-permute-start.3 = (f32[1,16,1536]{2,1,0:T(8,128)S(1)}, f32[1,16,1536]{2,1,0:T(8,128)S(1)}, u32[]{:S(2)}, u32[]{:S(2)}) collective-permute-start(f32[1,16,1536]{2,1,0:T(8,128)S(1)} %constant_dynamic-slice_fusion.9), channel_id=1, source_target_pairs={{0,2},{1,3},{2,0},{3,1},{4,6},{5,7},{6,4},{7,5},{8,10},{9,11},{10,... | collective-permute-start | bytes 294920 | tf_op jit(solution)/shard_map/ppermute | solution.py:68
  55.5 11.2 %copy-start.7 = (f32[1536]{0:T(1024)S(1)}, f32[1536]{0:T(1024)}, u32[]{:S(2)}) copy-start(f32[1536]{0:T(1024)} %param.10) | copy-start | bytes 18436
  66.6 7.8 %collective-permute-start.15 = (f32[4,192,2]{1,0,2:T(4,128)S(1)}, f32[4,192,2]{1,0,2:T(4,128)S(1)}, u32[]{:S(2)}, u32[]{:S(2)}) collective-permute-start(f32[4,192,2]{1,0,2:T(4,128)S(1)} %bitcast.110), channel_id=1, source_target_pairs={{0,4},{4,0},{8,12},{12,8},{16,20},{20,16},{24,28},{28,24},{1,5},{5... | collective-permute-start | bytes 18440 | tf_op jit(solution)/shard_map/ppermute | solution.py:94
  72.7 3.0 %copy-start.2 = (f32[1536,384]{1,0:T(8,128)}, f32[1536,384]{1,0:T(8,128)S(1)}, u32[]{:S(2)}) copy-start(f32[1536,384]{1,0:T(8,128)S(1)} %fusion.8) | copy-start | bytes 7077892
  73.9 11.7 %collective-permute-start.4 = (f32[4,192,384]{2,1,0:T(8,128)}, f32[4,192,384]{2,1,0:T(8,128)}, u32[]{:S(2)}, u32[]{:S(2)}) collective-permute-start(f32[4,192,384]{2,1,0:T(8,128)} %dynamic-slice_bitcast_fusion), channel_id=1, source_target_pairs={{0,4},{4,0},{8,12},{12,8},{16,20},{20,16},{24,28},{28,24},{1,5},{5... | collective-permute-start | bytes 3538952 | tf_op jit(solution)/shard_map/ppermute | solution.py:94
  75.0 3.9 %collective-permute-start.16 = (f32[2,192,2]{1,2,0:T(2,128)}, f32[2,192,2]{1,2,0:T(2,128)}, u32[]{:S(2)}, u32[]{:S(2)}) collective-permute-start(f32[2,192,2]{1,2,0:T(2,128)} %fusion.61), channel_id=1, source_target_pairs={{0,8},{4,12},{8,0},{12,4},{16,24},{20,28},{24,16},{28,20},{1,9},{5... | collective-permute-start | bytes 9224 | tf_op jit(solution)/shard_map/ppermute | solution.py:94
  79.7 4.5 %collective-permute-start.17 = (f32[1,192,2]{1,2,0:T(2,128)S(1)}, f32[1,192,2]{1,2,0:T(2,128)S(1)}, u32[]{:S(2)}, u32[]{:S(2)}) collective-permute-start(f32[1,192,2]{1,2,0:T(2,128)S(1)} %constant_dynamic-slice_fusion), channel_id=1, source_target_pairs={{0,16},{4,20},{8,24},{12,28},{16,0},{20,4},{24,8},{28,12},{1,17},{... | collective-permute-start | bytes 4616 | tf_op jit(solution)/shard_map/ppermute | solution.py:94
  84.1 11.3 %collective-permute-start.18 = (f32[1,192,2]{1,2,0:T(2,128)S(1)}, f32[1,192,2]{1,2,0:T(2,128)S(1)}, u32[]{:S(2)}, u32[]{:S(2)}) collective-permute-start(f32[1,192,2]{1,2,0:T(2,128)S(1)} %fusion.65), channel_id=1, source_target_pairs={{0,1},{1,0},{2,3},{3,2},{4,5},{5,4},{6,7},{7,6},{8,9},{9,8},{10,11... | collective-permute-start | bytes 4616 | tf_op jit(solution)/shard_map/ppermute | solution.py:79
  91.1 16.6 %copy-start.1 = (f32[4,192,192]{2,1,0:T(8,128)S(1)}, f32[4,192,192]{2,1,0:T(8,128)}, u32[]{:S(2)}) copy-start(f32[4,192,192]{2,1,0:T(8,128)} %get-tuple-element.25) | copy-start | bytes 1769476
  92.2 10.3 %collective-permute-start.9 = (f32[4,192,2,48]{1,3,2,0:T(8,128)S(1)}, f32[4,192,2,48]{1,3,2,0:T(8,128)S(1)}, u32[]{:S(2)}, u32[]{:S(2)}) collective-permute-start(f32[4,192,2,48]{1,3,2,0:T(8,128)S(1)} %dynamic-slice_bitcast_fusion.1), channel_id=1, source_target_pairs={{0,1},{1,0},{2,3},{3,2},{4,5},{5,4},{6,7},{7,6},{8,9},{9,8},{10,11... | collective-permute-start | bytes 884744 | tf_op jit(solution)/shard_map/ppermute | solution.py:94
  95.5 26.9 %collective-permute-start.19 = (f32[1,192,2]{1,2,0:T(2,128)S(1)}, f32[1,192,2]{1,2,0:T(2,128)S(1)}, u32[]{:S(2)}, u32[]{:S(2)}) collective-permute-start(f32[1,192,2]{1,2,0:T(2,128)S(1)} %add.357), channel_id=1, source_target_pairs={{0,2},{1,3},{2,0},{3,1},{4,6},{5,7},{6,4},{7,5},{8,10},{9,11},{10,... | collective-permute-start | bytes 4616 | tf_op jit(solution)/shard_map/ppermute | solution.py:79
  98.0 9.7 %collective-permute-start.5 = (f32[2,192,192]{2,1,0:T(8,128)S(1)}, f32[2,192,192]{2,1,0:T(8,128)S(1)}, u32[]{:S(2)}, u32[]{:S(2)}) collective-permute-start(f32[2,192,192]{2,1,0:T(8,128)S(1)} %dynamic-slice_bitcast_fusion.2), channel_id=1, source_target_pairs={{0,8},{4,12},{8,0},{12,4},{16,24},{20,28},{24,16},{28,20},{1,9},{5... | collective-permute-start | bytes 884744 | tf_op jit(solution)/shard_map/ppermute | solution.py:94
  103.6 5.7 %collective-permute-start.10 = (f32[4,192,1,48]{1,3,2,0:T(8,128)S(1)}, f32[4,192,1,48]{1,3,2,0:T(8,128)S(1)}, u32[]{:S(2)}, u32[]{:S(2)}) collective-permute-start(f32[4,192,1,48]{1,3,2,0:T(8,128)S(1)} %constant_dynamic-slice_fusion.7), channel_id=1, source_target_pairs={{0,2},{1,3},{2,0},{3,1},{4,6},{5,7},{6,4},{7,5},{8,10},{9,11},{10,... | collective-permute-start | bytes 442376 | tf_op jit(solution)/shard_map/ppermute | solution.py:94
  109.4 5.0 %collective-permute-start.11 = (f32[2,192,1,48]{1,3,2,0:T(8,128)S(1)}, f32[2,192,1,48]{1,3,2,0:T(8,128)S(1)}, u32[]{:S(2)}, u32[]{:S(2)}) collective-permute-start(f32[2,192,1,48]{1,3,2,0:T(8,128)S(1)} %dynamic-slice_bitcast_fusion.4), channel_id=1, source_target_pairs={{0,8},{4,12},{8,0},{12,4},{16,24},{20,28},{24,16},{28,20},{1,9},{5... | collective-permute-start | bytes 221192 | tf_op jit(solution)/shard_map/ppermute | solution.py:94
  110.6 9.5 %collective-permute-start.6 = (f32[1,192,192]{2,1,0:T(8,128)S(1)}, f32[1,192,192]{2,1,0:T(8,128)S(1)}, u32[]{:S(2)}, u32[]{:S(2)}) collective-permute-start(f32[1,192,192]{2,1,0:T(8,128)S(1)} %constant_dynamic-slice_fusion.8), channel_id=1, source_target_pairs={{0,16},{4,20},{8,24},{12,28},{16,0},{20,4},{24,8},{28,12},{1,17},{... | collective-permute-start | bytes 442376 | tf_op jit(solution)/shard_map/ppermute | solution.py:94
  114.4 6.8 %collective-permute-start.12 = (f32[1,192,1,48]{1,3,2,0:T(8,128)S(1)}, f32[1,192,1,48]{1,3,2,0:T(8,128)S(1)}, u32[]{:S(2)}, u32[]{:S(2)}) collective-permute-start(f32[1,192,1,48]{1,3,2,0:T(8,128)S(1)} %constant_dynamic-slice_fusion.6), channel_id=1, source_target_pairs={{0,16},{4,20},{8,24},{12,28},{16,0},{20,4},{24,8},{28,12},{1,17},{... | collective-permute-start | bytes 110600 | tf_op jit(solution)/shard_map/ppermute | solution.py:94
  120.2 7.9 %collective-permute-start.7 = (f32[1,192,192]{2,1,0:T(8,128)S(1)}, f32[1,192,192]{2,1,0:T(8,128)S(1)}, u32[]{:S(2)}, u32[]{:S(2)}) collective-permute-start(f32[1,192,192]{2,1,0:T(8,128)S(1)} %dynamic-slice_add_fusion.1), channel_id=1, source_target_pairs={{0,1},{1,0},{2,3},{3,2},{4,5},{5,4},{6,7},{7,6},{8,9},{9,8},{10,11... | collective-permute-start | bytes 442376 | tf_op jit(solution)/shard_map/ppermute | solution.py:79
  121.2 5.2 %collective-permute-start.13 = (f32[1,192,1,48]{1,3,2,0:T(8,128)S(1)}, f32[1,192,1,48]{1,3,2,0:T(8,128)S(1)}, u32[]{:S(2)}, u32[]{:S(2)}) collective-permute-start(f32[1,192,1,48]{1,3,2,0:T(8,128)S(1)} %dynamic-slice_add_fusion.2), channel_id=1, source_target_pairs={{0,1},{1,0},{2,3},{3,2},{4,5},{5,4},{6,7},{7,6},{8,9},{9,8},{10,11... | collective-permute-start | bytes 110600 | tf_op jit(solution)/shard_map/ppermute | solution.py:102
  126.5 4.7 %collective-permute-start.14 = (f32[1,192,2,48]{1,3,2,0:T(8,128)S(1)}, f32[1,192,2,48]{1,3,2,0:T(8,128)S(1)}, u32[]{:S(2)}, u32[]{:S(2)}) collective-permute-start(f32[1,192,2,48]{1,3,2,0:T(8,128)S(1)} %maximum_select_fusion.3), channel_id=1, source_target_pairs={{0,2},{1,3},{2,0},{3,1},{4,6},{5,7},{6,4},{7,5},{8,10},{9,11},{10,... | collective-permute-start | bytes 221192 | tf_op jit(solution)/shard_map/ppermute | solution.py:102
  128.8 6.0 %collective-permute-start.8 = (f32[1,192,192]{2,1,0:T(8,128)}, f32[1,192,192]{2,1,0:T(8,128)}, u32[]{:S(2)}, u32[]{:S(2)}) collective-permute-start(f32[1,192,192]{2,1,0:T(8,128)} %add.348), channel_id=1, source_target_pairs={{0,2},{1,3},{2,0},{3,1},{4,6},{5,7},{6,4},{7,5},{8,10},{9,11},{10,... | collective-permute-start | bytes 442376 | tf_op jit(solution)/shard_map/ppermute | solution.py:79

commit v6 on v2

--- a/solution.py
+++ b/solution.py
@@ -156,10 +156,18 @@
     )
     gain_term = jnp.sum(pixel_gradient * linear_scores, axis=0)
     shift_term = jnp.sum(pixel_gradient, axis=0)
-    side_terms = jnp.stack([gain_term, shift_term], axis=1)
-    head_part, side_part = halving_scatter([head_term, side_terms], "dp")
-    head_sum, side_sum = butterfly_sum([head_part, side_part], "leaf")
-    return (head_sum.T, side_sum[:, 0], side_sum[:, 1], node_grad)
+    e_size = head_term.shape[1]
+    chunk = width // n_dp
+    extra = -(-2 * chunk // e_size)
+    side_rows = jnp.stack([gain_term, shift_term], axis=1).reshape(n_dp, 2 * chunk)
+    side_rows = jnp.pad(side_rows, ((0, 0), (0, extra * e_size - 2 * chunk)))
+    stacked = jnp.concatenate(
+        [head_term.reshape(n_dp, chunk, e_size), side_rows.reshape(n_dp, extra, e_size)], axis=1
+    )
+    (part,) = halving_scatter([stacked], "dp")
+    (total,) = butterfly_sum([part[0]], "leaf")
+    side_sum = total[chunk:].reshape(-1)[: 2 * chunk].reshape(chunk, 2)
+    return (total[:chunk].T, side_sum[:, 0], side_sum[:, 1], node_grad)
 
 
 def solution(mesh):

time: 132 us -> 127 us (0.962); the launches traced: 132 us -> 125 us
  starting transfers between devices: 25.5 us -> 17.9 us
  waiting for transfers between devices: 44.1 us -> 40.3 us
  local copies, waits for them, and re-layouts: 18.9 us -> 21.7 us
  matrix products: 28.9 us -> 30.3 us
    all_to_all x1, waiting for transfers between devices: 11.5 us -> 0.01 us  [shards(): recv = lax.all_to_all(send, 'dp', split_axis=0, concat_axis=0, tiled=True)]
    ppermute x8 -> x5, waiting for transfers between devices: 24.4 us -> 33.4 us  [halving_scatter(): got = lax.ppermute(tuple(give), name, partners(size, bit))]
    ppermute x4 -> x2, starting transfers between devices: 5.21 us -> 2.1 us  [butterfly_sum(): got = lax.ppermute(cur, name, partners(size, bit))]
    ppermute x8 -> x5, starting transfers between devices: 9.96 us -> 7.11 us  [halving_scatter(): got = lax.ppermute(tuple(give), name, partners(size, bit))]
    another operation x0 -> x2, other arithmetic: none -> 1.82 us  [the longest x1 1.8 us: shards(): total, = butterfly_sum([part[0]], 'leaf')]
    reshape x2 -> x0, other arithmetic: 1.8 us -> none  [halving_scatter(): return [c.reshape(c.shape[1:]) for c in cur]]
    all_to_all x1, starting transfers between devices: 5.74 us -> 4.1 us  [shards(): recv = lax.all_to_all(send, 'dp', split_axis=0, concat_axis=0, tiled=True)]
    concatenate x0 -> x1, local copies, waits for them, and re-layouts: none -> 1.59 us  [shards(): jnp.concatenate([head_term.reshape(n_dp, chunk, e_size), side_rows.reshap...]
  transfers between devices with their start and end apart: 15 -> 10, of which waited for: 9 -> 8; matrix products, arithmetic and copies ran while one was open for 16% -> 14% of each run, Pallas kernels for 0% -> 0%
where the time goes in v6:
time: 127 us; the launch traced here: 125 us
  waiting for transfers between devices  40.3 us (32%)
  matrix products  30.3 us (24%)
  local copies, waits for them, and re-layouts  21.7 us (17%)
  starting transfers between devices  17.9 us (14%)
  other arithmetic  13.9 us (11%)
    ppermute x5, waiting for transfers between devices, halving_scatter(): got = lax.ppermute(tuple(give), name, partners(size, bit))  33.4 us
    dot_general x1, matrix products, shards(): jnp.dot(select.T, emb_grad / P_SIZE, precision=HIGHEST, preferred_element...  10.9 us
    ppermute x5, starting transfers between devices, halving_scatter(): got = lax.ppermute(tuple(give), name, partners(size, bit))  7.11 us
    unnamed x43, local copies, waits for them, and re-layouts  6.16 us
    dot_general x1, matrix products, shards(): jnp.dot(select, active, precision=HIGHEST, preferred_element_type=jnp.flo...  5.63 us
    ppermute x2, starting transfers between devices, doubling_gather(): other = lax.ppermute(cur, name, partners(size, bit))  4.58 us
    dot_general x1, matrix products, shards(): jnp.dot(features, head_weight, preferred_element_type=jnp.float32)  4.5 us
    ppermute x2, waiting for transfers between devices, butterfly_sum(): got = lax.ppermute(cur, name, partners(size, bit))  4.47 us
  transfers between devices with their start and end apart: 10, of which 8 were waited for; matrix products, arithmetic and copies ran while one was open for 14% of the time, Pallas kernels for 0%

profile of v6, /device:TPU:0, one launch (start us, length us, event | category | flops | bytes accessed | tf_op | source)
XLA Modules:
  0.0 125.4 jit_solution(9181416868049949678)
XLA Ops:
  0.7 4.5 %fusion.64 = f32[1600,1536]{1,0:T(8,128)S(1)} fusion(bf16[1600,384]{1,0:T(8,128)(2,1)} %param.8, bf16[384,1536]{1,0:T(8,128)(2,1)} %param.9), kind=kOutput, calls=%fused_computation.171 | convolution fusion | flops 1887436800 | bytes 12238848 | tf_op jit(solution)/shard_map/dot_general | solution.py:92
  5.3 5.6 %fusion.15 = bf16[1,16,1536]{2,1,0:T(8,128)(2,1)S(1)} fusion(f32[1600,1536]{1,0:T(8,128)S(1)} %fusion.64, f32[1536]{0:T(1024)S(1)} %copy-done.16, f32[1536]{0:T(1024)S(1)} %copy-done.17, s32[1600]{0:T(1024)S(1)} %add_select_fusion.7), kind=kOutput, calls=%fused_computation.21 | convolution fusion | flops 486679552 | bytes 9898240 | tf_op jit(solution)/shard_map/dot_general | solution.py:96
  10.9 3.0 %collective-permute-start = (bf16[1,16,1536]{2,1,0:T(8,128)(2,1)S(1)}, bf16[1,16,1536]{2,1,0:T(8,128)(2,1)S(1)}, u32[]{:S(2)}, u32[]{:S(2)}) collective-permute-start(bf16[1,16,1536]{2,1,0:T(8,128)(2,1)S(1)} %fusion.15), channel_id=1, source_target_pairs={{0,1},{1,0},{2,3},{3,2},{4,5},{5,4},{6,7},{7,6},{8,9},{9,8},{10,11... | collective-permute-start | bytes 147464 | tf_op jit(solution)/shard_map/ppermute | solution.py:44
  15.7 1.1 fusion.19
  17.9 1.6 %collective-permute-start.1 = (bf16[2,16,1536]{2,1,0:T(8,128)(2,1)S(1)}, bf16[2,16,1536]{2,1,0:T(8,128)(2,1)S(1)}, u32[]{:S(2)}, u32[]{:S(2)}) collective-permute-start(bf16[2,16,1536]{2,1,0:T(8,128)(2,1)S(1)} %maximum_select_fusion.1), channel_id=1, source_target_pairs={{0,2},{1,3},{2,0},{3,1},{4,6},{5,7},{6,4},{7,5},{8,10},{9,11},{10,... | collective-permute-start | bytes 294920 | tf_op jit(solution)/shard_map/ppermute | solution.py:44
  20.1 2.5 %collective-permute-done.1 = bf16[2,16,1536]{2,1,0:T(8,128)(2,1)S(1)} collective-permute-done((bf16[2,16,1536]{2,1,0:T(8,128)(2,1)S(1)}, bf16[2,16,1536]{2,1,0:T(8,128)(2,1)S(1)}, u32[]{:S(2)}, u32[]{:S(2)}) %collective-permute-start.1) | collective-permute-done | bytes 98336 | tf_op jit(solution)/shard_map/ppermute | solution.py:44
  22.6 1.8 %select_reduce_fusion = (f32[64,64]{1,0:T(8,128)S(1)}, f32[64,64]{1,0:T(8,128)S(1)}) fusion(pred[64,16]{0,1:T(8,128)(4,1)S(1)} %iota_compare_fusion.7, pred[64,16]{0,1:T(8,128)(4,1)S(1)} %iota_compare_fusion.8, bf16[64,1536,1]{1,0,2:T(8,128)(2,1)S(1)} %bitcast.76, bf16[16,64,1536]{2,1,0:T(8,128)(2,1)S(1)} %bitcast.66), kind=kOutput, calls=%fused_computation.35 | convolution fusion | flops 201580544 | bytes 3377152 | tf_op jit(solution)/shard_map/dot_general | solution.py:112
  26.4 1.7 %fusion.7 = f32[2,2,16,1536]{3,2,1,0:T(8,128)S(1)} fusion(bf16[1024,1536]{1,0:T(8,128)(2,1)S(1)} %copy-done, bf16[2,2,16,1024]{3,2,1,0:T(8,128)(2,1)} %tile.13, bf16[2,2,16,1024]{3,2,1,0:T(8,128)(2,1)} %tile.15, s32[2,2,16]{2,1,0:T(2,128)} %get-tuple-element.23, s32[2,2,16]{2,1,0:T(2,128)} %get-tuple-element.24, s32[1024]{0:T(1024)} %add_select_fusion.8), kind=kOutput, calls=%fused_computation.15 | convolution fusion | flops 201654272 | bytes 3805696 | tf_op jit(solution)/shard_map/dot_general | solution.py:122
  28.9 5.8 %collective-permute-done.2 = f32[2,16,1536]{2,1,0:T(8,128)} collective-permute-done((f32[2,16,1536]{2,1,0:T(8,128)}, f32[2,16,1536]{2,1,0:T(8,128)}, u32[]{:S(2)}, u32[]{:S(2)}) %collective-permute-start.2) | collective-permute-done | bytes 196640 | tf_op jit(solution)/shard_map/ppermute | solution.py:61
  36.4 1.6 %collective-permute-start.3 = (f32[1,16,1536]{2,1,0:T(8,128)S(1)}, f32[1,16,1536]{2,1,0:T(8,128)S(1)}, u32[]{:S(2)}, u32[]{:S(2)}) collective-permute-start(f32[1,16,1536]{2,1,0:T(8,128)S(1)} %constant_dynamic-slice_fusion.1), channel_id=1, source_target_pairs={{0,2},{1,3},{2,0},{3,1},{4,6},{5,7},{6,4},{7,5},{8,10},{9,11},{10,... | collective-permute-start | bytes 294920 | tf_op jit(solution)/shard_map/ppermute | solution.py:61
  38.0 3.1 %collective-permute-done.3 = f32[1,16,1536]{2,1,0:T(8,128)S(1)} collective-permute-done((f32[1,16,1536]{2,1,0:T(8,128)S(1)}, f32[1,16,1536]{2,1,0:T(8,128)S(1)}, u32[]{:S(2)}, u32[]{:S(2)}) %collective-permute-start.3) | collective-permute-done | bytes 98336 | tf_op jit(solution)/shard_map/ppermute | solution.py:61
  41.1 10.9 %multiply_reduce_fusion = (f32[1536]{0:T(1024)S(1)}, f32[1536]{0:T(1024)S(1)}, f32[1600,1536]{1,0:T(8,128)S(1)}) fusion(f32[1600,1536]{1,0:T(8,128)} %copy-done.1, f32[1536]{0:T(1024)} %param.11, f32[1536]{0:T(1024)} %param.10, f32[1,16,1536]{2,1,0:T(8,128)S(1)} %collective-permute-done.3, f32[2,16,1536]{2,1,0:T(8,128)} %copy-done.6, s32[]{:T(128)S(6)} %select_n.411, ...), kind=kOutput, calls=%fused_computation.1 | convolution fusion | flops 503879680 | bytes 19894276 | tf_op jit(solution)/shard_map/dot_general | solution.py:151
  52.0 4.5 %fusion.2 = f32[1536,384]{1,0:T(8,128)} fusion(bf16[1600,384]{1,0:T(8,128)(2,1)S(1)} %copy-done.4, f32[1600,1536]{1,0:T(8,128)S(1)} %get-tuple-element.22, f32[1536]{0:T(1024)S(1)} %copy-done.18), kind=kOutput, calls=%fused_computation.8 | convolution fusion | flops 1892352000 | bytes 13424640 | tf_op jit(solution)/shard_map/dot_general | solution.py:154
  56.5 1.2 copy.68
  57.7 1.6 %concatenate.35 = f32[4,2,1,1,384]{4,3,1,0,2:T(1,128)S(1)} reshape(f32[1536,2]{1,0:T(8,128)} %copy.68) | data formatting | bytes 24576 | tf_op jit(solution)/shard_map/concatenate | solution.py:164
  59.3 1.4 %fusion.20 = f32[4,1,1,193,384]{4,3,1,0,2:T(8,128)S(1)} fusion(s32[]{:T(128)S(6)} %select_n.415, f32[4,2,1,192,384]{4,3,1,0,2:T(8,128)} %bitcast.67, f32[4,2,1,1,384]{4,3,1,0,2:T(1,128)S(1)} %concatenate.35), kind=kLoop, calls=%fused_computation.27 | loop fusion | flops 296448 | bytes 3557380 | tf_op jit(solution)/shard_map/concatenate | solution.py:164
  60.6 1.4 %copy.96 = f32[4,1,1,193,384]{4,0,3,2,1:T(4,128)} copy(f32[4,1,1,193,384]{4,3,1,0,2:T(8,128)S(1)} %fusion.20) | data formatting | bytes 2371584 | tf_op jit(solution)/shard_map/jit(dynamic_index_in_dim)/dynamic_slice | solution.py:60
  62.0 3.2 %collective-permute-done.4 = f32[4,1,193,384]{3,0,2,1:T(4,128)} collective-permute-done((f32[4,1,193,384]{3,0,2,1:T(4,128)}, f32[4,1,193,384]{3,0,2,1:T(4,128)}, u32[]{:S(2)}, u32[]{:S(2)}) %collective-permute-start.4) | collective-permute-done | bytes 1185824 | tf_op jit(solution)/shard_map/ppermute | solution.py:61
  65.2 1.8 %fusion.23 = f32[4,1,193,384]{3,2,0,1:T(8,128)S(1)} fusion(s32[]{:T(128)S(6)} %select_n.414, f32[4,2,1,192,384]{4,3,1,0,2:T(8,128)} %bitcast.68, f32[4,2,1,1,384]{4,3,1,0,2:T(1,128)S(1)} %concatenate.35, f32[4,1,193,384]{3,0,2,1:T(4,128)} %collective-permute-done.4), kind=kLoop, calls=%fused_computation.30 | loop fusion | flops 592896 | bytes 4743172 | tf_op jit(solution)/shard_map/add | solution.py:62
  68.0 1.1 copy.72
  69.1 1.6 %collective-permute-start.5 = (f32[2,1,193,384]{3,0,2,1:T(2,128)}, f32[2,1,193,384]{3,0,2,1:T(2,128)}, u32[]{:S(2)}, u32[]{:S(2)}) collective-permute-start(f32[2,1,193,384]{3,0,2,1:T(2,128)} %copy.72), channel_id=1, source_target_pairs={{0,8},{4,12},{8,0},{12,4},{16,24},{20,28},{24,16},{28,20},{1,9},{5... | collective-permute-start | bytes 1778696 | tf_op jit(solution)/shard_map/ppermute | solution.py:61
  71.0 1.2 select_n.425
  73.3 4.1 %all-to-all-start = ((bf16[8,64,322]{2,1,0:T(8,128)(2,1)}), bf16[8,64,322]{2,1,0:T(8,128)(2,1)}, u32[]{:S(2)}, u32[]{:S(2)}) async-start(bf16[8,64,322]{2,1,0:T(8,128)(2,1)} %pad_maximum_fusion), calls=%async_computation | async-start | bytes 786432 | tf_op jit(solution)/shard_map/all_to_all | solution.py:139
  77.4 10.4 %collective-permute-done.5 = f32[2,1,193,384]{3,0,2,1:T(2,128)} collective-permute-done((f32[2,1,193,384]{3,0,2,1:T(2,128)}, f32[2,1,193,384]{3,0,2,1:T(2,128)}, u32[]{:S(2)}, u32[]{:S(2)}) %collective-permute-start.5) | collective-permute-done | bytes 592928 | tf_op jit(solution)/shard_map/ppermute | solution.py:61
  87.8 1.3 %bitcast_add_fusion = f32[2,1,193,384]{3,2,0,1:T(8,128)S(1)} fusion(f32[2,1,193,384]{3,0,2,1:T(2,128)} %collective-permute-done.5, f32[2,2,1,193,384]{4,3,1,0,2:T(8,128)} %bitcast.70, s32[]{:T(128)S(6)} %select_n.418), kind=kLoop, calls=%fused_computation.33 | loop fusion | flops 148224 | bytes 1778692 | tf_op jit(solution)/shard_map/add | solution.py:62
  90.7 3.8 %collective-permute-start.6 = (f32[1,1,193,384]{3,2,0,1:T(8,128)}, f32[1,1,193,384]{3,2,0,1:T(8,128)}, u32[]{:S(2)}, u32[]{:S(2)}) collective-permute-start(f32[1,1,193,384]{3,2,0,1:T(8,128)} %constant_dynamic-slice_fusion), channel_id=1, source_target_pairs={{0,16},{4,20},{8,24},{12,28},{16,0},{20,4},{24,8},{28,12},{1,17},{... | collective-permute-start | bytes 889352 | tf_op jit(solution)/shard_map/ppermute | solution.py:61
  95.6 10.8 %collective-permute-done.6 = f32[1,1,193,384]{3,2,0,1:T(8,128)} collective-permute-done((f32[1,1,193,384]{3,2,0,1:T(8,128)}, f32[1,1,193,384]{3,2,0,1:T(8,128)}, u32[]{:S(2)}, u32[]{:S(2)}) %collective-permute-start.6) | collective-permute-done | bytes 296480 | tf_op jit(solution)/shard_map/ppermute | solution.py:61
  106.4 1.8 %add_bitcast_fusion = f32[193,384]{1,0:T(8,128)} fusion(f32[1,1,193,384]{3,2,0,1:T(8,128)} %collective-permute-done.6, f32[2,1,193,384]{3,2,0,1:T(8,128)} %copy-done.3, s32[]{:T(128)S(6)} %select_n.422), kind=kLoop, calls=%fused_computation.41 | loop fusion | flops 74112 | bytes 889348 | tf_op jit(solution)/shard_map/squeeze;reshape | solution.py:168
  113.6 2.1 %collective-permute-done.7 = f32[193,384]{1,0:T(8,128)} collective-permute-done((f32[193,384]{1,0:T(8,128)}, f32[193,384]{1,0:T(8,128)}, u32[]{:S(2)}, u32[]{:S(2)}) %collective-permute-start.7) | collective-permute-done | bytes 296480 | tf_op jit(solution)/shard_map/ppermute | solution.py:72
  116.8 1.6 %collective-permute-start.8 = (f32[193,384]{1,0:T(8,128)S(1)}, f32[193,384]{1,0:T(8,128)S(1)}, u32[]{:S(2)}, u32[]{:S(2)}) collective-permute-start(f32[193,384]{1,0:T(8,128)S(1)} %add.289), channel_id=1, source_target_pairs={{0,2},{1,3},{2,0},{3,1},{4,6},{5,7},{6,4},{7,5},{8,10},{9,11},{10,... | collective-permute-start | bytes 889352 | tf_op jit(solution)/shard_map/ppermute | solution.py:72
  119.9 1.4 %fusion.65 = f32[1024,192]{0,1:T(8,128)} fusion(bf16[512,1024]{0,1:T(8,128)(2,1)S(1)} %bitcast.71, bf16[512,192]{1,0:T(8,128)(2,1)S(1)} %bitcast.75), kind=kOutput, calls=%fused_computation.172 | convolution fusion | flops 201326592 | bytes 2031616 | tf_op jit(solution)/shard_map/dot_general | solution.py:147
  121.3 2.4 %collective-permute-done.8 = f32[193,384]{1,0:T(8,128)S(1)} collective-permute-done((f32[193,384]{1,0:T(8,128)S(1)}, f32[193,384]{1,0:T(8,128)S(1)}, u32[]{:S(2)}, u32[]{:S(2)}) %collective-permute-start.8) | collective-permute-done | bytes 296480 | tf_op jit(solution)/shard_map/ppermute | solution.py:72
  (108 shorter events, 22.5 us)
Async XLA Ops:
  0.6 22.0 %copy-start = (bf16[1024,1536]{1,0:T(8,128)(2,1)S(1)}, bf16[1024,1536]{1,0:T(8,128)(2,1)}, u32[]{:S(2)}) copy-start(bf16[1024,1536]{1,0:T(8,128)(2,1)} %param.12) | copy-start | bytes 9437188
  0.7 4.5 %copy-start.14 = (s32[1600]{0:T(1024)}, s32[1600]{0:T(1024)S(1)}, u32[]{:S(2)}) copy-start(s32[1600]{0:T(1024)S(1)} %add_select_fusion.7) | copy-start | bytes 19204
  0.7 4.5 %copy-start.16 = (f32[1536]{0:T(1024)S(1)}, f32[1536]{0:T(1024)}, u32[]{:S(2)}) copy-start(f32[1536]{0:T(1024)} %param.11) | copy-start | bytes 18436
  0.7 4.5 %copy-start.17 = (f32[1536]{0:T(1024)S(1)}, f32[1536]{0:T(1024)}, u32[]{:S(2)}) copy-start(f32[1536]{0:T(1024)} %param.10) | copy-start | bytes 18436
  5.2 5.7 %copy-start.1 = (f32[1600,1536]{1,0:T(8,128)}, f32[1600,1536]{1,0:T(8,128)S(1)}, u32[]{:S(2)}) copy-start(f32[1600,1536]{1,0:T(8,128)S(1)} %fusion.64) | copy-start | bytes 29491204
  5.2 8.7 %copy-start.9 = (s32[64,64]{1,0:T(8,128)S(1)}, s32[64,64]{1,0:T(8,128)}, u32[]{:S(2)}) copy-start(s32[64,64]{1,0:T(8,128)} %param.14) | copy-start | bytes 49156
  5.3 9.4 %copy-start.15 = (s32[64]{0:T(128)S(1)}, s32[64]{0:T(128)}, u32[]{:S(2)}) copy-start(s32[64]{0:T(128)} %param.13) | copy-start | bytes 772
  10.9 6.9 %collective-permute-start = (bf16[1,16,1536]{2,1,0:T(8,128)(2,1)S(1)}, bf16[1,16,1536]{2,1,0:T(8,128)(2,1)S(1)}, u32[]{:S(2)}, u32[]{:S(2)}) collective-permute-start(bf16[1,16,1536]{2,1,0:T(8,128)(2,1)S(1)} %fusion.15), channel_id=1, source_target_pairs={{0,1},{1,0},{2,3},{3,2},{4,5},{5,4},{6,7},{7,6},{8,9},{9,8},{10,11... | collective-permute-start | bytes 147464 | tf_op jit(solution)/shard_map/ppermute | solution.py:44
  14.8 0.5 copy-start.10
  14.8 0.5 copy-start.12
  17.9 4.7 %collective-permute-start.1 = (bf16[2,16,1536]{2,1,0:T(8,128)(2,1)S(1)}, bf16[2,16,1536]{2,1,0:T(8,128)(2,1)S(1)}, u32[]{:S(2)}, u32[]{:S(2)}) collective-permute-start(bf16[2,16,1536]{2,1,0:T(8,128)(2,1)S(1)} %maximum_select_fusion.1), channel_id=1, source_target_pairs={{0,2},{1,3},{2,0},{3,1},{4,6},{5,7},{6,4},{7,5},{8,10},{9,11},{10,... | collective-permute-start | bytes 294920 | tf_op jit(solution)/shard_map/ppermute | solution.py:44
  22.6 1.8 %copy-start.5 = (bf16[4,16,1536]{2,1,0:T(8,128)(2,1)}, bf16[4,16,1536]{2,1,0:T(8,128)(2,1)S(1)}, u32[]{:S(2)}) copy-start(bf16[4,16,1536]{2,1,0:T(8,128)(2,1)S(1)} %maximum_select_fusion) | copy-start | bytes 589828
  25.5 0.9 copy-start.7
  28.8 6.0 %collective-permute-start.2 = (f32[2,16,1536]{2,1,0:T(8,128)}, f32[2,16,1536]{2,1,0:T(8,128)}, u32[]{:S(2)}, u32[]{:S(2)}) collective-permute-start(f32[2,16,1536]{2,1,0:T(8,128)} %dynamic-slice_bitcast_fusion.1), channel_id=1, source_target_pairs={{0,1},{1,0},{2,3},{3,2},{4,5},{5,4},{6,7},{7,6},{8,9},{9,8},{10,11... | collective-permute-start | bytes 589832 | tf_op jit(solution)/shard_map/ppermute | solution.py:61
  35.7 0.7 copy-start.6
  36.4 4.7 %collective-permute-start.3 = (f32[1,16,1536]{2,1,0:T(8,128)S(1)}, f32[1,16,1536]{2,1,0:T(8,128)S(1)}, u32[]{:S(2)}, u32[]{:S(2)}) collective-permute-start(f32[1,16,1536]{2,1,0:T(8,128)S(1)} %constant_dynamic-slice_fusion.1), channel_id=1, source_target_pairs={{0,2},{1,3},{2,0},{3,1},{4,6},{5,7},{6,4},{7,5},{8,10},{9,11},{10,... | collective-permute-start | bytes 294920 | tf_op jit(solution)/shard_map/ppermute | solution.py:61
  38.0 14.0 %copy-start.4 = (bf16[1600,384]{1,0:T(8,128)(2,1)S(1)}, bf16[1600,384]{1,0:T(8,128)(2,1)}, u32[]{:S(2)}) copy-start(bf16[1600,384]{1,0:T(8,128)(2,1)} %param.8) | copy-start | bytes 3686404
  38.0 14.0 %copy-start.18 = (f32[1536]{0:T(1024)S(1)}, f32[1536]{0:T(1024)}, u32[]{:S(2)}) copy-start(f32[1536]{0:T(1024)} %param.10) | copy-start | bytes 18436
  62.0 3.2 %collective-permute-start.4 = (f32[4,1,193,384]{3,0,2,1:T(4,128)}, f32[4,1,193,384]{3,0,2,1:T(4,128)}, u32[]{:S(2)}, u32[]{:S(2)}) collective-permute-start(f32[4,1,193,384]{3,0,2,1:T(4,128)} %bitcast.64), channel_id=1, source_target_pairs={{0,4},{4,0},{8,12},{12,8},{16,20},{20,16},{24,28},{28,24},{1,5},{5... | collective-permute-start | bytes 3557384 | tf_op jit(solution)/shard_map/ppermute | solution.py:61
  62.0 8.8 %copy-start.13 = (s32[64]{0:T(128)S(1)}, s32[64]{0:T(128)}, u32[]{:S(2)}) copy-start(s32[64]{0:T(128)} %copy-done.12) | copy-start | bytes 772
  62.0 8.8 %copy-start.11 = (s32[64]{0:T(128)S(1)}, s32[64]{0:T(128)}, u32[]{:S(2)}) copy-start(s32[64]{0:T(128)} %copy-done.10) | copy-start | bytes 772
  62.0 10.2 %copy-start.8 = (bf16[64,64]{1,0:T(8,128)(2,1)S(1)}, bf16[64,64]{1,0:T(8,128)(2,1)}, u32[]{:S(2)}) copy-start(bf16[64,64]{1,0:T(8,128)(2,1)} %copy-done.7) | copy-start | bytes 24580
  66.9 1.0 copy-start.2
  69.1 18.7 %collective-permute-start.5 = (f32[2,1,193,384]{3,0,2,1:T(2,128)}, f32[2,1,193,384]{3,0,2,1:T(2,128)}, u32[]{:S(2)}, u32[]{:S(2)}) collective-permute-start(f32[2,1,193,384]{3,0,2,1:T(2,128)} %copy.72), channel_id=1, source_target_pairs={{0,8},{4,12},{8,0},{12,4},{16,24},{20,28},{24,16},{28,20},{1,9},{5... | collective-permute-start | bytes 1778696 | tf_op jit(solution)/shard_map/ppermute | solution.py:61
  73.3 21.2 %all-to-all-start = ((bf16[8,64,322]{2,1,0:T(8,128)(2,1)}), bf16[8,64,322]{2,1,0:T(8,128)(2,1)}, u32[]{:S(2)}, u32[]{:S(2)}) async-start(bf16[8,64,322]{2,1,0:T(8,128)(2,1)} %pad_maximum_fusion), calls=%async_computation | async-start | bytes 786432 | tf_op jit(solution)/shard_map/all_to_all | solution.py:139
  89.1 0.8 copy-start.3
  90.7 15.7 %collective-permute-start.6 = (f32[1,1,193,384]{3,2,0,1:T(8,128)}, f32[1,1,193,384]{3,2,0,1:T(8,128)}, u32[]{:S(2)}, u32[]{:S(2)}) collective-permute-start(f32[1,1,193,384]{3,2,0,1:T(8,128)} %constant_dynamic-slice_fusion), channel_id=1, source_target_pairs={{0,16},{4,20},{8,24},{12,28},{16,0},{20,4},{24,8},{28,12},{1,17},{... | collective-permute-start | bytes 889352 | tf_op jit(solution)/shard_map/ppermute | solution.py:61
  108.2 7.4 %collective-permute-start.7 = (f32[193,384]{1,0:T(8,128)}, f32[193,384]{1,0:T(8,128)}, u32[]{:S(2)}, u32[]{:S(2)}) collective-permute-start(f32[193,384]{1,0:T(8,128)} %add_bitcast_fusion), channel_id=1, source_target_pairs={{0,1},{1,0},{2,3},{3,2},{4,5},{5,4},{6,7},{7,6},{8,9},{9,8},{10,11... | collective-permute-start | bytes 889352 | tf_op jit(solution)/shard_map/ppermute | solution.py:72
  116.8 6.9 %collective-permute-start.8 = (f32[193,384]{1,0:T(8,128)S(1)}, f32[193,384]{1,0:T(8,128)S(1)}, u32[]{:S(2)}, u32[]{:S(2)}) collective-permute-start(f32[193,384]{1,0:T(8,128)S(1)} %add.289), channel_id=1, source_target_pairs={{0,2},{1,3},{2,0},{3,1},{4,6},{5,7},{6,4},{7,5},{8,10},{9,11},{10,... | collective-permute-start | bytes 889352 | tf_op jit(solution)/shard_map/ppermute | solution.py:72

commit v7 on v6

--- a/solution.py
+++ b/solution.py
@@ -137,6 +137,7 @@
         [column_chunks, jnp.broadcast_to(compact[None], (n_dp,) + compact.shape)], axis=2
     )
     recv = lax.all_to_all(send, "dp", split_axis=0, concat_axis=0, tiled=True)
+    recv, emb_grad = lax.optimization_barrier((recv, emb_grad))
     columns = recv[:, :, :col_width].reshape(n_dp * group, col_width)
     info = recv[:, :, col_width:].reshape(n_dp * group, compact.shape[1])
     all_pos = info[:, :SUB_SIZE]

time: 127 us -> 145 us (1.14)
  waiting for transfers between devices: 40.3 us -> 48.9 us
  local copies, waits for them, and re-layouts: 21.7 us -> 27.8 us
  other arithmetic: 13.9 us -> 19 us
  starting transfers between devices: 17.9 us -> 15.2 us
  matrix products: 30.3 us -> 31.8 us
    ppermute x5, starting transfers between devices: 7.11 us -> 2.14 us  [halving_scatter(): got = lax.ppermute(tuple(give), name, partners(size, bit))]
    ppermute x5, waiting for transfers between devices: 33.4 us -> 37.5 us  [halving_scatter(): got = lax.ppermute(tuple(give), name, partners(size, bit))]
    all_to_all x1, waiting for transfers between devices: 0.01 us -> 3.06 us  [shards(): recv = lax.all_to_all(send, 'dp', split_axis=0, concat_axis=0, tiled=True)]
    unnamed x43, local copies, waits for them, and re-layouts: 6.16 us -> 9.19 us
    another operation x2, local copies, waits for them, and re-layouts: 0.9 us -> 2.54 us  [block_table(): neg_wide = jnp.tile(neg_vec, (1, blocks))]
    reshape x0 -> x1, other arithmetic: none -> 1.59 us  [halving_scatter(): return [c.reshape(c.shape[1:]) for c in cur]]
    dot_general x1, matrix products: 1.81 us -> 3.34 us  [shards(): lax.dot_general(grouped, node_weights, (((1,), (1,)), ((), ())), preferre...]
where the time goes in v7:
time: 145 us; the launch traced here: 144 us
  waiting for transfers between devices  48.9 us (34%)
  matrix products  31.8 us (22%)
  local copies, waits for them, and re-layouts  27.8 us (19%)
  other arithmetic  19 us (13%)
  starting transfers between devices  15.2 us (10%)
    ppermute x5, waiting for transfers between devices, halving_scatter(): got = lax.ppermute(tuple(give), name, partners(size, bit))  37.5 us
    dot_general x1, matrix products, shards(): jnp.dot(select.T, emb_grad / P_SIZE, precision=HIGHEST, preferred_element...  10.9 us
    unnamed x43, local copies, waits for them, and re-layouts  9.19 us
    ppermute x2, waiting for transfers between devices, butterfly_sum(): got = lax.ppermute(cur, name, partners(size, bit))  5.76 us
    dot_general x1, matrix products, shards(): jnp.dot(select, active, precision=HIGHEST, preferred_element_type=jnp.flo...  5.64 us
    all_to_all x1, starting transfers between devices, shards(): recv = lax.all_to_all(send, 'dp', split_axis=0, concat_axis=0, tiled=True)  5.37 us
    ppermute x2, starting transfers between devices, doubling_gather(): other = lax.ppermute(cur, name, partners(size, bit))  4.58 us
    dot_general x1, matrix products, shards(): jnp.dot(features, head_weight, preferred_element_type=jnp.float32)  4.5 us
  transfers between devices with their start and end apart: 10, of which 8 were waited for; matrix products, arithmetic and copies ran while one was open for 14% of the time, Pallas kernels for 0%

profile of v7, /device:TPU:0, one launch (start us, length us, event | category | flops | bytes accessed | tf_op | source)
XLA Modules:
  0.0 143.7 jit_solution(9484194451069173363)
XLA Ops:
  0.7 4.5 %fusion.60 = f32[1600,1536]{1,0:T(8,128)S(1)} fusion(bf16[1600,384]{1,0:T(8,128)(2,1)} %param.8, bf16[384,1536]{1,0:T(8,128)(2,1)} %param.9), kind=kOutput, calls=%fused_computation.168 | convolution fusion | flops 1887436800 | bytes 12238848 | tf_op jit(solution)/shard_map/dot_general | solution.py:92
  5.3 5.6 %fusion.15 = bf16[1,16,1536]{2,1,0:T(8,128)(2,1)S(1)} fusion(f32[1600,1536]{1,0:T(8,128)S(1)} %fusion.60, f32[1536]{0:T(1024)S(1)} %copy-done.16, f32[1536]{0:T(1024)S(1)} %copy-done.17, s32[1600]{0:T(1024)S(1)} %add_select_fusion.7), kind=kOutput, calls=%fused_computation.21 | convolution fusion | flops 486679552 | bytes 9898240 | tf_op jit(solution)/shard_map/dot_general | solution.py:96
  10.9 3.0 %collective-permute-start = (bf16[1,16,1536]{2,1,0:T(8,128)(2,1)S(1)}, bf16[1,16,1536]{2,1,0:T(8,128)(2,1)S(1)}, u32[]{:S(2)}, u32[]{:S(2)}) collective-permute-start(bf16[1,16,1536]{2,1,0:T(8,128)(2,1)S(1)} %fusion.15), channel_id=1, source_target_pairs={{0,1},{1,0},{2,3},{3,2},{4,5},{5,4},{6,7},{7,6},{8,9},{9,8},{10,11... | collective-permute-start | bytes 147464 | tf_op jit(solution)/shard_map/ppermute | solution.py:44
  16.8 1.7 %fusion.19 = pred[64,64]{1,0:T(8,128)(4,1)} fusion(s32[64,48]{1,0:T(8,128)S(1)} %copy.67, pred[64,48]{1,0:T(8,128)(4,1)S(1)} %copy.68), kind=kLoop, calls=%fused_computation.26 | loop fusion | flops 585728 | bytes 19456 | tf_op jit(solution)/shard_map/reduce_or | solution.py:31
  19.5 1.6 %collective-permute-start.1 = (bf16[2,16,1536]{2,1,0:T(8,128)(2,1)S(1)}, bf16[2,16,1536]{2,1,0:T(8,128)(2,1)S(1)}, u32[]{:S(2)}, u32[]{:S(2)}) collective-permute-start(bf16[2,16,1536]{2,1,0:T(8,128)(2,1)S(1)} %maximum_select_fusion.1), channel_id=1, source_target_pairs={{0,2},{1,3},{2,0},{3,1},{4,6},{5,7},{6,4},{7,5},{8,10},{9,11},{10,... | collective-permute-start | bytes 294920 | tf_op jit(solution)/shard_map/ppermute | solution.py:44
  21.7 2.5 %collective-permute-done.1 = bf16[2,16,1536]{2,1,0:T(8,128)(2,1)S(1)} collective-permute-done((bf16[2,16,1536]{2,1,0:T(8,128)(2,1)S(1)}, bf16[2,16,1536]{2,1,0:T(8,128)(2,1)S(1)}, u32[]{:S(2)}, u32[]{:S(2)}) %collective-permute-start.1) | collective-permute-done | bytes 98336 | tf_op jit(solution)/shard_map/ppermute | solution.py:44
  26.9 3.3 %select_reduce_fusion.1 = (f32[64,64]{1,0:T(8,128)S(1)}, f32[64,64]{1,0:T(8,128)}) fusion(pred[64,16]{0,1:T(8,128)(4,1)S(1)} %iota_compare_fusion.8, pred[64,16]{0,1:T(8,128)(4,1)S(1)} %iota_compare_fusion.7, bf16[64,1536,1]{1,0,2:T(8,128)(2,1)} %bitcast.73, bf16[16,64,1536]{2,1,0:T(8,128)(2,1)S(1)} %bitcast.63), kind=kOutput, calls=%fused_computation.36 | convolution fusion | flops 201580544 | bytes 3377152 | tf_op jit(solution)/shard_map/dot_general | solution.py:112
  34.4 1.8 %tile.15 = bf16[2,2,16,1024]{3,2,1,0:T(8,128)(2,1)} reshape(bf16[64,16,64]{2,1,0:T(8,128)(2,1)} %tile.14) | data formatting | bytes 262144 | tf_op jit(solution)/shard_map/tile | solution.py:15
  36.2 1.6 %fusion.7 = f32[2,2,16,1536]{3,2,1,0:T(8,128)S(1)} fusion(bf16[1024,1536]{1,0:T(8,128)(2,1)S(1)} %copy-done, bf16[2,2,16,1024]{3,2,1,0:T(8,128)(2,1)S(1)} %tile.13, bf16[2,2,16,1024]{3,2,1,0:T(8,128)(2,1)} %tile.15, s32[2,2,16]{2,1,0:T(2,128)} %get-tuple-element.27, s32[2,2,16]{2,1,0:T(2,128)} %get-tuple-element.28, s32[1024]{0:T(1024)} %add_select_fusion.8), kind=kOutput, calls=%fused_computation.15 | convolution fusion | flops 201654272 | bytes 3805696 | tf_op jit(solution)/shard_map/dot_general | solution.py:122
  40.3 5.4 %all-to-all-start = ((bf16[8,64,322]{2,1,0:T(8,128)(2,1)}), bf16[8,64,322]{2,1,0:T(8,128)(2,1)S(1)}, u32[]{:S(2)}, u32[]{:S(2)}) async-start(bf16[8,64,322]{2,1,0:T(8,128)(2,1)} %pad_maximum_fusion), calls=%async_computation | async-start | bytes 786432 | tf_op jit(solution)/shard_map/all_to_all | solution.py:139
  48.1 1.5 %collective-permute-start.3 = (f32[1,16,1536]{2,1,0:T(8,128)}, f32[1,16,1536]{2,1,0:T(8,128)}, u32[]{:S(2)}, u32[]{:S(2)}) collective-permute-start(f32[1,16,1536]{2,1,0:T(8,128)} %constant_dynamic-slice_fusion.1), channel_id=1, source_target_pairs={{0,2},{1,3},{2,0},{3,1},{4,6},{5,7},{6,4},{7,5},{8,10},{9,11},{10,... | collective-permute-start | bytes 294920 | tf_op jit(solution)/shard_map/ppermute | solution.py:61
  49.6 4.0 %collective-permute-done.3 = f32[1,16,1536]{2,1,0:T(8,128)} collective-permute-done((f32[1,16,1536]{2,1,0:T(8,128)}, f32[1,16,1536]{2,1,0:T(8,128)}, u32[]{:S(2)}, u32[]{:S(2)}) %collective-permute-start.3) | collective-permute-done | bytes 98336 | tf_op jit(solution)/shard_map/ppermute | solution.py:61
  53.6 1.6 %add_bitcast_fusion.1 = f32[16,1536]{1,0:T(8,128)} fusion(f32[1,16,1536]{2,1,0:T(8,128)} %collective-permute-done.3, f32[2,16,1536]{2,1,0:T(8,128)} %copy-done.8, s32[]{:T(128)S(6)} %select_n.418), kind=kLoop, calls=%fused_computation.60 | loop fusion | flops 24576 | bytes 294916 | tf_op jit(solution)/shard_map/reshape | solution.py:64
  55.2 3.1 %all-to-all-done = bf16[8,64,322]{2,1,0:T(8,128)(2,1)S(1)} async-done(((bf16[8,64,322]{2,1,0:T(8,128)(2,1)}), bf16[8,64,322]{2,1,0:T(8,128)(2,1)S(1)}, u32[]{:S(2)}, u32[]{:S(2)}) %all-to-all-start) | async-done | bytes 329760 | tf_op jit(solution)/shard_map/all_to_all | solution.py:139
  58.3 10.9 %multiply_reduce_fusion = (f32[1536]{0:T(1024)S(1)}, f32[1536]{0:T(1024)S(1)}, f32[1600,1536]{1,0:T(8,128)S(1)}) fusion(f32[1600,1536]{1,0:T(8,128)} %copy-done.1, f32[1536]{0:T(1024)} %param.11, f32[1536]{0:T(1024)} %param.10, f32[16,1536]{1,0:T(8,128)} %add_bitcast_fusion.1, s32[1600]{0:T(1024)} %copy-done.14), kind=kOutput, calls=%fused_computation.1 | convolution fusion | flops 503855104 | bytes 19790080 | tf_op jit(solution)/shard_map/dot_general | solution.py:152
  69.2 4.5 %fusion.2 = f32[1536,384]{1,0:T(8,128)} fusion(bf16[1600,384]{1,0:T(8,128)(2,1)S(1)} %copy-done.6, f32[1600,1536]{1,0:T(8,128)S(1)} %get-tuple-element.26, f32[1536]{0:T(1024)S(1)} %copy-done.18), kind=kOutput, calls=%fused_computation.8 | convolution fusion | flops 1892352000 | bytes 13424640 | tf_op jit(solution)/shard_map/dot_general | solution.py:155
  74.8 1.6 %concatenate.35 = f32[4,2,1,1,384]{4,3,1,0,2:T(1,128)S(1)} reshape(f32[1536,2]{1,0:T(8,128)} %copy.77) | data formatting | bytes 24576 | tf_op jit(solution)/shard_map/concatenate | solution.py:165
  76.4 1.4 fusion.20
  77.8 1.3 copy.96
  79.2 3.2 %collective-permute-done.4 = f32[4,1,193,384]{3,0,2,1:T(4,128)} collective-permute-done((f32[4,1,193,384]{3,0,2,1:T(4,128)}, f32[4,1,193,384]{3,0,2,1:T(4,128)}, u32[]{:S(2)}, u32[]{:S(2)}) %collective-permute-start.4) | collective-permute-done | bytes 1185824 | tf_op jit(solution)/shard_map/ppermute | solution.py:61
  82.4 1.8 %fusion.23 = f32[4,1,193,384]{3,2,0,1:T(8,128)S(1)} fusion(s32[]{:T(128)S(6)} %select_n.421, f32[4,2,1,192,384]{4,3,1,0,2:T(8,128)} %bitcast.65, f32[4,2,1,1,384]{4,3,1,0,2:T(1,128)S(1)} %concatenate.35, f32[4,1,193,384]{3,0,2,1:T(4,128)} %collective-permute-done.4), kind=kLoop, calls=%fused_computation.30 | loop fusion | flops 592896 | bytes 4743172 | tf_op jit(solution)/shard_map/add | solution.py:62
  86.3 15.7 %collective-permute-done.5 = f32[2,1,193,384]{3,0,2,1:T(2,128)} collective-permute-done((f32[2,1,193,384]{3,0,2,1:T(2,128)}, f32[2,1,193,384]{3,0,2,1:T(2,128)}, u32[]{:S(2)}, u32[]{:S(2)}) %collective-permute-start.5) | collective-permute-done | bytes 592928 | tf_op jit(solution)/shard_map/ppermute | solution.py:61
  102.1 1.3 bitcast_add_fusion
  106.7 14.6 %collective-permute-done.6 = f32[1,1,193,384]{3,2,0,1:T(8,128)} collective-permute-done((f32[1,1,193,384]{3,2,0,1:T(8,128)}, f32[1,1,193,384]{3,2,0,1:T(8,128)}, u32[]{:S(2)}, u32[]{:S(2)}) %collective-permute-start.6) | collective-permute-done | bytes 296480 | tf_op jit(solution)/shard_map/ppermute | solution.py:61
  121.3 1.8 %add_bitcast_fusion = f32[193,384]{1,0:T(8,128)} fusion(f32[1,1,193,384]{3,2,0,1:T(8,128)} %collective-permute-done.6, f32[2,1,193,384]{3,2,0,1:T(8,128)} %copy-done.3, s32[]{:T(128)S(6)} %select_n.429), kind=kLoop, calls=%fused_computation.41 | loop fusion | flops 74112 | bytes 889348 | tf_op jit(solution)/shard_map/squeeze;reshape | solution.py:169
  123.1 1.5 %collective-permute-start.7 = (f32[193,384]{1,0:T(8,128)}, f32[193,384]{1,0:T(8,128)}, u32[]{:S(2)}, u32[]{:S(2)}) collective-permute-start(f32[193,384]{1,0:T(8,128)} %add_bitcast_fusion), channel_id=1, source_target_pairs={{0,1},{1,0},{2,3},{3,2},{4,5},{5,4},{6,7},{7,6},{8,9},{9,8},{10,11... | collective-permute-start | bytes 889352 | tf_op jit(solution)/shard_map/ppermute | solution.py:72
  128.3 1.7 %copy.89 = bf16[512,64]{0,1:T(8,128)(2,1)} copy(bf16[512,64]{1,0:T(8,128)(2,1)} %get-tuple-element.21) | data formatting | bytes 131072
  130.7 1.8 %collective-permute-done.7 = f32[193,384]{1,0:T(8,128)} collective-permute-done((f32[193,384]{1,0:T(8,128)}, f32[193,384]{1,0:T(8,128)}, u32[]{:S(2)}, u32[]{:S(2)}) %collective-permute-start.7) | collective-permute-done | bytes 296480 | tf_op jit(solution)/shard_map/ppermute | solution.py:72
  133.6 1.6 %collective-permute-start.8 = (f32[193,384]{1,0:T(8,128)S(1)}, f32[193,384]{1,0:T(8,128)S(1)}, u32[]{:S(2)}, u32[]{:S(2)}) collective-permute-start(f32[193,384]{1,0:T(8,128)S(1)} %add.291), channel_id=1, source_target_pairs={{0,2},{1,3},{2,0},{3,1},{4,6},{5,7},{6,4},{7,5},{8,10},{9,11},{10,... | collective-permute-start | bytes 889352 | tf_op jit(solution)/shard_map/ppermute | solution.py:72
  135.2 1.4 %fusion.24 = bf16[512,16,64]{0,2,1:T(8,128)(2,1)S(1)} fusion(s32[512]{0:T(512)S(1)} %bitcast.74, s32[512]{0:T(512)S(1)} %bitcast.75, s32[16,64]{1,0:T(8,128)S(1)} %add_select_fusion.5, bf16[512,64]{0,1:T(8,128)(2,1)} %copy.89, bf16[512,64]{0,1:T(8,128)(2,1)} %copy.87), kind=kLoop, calls=%fused_computation.32 | loop fusion | flops 2621440 | bytes 1187840 | tf_op jit(solution)/shard_map/add | solution.py:18
  136.7 1.4 fusion.61
  138.1 3.9 %collective-permute-done.8 = f32[193,384]{1,0:T(8,128)S(1)} collective-permute-done((f32[193,384]{1,0:T(8,128)S(1)}, f32[193,384]{1,0:T(8,128)S(1)}, u32[]{:S(2)}, u32[]{:S(2)}) %collective-permute-start.8) | collective-permute-done | bytes 296480 | tf_op jit(solution)/shard_map/ppermute | solution.py:72
  (110 shorter events, 29.9 us)
Async XLA Ops:
  0.6 26.2 %copy-start = (bf16[1024,1536]{1,0:T(8,128)(2,1)S(1)}, bf16[1024,1536]{1,0:T(8,128)(2,1)}, u32[]{:S(2)}) copy-start(bf16[1024,1536]{1,0:T(8,128)(2,1)} %param.12) | copy-start | bytes 9437188
  0.7 4.5 %copy-start.14 = (s32[1600]{0:T(1024)}, s32[1600]{0:T(1024)S(1)}, u32[]{:S(2)}) copy-start(s32[1600]{0:T(1024)S(1)} %add_select_fusion.7) | copy-start | bytes 19204
  0.7 4.5 %copy-start.16 = (f32[1536]{0:T(1024)S(1)}, f32[1536]{0:T(1024)}, u32[]{:S(2)}) copy-start(f32[1536]{0:T(1024)} %param.11) | copy-start | bytes 18436
  0.7 4.5 %copy-start.17 = (f32[1536]{0:T(1024)S(1)}, f32[1536]{0:T(1024)}, u32[]{:S(2)}) copy-start(f32[1536]{0:T(1024)} %param.10) | copy-start | bytes 18436
  5.2 5.7 %copy-start.1 = (f32[1600,1536]{1,0:T(8,128)}, f32[1600,1536]{1,0:T(8,128)S(1)}, u32[]{:S(2)}) copy-start(f32[1600,1536]{1,0:T(8,128)S(1)} %fusion.60) | copy-start | bytes 29491204
  5.2 8.7 %copy-start.13 = (s32[64,64]{1,0:T(8,128)S(1)}, s32[64,64]{1,0:T(8,128)}, u32[]{:S(2)}) copy-start(s32[64,64]{1,0:T(8,128)} %param.14) | copy-start | bytes 49156
  5.3 9.4 %copy-start.15 = (s32[64]{0:T(128)S(1)}, s32[64]{0:T(128)}, u32[]{:S(2)}) copy-start(s32[64]{0:T(128)} %param.13) | copy-start | bytes 772
  10.9 8.6 %collective-permute-start = (bf16[1,16,1536]{2,1,0:T(8,128)(2,1)S(1)}, bf16[1,16,1536]{2,1,0:T(8,128)(2,1)S(1)}, u32[]{:S(2)}, u32[]{:S(2)}) collective-permute-start(bf16[1,16,1536]{2,1,0:T(8,128)(2,1)S(1)} %fusion.15), channel_id=1, source_target_pairs={{0,1},{1,0},{2,3},{3,2},{4,5},{5,4},{6,7},{7,6},{8,9},{9,8},{10,11... | collective-permute-start | bytes 147464 | tf_op jit(solution)/shard_map/ppermute | solution.py:44
  19.5 4.7 %collective-permute-start.1 = (bf16[2,16,1536]{2,1,0:T(8,128)(2,1)S(1)}, bf16[2,16,1536]{2,1,0:T(8,128)(2,1)S(1)}, u32[]{:S(2)}, u32[]{:S(2)}) collective-permute-start(bf16[2,16,1536]{2,1,0:T(8,128)(2,1)S(1)} %maximum_select_fusion.1), channel_id=1, source_target_pairs={{0,2},{1,3},{2,0},{3,1},{4,6},{5,7},{6,4},{7,5},{8,10},{9,11},{10,... | collective-permute-start | bytes 294920 | tf_op jit(solution)/shard_map/ppermute | solution.py:44
  24.2 0.7 copy-start.7
  33.0 0.6 copy-start.9
  36.2 3.1 %copy-start.10 = (bf16[64,64]{1,0:T(8,128)(2,1)S(1)}, bf16[64,64]{1,0:T(8,128)(2,1)}, u32[]{:S(2)}) copy-start(bf16[64,64]{1,0:T(8,128)(2,1)} %copy-done.9) | copy-start | bytes 24580
  36.2 3.1 %copy-start.11 = (bf16[64,1]{1,0:T(8,128)(2,1)S(1)}, bf16[64,1]{1,0:T(8,128)(2,1)}, u32[]{:S(2)}) copy-start(bf16[64,1]{1,0:T(8,128)(2,1)} %get-tuple-element.31) | copy-start | bytes 388
  36.2 3.1 %copy-start.12 = (bf16[64,1]{1,0:T(8,128)(2,1)S(1)}, bf16[64,1]{1,0:T(8,128)(2,1)}, u32[]{:S(2)}) copy-start(bf16[64,1]{1,0:T(8,128)(2,1)} %get-tuple-element.32) | copy-start | bytes 388
  37.8 0.8 copy-start.5
  39.3 6.4 %collective-permute-start.2 = (f32[2,16,1536]{2,1,0:T(8,128)}, f32[2,16,1536]{2,1,0:T(8,128)}, u32[]{:S(2)}, u32[]{:S(2)}) collective-permute-start(f32[2,16,1536]{2,1,0:T(8,128)} %dynamic-slice_bitcast_fusion.1), channel_id=1, source_target_pairs={{0,1},{1,0},{2,3},{3,2},{4,5},{5,4},{6,7},{7,6},{8,9},{9,8},{10,11... | collective-permute-start | bytes 589832 | tf_op jit(solution)/shard_map/ppermute | solution.py:61
  40.3 17.9 %all-to-all-start = ((bf16[8,64,322]{2,1,0:T(8,128)(2,1)}), bf16[8,64,322]{2,1,0:T(8,128)(2,1)S(1)}, u32[]{:S(2)}, u32[]{:S(2)}) async-start(bf16[8,64,322]{2,1,0:T(8,128)(2,1)} %pad_maximum_fusion), calls=%async_computation | async-start | bytes 786432 | tf_op jit(solution)/shard_map/all_to_all | solution.py:139
  46.8 0.7 copy-start.8
  48.1 5.5 %collective-permute-start.3 = (f32[1,16,1536]{2,1,0:T(8,128)}, f32[1,16,1536]{2,1,0:T(8,128)}, u32[]{:S(2)}, u32[]{:S(2)}) collective-permute-start(f32[1,16,1536]{2,1,0:T(8,128)} %constant_dynamic-slice_fusion.1), channel_id=1, source_target_pairs={{0,2},{1,3},{2,0},{3,1},{4,6},{5,7},{6,4},{7,5},{8,10},{9,11},{10,... | collective-permute-start | bytes 294920 | tf_op jit(solution)/shard_map/ppermute | solution.py:61
  55.2 13.9 %copy-start.18 = (f32[1536]{0:T(1024)S(1)}, f32[1536]{0:T(1024)}, u32[]{:S(2)}) copy-start(f32[1536]{0:T(1024)} %param.10) | copy-start | bytes 18436
  58.3 10.9 %copy-start.4 = (bf16[8,64,322]{2,1,0:T(8,128)(2,1)}, bf16[8,64,322]{2,1,0:T(8,128)(2,1)S(1)}, u32[]{:S(2)}) copy-start(bf16[8,64,322]{2,1,0:T(8,128)(2,1)S(1)} %all-to-all-done) | copy-start | bytes 989188
  58.3 10.9 %copy-start.6 = (bf16[1600,384]{1,0:T(8,128)(2,1)S(1)}, bf16[1600,384]{1,0:T(8,128)(2,1)}, u32[]{:S(2)}) copy-start(bf16[1600,384]{1,0:T(8,128)(2,1)} %param.8) | copy-start | bytes 3686404
  79.2 3.2 %collective-permute-start.4 = (f32[4,1,193,384]{3,0,2,1:T(4,128)}, f32[4,1,193,384]{3,0,2,1:T(4,128)}, u32[]{:S(2)}, u32[]{:S(2)}) collective-permute-start(f32[4,1,193,384]{3,0,2,1:T(4,128)} %bitcast.61), channel_id=1, source_target_pairs={{0,4},{4,0},{8,12},{12,8},{16,20},{20,16},{24,28},{28,24},{1,5},{5... | collective-permute-start | bytes 3557384 | tf_op jit(solution)/shard_map/ppermute | solution.py:61
  84.1 1.0 copy-start.2
  86.3 15.8 %collective-permute-start.5 = (f32[2,1,193,384]{3,0,2,1:T(2,128)}, f32[2,1,193,384]{3,0,2,1:T(2,128)}, u32[]{:S(2)}, u32[]{:S(2)}) collective-permute-start(f32[2,1,193,384]{3,0,2,1:T(2,128)} %copy.81), channel_id=1, source_target_pairs={{0,8},{4,12},{8,0},{12,4},{16,24},{20,28},{24,16},{28,20},{1,9},{5... | collective-permute-start | bytes 1778696 | tf_op jit(solution)/shard_map/ppermute | solution.py:61
  103.4 0.8 copy-start.3
  105.0 16.3 %collective-permute-start.6 = (f32[1,1,193,384]{3,2,0,1:T(8,128)}, f32[1,1,193,384]{3,2,0,1:T(8,128)}, u32[]{:S(2)}, u32[]{:S(2)}) collective-permute-start(f32[1,1,193,384]{3,2,0,1:T(8,128)} %constant_dynamic-slice_fusion), channel_id=1, source_target_pairs={{0,16},{4,20},{8,24},{12,28},{16,0},{20,4},{24,8},{28,12},{1,17},{... | collective-permute-start | bytes 889352 | tf_op jit(solution)/shard_map/ppermute | solution.py:61
  123.1 9.5 %collective-permute-start.7 = (f32[193,384]{1,0:T(8,128)}, f32[193,384]{1,0:T(8,128)}, u32[]{:S(2)}, u32[]{:S(2)}) collective-permute-start(f32[193,384]{1,0:T(8,128)} %add_bitcast_fusion), channel_id=1, source_target_pairs={{0,1},{1,0},{2,3},{3,2},{4,5},{5,4},{6,7},{7,6},{8,9},{9,8},{10,11... | collective-permute-start | bytes 889352 | tf_op jit(solution)/shard_map/ppermute | solution.py:72
  128.3 8.4 %slice-start = ((bf16[8,64,322]{2,1,0:T(8,128)(2,1)}), bf16[8,64,192]{2,1,0:T(8,128)(2,1)S(1)}, s32[]{:S(2)}) async-start(bf16[8,64,322]{2,1,0:T(8,128)(2,1)} %copy-done.4), calls=%async_computation.1 | async-start | bytes 524288 | tf_op jit(solution)/shard_map/slice | solution.py:141
  133.6 8.4 %collective-permute-start.8 = (f32[193,384]{1,0:T(8,128)S(1)}, f32[193,384]{1,0:T(8,128)S(1)}, u32[]{:S(2)}, u32[]{:S(2)}) collective-permute-start(f32[193,384]{1,0:T(8,128)S(1)} %add.291), channel_id=1, source_target_pairs={{0,2},{1,3},{2,0},{3,1},{4,6},{5,7},{6,4},{7,5},{8,10},{9,11},{10,... | collective-permute-start | bytes 889352 | tf_op jit(solution)/shard_map/ppermute | solution.py:72

commit v8 on v6

--- a/solution.py
+++ b/solution.py
@@ -73,6 +73,37 @@
         cur = tuple(c + g for c, g in zip(cur, got))
         bit += 1
     return cur
+
+
+def halve_steps(x, name, axis, bits):
+    idx = lax.axis_index(name)
+    size = lax.axis_size(name)
+    for bit in bits:
+        n = x.shape[axis]
+        pairs = x.reshape(x.shape[:axis] + (n // 2, 2) + x.shape[axis + 1 :])
+        mine = (idx // (1 << bit)) % 2
+        keep = lax.dynamic_index_in_dim(pairs, mine, axis + 1, keepdims=False)
+        give = lax.dynamic_index_in_dim(pairs, 1 - mine, axis + 1, keepdims=False)
+        x = keep + lax.ppermute(give, name, partners(size, bit))
+    return x
+
+
+def double_steps(x, name, axis, bits):
+    idx = lax.axis_index(name)
+    size = lax.axis_size(name)
+    for bit in bits:
+        other = lax.ppermute(x, name, partners(size, bit))
+        low = (idx // (1 << bit)) % 2 == 0
+        x = jnp.where(low, jnp.concatenate([x, other], axis), jnp.concatenate([other, x], axis))
+    return x
+
+
+def axis_bits(name):
+    size = lax.axis_size(name)
+    bit = 0
+    while (1 << bit) < size:
+        bit += 1
+    return list(range(bit))
 
 
 def shards(features, head_weight, gain, shift, node_weights, subtree_map, node_ids):
@@ -159,14 +190,26 @@
     e_size = head_term.shape[1]
     chunk = width // n_dp
     extra = -(-2 * chunk // e_size)
+    n_leaf = lax.axis_size("leaf")
+    padded = -(-(chunk + extra) // (8 * n_leaf)) * 8 * n_leaf
     side_rows = jnp.stack([gain_term, shift_term], axis=1).reshape(n_dp, 2 * chunk)
     side_rows = jnp.pad(side_rows, ((0, 0), (0, extra * e_size - 2 * chunk)))
     stacked = jnp.concatenate(
-        [head_term.reshape(n_dp, chunk, e_size), side_rows.reshape(n_dp, extra, e_size)], axis=1
-    )
-    (part,) = halving_scatter([stacked], "dp")
-    (total,) = butterfly_sum([part[0]], "leaf")
-    side_sum = total[chunk:].reshape(-1)[: 2 * chunk].reshape(chunk, 2)
+        [
+            head_term.reshape(n_dp, chunk, e_size),
+            side_rows.reshape(n_dp, extra, e_size),
+            jnp.zeros((n_dp, padded - chunk - extra, e_size), jnp.float32),
+        ],
+        axis=1,
+    )
+    dbits = axis_bits("dp")
+    lbits = axis_bits("leaf")
+    part = halve_steps(stacked, "dp", 0, dbits[:1])
+    part = part.reshape(part.shape[0], n_leaf, padded // n_leaf, e_size)
+    part = halve_steps(part, "leaf", 1, lbits)
+    part = halve_steps(part, "dp", 0, dbits[1:])
+    total = double_steps(part, "leaf", 1, lbits).reshape(padded, e_size)
+    side_sum = total[chunk : chunk + extra].reshape(-1)[: 2 * chunk].reshape(chunk, 2)
     return (total[:chunk].T, side_sum[:, 0], side_sum[:, 1], node_grad)
 
 

time: 127 us -> 134 us (1.055)
  matrix products: 30.3 us -> 35.2 us
  local copies, waits for them, and re-layouts: 21.7 us -> 24 us
  starting transfers between devices: 17.9 us -> 19.6 us
    ppermute x2 -> x7, waiting for transfers between devices: 4.47 us -> 29.1 us  [the longest x5 24.2 us: halve_steps(): x = keep + lax.ppermute(give, name, partners(size, bit))]
    ppermute x5 -> x2, waiting for transfers between devices: 33.4 us -> 8.87 us  [halving_scatter(): got = lax.ppermute(tuple(give), name, partners(size, bit))]
    ppermute x2 -> x7, starting transfers between devices: 2.1 us -> 8.06 us  [the longest x5 5.87 us: halve_steps(): x = keep + lax.ppermute(give, name, partners(size, bit))]
    ppermute x5 -> x2, starting transfers between devices: 7.11 us -> 1.71 us  [halving_scatter(): got = lax.ppermute(tuple(give), name, partners(size, bit))]
    add x2 -> x5, other arithmetic: 1.13 us -> 5.35 us  [halve_steps(): x = keep + lax.ppermute(give, name, partners(size, bit))]
    unnamed x43 -> x45, local copies, waits for them, and re-layouts: 6.16 us -> 9.95 us
    squeeze x0 -> x5, local copies, waits for them, and re-layouts: none -> 3.54 us  [halve_steps(): give = lax.dynamic_index_in_dim(pairs, 1 - mine, axis + 1, keepdims=False)]
    dot_general x1, matrix products: 10.9 us -> 14 us  [shards(): jnp.dot(select.T, emb_grad / P_SIZE, precision=HIGHEST, preferred_element...]
  transfers between devices with their start and end apart: 10 -> 12, of which waited for: 8 -> 9; matrix products, arithmetic and copies ran while one was open for 14% -> 14% of each run, Pallas kernels for 0% -> 0%
where the time goes in v8:
time: 134 us
  waiting for transfers between devices  40.5 us (30%)
  matrix products  35.2 us (26%)
  local copies, waits for them, and re-layouts  24 us (18%)
  starting transfers between devices  19.6 us (15%)
  other arithmetic  13.2 us (10%)
    ppermute x5, waiting for transfers between devices, halve_steps(): x = keep + lax.ppermute(give, name, partners(size, bit))  24.2 us
    dot_general x1, matrix products, shards(): jnp.dot(select.T, emb_grad / P_SIZE, precision=HIGHEST, preferred_element...  14 us
    unnamed x45, local copies, waits for them, and re-layouts  9.95 us
    ppermute x2, waiting for transfers between devices, halving_scatter(): got = lax.ppermute(tuple(give), name, partners(size, bit))  8.87 us
    dot_general x1, matrix products, shards(): lax.dot_general(lin_grad, features, (((0,), (0,)), ((), ())), preferred_e...  6.19 us
    ppermute x5, starting transfers between devices, halve_steps(): x = keep + lax.ppermute(give, name, partners(size, bit))  5.87 us
    dot_general x1, matrix products, shards(): jnp.dot(select, active, precision=HIGHEST, preferred_element_type=jnp.flo...  5.63 us
    add x5, other arithmetic, halve_steps(): x = keep + lax.ppermute(give, name, partners(size, bit))  5.35 us
  transfers between devices with their start and end apart: 12, of which 9 were waited for; matrix products, arithmetic and copies ran while one was open for 14% of the time, Pallas kernels for 0%

profile of v8, /device:TPU:0, one launch (start us, length us, event | category | flops | bytes accessed | tf_op | source)
XLA Modules:
  0.0 133.7 jit_solution(224924918854101598)
XLA Ops:
  0.7 4.5 %fusion.62 = f32[1600,1536]{1,0:T(8,128)S(1)} fusion(bf16[1600,384]{1,0:T(8,128)(2,1)} %param.8, bf16[384,1536]{1,0:T(8,128)(2,1)} %param.9), kind=kOutput, calls=%fused_computation.173 | convolution fusion | flops 1887436800 | bytes 12238848 | tf_op jit(solution)/shard_map/dot_general | solution.py:123
  5.3 5.6 %fusion.15 = bf16[1,16,1536]{2,1,0:T(8,128)(2,1)S(1)} fusion(f32[1600,1536]{1,0:T(8,128)S(1)} %fusion.62, f32[1536]{0:T(1024)S(1)} %copy-done.17, f32[1536]{0:T(1024)S(1)} %copy-done.18, s32[1600]{0:T(1024)S(1)} %add_select_fusion.7), kind=kOutput, calls=%fused_computation.18 | convolution fusion | flops 486679552 | bytes 9898240 | tf_op jit(solution)/shard_map/dot_general | solution.py:127
  10.9 3.0 %collective-permute-start = (bf16[1,16,1536]{2,1,0:T(8,128)(2,1)S(1)}, bf16[1,16,1536]{2,1,0:T(8,128)(2,1)S(1)}, u32[]{:S(2)}, u32[]{:S(2)}) collective-permute-start(bf16[1,16,1536]{2,1,0:T(8,128)(2,1)S(1)} %fusion.15), channel_id=1, source_target_pairs={{0,1},{1,0},{2,3},{3,2},{4,5},{5,4},{6,7},{7,6},{8,9},{9,8},{10,11... | collective-permute-start | bytes 147464 | tf_op jit(solution)/shard_map/ppermute | solution.py:44
  17.9 1.6 %collective-permute-start.1 = (bf16[2,16,1536]{2,1,0:T(8,128)(2,1)S(1)}, bf16[2,16,1536]{2,1,0:T(8,128)(2,1)S(1)}, u32[]{:S(2)}, u32[]{:S(2)}) collective-permute-start(bf16[2,16,1536]{2,1,0:T(8,128)(2,1)S(1)} %maximum_select_fusion.1), channel_id=1, source_target_pairs={{0,2},{1,3},{2,0},{3,1},{4,6},{5,7},{6,4},{7,5},{8,10},{9,11},{10,... | collective-permute-start | bytes 294920 | tf_op jit(solution)/shard_map/ppermute | solution.py:44
  20.1 2.5 %collective-permute-done.1 = bf16[2,16,1536]{2,1,0:T(8,128)(2,1)S(1)} collective-permute-done((bf16[2,16,1536]{2,1,0:T(8,128)(2,1)S(1)}, bf16[2,16,1536]{2,1,0:T(8,128)(2,1)S(1)}, u32[]{:S(2)}, u32[]{:S(2)}) %collective-permute-start.1) | collective-permute-done | bytes 98336 | tf_op jit(solution)/shard_map/ppermute | solution.py:44
  22.6 1.8 %select_reduce_fusion = (f32[64,64]{1,0:T(8,128)S(1)}, f32[64,64]{1,0:T(8,128)S(1)}) fusion(pred[64,16]{0,1:T(8,128)(4,1)S(1)} %iota_compare_fusion.7, pred[64,16]{0,1:T(8,128)(4,1)S(1)} %iota_compare_fusion.8, bf16[64,1536,1]{1,0,2:T(8,128)(2,1)S(1)} %bitcast.102, bf16[16,64,1536]{2,1,0:T(8,128)(2,1)S(1)} %bitcast.84), kind=kOutput, calls=%fused_computation.29 | convolution fusion | flops 201580544 | bytes 3377152 | tf_op jit(solution)/shard_map/dot_general | solution.py:143
  26.4 1.7 %fusion.7 = f32[2,2,16,1536]{3,2,1,0:T(8,128)S(1)} fusion(bf16[1024,1536]{1,0:T(8,128)(2,1)S(1)} %copy-done, bf16[2,2,16,1024]{3,2,1,0:T(8,128)(2,1)} %tile.13, bf16[2,2,16,1024]{3,2,1,0:T(8,128)(2,1)} %tile.15, s32[2,2,16]{2,1,0:T(2,128)} %get-tuple-element.23, s32[2,2,16]{2,1,0:T(2,128)} %get-tuple-element.24, s32[1024]{0:T(1024)} %add_select_fusion.8), kind=kOutput, calls=%fused_computation.13 | convolution fusion | flops 201654272 | bytes 3805696 | tf_op jit(solution)/shard_map/dot_general | solution.py:153
  28.9 5.9 %collective-permute-done.2 = f32[2,16,1536]{2,1,0:T(8,128)} collective-permute-done((f32[2,16,1536]{2,1,0:T(8,128)}, f32[2,16,1536]{2,1,0:T(8,128)}, u32[]{:S(2)}, u32[]{:S(2)}) %collective-permute-start.2) | collective-permute-done | bytes 196640 | tf_op jit(solution)/shard_map/ppermute | solution.py:61
  36.4 1.6 %collective-permute-start.3 = (f32[1,16,1536]{2,1,0:T(8,128)S(1)}, f32[1,16,1536]{2,1,0:T(8,128)S(1)}, u32[]{:S(2)}, u32[]{:S(2)}) collective-permute-start(f32[1,16,1536]{2,1,0:T(8,128)S(1)} %constant_dynamic-slice_fusion.2), channel_id=1, source_target_pairs={{0,2},{1,3},{2,0},{3,1},{4,6},{5,7},{6,4},{7,5},{8,10},{9,11},{10,... | collective-permute-start | bytes 294920 | tf_op jit(solution)/shard_map/ppermute | solution.py:61
  38.1 3.0 %collective-permute-done.3 = f32[1,16,1536]{2,1,0:T(8,128)S(1)} collective-permute-done((f32[1,16,1536]{2,1,0:T(8,128)S(1)}, f32[1,16,1536]{2,1,0:T(8,128)S(1)}, u32[]{:S(2)}, u32[]{:S(2)}) %collective-permute-start.3) | collective-permute-done | bytes 98336 | tf_op jit(solution)/shard_map/ppermute | solution.py:61
  41.1 14.0 %multiply_reduce_fusion = (f32[1536]{0:T(1024)S(1)}, f32[1536]{0:T(1024)S(1)}, f32[1600,1536]{1,0:T(8,128)}) fusion(f32[1600,1536]{1,0:T(8,128)} %copy-done.1, f32[1536]{0:T(1024)} %param.11, f32[1536]{0:T(1024)} %param.10, f32[1,16,1536]{2,1,0:T(8,128)S(1)} %collective-permute-done.3, f32[2,16,1536]{2,1,0:T(8,128)} %copy-done.7, s32[]{:T(128)S(6)} %select_n.464, ...), kind=kOutput, calls=%fused_computation.1 | convolution fusion | flops 503879680 | bytes 19894276 | tf_op jit(solution)/shard_map/dot_general | solution.py:182
  56.4 1.6 %concatenate.77 = f32[4,2,1,384]{3,2,1,0:T(1,128)S(1)} reshape(f32[1536,2]{1,0:T(8,128)} %copy.86) | data formatting | bytes 24576 | tf_op jit(solution)/shard_map/concatenate | solution.py:197
  58.0 6.2 %fusion.2 = f32[1536,384]{1,0:T(8,128)S(1)} fusion(bf16[1600,384]{1,0:T(8,128)(2,1)} %param.8, f32[1600,1536]{1,0:T(8,128)} %get-tuple-element.22, f32[1536]{0:T(1024)S(1)} %copy-done.19), kind=kOutput, calls=%fused_computation.8 | convolution fusion | flops 1892352000 | bytes 13424640 | tf_op jit(solution)/shard_map/dot_general | solution.py:185
  64.5 1.5 %copy-done.2 = f32[4,2,224,384]{3,2,1,0:T(8,128)} copy-done((f32[4,2,224,384]{3,2,1,0:T(8,128)}, f32[4,2,224,384]{3,2,1,0:T(8,128)S(1)}, u32[]{:S(2)}) %copy-start.2) | copy-done | bytes 2752536
  66.0 1.2 dynamic-slice_bitcast_fusion
  67.2 3.5 %collective-permute-done.4 = f32[4,224,384]{2,1,0:T(8,128)} collective-permute-done((f32[4,224,384]{2,1,0:T(8,128)}, f32[4,224,384]{2,1,0:T(8,128)}, u32[]{:S(2)}, u32[]{:S(2)}) %collective-permute-start.4) | collective-permute-done | bytes 1376288 | tf_op jit(solution)/shard_map/ppermute | solution.py:87
  70.7 1.9 %bitcast_add_fusion = f32[4,224,384]{2,1,0:T(8,128)S(1)} fusion(f32[4,224,384]{2,1,0:T(8,128)} %collective-permute-done.4, f32[4,2,224,384]{3,2,1,0:T(8,128)} %copy-done.2, s32[]{:T(128)S(6)} %select_n.467), kind=kLoop, calls=%fused_computation.24 | loop fusion | flops 344064 | bytes 4128772 | tf_op jit(solution)/shard_map/add | solution.py:87
  77.2 5.3 %all-to-all-start = ((bf16[8,64,322]{2,1,0:T(8,128)(2,1)}), bf16[8,64,322]{2,1,0:T(8,128)(2,1)S(1)}, u32[]{:S(2)}, u32[]{:S(2)}) async-start(bf16[8,64,322]{2,1,0:T(8,128)(2,1)} %pad_maximum_fusion), calls=%async_computation | async-start | bytes 786432 | tf_op jit(solution)/shard_map/all_to_all | solution.py:170
  82.5 9.8 %collective-permute-done.5 = f32[4,2,56,384]{3,2,1,0:T(8,128)} collective-permute-done((f32[4,2,56,384]{3,2,1,0:T(8,128)}, f32[4,2,56,384]{3,2,1,0:T(8,128)}, u32[]{:S(2)}, u32[]{:S(2)}) %collective-permute-start.5) | collective-permute-done | bytes 688160 | tf_op jit(solution)/shard_map/ppermute | solution.py:87
  92.3 1.4 %bitcast_add_fusion.1 = f32[4,2,56,384]{3,2,1,0:T(8,128)S(1)} fusion(f32[4,2,56,384]{3,2,1,0:T(8,128)} %collective-permute-done.5, f32[4,2,2,56,384]{4,3,2,1,0:T(8,128)} %bitcast.86, s32[]{:T(128)S(6)} %select_n.462), kind=kLoop, calls=%fused_computation.27 | loop fusion | flops 172032 | bytes 2064388 | tf_op jit(solution)/shard_map/add | solution.py:87
  95.3 1.5 %collective-permute-start.6 = (f32[4,1,56,384]{3,2,1,0:T(8,128)}, f32[4,1,56,384]{3,2,1,0:T(8,128)}, u32[]{:S(2)}, u32[]{:S(2)}) collective-permute-start(f32[4,1,56,384]{3,2,1,0:T(8,128)} %constant_dynamic-slice_fusion.1), channel_id=1, source_target_pairs={{0,2},{1,3},{2,0},{3,1},{4,6},{5,7},{6,4},{7,5},{8,10},{9,11},{10,... | collective-permute-start | bytes 1032200 | tf_op jit(solution)/shard_map/ppermute | solution.py:87
  97.0 7.9 %collective-permute-done.6 = f32[4,1,56,384]{3,2,1,0:T(8,128)} collective-permute-done((f32[4,1,56,384]{3,2,1,0:T(8,128)}, f32[4,1,56,384]{3,2,1,0:T(8,128)}, u32[]{:S(2)}, u32[]{:S(2)}) %collective-permute-start.6) | collective-permute-done | bytes 344096 | tf_op jit(solution)/shard_map/ppermute | solution.py:87
  106.1 1.6 %collective-permute-start.7 = (f32[2,1,56,384]{3,2,1,0:T(8,128)S(1)}, f32[2,1,56,384]{3,2,1,0:T(8,128)S(1)}, u32[]{:S(2)}, u32[]{:S(2)}) collective-permute-start(f32[2,1,56,384]{3,2,1,0:T(8,128)S(1)} %dynamic-slice_bitcast_fusion.3), channel_id=1, source_target_pairs={{0,8},{4,12},{8,0},{12,4},{16,24},{20,28},{24,16},{28,20},{1,9},{5... | collective-permute-start | bytes 516104 | tf_op jit(solution)/shard_map/ppermute | solution.py:87
  108.5 3.0 %collective-permute-done.7 = f32[2,1,56,384]{3,2,1,0:T(8,128)S(1)} collective-permute-done((f32[2,1,56,384]{3,2,1,0:T(8,128)S(1)}, f32[2,1,56,384]{3,2,1,0:T(8,128)S(1)}, u32[]{:S(2)}, u32[]{:S(2)}) %collective-permute-start.7) | collective-permute-done | bytes 172064 | tf_op jit(solution)/shard_map/ppermute | solution.py:87
  112.2 2.6 %collective-permute-start.8 = (f32[1,1,56,384]{3,2,1,0:T(8,128)}, f32[1,1,56,384]{3,2,1,0:T(8,128)}, u32[]{:S(2)}, u32[]{:S(2)}) collective-permute-start(f32[1,1,56,384]{3,2,1,0:T(8,128)} %constant_dynamic-slice_fusion), channel_id=1, source_target_pairs={{0,16},{4,20},{8,24},{12,28},{16,0},{20,4},{24,8},{28,12},{1,17},{... | collective-permute-start | bytes 258056 | tf_op jit(solution)/shard_map/ppermute | solution.py:87
  117.7 1.6 %copy.111 = bf16[512,64]{0,1:T(8,128)(2,1)} copy(bf16[512,64]{1,0:T(8,128)(2,1)} %get-tuple-element.17) | data formatting | bytes 131072
  119.4 1.6 %copy.109 = bf16[512,64]{0,1:T(8,128)(2,1)} copy(bf16[512,64]{1,0:T(8,128)(2,1)} %get-tuple-element.16) | data formatting | bytes 131072
  122.5 1.4 %fusion.20 = bf16[512,16,64]{0,2,1:T(8,128)(2,1)S(1)} fusion(s32[512]{0:T(512)S(1)} %bitcast.104, s32[512]{0:T(512)S(1)} %bitcast.105, s32[16,64]{1,0:T(8,128)S(1)} %add_select_fusion.5, bf16[512,64]{0,1:T(8,128)(2,1)} %copy.111, bf16[512,64]{0,1:T(8,128)(2,1)} %copy.109), kind=kLoop, calls=%fused_computation.26 | loop fusion | flops 2621440 | bytes 1187840 | tf_op jit(solution)/shard_map/add | solution.py:18
  124.0 2.5 %collective-permute-done.9 = f32[1,1,56,384]{3,2,0,1:T(8,128)S(1)} collective-permute-done((f32[1,1,56,384]{3,2,0,1:T(8,128)S(1)}, f32[1,1,56,384]{3,2,0,1:T(8,128)S(1)}, u32[]{:S(2)}, u32[]{:S(2)}) %collective-permute-start.9) | collective-permute-done | bytes 86048 | tf_op jit(solution)/shard_map/ppermute | solution.py:95
  126.5 1.6 %collective-permute-start.10 = (f32[1,2,56,384]{3,2,0,1:T(8,128)S(1)}, f32[1,2,56,384]{3,2,0,1:T(8,128)S(1)}, u32[]{:S(2)}, u32[]{:S(2)}) collective-permute-start(f32[1,2,56,384]{3,2,0,1:T(8,128)S(1)} %fusion.71), channel_id=1, source_target_pairs={{0,2},{1,3},{2,0},{3,1},{4,6},{5,7},{6,4},{7,5},{8,10},{9,11},{10,... | collective-permute-start | bytes 516104 | tf_op jit(solution)/shard_map/ppermute | solution.py:95
  128.1 1.4 %fusion.63 = f32[1024,192]{0,1:T(8,128)} fusion(bf16[512,1024]{0,1:T(8,128)(2,1)S(1)} %bitcast.87, bf16[512,192]{1,0:T(8,128)(2,1)S(1)} %bitcast.101), kind=kOutput, calls=%fused_computation.174 | convolution fusion | flops 201326592 | bytes 2031616 | tf_op jit(solution)/shard_map/dot_general | solution.py:178
  129.5 2.5 %collective-permute-done.10 = f32[1,2,56,384]{3,2,0,1:T(8,128)S(1)} collective-permute-done((f32[1,2,56,384]{3,2,0,1:T(8,128)S(1)}, f32[1,2,56,384]{3,2,0,1:T(8,128)S(1)}, u32[]{:S(2)}, u32[]{:S(2)}) %collective-permute-start.10) | collective-permute-done | bytes 172064 | tf_op jit(solution)/shard_map/ppermute | solution.py:95
  (120 shorter events, 25.7 us)
Async XLA Ops:
  0.6 22.0 %copy-start = (bf16[1024,1536]{1,0:T(8,128)(2,1)S(1)}, bf16[1024,1536]{1,0:T(8,128)(2,1)}, u32[]{:S(2)}) copy-start(bf16[1024,1536]{1,0:T(8,128)(2,1)} %param.12) | copy-start | bytes 9437188
  0.7 4.5 %copy-start.15 = (s32[1600]{0:T(1024)}, s32[1600]{0:T(1024)S(1)}, u32[]{:S(2)}) copy-start(s32[1600]{0:T(1024)S(1)} %add_select_fusion.7) | copy-start | bytes 19204
  0.7 4.5 %copy-start.17 = (f32[1536]{0:T(1024)S(1)}, f32[1536]{0:T(1024)}, u32[]{:S(2)}) copy-start(f32[1536]{0:T(1024)} %param.11) | copy-start | bytes 18436
  0.7 4.5 %copy-start.18 = (f32[1536]{0:T(1024)S(1)}, f32[1536]{0:T(1024)}, u32[]{:S(2)}) copy-start(f32[1536]{0:T(1024)} %param.10) | copy-start | bytes 18436
  5.2 5.7 %copy-start.1 = (f32[1600,1536]{1,0:T(8,128)}, f32[1600,1536]{1,0:T(8,128)S(1)}, u32[]{:S(2)}) copy-start(f32[1600,1536]{1,0:T(8,128)S(1)} %fusion.62) | copy-start | bytes 29491204
  5.2 8.7 %copy-start.10 = (s32[64,64]{1,0:T(8,128)S(1)}, s32[64,64]{1,0:T(8,128)}, u32[]{:S(2)}) copy-start(s32[64,64]{1,0:T(8,128)} %param.14) | copy-start | bytes 49156
  5.3 9.4 %copy-start.16 = (s32[64]{0:T(128)S(1)}, s32[64]{0:T(128)}, u32[]{:S(2)}) copy-start(s32[64]{0:T(128)} %param.13) | copy-start | bytes 772
  10.9 6.9 %collective-permute-start = (bf16[1,16,1536]{2,1,0:T(8,128)(2,1)S(1)}, bf16[1,16,1536]{2,1,0:T(8,128)(2,1)S(1)}, u32[]{:S(2)}, u32[]{:S(2)}) collective-permute-start(bf16[1,16,1536]{2,1,0:T(8,128)(2,1)S(1)} %fusion.15), channel_id=1, source_target_pairs={{0,1},{1,0},{2,3},{3,2},{4,5},{5,4},{6,7},{7,6},{8,9},{9,8},{10,11... | collective-permute-start | bytes 147464 | tf_op jit(solution)/shard_map/ppermute | solution.py:44
  14.8 0.5 copy-start.11
  14.8 0.5 copy-start.13
  17.9 4.7 %collective-permute-start.1 = (bf16[2,16,1536]{2,1,0:T(8,128)(2,1)S(1)}, bf16[2,16,1536]{2,1,0:T(8,128)(2,1)S(1)}, u32[]{:S(2)}, u32[]{:S(2)}) collective-permute-start(bf16[2,16,1536]{2,1,0:T(8,128)(2,1)S(1)} %maximum_select_fusion.1), channel_id=1, source_target_pairs={{0,2},{1,3},{2,0},{3,1},{4,6},{5,7},{6,4},{7,5},{8,10},{9,11},{10,... | collective-permute-start | bytes 294920 | tf_op jit(solution)/shard_map/ppermute | solution.py:44
  22.6 1.8 %copy-start.5 = (bf16[4,16,1536]{2,1,0:T(8,128)(2,1)}, bf16[4,16,1536]{2,1,0:T(8,128)(2,1)S(1)}, u32[]{:S(2)}) copy-start(bf16[4,16,1536]{2,1,0:T(8,128)(2,1)S(1)} %maximum_select_fusion) | copy-start | bytes 589828
  25.5 0.9 copy-start.8
  28.8 6.0 %collective-permute-start.2 = (f32[2,16,1536]{2,1,0:T(8,128)}, f32[2,16,1536]{2,1,0:T(8,128)}, u32[]{:S(2)}, u32[]{:S(2)}) collective-permute-start(f32[2,16,1536]{2,1,0:T(8,128)} %dynamic-slice_bitcast_fusion.2), channel_id=1, source_target_pairs={{0,1},{1,0},{2,3},{3,2},{4,5},{5,4},{6,7},{7,6},{8,9},{9,8},{10,11... | collective-permute-start | bytes 589832 | tf_op jit(solution)/shard_map/ppermute | solution.py:61
  35.7 0.7 copy-start.7
  36.4 4.7 %collective-permute-start.3 = (f32[1,16,1536]{2,1,0:T(8,128)S(1)}, f32[1,16,1536]{2,1,0:T(8,128)S(1)}, u32[]{:S(2)}, u32[]{:S(2)}) collective-permute-start(f32[1,16,1536]{2,1,0:T(8,128)S(1)} %constant_dynamic-slice_fusion.2), channel_id=1, source_target_pairs={{0,2},{1,3},{2,0},{3,1},{4,6},{5,7},{6,4},{7,5},{8,10},{9,11},{10,... | collective-permute-start | bytes 294920 | tf_op jit(solution)/shard_map/ppermute | solution.py:61
  38.1 19.9 %copy-start.19 = (f32[1536]{0:T(1024)S(1)}, f32[1536]{0:T(1024)}, u32[]{:S(2)}) copy-start(f32[1536]{0:T(1024)} %param.10) | copy-start | bytes 18436
  64.4 1.5 %copy-start.2 = (f32[4,2,224,384]{3,2,1,0:T(8,128)}, f32[4,2,224,384]{3,2,1,0:T(8,128)S(1)}, u32[]{:S(2)}) copy-start(f32[4,2,224,384]{3,2,1,0:T(8,128)S(1)} %maximum_maximum_fusion) | copy-start | bytes 8257540
  67.2 7.5 %copy-start.14 = (s32[64]{0:T(128)S(1)}, s32[64]{0:T(128)}, u32[]{:S(2)}) copy-start(s32[64]{0:T(128)} %copy-done.13) | copy-start | bytes 772
  67.2 7.6 %copy-start.12 = (s32[64]{0:T(128)S(1)}, s32[64]{0:T(128)}, u32[]{:S(2)}) copy-start(s32[64]{0:T(128)} %copy-done.11) | copy-start | bytes 772
  67.2 3.5 %collective-permute-start.4 = (f32[4,224,384]{2,1,0:T(8,128)}, f32[4,224,384]{2,1,0:T(8,128)}, u32[]{:S(2)}, u32[]{:S(2)}) collective-permute-start(f32[4,224,384]{2,1,0:T(8,128)} %dynamic-slice_bitcast_fusion), channel_id=1, source_target_pairs={{0,4},{4,0},{8,12},{12,8},{16,20},{20,16},{24,28},{28,24},{1,5},{5... | collective-permute-start | bytes 4128776 | tf_op jit(solution)/shard_map/ppermute | solution.py:87
  67.2 9.0 %copy-start.9 = (bf16[64,64]{1,0:T(8,128)(2,1)S(1)}, bf16[64,64]{1,0:T(8,128)(2,1)}, u32[]{:S(2)}) copy-start(bf16[64,64]{1,0:T(8,128)(2,1)} %copy-done.8) | copy-start | bytes 24580
  72.5 1.1 copy-start.3
  74.5 17.8 %collective-permute-start.5 = (f32[4,2,56,384]{3,2,1,0:T(8,128)}, f32[4,2,56,384]{3,2,1,0:T(8,128)}, u32[]{:S(2)}, u32[]{:S(2)}) collective-permute-start(f32[4,2,56,384]{3,2,1,0:T(8,128)} %dynamic-slice_bitcast_fusion.1), channel_id=1, source_target_pairs={{0,1},{1,0},{2,3},{3,2},{4,5},{5,4},{6,7},{7,6},{8,9},{9,8},{10,11... | collective-permute-start | bytes 2064392 | tf_op jit(solution)/shard_map/ppermute | solution.py:87
  77.2 19.6 %all-to-all-start = ((bf16[8,64,322]{2,1,0:T(8,128)(2,1)}), bf16[8,64,322]{2,1,0:T(8,128)(2,1)S(1)}, u32[]{:S(2)}, u32[]{:S(2)}) async-start(bf16[8,64,322]{2,1,0:T(8,128)(2,1)} %pad_maximum_fusion), calls=%async_computation | async-start | bytes 786432 | tf_op jit(solution)/shard_map/all_to_all | solution.py:170
  93.7 0.8 copy-start.4
  95.3 9.6 %collective-permute-start.6 = (f32[4,1,56,384]{3,2,1,0:T(8,128)}, f32[4,1,56,384]{3,2,1,0:T(8,128)}, u32[]{:S(2)}, u32[]{:S(2)}) collective-permute-start(f32[4,1,56,384]{3,2,1,0:T(8,128)} %constant_dynamic-slice_fusion.1), channel_id=1, source_target_pairs={{0,2},{1,3},{2,0},{3,1},{4,6},{5,7},{6,4},{7,5},{8,10},{9,11},{10,... | collective-permute-start | bytes 1032200 | tf_op jit(solution)/shard_map/ppermute | solution.py:87
  106.1 5.5 %collective-permute-start.7 = (f32[2,1,56,384]{3,2,1,0:T(8,128)S(1)}, f32[2,1,56,384]{3,2,1,0:T(8,128)S(1)}, u32[]{:S(2)}, u32[]{:S(2)}) collective-permute-start(f32[2,1,56,384]{3,2,1,0:T(8,128)S(1)} %dynamic-slice_bitcast_fusion.3), channel_id=1, source_target_pairs={{0,8},{4,12},{8,0},{12,4},{16,24},{20,28},{24,16},{28,20},{1,9},{5... | collective-permute-start | bytes 516104 | tf_op jit(solution)/shard_map/ppermute | solution.py:87
  111.6 4.0 %copy-start.6 = (f32[2,1,56,384]{3,2,1,0:T(8,128)}, f32[2,1,56,384]{3,2,1,0:T(8,128)S(1)}, u32[]{:S(2)}) copy-start(f32[2,1,56,384]{3,2,1,0:T(8,128)S(1)} %bitcast_add_fusion.3) | copy-start | bytes 516100
  112.2 8.7 %collective-permute-start.8 = (f32[1,1,56,384]{3,2,1,0:T(8,128)}, f32[1,1,56,384]{3,2,1,0:T(8,128)}, u32[]{:S(2)}, u32[]{:S(2)}) collective-permute-start(f32[1,1,56,384]{3,2,1,0:T(8,128)} %constant_dynamic-slice_fusion), channel_id=1, source_target_pairs={{0,16},{4,20},{8,24},{12,28},{16,0},{20,4},{24,8},{28,12},{1,17},{... | collective-permute-start | bytes 258056 | tf_op jit(solution)/shard_map/ppermute | solution.py:87
  121.9 4.6 %collective-permute-start.9 = (f32[1,1,56,384]{3,2,0,1:T(8,128)S(1)}, f32[1,1,56,384]{3,2,0,1:T(8,128)S(1)}, u32[]{:S(2)}, u32[]{:S(2)}) collective-permute-start(f32[1,1,56,384]{3,2,0,1:T(8,128)S(1)} %bitcast.91), channel_id=1, source_target_pairs={{0,1},{1,0},{2,3},{3,2},{4,5},{5,4},{6,7},{7,6},{8,9},{9,8},{10,11... | collective-permute-start | bytes 258056 | tf_op jit(solution)/shard_map/ppermute | solution.py:95
  126.5 5.5 %collective-permute-start.10 = (f32[1,2,56,384]{3,2,0,1:T(8,128)S(1)}, f32[1,2,56,384]{3,2,0,1:T(8,128)S(1)}, u32[]{:S(2)}, u32[]{:S(2)}) collective-permute-start(f32[1,2,56,384]{3,2,0,1:T(8,128)S(1)} %fusion.71), channel_id=1, source_target_pairs={{0,2},{1,3},{2,0},{3,1},{4,6},{5,7},{6,4},{7,5},{8,10},{9,11},{10,... | collective-permute-start | bytes 516104 | tf_op jit(solution)/shard_map/ppermute | solution.py:95

commit v9 on v6

--- a/solution.py
+++ b/solution.py
@@ -75,6 +75,25 @@
     return cur
 
 
+def direct_gather(x, name):
+    size = lax.axis_size(name)
+    idx = lax.axis_index(name)
+    got = [x] + [lax.ppermute(x, name, [(i, i ^ k) for i in range(size)]) for k in range(1, size)]
+    order = jnp.bitwise_xor(jnp.arange(size, dtype=jnp.int32), idx)
+    return jnp.take(jnp.stack(got), order, axis=0).reshape((size * x.shape[0],) + x.shape[1:])
+
+
+def direct_scatter(x, name):
+    size = lax.axis_size(name)
+    idx = lax.axis_index(name)
+    blocks = x.reshape((size, x.shape[0] // size) + x.shape[1:])
+    total = lax.dynamic_index_in_dim(blocks, idx, 0, keepdims=False)
+    for k in range(1, size):
+        give = lax.dynamic_index_in_dim(blocks, jnp.bitwise_xor(idx, k), 0, keepdims=False)
+        total = total + lax.ppermute(give, name, [(i, i ^ k) for i in range(size)])
+    return total
+
+
 def shards(features, head_weight, gain, shift, node_weights, subtree_map, node_ids):
     rows = features.shape[0]
     images_here = rows // P_SIZE
@@ -95,7 +114,8 @@
     active = shifted * sig
     image_sum = jnp.dot(select, active, precision=HIGHEST, preferred_element_type=jnp.float32)
     embedded = (image_sum / P_SIZE).astype(jnp.bfloat16)
-    grouped = doubling_gather(embedded, "leaf")
+    direct = lax.axis_size("leaf") <= 4
+    grouped = direct_gather(embedded, "leaf") if direct else doubling_gather(embedded, "leaf")
     group = grouped.shape[0]
 
     valid = node_ids >= 0
@@ -120,7 +140,10 @@
     neg_coef = neg_coef.astype(jnp.bfloat16)
     table = block_table(pos_coef, pos_here, neg_coef, neg_here, blocks).astype(jnp.bfloat16)
     grad_part = jnp.dot(table, node_weights, preferred_element_type=jnp.float32)
-    (emb_grad,) = halving_scatter([grad_part], "leaf")
+    if direct:
+        emb_grad = direct_scatter(grad_part, "leaf")
+    else:
+        (emb_grad,) = halving_scatter([grad_part], "leaf")
 
     col_width = width // n_dp
     column_chunks = grouped.reshape(group, n_dp, col_width).transpose(1, 0, 2)

time: 127 us -> 131 us (1.031)
  waiting for transfers between devices: 40.3 us -> 32.2 us
  other arithmetic: 13.9 us -> 19 us
  local copies, waits for them, and re-layouts: 21.7 us -> 25.3 us
  starting transfers between devices: 17.9 us -> 20.1 us
    ppermute x5 -> x3, waiting for transfers between devices: 33.4 us -> 23.6 us  [halving_scatter(): got = lax.ppermute(tuple(give), name, partners(size, bit))]
    ppermute x2 -> x6, starting transfers between devices: 4.58 us -> 8.08 us  [the longest x3 4.59 us: direct_gather(): lax.ppermute(x, name, [(i, i ^ k) for i in range(size)])]
    ppermute x2 -> x6, waiting for transfers between devices: 2.5 us -> 4.59 us  [the longest x3 4.58 us: direct_scatter(): total = total + lax.ppermute(give, name, [(i, i ^ k) for i in range(size)])]
    ppermute x5 -> x3, starting transfers between devices: 7.11 us -> 5.38 us  [halving_scatter(): got = lax.ppermute(tuple(give), name, partners(size, bit))]
    another operation x2, local copies, waits for them, and re-layouts: 0.9 us -> 2.54 us  [block_table(): neg_wide = jnp.tile(neg_vec, (1, blocks))]
    gather x0 -> x2, local copies, waits for them, and re-layouts: none -> 1.61 us  [direct_gather(): jnp.take(jnp.stack(got), order, axis=0)]
    add x3 -> x2, other arithmetic: 4.04 us -> 3.09 us  [halving_scatter(): cur = [k + g for k, g in zip(keep, got)]]
    unnamed x43 -> x51, local copies, waits for them, and re-layouts: 6.16 us -> 6.6 us
  transfers between devices with their start and end apart: 10 -> 12, of which waited for: 8 -> 8; matrix products, arithmetic and copies ran while one was open for 14% -> 16% of each run, Pallas kernels for 0% -> 0%
where the time goes in v9:
time: 131 us; the launch traced here: 129 us
  waiting for transfers between devices  32.2 us (25%)
  matrix products  31.1 us (24%)
  local copies, waits for them, and re-layouts  25.3 us (19%)
  starting transfers between devices  20.1 us (15%)
  other arithmetic  19 us (15%)
    ppermute x3, waiting for transfers between devices, halving_scatter(): got = lax.ppermute(tuple(give), name, partners(size, bit))  23.6 us
    dot_general x1, matrix products, shards(): jnp.dot(select.T, emb_grad / P_SIZE, precision=HIGHEST, preferred_element...  10.9 us
    unnamed x51, local copies, waits for them, and re-layouts  6.6 us
    dot_general x1, matrix products, shards(): jnp.dot(select, active, precision=HIGHEST, preferred_element_type=jnp.flo...  5.63 us
    ppermute x3, starting transfers between devices, halving_scatter(): got = lax.ppermute(tuple(give), name, partners(size, bit))  5.38 us
    ppermute x3, starting transfers between devices, direct_gather(): lax.ppermute(x, name, [(i, i ^ k) for i in range(size)])  4.59 us
    ppermute x3, waiting for transfers between devices, direct_scatter(): total = total + lax.ppermute(give, name, [(i, i ^ k) for i in range(size)])  4.58 us
    dot_general x1, matrix products, shards(): jnp.dot(features, head_weight, preferred_element_type=jnp.float32)  4.5 us
  transfers between devices with their start and end apart: 12, of which 8 were waited for; matrix products, arithmetic and copies ran while one was open for 16% of the time, Pallas kernels for 0%

profile of v9, /device:TPU:0, one launch (start us, length us, event | category | flops | bytes accessed | tf_op | source)
XLA Modules:
  0.0 128.8 jit_solution(15620584104340732583)
XLA Ops:
  0.7 4.5 %fusion.72 = f32[1600,1536]{1,0:T(8,128)S(1)} fusion(bf16[1600,384]{1,0:T(8,128)(2,1)} %param.8, bf16[384,1536]{1,0:T(8,128)(2,1)} %param.9), kind=kOutput, calls=%fused_computation.186 | convolution fusion | flops 1887436800 | bytes 12238848 | tf_op jit(solution)/shard_map/dot_general | solution.py:111
  5.3 5.6 %fusion.12 = bf16[16,1536]{1,0:T(8,128)(2,1)S(1)} fusion(f32[1600,1536]{1,0:T(8,128)S(1)} %fusion.72, f32[1536]{0:T(1024)S(1)} %copy-done.19, f32[1536]{0:T(1024)S(1)} %copy-done.21, s32[1600]{0:T(1024)S(1)} %add_select_fusion.7), kind=kOutput, calls=%fused_computation.21 | convolution fusion | flops 486679552 | bytes 9898240 | tf_op jit(solution)/shard_map/dot_general | solution.py:115
  10.9 4.0 %collective-permute-start.2 = (bf16[16,1536]{1,0:T(8,128)(2,1)S(1)}, bf16[16,1536]{1,0:T(8,128)(2,1)S(1)}, u32[]{:S(2)}, u32[]{:S(2)}) collective-permute-start(bf16[16,1536]{1,0:T(8,128)(2,1)S(1)} %fusion.12), channel_id=1, source_target_pairs={{0,3},{1,2},{2,1},{3,0},{4,7},{5,6},{6,5},{7,4},{8,11},{9,10},{10,... | collective-permute-start | bytes 147464 | tf_op jit(solution)/shard_map/ppermute | solution.py:81
  20.2 1.1 fusion.16
  25.4 2.5 %select_reduce_fusion = (f32[64,64]{1,0:T(8,128)S(1)}, f32[64,64]{1,0:T(8,128)S(1)}) fusion(pred[64,16]{0,1:T(8,128)(4,1)} %iota_compare_fusion.7, pred[64,16]{0,1:T(8,128)(4,1)} %iota_compare_fusion.8, bf16[64,1536,1]{1,0,2:T(8,128)(2,1)S(1)} %bitcast.84, bf16[16,64,1536]{2,1,0:T(8,128)(2,1)S(1)} %bitcast.75), kind=kOutput, calls=%fused_computation.35 | convolution fusion | flops 201580544 | bytes 3377152 | tf_op jit(solution)/shard_map/dot_general | solution.py:132
  28.8 1.1 tile.13
  31.4 1.8 %tile.15 = bf16[4,16,1024]{2,1,0:T(8,128)(2,1)} reshape(bf16[64,16,64]{2,1,0:T(8,128)(2,1)} %tile.14) | data formatting | bytes 262144 | tf_op jit(solution)/shard_map/tile | solution.py:15
  33.2 1.6 %fusion.7 = f32[4,16,1536]{2,1,0:T(8,128)S(1)} fusion(bf16[1024,1536]{1,0:T(8,128)(2,1)S(1)} %copy-done, bf16[4,16,1024]{2,1,0:T(8,128)(2,1)S(1)} %tile.13, bf16[4,16,1024]{2,1,0:T(8,128)(2,1)} %tile.15, s32[4,16]{1,0:T(4,128)} %get-tuple-element.27, s32[4,16]{1,0:T(4,128)S(1)} %get-tuple-element.26, s32[1024]{0:T(1024)S(1)} %add_select_fusion.8), kind=kOutput, calls=%fused_computation.16 | convolution fusion | flops 201654272 | bytes 3805696 | tf_op jit(solution)/shard_map/dot_general | solution.py:142
  36.3 2.8 %collective-permute-start.5 = (f32[16,1536]{1,0:T(8,128)}, f32[16,1536]{1,0:T(8,128)}, u32[]{:S(2)}, u32[]{:S(2)}) collective-permute-start(f32[16,1536]{1,0:T(8,128)} %get-tuple-element.17), channel_id=1, source_target_pairs={{0,3},{1,2},{2,1},{3,0},{4,7},{5,6},{6,5},{7,4},{8,11},{9,10},{10,... | collective-permute-start | bytes 294920 | tf_op jit(solution)/shard_map/ppermute | solution.py:93
  39.8 2.8 %collective-permute-done.5 = f32[16,1536]{1,0:T(8,128)} collective-permute-done((f32[16,1536]{1,0:T(8,128)}, f32[16,1536]{1,0:T(8,128)}, u32[]{:S(2)}, u32[]{:S(2)}) %collective-permute-start.5) | collective-permute-done | bytes 98336 | tf_op jit(solution)/shard_map/ppermute | solution.py:93
  42.6 1.5 %collective-permute-done.4 = f32[16,1536]{1,0:T(8,128)} collective-permute-done((f32[16,1536]{1,0:T(8,128)}, f32[16,1536]{1,0:T(8,128)}, u32[]{:S(2)}, u32[]{:S(2)}) %collective-permute-start.4) | collective-permute-done | bytes 98336 | tf_op jit(solution)/shard_map/ppermute | solution.py:93
  44.4 10.9 %multiply_reduce_fusion = (f32[1536]{0:T(1024)S(1)}, f32[1536]{0:T(1024)S(1)}, f32[1600,1536]{1,0:T(8,128)S(1)}) fusion(f32[1600,1536]{1,0:T(8,128)} %copy-done.1, f32[1536]{0:T(1024)S(1)} %copy-done.20, f32[1536]{0:T(1024)S(1)} %copy-done.22, f32[16,1536]{1,0:T(8,128)} %collective-permute-done.5, f32[16,1536]{1,0:T(8,128)} %collective-permute-done.4, ...), kind=kOutput, calls=%fused_computation.2 | convolution fusion | flops 503928832 | bytes 20084996 | tf_op jit(solution)/shard_map/dot_general | solution.py:174
  55.4 4.5 %fusion.2 = f32[1536,384]{1,0:T(8,128)} fusion(bf16[1600,384]{1,0:T(8,128)(2,1)S(1)} %copy-done.4, f32[1600,1536]{1,0:T(8,128)S(1)} %get-tuple-element.25, f32[1536]{0:T(1024)S(1)} %copy-done.22), kind=kOutput, calls=%fused_computation.9 | convolution fusion | flops 1892352000 | bytes 13424640 | tf_op jit(solution)/shard_map/dot_general | solution.py:177
  59.9 1.2 copy.68
  61.1 1.6 %concatenate.19 = f32[4,2,1,1,384]{4,3,1,0,2:T(1,128)S(1)} reshape(f32[1536,2]{1,0:T(8,128)} %copy.68) | data formatting | bytes 24576 | tf_op jit(solution)/shard_map/concatenate | solution.py:187
  62.7 1.4 %fusion.17 = f32[4,1,1,193,384]{4,3,1,0,2:T(8,128)S(1)} fusion(s32[]{:T(128)S(6)} %select_n.395, f32[4,2,1,192,384]{4,3,1,0,2:T(8,128)} %bitcast.76, f32[4,2,1,1,384]{4,3,1,0,2:T(1,128)S(1)} %concatenate.19), kind=kLoop, calls=%fused_computation.27 | loop fusion | flops 296448 | bytes 3557380 | tf_op jit(solution)/shard_map/concatenate | solution.py:187
  64.1 1.3 %copy.97 = f32[4,1,1,193,384]{4,0,3,2,1:T(4,128)} copy(f32[4,1,1,193,384]{4,3,1,0,2:T(8,128)S(1)} %fusion.17) | data formatting | bytes 2371584 | tf_op jit(solution)/shard_map/jit(dynamic_index_in_dim)/dynamic_slice | solution.py:60
  65.8 2.8 %collective-permute-done.6 = f32[4,1,193,384]{3,0,2,1:T(4,128)} collective-permute-done((f32[4,1,193,384]{3,0,2,1:T(4,128)}, f32[4,1,193,384]{3,0,2,1:T(4,128)}, u32[]{:S(2)}, u32[]{:S(2)}) %collective-permute-start.6) | collective-permute-done | bytes 1185824 | tf_op jit(solution)/shard_map/ppermute | solution.py:61
  68.6 1.8 %fusion.20 = f32[4,1,193,384]{3,2,0,1:T(8,128)S(1)} fusion(s32[]{:T(128)S(6)} %select_n.394, f32[4,2,1,192,384]{4,3,1,0,2:T(8,128)} %bitcast.77, f32[4,2,1,1,384]{4,3,1,0,2:T(1,128)S(1)} %concatenate.19, f32[4,1,193,384]{3,0,2,1:T(4,128)} %collective-permute-done.6), kind=kLoop, calls=%fused_computation.30 | loop fusion | flops 592896 | bytes 4743172 | tf_op jit(solution)/shard_map/add | solution.py:62
  71.5 1.1 copy.72
  72.6 1.6 %collective-permute-start.7 = (f32[2,1,193,384]{3,0,2,1:T(2,128)}, f32[2,1,193,384]{3,0,2,1:T(2,128)}, u32[]{:S(2)}, u32[]{:S(2)}) collective-permute-start(f32[2,1,193,384]{3,0,2,1:T(2,128)} %copy.72), channel_id=1, source_target_pairs={{0,8},{4,12},{8,0},{12,4},{16,24},{20,28},{24,16},{28,20},{1,9},{5... | collective-permute-start | bytes 1778696 | tf_op jit(solution)/shard_map/ppermute | solution.py:61
  77.2 4.1 %all-to-all-start = ((bf16[8,64,322]{2,1,0:T(8,128)(2,1)}), bf16[8,64,322]{2,1,0:T(8,128)(2,1)}, u32[]{:S(2)}, u32[]{:S(2)}) async-start(bf16[8,64,322]{2,1,0:T(8,128)(2,1)} %pad_maximum_fusion), calls=%async_computation | async-start | bytes 786432 | tf_op jit(solution)/shard_map/all_to_all | solution.py:162
  81.3 9.9 %collective-permute-done.7 = f32[2,1,193,384]{3,0,2,1:T(2,128)} collective-permute-done((f32[2,1,193,384]{3,0,2,1:T(2,128)}, f32[2,1,193,384]{3,0,2,1:T(2,128)}, u32[]{:S(2)}, u32[]{:S(2)}) %collective-permute-start.7) | collective-permute-done | bytes 592928 | tf_op jit(solution)/shard_map/ppermute | solution.py:61
  91.2 1.3 %bitcast_add_fusion = f32[2,1,193,384]{3,2,0,1:T(8,128)S(1)} fusion(f32[2,1,193,384]{3,0,2,1:T(2,128)} %collective-permute-done.7, f32[2,2,1,193,384]{4,3,1,0,2:T(8,128)} %bitcast.79, s32[]{:T(128)S(6)} %select_n.398), kind=kLoop, calls=%fused_computation.33 | loop fusion | flops 148224 | bytes 1778692 | tf_op jit(solution)/shard_map/add | solution.py:62
  94.1 3.8 %collective-permute-start.8 = (f32[1,1,193,384]{3,2,0,1:T(8,128)}, f32[1,1,193,384]{3,2,0,1:T(8,128)}, u32[]{:S(2)}, u32[]{:S(2)}) collective-permute-start(f32[1,1,193,384]{3,2,0,1:T(8,128)} %constant_dynamic-slice_fusion), channel_id=1, source_target_pairs={{0,16},{4,20},{8,24},{12,28},{16,0},{20,4},{24,8},{28,12},{1,17},{... | collective-permute-start | bytes 889352 | tf_op jit(solution)/shard_map/ppermute | solution.py:61
  99.0 10.8 %collective-permute-done.8 = f32[1,1,193,384]{3,2,0,1:T(8,128)} collective-permute-done((f32[1,1,193,384]{3,2,0,1:T(8,128)}, f32[1,1,193,384]{3,2,0,1:T(8,128)}, u32[]{:S(2)}, u32[]{:S(2)}) %collective-permute-start.8) | collective-permute-done | bytes 296480 | tf_op jit(solution)/shard_map/ppermute | solution.py:61
  109.9 1.8 %add_bitcast_fusion = f32[193,384]{1,0:T(8,128)} fusion(f32[1,1,193,384]{3,2,0,1:T(8,128)} %collective-permute-done.8, f32[2,1,193,384]{3,2,0,1:T(8,128)} %copy-done.3, s32[]{:T(128)S(6)} %select_n.402), kind=kLoop, calls=%fused_computation.41 | loop fusion | flops 74112 | bytes 889348 | tf_op jit(solution)/shard_map/squeeze;reshape | solution.py:191
  117.5 1.6 %collective-permute-done.9 = f32[193,384]{1,0:T(8,128)} collective-permute-done((f32[193,384]{1,0:T(8,128)}, f32[193,384]{1,0:T(8,128)}, u32[]{:S(2)}, u32[]{:S(2)}) %collective-permute-start.9) | collective-permute-done | bytes 296480 | tf_op jit(solution)/shard_map/ppermute | solution.py:72
  119.1 1.1 add.295
  120.2 1.6 %collective-permute-start.10 = (f32[193,384]{1,0:T(8,128)S(1)}, f32[193,384]{1,0:T(8,128)S(1)}, u32[]{:S(2)}, u32[]{:S(2)}) collective-permute-start(f32[193,384]{1,0:T(8,128)S(1)} %add.295), channel_id=1, source_target_pairs={{0,2},{1,3},{2,0},{3,1},{4,6},{5,7},{6,4},{7,5},{8,10},{9,11},{10,... | collective-permute-start | bytes 889352 | tf_op jit(solution)/shard_map/ppermute | solution.py:72
  123.3 1.4 %fusion.73 = f32[1024,192]{0,1:T(8,128)} fusion(bf16[512,1024]{0,1:T(8,128)(2,1)S(1)} %bitcast.80, bf16[512,192]{1,0:T(8,128)(2,1)S(1)} %bitcast.83), kind=kOutput, calls=%fused_computation.187 | convolution fusion | flops 201326592 | bytes 2031616 | tf_op jit(solution)/shard_map/dot_general | solution.py:170
  124.7 2.4 %collective-permute-done.10 = f32[193,384]{1,0:T(8,128)S(1)} collective-permute-done((f32[193,384]{1,0:T(8,128)S(1)}, f32[193,384]{1,0:T(8,128)S(1)}, u32[]{:S(2)}, u32[]{:S(2)}) %collective-permute-start.10) | collective-permute-done | bytes 296480 | tf_op jit(solution)/shard_map/ppermute | solution.py:72
  (124 shorter events, 30.3 us)
Async XLA Ops:
  0.6 24.8 %copy-start = (bf16[1024,1536]{1,0:T(8,128)(2,1)S(1)}, bf16[1024,1536]{1,0:T(8,128)(2,1)}, u32[]{:S(2)}) copy-start(bf16[1024,1536]{1,0:T(8,128)(2,1)} %param.12) | copy-start | bytes 9437188
  0.7 4.5 %copy-start.14 = (s32[1600]{0:T(1024)}, s32[1600]{0:T(1024)S(1)}, u32[]{:S(2)}) copy-start(s32[1600]{0:T(1024)S(1)} %add_select_fusion.7) | copy-start | bytes 19204
  0.7 4.5 %copy-start.19 = (f32[1536]{0:T(1024)S(1)}, f32[1536]{0:T(1024)}, u32[]{:S(2)}) copy-start(f32[1536]{0:T(1024)} %param.11) | copy-start | bytes 18436
  0.7 4.5 %copy-start.21 = (f32[1536]{0:T(1024)S(1)}, f32[1536]{0:T(1024)}, u32[]{:S(2)}) copy-start(f32[1536]{0:T(1024)} %param.10) | copy-start | bytes 18436
  5.2 5.7 %copy-start.1 = (f32[1600,1536]{1,0:T(8,128)}, f32[1600,1536]{1,0:T(8,128)S(1)}, u32[]{:S(2)}) copy-start(f32[1600,1536]{1,0:T(8,128)S(1)} %fusion.72) | copy-start | bytes 29491204
  5.2 10.3 %copy-start.8 = (s32[64,64]{1,0:T(8,128)S(1)}, s32[64,64]{1,0:T(8,128)}, u32[]{:S(2)}) copy-start(s32[64,64]{1,0:T(8,128)} %param.14) | copy-start | bytes 49156
  5.3 11.0 %copy-start.18 = (s32[64]{0:T(128)S(1)}, s32[64]{0:T(128)}, u32[]{:S(2)}) copy-start(s32[64]{0:T(128)} %param.13) | copy-start | bytes 772
  10.9 11.5 %collective-permute-start.2 = (bf16[16,1536]{1,0:T(8,128)(2,1)S(1)}, bf16[16,1536]{1,0:T(8,128)(2,1)S(1)}, u32[]{:S(2)}, u32[]{:S(2)}) collective-permute-start(bf16[16,1536]{1,0:T(8,128)(2,1)S(1)} %fusion.12), channel_id=1, source_target_pairs={{0,3},{1,2},{2,1},{3,0},{4,7},{5,6},{6,5},{7,4},{8,11},{9,10},{10,... | collective-permute-start | bytes 147464 | tf_op jit(solution)/shard_map/ppermute | solution.py:81
  14.9 7.6 %collective-permute-start.1 = (bf16[16,1536]{1,0:T(8,128)(2,1)S(1)}, bf16[16,1536]{1,0:T(8,128)(2,1)S(1)}, u32[]{:S(2)}, u32[]{:S(2)}) collective-permute-start(bf16[16,1536]{1,0:T(8,128)(2,1)S(1)} %fusion.12), channel_id=1, source_target_pairs={{0,2},{1,3},{2,0},{3,1},{4,6},{5,7},{6,4},{7,5},{8,10},{9,11},{10,... | collective-permute-start | bytes 147464 | tf_op jit(solution)/shard_map/ppermute | solution.py:81
  15.4 7.1 %collective-permute-start = (bf16[16,1536]{1,0:T(8,128)(2,1)S(1)}, bf16[16,1536]{1,0:T(8,128)(2,1)S(1)}, u32[]{:S(2)}, u32[]{:S(2)}) collective-permute-start(bf16[16,1536]{1,0:T(8,128)(2,1)S(1)} %fusion.12), channel_id=1, source_target_pairs={{0,1},{1,0},{2,3},{3,2},{4,5},{5,4},{6,7},{7,6},{8,9},{9,8},{10,11... | collective-permute-start | bytes 147464 | tf_op jit(solution)/shard_map/ppermute | solution.py:81
  16.4 2.4 %copy-start.10 = (s32[64]{0:T(128)}, s32[64]{0:T(128)S(1)}, u32[]{:S(2)}) copy-start(s32[64]{0:T(128)S(1)} %get-tuple-element.10) | copy-start | bytes 772
  16.4 2.4 %copy-start.12 = (s32[64]{0:T(128)}, s32[64]{0:T(128)S(1)}, u32[]{:S(2)}) copy-start(s32[64]{0:T(128)S(1)} %get-tuple-element.11) | copy-start | bytes 772
  24.6 3.3 %copy-start.9 = (pred[64,64]{1,0:T(8,128)(4,1)S(1)}, pred[64,64]{1,0:T(8,128)(4,1)}, u32[]{:S(2)}) copy-start(pred[64,64]{1,0:T(8,128)(4,1)} %fusion.23) | copy-start | bytes 12292
  24.7 3.3 %copy-start.16 = (pred[64]{0:T(512)(128)(4,1)S(1)}, pred[64]{0:T(512)(128)(4,1)}, u32[]{:S(2)}) copy-start(pred[64]{0:T(512)(128)(4,1)} %get-tuple-element.14) | copy-start | bytes 196
  33.2 11.2 %copy-start.15 = (s32[1600]{0:T(1024)S(1)}, s32[1600]{0:T(1024)}, u32[]{:S(2)}) copy-start(s32[1600]{0:T(1024)} %copy-done.14) | copy-start | bytes 19204
  33.2 11.2 %copy-start.20 = (f32[1536]{0:T(1024)S(1)}, f32[1536]{0:T(1024)}, u32[]{:S(2)}) copy-start(f32[1536]{0:T(1024)} %param.11) | copy-start | bytes 18436
  33.2 11.2 %copy-start.22 = (f32[1536]{0:T(1024)S(1)}, f32[1536]{0:T(1024)}, u32[]{:S(2)}) copy-start(f32[1536]{0:T(1024)} %param.10) | copy-start | bytes 18436
  36.3 6.3 %collective-permute-start.5 = (f32[16,1536]{1,0:T(8,128)}, f32[16,1536]{1,0:T(8,128)}, u32[]{:S(2)}, u32[]{:S(2)}) collective-permute-start(f32[16,1536]{1,0:T(8,128)} %get-tuple-element.17), channel_id=1, source_target_pairs={{0,3},{1,2},{2,1},{3,0},{4,7},{5,6},{6,5},{7,4},{8,11},{9,10},{10,... | collective-permute-start | bytes 294920 | tf_op jit(solution)/shard_map/ppermute | solution.py:93
  39.2 4.9 %collective-permute-start.4 = (f32[16,1536]{1,0:T(8,128)}, f32[16,1536]{1,0:T(8,128)}, u32[]{:S(2)}, u32[]{:S(2)}) collective-permute-start(f32[16,1536]{1,0:T(8,128)} %get-tuple-element.18), channel_id=1, source_target_pairs={{0,2},{1,3},{2,0},{3,1},{4,6},{5,7},{6,4},{7,5},{8,10},{9,11},{10,... | collective-permute-start | bytes 294920 | tf_op jit(solution)/shard_map/ppermute | solution.py:93
  39.7 4.7 %collective-permute-start.3 = (f32[16,1536]{1,0:T(8,128)S(1)}, f32[16,1536]{1,0:T(8,128)}, u32[]{:S(2)}, u32[]{:S(2)}) collective-permute-start(f32[16,1536]{1,0:T(8,128)S(1)} %get-tuple-element.16), channel_id=1, source_target_pairs={{0,1},{1,0},{2,3},{3,2},{4,5},{5,4},{6,7},{7,6},{8,9},{9,8},{10,11... | collective-permute-start | bytes 294920 | tf_op jit(solution)/shard_map/ppermute | solution.py:93
  39.8 15.5 %copy-start.4 = (bf16[1600,384]{1,0:T(8,128)(2,1)S(1)}, bf16[1600,384]{1,0:T(8,128)(2,1)}, u32[]{:S(2)}) copy-start(bf16[1600,384]{1,0:T(8,128)(2,1)} %param.8) | copy-start | bytes 3686404
  62.7 2.7 %copy-start.13 = (s32[64]{0:T(128)S(1)}, s32[64]{0:T(128)}, u32[]{:S(2)}) copy-start(s32[64]{0:T(128)} %copy-done.12) | copy-start | bytes 772
  62.7 2.8 %copy-start.11 = (s32[64]{0:T(128)S(1)}, s32[64]{0:T(128)}, u32[]{:S(2)}) copy-start(s32[64]{0:T(128)} %copy-done.10) | copy-start | bytes 772
  62.7 2.9 %copy-start.17 = (pred[4]{0:T(512)(128)(4,1)S(1)}, pred[4]{0:T(512)(128)(4,1)}, u32[]{:S(2)}) copy-start(pred[4]{0:T(512)(128)(4,1)} %compare_and_fusion) | copy-start | bytes 16
  65.4 3.2 %collective-permute-start.6 = (f32[4,1,193,384]{3,0,2,1:T(4,128)}, f32[4,1,193,384]{3,0,2,1:T(4,128)}, u32[]{:S(2)}, u32[]{:S(2)}) collective-permute-start(f32[4,1,193,384]{3,0,2,1:T(4,128)} %bitcast.74), channel_id=1, source_target_pairs={{0,4},{4,0},{8,12},{12,8},{16,20},{20,16},{24,28},{28,24},{1,5},{5... | collective-permute-start | bytes 3557384 | tf_op jit(solution)/shard_map/ppermute | solution.py:61
  70.4 1.1 copy-start.2
  72.6 18.7 %collective-permute-start.7 = (f32[2,1,193,384]{3,0,2,1:T(2,128)}, f32[2,1,193,384]{3,0,2,1:T(2,128)}, u32[]{:S(2)}, u32[]{:S(2)}) collective-permute-start(f32[2,1,193,384]{3,0,2,1:T(2,128)} %copy.72), channel_id=1, source_target_pairs={{0,8},{4,12},{8,0},{12,4},{16,24},{20,28},{24,16},{28,20},{1,9},{5... | collective-permute-start | bytes 1778696 | tf_op jit(solution)/shard_map/ppermute | solution.py:61
  77.2 20.7 %all-to-all-start = ((bf16[8,64,322]{2,1,0:T(8,128)(2,1)}), bf16[8,64,322]{2,1,0:T(8,128)(2,1)}, u32[]{:S(2)}, u32[]{:S(2)}) async-start(bf16[8,64,322]{2,1,0:T(8,128)(2,1)} %pad_maximum_fusion), calls=%async_computation | async-start | bytes 786432 | tf_op jit(solution)/shard_map/all_to_all | solution.py:162
  92.6 0.8 copy-start.3
  94.1 15.7 %collective-permute-start.8 = (f32[1,1,193,384]{3,2,0,1:T(8,128)}, f32[1,1,193,384]{3,2,0,1:T(8,128)}, u32[]{:S(2)}, u32[]{:S(2)}) collective-permute-start(f32[1,1,193,384]{3,2,0,1:T(8,128)} %constant_dynamic-slice_fusion), channel_id=1, source_target_pairs={{0,16},{4,20},{8,24},{12,28},{16,0},{20,4},{24,8},{28,12},{1,17},{... | collective-permute-start | bytes 889352 | tf_op jit(solution)/shard_map/ppermute | solution.py:61
  111.7 7.5 %collective-permute-start.9 = (f32[193,384]{1,0:T(8,128)}, f32[193,384]{1,0:T(8,128)}, u32[]{:S(2)}, u32[]{:S(2)}) collective-permute-start(f32[193,384]{1,0:T(8,128)} %add_bitcast_fusion), channel_id=1, source_target_pairs={{0,1},{1,0},{2,3},{3,2},{4,5},{5,4},{6,7},{7,6},{8,9},{9,8},{10,11... | collective-permute-start | bytes 889352 | tf_op jit(solution)/shard_map/ppermute | solution.py:72
  120.2 6.9 %collective-permute-start.10 = (f32[193,384]{1,0:T(8,128)S(1)}, f32[193,384]{1,0:T(8,128)S(1)}, u32[]{:S(2)}, u32[]{:S(2)}) collective-permute-start(f32[193,384]{1,0:T(8,128)S(1)} %add.295), channel_id=1, source_target_pairs={{0,2},{1,3},{2,0},{3,1},{4,6},{5,7},{6,4},{7,5},{8,10},{9,11},{10,... | collective-permute-start | bytes 889352 | tf_op jit(solution)/shard_map/ppermute | solution.py:72
  (3 other events, 2.0 us)

commit v10 on v6

--- a/solution.py
+++ b/solution.py
@@ -159,14 +159,18 @@
     e_size = head_term.shape[1]
     chunk = width // n_dp
     extra = -(-2 * chunk // e_size)
-    side_rows = jnp.stack([gain_term, shift_term], axis=1).reshape(n_dp, 2 * chunk)
-    side_rows = jnp.pad(side_rows, ((0, 0), (0, extra * e_size - 2 * chunk)))
+    pad_rows = -(-extra // 8) * 8
+    side_rows = jnp.concatenate(
+        [gain_term.reshape(n_dp, chunk), shift_term.reshape(n_dp, chunk)], axis=1
+    )
+    side_rows = jnp.pad(side_rows, ((0, 0), (0, pad_rows * e_size - 2 * chunk)))
     stacked = jnp.concatenate(
-        [head_term.reshape(n_dp, chunk, e_size), side_rows.reshape(n_dp, extra, e_size)], axis=1
+        [head_term.reshape(n_dp, chunk, e_size), side_rows.reshape(n_dp, pad_rows, e_size)], axis=1
     )
     (part,) = halving_scatter([stacked], "dp")
     (total,) = butterfly_sum([part[0]], "leaf")
-    side_sum = total[chunk:].reshape(-1)[: 2 * chunk].reshape(chunk, 2)
+    side_flat = total[chunk:].reshape(-1)
+    side_sum = jnp.stack([side_flat[:chunk], side_flat[chunk : 2 * chunk]], axis=1)
     return (total[:chunk].T, side_sum[:, 0], side_sum[:, 1], node_grad)
 
 

time: 127 us -> 124 us (0.976)
  local copies, waits for them, and re-layouts: 21.7 us -> 17.2 us
    squeeze x0 -> x1, other arithmetic: none -> 2.41 us  [halving_scatter(): lax.dynamic_index_in_dim(p, 1 - mine, axis=1, keepdims=False)]
    concatenate x1 -> x0, local copies, waits for them, and re-layouts: 1.59 us -> none  [shards(): jnp.concatenate([head_term.reshape(n_dp, chunk, e_size), side_rows.reshap...]
    dynamic_slice x1 -> x0, local copies, waits for them, and re-layouts: 1.35 us -> none  [halving_scatter(): lax.dynamic_index_in_dim(p, 1 - mine, axis=1, keepdims=False)]
    another operation x4 -> x0, local copies, waits for them, and re-layouts: 1.33 us -> none  [the longest x3 1.19 us: shards(): jnp.stack([gain_term, shift_term], axis=1).reshape(n_dp, 2 * chunk)]
    concatenate x1, other arithmetic: 1.36 us -> 0.08 us  [shards(): jnp.concatenate([gain_term.reshape(n_dp, chunk), shift_term.reshape(n_dp,...]
    squeeze x5 -> x4, local copies, waits for them, and re-layouts: 2.6 us -> 2.32 us  [halving_scatter(): lax.dynamic_index_in_dim(p, 1 - mine, axis=1, keepdims=False)]
    unnamed x43 -> x44, local copies, waits for them, and re-layouts: 6.16 us -> 6.21 us
where the time goes in v10:
time: 124 us; the launch traced here: 123 us
  waiting for transfers between devices  40.8 us (33%)
  matrix products  30.4 us (25%)
  starting transfers between devices  17.9 us (14%)
  local copies, waits for them, and re-layouts  17.2 us (14%)
  other arithmetic  15.1 us (12%)
    ppermute x5, waiting for transfers between devices, halving_scatter(): got = lax.ppermute(tuple(give), name, partners(size, bit))  33.9 us
    dot_general x1, matrix products, shards(): jnp.dot(select.T, emb_grad / P_SIZE, precision=HIGHEST, preferred_element...  10.9 us
    ppermute x5, starting transfers between devices, halving_scatter(): got = lax.ppermute(tuple(give), name, partners(size, bit))  7.1 us
    unnamed x44, local copies, waits for them, and re-layouts  6.21 us
    dot_general x1, matrix products, shards(): jnp.dot(select, active, precision=HIGHEST, preferred_element_type=jnp.flo...  5.63 us
    ppermute x2, starting transfers between devices, doubling_gather(): other = lax.ppermute(cur, name, partners(size, bit))  4.58 us
    dot_general x1, matrix products, shards(): jnp.dot(features, head_weight, preferred_element_type=jnp.float32)  4.5 us
    dot_general x1, matrix products, shards(): lax.dot_general(lin_grad, features, (((0,), (0,)), ((), ())), preferred_e...  4.5 us
  transfers between devices with their start and end apart: 10, of which 8 were waited for; matrix products, arithmetic and copies ran while one was open for 14% of the time, Pallas kernels for 0%

profile of v10, /device:TPU:0, one launch (start us, length us, event | category | flops | bytes accessed | tf_op | source)
XLA Modules:
  0.0 122.5 jit_solution(3413710358307263353)
XLA Ops:
  0.7 4.5 %fusion.66 = f32[1600,1536]{1,0:T(8,128)S(1)} fusion(bf16[1600,384]{1,0:T(8,128)(2,1)} %param.8, bf16[384,1536]{1,0:T(8,128)(2,1)} %param.9), kind=kOutput, calls=%fused_computation.170 | convolution fusion | flops 1887436800 | bytes 12238848 | tf_op jit(solution)/shard_map/dot_general | solution.py:92
  5.3 5.6 %fusion.15 = bf16[1,16,1536]{2,1,0:T(8,128)(2,1)S(1)} fusion(f32[1600,1536]{1,0:T(8,128)S(1)} %fusion.66, f32[1536]{0:T(1024)S(1)} %copy-done.16, f32[1536]{0:T(1024)S(1)} %copy-done.17, s32[1600]{0:T(1024)S(1)} %add_select_fusion.7), kind=kOutput, calls=%fused_computation.21 | convolution fusion | flops 486679552 | bytes 9898240 | tf_op jit(solution)/shard_map/dot_general | solution.py:96
  10.9 3.0 %collective-permute-start = (bf16[1,16,1536]{2,1,0:T(8,128)(2,1)S(1)}, bf16[1,16,1536]{2,1,0:T(8,128)(2,1)S(1)}, u32[]{:S(2)}, u32[]{:S(2)}) collective-permute-start(bf16[1,16,1536]{2,1,0:T(8,128)(2,1)S(1)} %fusion.15), channel_id=1, source_target_pairs={{0,1},{1,0},{2,3},{3,2},{4,5},{5,4},{6,7},{7,6},{8,9},{9,8},{10,11... | collective-permute-start | bytes 147464 | tf_op jit(solution)/shard_map/ppermute | solution.py:44
  15.7 1.1 fusion.19
  17.9 1.6 %collective-permute-start.1 = (bf16[2,16,1536]{2,1,0:T(8,128)(2,1)S(1)}, bf16[2,16,1536]{2,1,0:T(8,128)(2,1)S(1)}, u32[]{:S(2)}, u32[]{:S(2)}) collective-permute-start(bf16[2,16,1536]{2,1,0:T(8,128)(2,1)S(1)} %maximum_select_fusion.1), channel_id=1, source_target_pairs={{0,2},{1,3},{2,0},{3,1},{4,6},{5,7},{6,4},{7,5},{8,10},{9,11},{10,... | collective-permute-start | bytes 294920 | tf_op jit(solution)/shard_map/ppermute | solution.py:44
  20.1 2.5 %collective-permute-done.1 = bf16[2,16,1536]{2,1,0:T(8,128)(2,1)S(1)} collective-permute-done((bf16[2,16,1536]{2,1,0:T(8,128)(2,1)S(1)}, bf16[2,16,1536]{2,1,0:T(8,128)(2,1)S(1)}, u32[]{:S(2)}, u32[]{:S(2)}) %collective-permute-start.1) | collective-permute-done | bytes 98336 | tf_op jit(solution)/shard_map/ppermute | solution.py:44
  22.6 1.8 %select_reduce_fusion = (f32[64,64]{1,0:T(8,128)S(1)}, f32[64,64]{1,0:T(8,128)S(1)}) fusion(pred[64,16]{0,1:T(8,128)(4,1)S(1)} %iota_compare_fusion.8, pred[64,16]{0,1:T(8,128)(4,1)S(1)} %iota_compare_fusion.9, bf16[64,1536,1]{1,0,2:T(8,128)(2,1)S(1)} %bitcast.81, bf16[16,64,1536]{2,1,0:T(8,128)(2,1)S(1)} %bitcast.69), kind=kOutput, calls=%fused_computation.35 | convolution fusion | flops 201580544 | bytes 3377152 | tf_op jit(solution)/shard_map/dot_general | solution.py:112
  26.4 1.7 %fusion.7 = f32[2,2,16,1536]{3,2,1,0:T(8,128)S(1)} fusion(bf16[1024,1536]{1,0:T(8,128)(2,1)S(1)} %copy-done, bf16[2,2,16,1024]{3,2,1,0:T(8,128)(2,1)} %tile.13, bf16[2,2,16,1024]{3,2,1,0:T(8,128)(2,1)} %tile.15, s32[2,2,16]{2,1,0:T(2,128)} %get-tuple-element.23, s32[2,2,16]{2,1,0:T(2,128)} %get-tuple-element.24, s32[1024]{0:T(1024)} %add_select_fusion.8), kind=kOutput, calls=%fused_computation.15 | convolution fusion | flops 201654272 | bytes 3805696 | tf_op jit(solution)/shard_map/dot_general | solution.py:122
  28.9 5.9 %collective-permute-done.2 = f32[2,16,1536]{2,1,0:T(8,128)} collective-permute-done((f32[2,16,1536]{2,1,0:T(8,128)}, f32[2,16,1536]{2,1,0:T(8,128)}, u32[]{:S(2)}, u32[]{:S(2)}) %collective-permute-start.2) | collective-permute-done | bytes 196640 | tf_op jit(solution)/shard_map/ppermute | solution.py:61
  36.4 1.6 %collective-permute-start.3 = (f32[1,16,1536]{2,1,0:T(8,128)S(1)}, f32[1,16,1536]{2,1,0:T(8,128)S(1)}, u32[]{:S(2)}, u32[]{:S(2)}) collective-permute-start(f32[1,16,1536]{2,1,0:T(8,128)S(1)} %constant_dynamic-slice_fusion.1), channel_id=1, source_target_pairs={{0,2},{1,3},{2,0},{3,1},{4,6},{5,7},{6,4},{7,5},{8,10},{9,11},{10,... | collective-permute-start | bytes 294920 | tf_op jit(solution)/shard_map/ppermute | solution.py:61
  38.0 3.1 %collective-permute-done.3 = f32[1,16,1536]{2,1,0:T(8,128)S(1)} collective-permute-done((f32[1,16,1536]{2,1,0:T(8,128)S(1)}, f32[1,16,1536]{2,1,0:T(8,128)S(1)}, u32[]{:S(2)}, u32[]{:S(2)}) %collective-permute-start.3) | collective-permute-done | bytes 98336 | tf_op jit(solution)/shard_map/ppermute | solution.py:61
  41.1 10.9 %multiply_reduce_fusion = (f32[1536]{0:T(1024)S(1)}, f32[1536]{0:T(1024)S(1)}, f32[1600,1536]{1,0:T(8,128)S(1)}) fusion(f32[1600,1536]{1,0:T(8,128)} %copy-done.1, f32[1536]{0:T(1024)} %param.11, f32[1536]{0:T(1024)} %param.10, f32[1,16,1536]{2,1,0:T(8,128)S(1)} %collective-permute-done.3, f32[2,16,1536]{2,1,0:T(8,128)} %copy-done.6, s32[]{:T(128)S(6)} %select_n.411, ...), kind=kOutput, calls=%fused_computation.1 | convolution fusion | flops 503879680 | bytes 19894276 | tf_op jit(solution)/shard_map/dot_general | solution.py:151
  52.0 4.5 %fusion.2 = f32[1536,384]{1,0:T(8,128)} fusion(bf16[1600,384]{1,0:T(8,128)(2,1)S(1)} %copy-done.4, f32[1600,1536]{1,0:T(8,128)S(1)} %get-tuple-element.22, f32[1536]{0:T(1024)S(1)} %copy-done.18), kind=kOutput, calls=%fused_computation.8 | convolution fusion | flops 1892352000 | bytes 13424640 | tf_op jit(solution)/shard_map/dot_general | solution.py:154
  56.7 2.4 %fusion.21 = f32[4,1,200,384]{3,2,0,1:T(8,128)} fusion(s32[]{:T(128)S(6)} %select_n.415, f32[4,2,1,192,384]{4,3,1,0,2:T(8,128)} %bitcast.70, f32[4,2,1,8,384]{4,3,1,0,2:T(8,128)S(1)} %bitcast.79), kind=kLoop, calls=%fused_computation.28 | loop fusion | flops 307200 | bytes 3686404 | tf_op jit(solution)/shard_map/jit(dynamic_index_in_dim)/squeeze | solution.py:60
  59.1 3.3 %collective-permute-done.4 = f32[4,1,200,384]{3,2,0,1:T(8,128)} collective-permute-done((f32[4,1,200,384]{3,2,0,1:T(8,128)}, f32[4,1,200,384]{3,2,0,1:T(8,128)}, u32[]{:S(2)}, u32[]{:S(2)}) %collective-permute-start.4) | collective-permute-done | bytes 1228832 | tf_op jit(solution)/shard_map/ppermute | solution.py:61
  62.4 1.8 %fusion.24 = f32[4,1,200,384]{3,2,0,1:T(8,128)S(1)} fusion(f32[4,1,200,384]{3,2,0,1:T(8,128)} %collective-permute-done.4, s32[]{:T(128)S(6)} %select_n.414, f32[4,2,1,192,384]{4,3,1,0,2:T(8,128)} %bitcast.71, f32[4,2,1,8,384]{4,3,1,0,2:T(8,128)S(1)} %bitcast.80), kind=kLoop, calls=%fused_computation.31 | loop fusion | flops 614400 | bytes 4915204 | tf_op jit(solution)/shard_map/add | solution.py:62
  64.2 1.1 copy-done.2
  66.1 1.6 %collective-permute-start.5 = (f32[2,1,200,384]{3,2,1,0:T(8,128)}, f32[2,1,200,384]{3,2,1,0:T(8,128)}, u32[]{:S(2)}, u32[]{:S(2)}) collective-permute-start(f32[2,1,200,384]{3,2,1,0:T(8,128)} %dynamic-slice_bitcast_fusion), channel_id=1, source_target_pairs={{0,8},{4,12},{8,0},{12,4},{16,24},{20,28},{24,16},{28,20},{1,9},{5... | collective-permute-start | bytes 1843208 | tf_op jit(solution)/shard_map/ppermute | solution.py:61
  67.9 1.2 select_n.425
  70.2 4.1 %all-to-all-start = ((bf16[8,64,322]{2,1,0:T(8,128)(2,1)}), bf16[8,64,322]{2,1,0:T(8,128)(2,1)}, u32[]{:S(2)}, u32[]{:S(2)}) async-start(bf16[8,64,322]{2,1,0:T(8,128)(2,1)} %pad_maximum_fusion), calls=%async_computation | async-start | bytes 786432 | tf_op jit(solution)/shard_map/all_to_all | solution.py:139
  74.3 10.9 %collective-permute-done.5 = f32[2,1,200,384]{3,2,1,0:T(8,128)} collective-permute-done((f32[2,1,200,384]{3,2,1,0:T(8,128)}, f32[2,1,200,384]{3,2,1,0:T(8,128)}, u32[]{:S(2)}, u32[]{:S(2)}) %collective-permute-start.5) | collective-permute-done | bytes 614432 | tf_op jit(solution)/shard_map/ppermute | solution.py:61
  85.2 1.3 %bitcast_add_fusion = f32[2,1,200,384]{3,2,1,0:T(8,128)S(1)} fusion(f32[2,1,200,384]{3,2,1,0:T(8,128)} %collective-permute-done.5, f32[2,2,1,200,384]{4,3,1,0,2:T(8,128)} %bitcast.73, s32[]{:T(128)S(6)} %select_n.418), kind=kLoop, calls=%fused_computation.33 | loop fusion | flops 153600 | bytes 1843204 | tf_op jit(solution)/shard_map/add | solution.py:62
  88.1 3.8 %collective-permute-start.6 = (f32[1,1,200,384]{3,2,1,0:T(8,128)}, f32[1,1,200,384]{3,2,1,0:T(8,128)}, u32[]{:S(2)}, u32[]{:S(2)}) collective-permute-start(f32[1,1,200,384]{3,2,1,0:T(8,128)} %constant_dynamic-slice_fusion), channel_id=1, source_target_pairs={{0,16},{4,20},{8,24},{12,28},{16,0},{20,4},{24,8},{28,12},{1,17},{... | collective-permute-start | bytes 921608 | tf_op jit(solution)/shard_map/ppermute | solution.py:61
  91.9 1.1 slice.74
  93.0 10.8 %collective-permute-done.6 = f32[1,1,200,384]{3,2,1,0:T(8,128)} collective-permute-done((f32[1,1,200,384]{3,2,1,0:T(8,128)}, f32[1,1,200,384]{3,2,1,0:T(8,128)}, u32[]{:S(2)}, u32[]{:S(2)}) %collective-permute-start.6) | collective-permute-done | bytes 307232 | tf_op jit(solution)/shard_map/ppermute | solution.py:61
  103.8 1.8 %add_bitcast_fusion = f32[200,384]{1,0:T(8,128)} fusion(f32[1,1,200,384]{3,2,1,0:T(8,128)} %collective-permute-done.6, f32[2,1,200,384]{3,2,1,0:T(8,128)} %copy-done.3, s32[]{:T(128)S(6)} %select_n.422), kind=kLoop, calls=%fused_computation.41 | loop fusion | flops 76800 | bytes 921604 | tf_op jit(solution)/shard_map/squeeze;reshape | solution.py:171
  108.1 1.1 copy.53
  111.0 2.0 %collective-permute-done.7 = f32[200,384]{1,0:T(8,128)} collective-permute-done((f32[200,384]{1,0:T(8,128)}, f32[200,384]{1,0:T(8,128)}, u32[]{:S(2)}, u32[]{:S(2)}) %collective-permute-start.7) | collective-permute-done | bytes 307232 | tf_op jit(solution)/shard_map/ppermute | solution.py:72
  113.1 1.1 add.291
  114.2 1.6 %collective-permute-start.8 = (f32[200,384]{1,0:T(8,128)S(1)}, f32[200,384]{1,0:T(8,128)S(1)}, u32[]{:S(2)}, u32[]{:S(2)}) collective-permute-start(f32[200,384]{1,0:T(8,128)S(1)} %add.291), channel_id=1, source_target_pairs={{0,2},{1,3},{2,0},{3,1},{4,6},{5,7},{6,4},{7,5},{8,10},{9,11},{10,... | collective-permute-start | bytes 921608 | tf_op jit(solution)/shard_map/ppermute | solution.py:72
  117.3 1.4 %fusion.67 = f32[1024,192]{0,1:T(8,128)} fusion(bf16[512,1024]{0,1:T(8,128)(2,1)S(1)} %bitcast.74, bf16[512,192]{1,0:T(8,128)(2,1)S(1)} %bitcast.78), kind=kOutput, calls=%fused_computation.171 | convolution fusion | flops 201326592 | bytes 2031616 | tf_op jit(solution)/shard_map/dot_general | solution.py:147
  118.7 2.4 %collective-permute-done.8 = f32[200,384]{1,0:T(8,128)S(1)} collective-permute-done((f32[200,384]{1,0:T(8,128)S(1)}, f32[200,384]{1,0:T(8,128)S(1)}, u32[]{:S(2)}, u32[]{:S(2)}) %collective-permute-start.8) | collective-permute-done | bytes 307232 | tf_op jit(solution)/shard_map/ppermute | solution.py:72
  (105 shorter events, 19.0 us)
Async XLA Ops:
  0.6 22.0 %copy-start = (bf16[1024,1536]{1,0:T(8,128)(2,1)S(1)}, bf16[1024,1536]{1,0:T(8,128)(2,1)}, u32[]{:S(2)}) copy-start(bf16[1024,1536]{1,0:T(8,128)(2,1)} %param.12) | copy-start | bytes 9437188
  0.7 4.5 %copy-start.14 = (s32[1600]{0:T(1024)}, s32[1600]{0:T(1024)S(1)}, u32[]{:S(2)}) copy-start(s32[1600]{0:T(1024)S(1)} %add_select_fusion.7) | copy-start | bytes 19204
  0.7 4.5 %copy-start.16 = (f32[1536]{0:T(1024)S(1)}, f32[1536]{0:T(1024)}, u32[]{:S(2)}) copy-start(f32[1536]{0:T(1024)} %param.11) | copy-start | bytes 18436
  0.7 4.5 %copy-start.17 = (f32[1536]{0:T(1024)S(1)}, f32[1536]{0:T(1024)}, u32[]{:S(2)}) copy-start(f32[1536]{0:T(1024)} %param.10) | copy-start | bytes 18436
  5.2 5.7 %copy-start.1 = (f32[1600,1536]{1,0:T(8,128)}, f32[1600,1536]{1,0:T(8,128)S(1)}, u32[]{:S(2)}) copy-start(f32[1600,1536]{1,0:T(8,128)S(1)} %fusion.66) | copy-start | bytes 29491204
  5.2 8.7 %copy-start.9 = (s32[64,64]{1,0:T(8,128)S(1)}, s32[64,64]{1,0:T(8,128)}, u32[]{:S(2)}) copy-start(s32[64,64]{1,0:T(8,128)} %param.14) | copy-start | bytes 49156
  5.3 9.4 %copy-start.15 = (s32[64]{0:T(128)S(1)}, s32[64]{0:T(128)}, u32[]{:S(2)}) copy-start(s32[64]{0:T(128)} %param.13) | copy-start | bytes 772
  10.9 6.9 %collective-permute-start = (bf16[1,16,1536]{2,1,0:T(8,128)(2,1)S(1)}, bf16[1,16,1536]{2,1,0:T(8,128)(2,1)S(1)}, u32[]{:S(2)}, u32[]{:S(2)}) collective-permute-start(bf16[1,16,1536]{2,1,0:T(8,128)(2,1)S(1)} %fusion.15), channel_id=1, source_target_pairs={{0,1},{1,0},{2,3},{3,2},{4,5},{5,4},{6,7},{7,6},{8,9},{9,8},{10,11... | collective-permute-start | bytes 147464 | tf_op jit(solution)/shard_map/ppermute | solution.py:44
  14.8 0.5 copy-start.10
  14.8 0.5 copy-start.12
  17.9 4.7 %collective-permute-start.1 = (bf16[2,16,1536]{2,1,0:T(8,128)(2,1)S(1)}, bf16[2,16,1536]{2,1,0:T(8,128)(2,1)S(1)}, u32[]{:S(2)}, u32[]{:S(2)}) collective-permute-start(bf16[2,16,1536]{2,1,0:T(8,128)(2,1)S(1)} %maximum_select_fusion.1), channel_id=1, source_target_pairs={{0,2},{1,3},{2,0},{3,1},{4,6},{5,7},{6,4},{7,5},{8,10},{9,11},{10,... | collective-permute-start | bytes 294920 | tf_op jit(solution)/shard_map/ppermute | solution.py:44
  22.6 1.8 %copy-start.5 = (bf16[4,16,1536]{2,1,0:T(8,128)(2,1)}, bf16[4,16,1536]{2,1,0:T(8,128)(2,1)S(1)}, u32[]{:S(2)}) copy-start(bf16[4,16,1536]{2,1,0:T(8,128)(2,1)S(1)} %maximum_select_fusion) | copy-start | bytes 589828
  25.5 0.9 copy-start.7
  28.8 6.0 %collective-permute-start.2 = (f32[2,16,1536]{2,1,0:T(8,128)}, f32[2,16,1536]{2,1,0:T(8,128)}, u32[]{:S(2)}, u32[]{:S(2)}) collective-permute-start(f32[2,16,1536]{2,1,0:T(8,128)} %dynamic-slice_bitcast_fusion.1), channel_id=1, source_target_pairs={{0,1},{1,0},{2,3},{3,2},{4,5},{5,4},{6,7},{7,6},{8,9},{9,8},{10,11... | collective-permute-start | bytes 589832 | tf_op jit(solution)/shard_map/ppermute | solution.py:61
  35.7 0.7 copy-start.6
  36.4 4.7 %collective-permute-start.3 = (f32[1,16,1536]{2,1,0:T(8,128)S(1)}, f32[1,16,1536]{2,1,0:T(8,128)S(1)}, u32[]{:S(2)}, u32[]{:S(2)}) collective-permute-start(f32[1,16,1536]{2,1,0:T(8,128)S(1)} %constant_dynamic-slice_fusion.1), channel_id=1, source_target_pairs={{0,2},{1,3},{2,0},{3,1},{4,6},{5,7},{6,4},{7,5},{8,10},{9,11},{10,... | collective-permute-start | bytes 294920 | tf_op jit(solution)/shard_map/ppermute | solution.py:61
  38.0 14.0 %copy-start.4 = (bf16[1600,384]{1,0:T(8,128)(2,1)S(1)}, bf16[1600,384]{1,0:T(8,128)(2,1)}, u32[]{:S(2)}) copy-start(bf16[1600,384]{1,0:T(8,128)(2,1)} %param.8) | copy-start | bytes 3686404
  38.0 14.0 %copy-start.18 = (f32[1536]{0:T(1024)S(1)}, f32[1536]{0:T(1024)}, u32[]{:S(2)}) copy-start(f32[1536]{0:T(1024)} %param.10) | copy-start | bytes 18436
  59.1 8.5 %copy-start.13 = (s32[64]{0:T(128)S(1)}, s32[64]{0:T(128)}, u32[]{:S(2)}) copy-start(s32[64]{0:T(128)} %copy-done.12) | copy-start | bytes 772
  59.1 8.6 %copy-start.11 = (s32[64]{0:T(128)S(1)}, s32[64]{0:T(128)}, u32[]{:S(2)}) copy-start(s32[64]{0:T(128)} %copy-done.10) | copy-start | bytes 772
  59.1 3.3 %collective-permute-start.4 = (f32[4,1,200,384]{3,2,0,1:T(8,128)}, f32[4,1,200,384]{3,2,0,1:T(8,128)}, u32[]{:S(2)}, u32[]{:S(2)}) collective-permute-start(f32[4,1,200,384]{3,2,0,1:T(8,128)} %fusion.21), channel_id=1, source_target_pairs={{0,4},{4,0},{8,12},{12,8},{16,20},{20,16},{24,28},{28,24},{1,5},{5... | collective-permute-start | bytes 3686408 | tf_op jit(solution)/shard_map/ppermute | solution.py:61
  59.1 10.0 %copy-start.8 = (bf16[64,64]{1,0:T(8,128)(2,1)S(1)}, bf16[64,64]{1,0:T(8,128)(2,1)}, u32[]{:S(2)}) copy-start(bf16[64,64]{1,0:T(8,128)(2,1)} %copy-done.7) | copy-start | bytes 24580
  64.2 1.1 copy-start.2
  66.1 19.1 %collective-permute-start.5 = (f32[2,1,200,384]{3,2,1,0:T(8,128)}, f32[2,1,200,384]{3,2,1,0:T(8,128)}, u32[]{:S(2)}, u32[]{:S(2)}) collective-permute-start(f32[2,1,200,384]{3,2,1,0:T(8,128)} %dynamic-slice_bitcast_fusion), channel_id=1, source_target_pairs={{0,8},{4,12},{8,0},{12,4},{16,24},{20,28},{24,16},{28,20},{1,9},{5... | collective-permute-start | bytes 1843208 | tf_op jit(solution)/shard_map/ppermute | solution.py:61
  70.2 21.7 %all-to-all-start = ((bf16[8,64,322]{2,1,0:T(8,128)(2,1)}), bf16[8,64,322]{2,1,0:T(8,128)(2,1)}, u32[]{:S(2)}, u32[]{:S(2)}) async-start(bf16[8,64,322]{2,1,0:T(8,128)(2,1)} %pad_maximum_fusion), calls=%async_computation | async-start | bytes 786432 | tf_op jit(solution)/shard_map/all_to_all | solution.py:139
  86.5 0.8 copy-start.3
  88.1 15.7 %collective-permute-start.6 = (f32[1,1,200,384]{3,2,1,0:T(8,128)}, f32[1,1,200,384]{3,2,1,0:T(8,128)}, u32[]{:S(2)}, u32[]{:S(2)}) collective-permute-start(f32[1,1,200,384]{3,2,1,0:T(8,128)} %constant_dynamic-slice_fusion), channel_id=1, source_target_pairs={{0,16},{4,20},{8,24},{12,28},{16,0},{20,4},{24,8},{28,12},{1,17},{... | collective-permute-start | bytes 921608 | tf_op jit(solution)/shard_map/ppermute | solution.py:61
  105.6 7.4 %collective-permute-start.7 = (f32[200,384]{1,0:T(8,128)}, f32[200,384]{1,0:T(8,128)}, u32[]{:S(2)}, u32[]{:S(2)}) collective-permute-start(f32[200,384]{1,0:T(8,128)} %add_bitcast_fusion), channel_id=1, source_target_pairs={{0,1},{1,0},{2,3},{3,2},{4,5},{5,4},{6,7},{7,6},{8,9},{9,8},{10,11... | collective-permute-start | bytes 921608 | tf_op jit(solution)/shard_map/ppermute | solution.py:72
  114.2 6.9 %collective-permute-start.8 = (f32[200,384]{1,0:T(8,128)S(1)}, f32[200,384]{1,0:T(8,128)S(1)}, u32[]{:S(2)}, u32[]{:S(2)}) collective-permute-start(f32[200,384]{1,0:T(8,128)S(1)} %add.291), channel_id=1, source_target_pairs={{0,2},{1,3},{2,0},{3,1},{4,6},{5,7},{6,4},{7,5},{8,10},{9,11},{10,... | collective-permute-start | bytes 921608 | tf_op jit(solution)/shard_map/ppermute | solution.py:72

commit v11 on v10

--- a/solution.py
+++ b/solution.py
@@ -29,6 +29,14 @@
     column = jnp.arange(SUB_SIZE, dtype=jnp.int32)[None, None, :]
     hit = ((ids % SUB_SIZE)[:, :, None] == column) & valid[:, :, None]
     return jnp.any(hit, axis=1)
+
+
+def split3(x):
+    hi = lax.reduce_precision(x, exponent_bits=8, mantissa_bits=7)
+    rest = x - hi
+    mid = lax.reduce_precision(rest, exponent_bits=8, mantissa_bits=7)
+    lo = rest - mid
+    return hi.astype(jnp.bfloat16), mid.astype(jnp.bfloat16), lo.astype(jnp.bfloat16)
 
 
 def partners(size, bit):
@@ -148,7 +156,11 @@
         all_table, columns, (((0,), (0,)), ((), ())), preferred_element_type=jnp.float32
     )
 
-    spread = jnp.dot(select.T, emb_grad / P_SIZE, precision=HIGHEST, preferred_element_type=jnp.float32)
+    spread = jnp.dot(
+        jnp.concatenate([select.T.astype(jnp.bfloat16)] * 3, axis=1),
+        jnp.concatenate(split3(emb_grad / P_SIZE), axis=0),
+        preferred_element_type=jnp.float32,
+    )
     pixel_gradient = spread * (sig * (1.0 + shifted * (1.0 - sig)))
     lin_grad = (pixel_gradient * gain).astype(jnp.bfloat16)
     head_term = lax.dot_general(

time: 124 us -> 122 us (0.984)
  matrix products: 30.4 us -> 26.8 us
  other arithmetic: 15.1 us -> 16.7 us
    dot_general x1, matrix products: 10.9 us -> 7.35 us  [shards(): jnp.dot(jnp.concatenate([select.T.astype(jnp.bfloat16)] * 3, axis=1), jnp...]
    convert_element_type x0 -> x3, other arithmetic: none -> 1.64 us  [the longest x1 0.91 us: split3(): hi.astype(jnp.bfloat16)]
  transfers between devices with their start and end apart: 10 -> 10, of which waited for: 8 -> 8; matrix products, arithmetic and copies ran while one was open for 14% -> 15% of each run, Pallas kernels for 0% -> 0%
where the time goes in v11:
time: 122 us; the launch traced here: 120 us
  waiting for transfers between devices  40.1 us (33%)
  matrix products  26.8 us (22%)
  starting transfers between devices  17.9 us (15%)
  local copies, waits for them, and re-layouts  17.2 us (14%)
  other arithmetic  16.7 us (14%)
    ppermute x5, waiting for transfers between devices, halving_scatter(): got = lax.ppermute(tuple(give), name, partners(size, bit))  33.2 us
    dot_general x1, matrix products, shards(): jnp.dot(jnp.concatenate([select.T.astype(jnp.bfloat16)] * 3, axis=1), jnp...  7.35 us
    ppermute x5, starting transfers between devices, halving_scatter(): got = lax.ppermute(tuple(give), name, partners(size, bit))  7.1 us
    unnamed x44, local copies, waits for them, and re-layouts  6.21 us
    dot_general x1, matrix products, shards(): jnp.dot(select, active, precision=HIGHEST, preferred_element_type=jnp.flo...  5.63 us
    ppermute x2, starting transfers between devices, doubling_gather(): other = lax.ppermute(cur, name, partners(size, bit))  4.59 us
    dot_general x1, matrix products, shards(): jnp.dot(features, head_weight, preferred_element_type=jnp.float32)  4.5 us
    dot_general x1, matrix products, shards(): lax.dot_general(lin_grad, features, (((0,), (0,)), ((), ())), preferred_e...  4.49 us
  transfers between devices with their start and end apart: 10, of which 8 were waited for; matrix products, arithmetic and copies ran while one was open for 15% of the time, Pallas kernels for 0%

profile of v11, /device:TPU:0, one launch (start us, length us, event | category | flops | bytes accessed | tf_op | source)
XLA Modules:
  0.0 119.9 jit_solution(11330126142357753679)
XLA Ops:
  0.7 4.5 %fusion.70 = f32[1600,1536]{1,0:T(8,128)S(1)} fusion(bf16[1600,384]{1,0:T(8,128)(2,1)} %param.8, bf16[384,1536]{1,0:T(8,128)(2,1)} %param.9), kind=kOutput, calls=%fused_computation.181 | convolution fusion | flops 1887436800 | bytes 12238848 | tf_op jit(solution)/shard_map/dot_general | solution.py:100
  5.3 5.6 %fusion.15 = bf16[1,16,1536]{2,1,0:T(8,128)(2,1)S(1)} fusion(f32[1600,1536]{1,0:T(8,128)S(1)} %fusion.70, f32[1536]{0:T(1024)S(1)} %copy-done.16, f32[1536]{0:T(1024)S(1)} %copy-done.17, s32[1600]{0:T(1024)S(1)} %add_select_fusion.7), kind=kOutput, calls=%fused_computation.21 | convolution fusion | flops 486679552 | bytes 9898240 | tf_op jit(solution)/shard_map/dot_general | solution.py:104
  10.9 3.0 %collective-permute-start = (bf16[1,16,1536]{2,1,0:T(8,128)(2,1)S(1)}, bf16[1,16,1536]{2,1,0:T(8,128)(2,1)S(1)}, u32[]{:S(2)}, u32[]{:S(2)}) collective-permute-start(bf16[1,16,1536]{2,1,0:T(8,128)(2,1)S(1)} %fusion.15), channel_id=1, source_target_pairs={{0,1},{1,0},{2,3},{3,2},{4,5},{5,4},{6,7},{7,6},{8,9},{9,8},{10,11... | collective-permute-start | bytes 147464 | tf_op jit(solution)/shard_map/ppermute | solution.py:52
  15.7 1.1 fusion.19
  17.9 1.6 %collective-permute-start.1 = (bf16[2,16,1536]{2,1,0:T(8,128)(2,1)S(1)}, bf16[2,16,1536]{2,1,0:T(8,128)(2,1)S(1)}, u32[]{:S(2)}, u32[]{:S(2)}) collective-permute-start(bf16[2,16,1536]{2,1,0:T(8,128)(2,1)S(1)} %maximum_select_fusion.1), channel_id=1, source_target_pairs={{0,2},{1,3},{2,0},{3,1},{4,6},{5,7},{6,4},{7,5},{8,10},{9,11},{10,... | collective-permute-start | bytes 294920 | tf_op jit(solution)/shard_map/ppermute | solution.py:52
  20.1 2.5 %collective-permute-done.1 = bf16[2,16,1536]{2,1,0:T(8,128)(2,1)S(1)} collective-permute-done((bf16[2,16,1536]{2,1,0:T(8,128)(2,1)S(1)}, bf16[2,16,1536]{2,1,0:T(8,128)(2,1)S(1)}, u32[]{:S(2)}, u32[]{:S(2)}) %collective-permute-start.1) | collective-permute-done | bytes 98336 | tf_op jit(solution)/shard_map/ppermute | solution.py:52
  22.6 1.8 %select_reduce_fusion = (f32[64,64]{1,0:T(8,128)S(1)}, f32[64,64]{1,0:T(8,128)S(1)}) fusion(pred[64,16]{0,1:T(8,128)(4,1)S(1)} %iota_compare_fusion.8, pred[64,16]{0,1:T(8,128)(4,1)S(1)} %iota_compare_fusion.9, bf16[64,1536,1]{1,0,2:T(8,128)(2,1)S(1)} %bitcast.83, bf16[16,64,1536]{2,1,0:T(8,128)(2,1)S(1)} %bitcast.71), kind=kOutput, calls=%fused_computation.35 | convolution fusion | flops 201580544 | bytes 3377152 | tf_op jit(solution)/shard_map/dot_general | solution.py:120
  26.4 1.7 %fusion.7 = f32[2,2,16,1536]{3,2,1,0:T(8,128)S(1)} fusion(bf16[1024,1536]{1,0:T(8,128)(2,1)S(1)} %copy-done, bf16[2,2,16,1024]{3,2,1,0:T(8,128)(2,1)} %tile.13, bf16[2,2,16,1024]{3,2,1,0:T(8,128)(2,1)} %tile.15, s32[2,2,16]{2,1,0:T(2,128)} %get-tuple-element.27, s32[2,2,16]{2,1,0:T(2,128)} %get-tuple-element.28, s32[1024]{0:T(1024)} %add_select_fusion.8), kind=kOutput, calls=%fused_computation.15 | convolution fusion | flops 201654272 | bytes 3805696 | tf_op jit(solution)/shard_map/dot_general | solution.py:130
  28.9 5.8 %collective-permute-done.2 = f32[2,16,1536]{2,1,0:T(8,128)} collective-permute-done((f32[2,16,1536]{2,1,0:T(8,128)}, f32[2,16,1536]{2,1,0:T(8,128)}, u32[]{:S(2)}, u32[]{:S(2)}) %collective-permute-start.2) | collective-permute-done | bytes 196640 | tf_op jit(solution)/shard_map/ppermute | solution.py:69
  36.4 1.6 %collective-permute-start.3 = (f32[1,16,1536]{2,1,0:T(8,128)S(1)}, f32[1,16,1536]{2,1,0:T(8,128)S(1)}, u32[]{:S(2)}, u32[]{:S(2)}) collective-permute-start(f32[1,16,1536]{2,1,0:T(8,128)S(1)} %constant_dynamic-slice_fusion.1), channel_id=1, source_target_pairs={{0,2},{1,3},{2,0},{3,1},{4,6},{5,7},{6,4},{7,5},{8,10},{9,11},{10,... | collective-permute-start | bytes 294920 | tf_op jit(solution)/shard_map/ppermute | solution.py:69
  38.7 2.4 %collective-permute-done.3 = f32[1,16,1536]{2,1,0:T(8,128)S(1)} collective-permute-done((f32[1,16,1536]{2,1,0:T(8,128)S(1)}, f32[1,16,1536]{2,1,0:T(8,128)S(1)}, u32[]{:S(2)}, u32[]{:S(2)}) %collective-permute-start.3) | collective-permute-done | bytes 98336 | tf_op jit(solution)/shard_map/ppermute | solution.py:69
  42.1 7.4 %multiply_reduce_fusion = (f32[1536]{0:T(1024)S(1)}, f32[1536]{0:T(1024)S(1)}, f32[1600,1536]{1,0:T(8,128)S(1)}) fusion(f32[1600,1536]{1,0:T(8,128)} %copy-done.1, f32[1536]{0:T(1024)} %param.11, f32[1536]{0:T(1024)} %param.10, bf16[16,1536]{1,0:T(8,128)(2,1)S(1)} %get-tuple-element.21, bf16[16,1536]{1,0:T(8,128)(2,1)S(1)} %get-tuple-element.20, ...), kind=kOutput, calls=%fused_computation.1 | convolution fusion | flops 268778496 | bytes 19884032 | tf_op jit(solution)/shard_map/dot_general | solution.py:159
  49.4 4.5 %fusion.2 = f32[1536,384]{1,0:T(8,128)} fusion(bf16[1600,384]{1,0:T(8,128)(2,1)S(1)} %copy-done.4, f32[1600,1536]{1,0:T(8,128)S(1)} %get-tuple-element.26, f32[1536]{0:T(1024)S(1)} %copy-done.18), kind=kOutput, calls=%fused_computation.8 | convolution fusion | flops 1892352000 | bytes 13424640 | tf_op jit(solution)/shard_map/dot_general | solution.py:166
  54.2 2.4 %fusion.21 = f32[4,1,200,384]{3,2,0,1:T(8,128)} fusion(s32[]{:T(128)S(6)} %select_n.419, f32[4,2,1,192,384]{4,3,1,0,2:T(8,128)} %bitcast.72, f32[4,2,1,8,384]{4,3,1,0,2:T(8,128)S(1)} %bitcast.81), kind=kLoop, calls=%fused_computation.28 | loop fusion | flops 307200 | bytes 3686404 | tf_op jit(solution)/shard_map/jit(dynamic_index_in_dim)/squeeze | solution.py:68
  56.6 3.3 %collective-permute-done.4 = f32[4,1,200,384]{3,2,0,1:T(8,128)} collective-permute-done((f32[4,1,200,384]{3,2,0,1:T(8,128)}, f32[4,1,200,384]{3,2,0,1:T(8,128)}, u32[]{:S(2)}, u32[]{:S(2)}) %collective-permute-start.4) | collective-permute-done | bytes 1228832 | tf_op jit(solution)/shard_map/ppermute | solution.py:69
  59.9 1.8 %fusion.24 = f32[4,1,200,384]{3,2,0,1:T(8,128)S(1)} fusion(f32[4,1,200,384]{3,2,0,1:T(8,128)} %collective-permute-done.4, s32[]{:T(128)S(6)} %select_n.418, f32[4,2,1,192,384]{4,3,1,0,2:T(8,128)} %bitcast.73, f32[4,2,1,8,384]{4,3,1,0,2:T(8,128)S(1)} %bitcast.82), kind=kLoop, calls=%fused_computation.31 | loop fusion | flops 614400 | bytes 4915204 | tf_op jit(solution)/shard_map/add | solution.py:70
  63.5 1.6 %collective-permute-start.5 = (f32[2,1,200,384]{3,2,1,0:T(8,128)}, f32[2,1,200,384]{3,2,1,0:T(8,128)}, u32[]{:S(2)}, u32[]{:S(2)}) collective-permute-start(f32[2,1,200,384]{3,2,1,0:T(8,128)} %dynamic-slice_bitcast_fusion), channel_id=1, source_target_pairs={{0,8},{4,12},{8,0},{12,4},{16,24},{20,28},{24,16},{28,20},{1,9},{5... | collective-permute-start | bytes 1843208 | tf_op jit(solution)/shard_map/ppermute | solution.py:69
  65.4 1.2 select_n.429
  67.6 4.1 %all-to-all-start = ((bf16[8,64,322]{2,1,0:T(8,128)(2,1)}), bf16[8,64,322]{2,1,0:T(8,128)(2,1)}, u32[]{:S(2)}, u32[]{:S(2)}) async-start(bf16[8,64,322]{2,1,0:T(8,128)(2,1)} %pad_maximum_fusion), calls=%async_computation | async-start | bytes 786432 | tf_op jit(solution)/shard_map/all_to_all | solution.py:147
  71.7 10.9 %collective-permute-done.5 = f32[2,1,200,384]{3,2,1,0:T(8,128)} collective-permute-done((f32[2,1,200,384]{3,2,1,0:T(8,128)}, f32[2,1,200,384]{3,2,1,0:T(8,128)}, u32[]{:S(2)}, u32[]{:S(2)}) %collective-permute-start.5) | collective-permute-done | bytes 614432 | tf_op jit(solution)/shard_map/ppermute | solution.py:69
  82.7 1.3 %bitcast_add_fusion = f32[2,1,200,384]{3,2,1,0:T(8,128)S(1)} fusion(f32[2,1,200,384]{3,2,1,0:T(8,128)} %collective-permute-done.5, f32[2,2,1,200,384]{4,3,1,0,2:T(8,128)} %bitcast.75, s32[]{:T(128)S(6)} %select_n.422), kind=kLoop, calls=%fused_computation.33 | loop fusion | flops 153600 | bytes 1843204 | tf_op jit(solution)/shard_map/add | solution.py:70
  85.5 3.8 %collective-permute-start.6 = (f32[1,1,200,384]{3,2,1,0:T(8,128)}, f32[1,1,200,384]{3,2,1,0:T(8,128)}, u32[]{:S(2)}, u32[]{:S(2)}) collective-permute-start(f32[1,1,200,384]{3,2,1,0:T(8,128)} %constant_dynamic-slice_fusion), channel_id=1, source_target_pairs={{0,16},{4,20},{8,24},{12,28},{16,0},{20,4},{24,8},{28,12},{1,17},{... | collective-permute-start | bytes 921608 | tf_op jit(solution)/shard_map/ppermute | solution.py:69
  89.4 1.1 slice.74
  90.5 10.8 %collective-permute-done.6 = f32[1,1,200,384]{3,2,1,0:T(8,128)} collective-permute-done((f32[1,1,200,384]{3,2,1,0:T(8,128)}, f32[1,1,200,384]{3,2,1,0:T(8,128)}, u32[]{:S(2)}, u32[]{:S(2)}) %collective-permute-start.6) | collective-permute-done | bytes 307232 | tf_op jit(solution)/shard_map/ppermute | solution.py:69
  101.3 1.8 %add_bitcast_fusion = f32[200,384]{1,0:T(8,128)} fusion(f32[1,1,200,384]{3,2,1,0:T(8,128)} %collective-permute-done.6, f32[2,1,200,384]{3,2,1,0:T(8,128)} %copy-done.3, s32[]{:T(128)S(6)} %select_n.426), kind=kLoop, calls=%fused_computation.41 | loop fusion | flops 76800 | bytes 921604 | tf_op jit(solution)/shard_map/squeeze;reshape | solution.py:183
  104.4 1.1 copy.64
  105.5 1.1 copy.63
  108.4 2.1 %collective-permute-done.7 = f32[200,384]{1,0:T(8,128)} collective-permute-done((f32[200,384]{1,0:T(8,128)}, f32[200,384]{1,0:T(8,128)}, u32[]{:S(2)}, u32[]{:S(2)}) %collective-permute-start.7) | collective-permute-done | bytes 307232 | tf_op jit(solution)/shard_map/ppermute | solution.py:80
  110.5 1.1 add.291
  111.6 1.6 %collective-permute-start.8 = (f32[200,384]{1,0:T(8,128)S(1)}, f32[200,384]{1,0:T(8,128)S(1)}, u32[]{:S(2)}, u32[]{:S(2)}) collective-permute-start(f32[200,384]{1,0:T(8,128)S(1)} %add.291), channel_id=1, source_target_pairs={{0,2},{1,3},{2,0},{3,1},{4,6},{5,7},{6,4},{7,5},{8,10},{9,11},{10,... | collective-permute-start | bytes 921608 | tf_op jit(solution)/shard_map/ppermute | solution.py:80
  114.8 1.4 %fusion.71 = f32[1024,192]{0,1:T(8,128)} fusion(bf16[512,1024]{0,1:T(8,128)(2,1)S(1)} %bitcast.76, bf16[512,192]{1,0:T(8,128)(2,1)S(1)} %bitcast.80), kind=kOutput, calls=%fused_computation.182 | convolution fusion | flops 201326592 | bytes 2031616 | tf_op jit(solution)/shard_map/dot_general | solution.py:155
  116.1 2.4 %collective-permute-done.8 = f32[200,384]{1,0:T(8,128)S(1)} collective-permute-done((f32[200,384]{1,0:T(8,128)S(1)}, f32[200,384]{1,0:T(8,128)S(1)}, u32[]{:S(2)}, u32[]{:S(2)}) %collective-permute-start.8) | collective-permute-done | bytes 307232 | tf_op jit(solution)/shard_map/ppermute | solution.py:80
  (108 shorter events, 20.6 us)
Async XLA Ops:
  0.6 22.0 %copy-start = (bf16[1024,1536]{1,0:T(8,128)(2,1)S(1)}, bf16[1024,1536]{1,0:T(8,128)(2,1)}, u32[]{:S(2)}) copy-start(bf16[1024,1536]{1,0:T(8,128)(2,1)} %param.12) | copy-start | bytes 9437188
  0.7 4.5 %copy-start.9 = (s32[1600]{0:T(1024)}, s32[1600]{0:T(1024)S(1)}, u32[]{:S(2)}) copy-start(s32[1600]{0:T(1024)S(1)} %add_select_fusion.7) | copy-start | bytes 19204
  0.7 4.5 %copy-start.16 = (f32[1536]{0:T(1024)S(1)}, f32[1536]{0:T(1024)}, u32[]{:S(2)}) copy-start(f32[1536]{0:T(1024)} %param.11) | copy-start | bytes 18436
  0.7 4.5 %copy-start.17 = (f32[1536]{0:T(1024)S(1)}, f32[1536]{0:T(1024)}, u32[]{:S(2)}) copy-start(f32[1536]{0:T(1024)} %param.10) | copy-start | bytes 18436
  5.2 5.7 %copy-start.1 = (f32[1600,1536]{1,0:T(8,128)}, f32[1600,1536]{1,0:T(8,128)S(1)}, u32[]{:S(2)}) copy-start(f32[1600,1536]{1,0:T(8,128)S(1)} %fusion.70) | copy-start | bytes 29491204
  5.2 8.7 %copy-start.10 = (s32[64,64]{1,0:T(8,128)S(1)}, s32[64,64]{1,0:T(8,128)}, u32[]{:S(2)}) copy-start(s32[64,64]{1,0:T(8,128)} %param.14) | copy-start | bytes 49156
  5.3 9.4 %copy-start.15 = (s32[64]{0:T(128)S(1)}, s32[64]{0:T(128)}, u32[]{:S(2)}) copy-start(s32[64]{0:T(128)} %param.13) | copy-start | bytes 772
  10.9 6.9 %collective-permute-start = (bf16[1,16,1536]{2,1,0:T(8,128)(2,1)S(1)}, bf16[1,16,1536]{2,1,0:T(8,128)(2,1)S(1)}, u32[]{:S(2)}, u32[]{:S(2)}) collective-permute-start(bf16[1,16,1536]{2,1,0:T(8,128)(2,1)S(1)} %fusion.15), channel_id=1, source_target_pairs={{0,1},{1,0},{2,3},{3,2},{4,5},{5,4},{6,7},{7,6},{8,9},{9,8},{10,11... | collective-permute-start | bytes 147464 | tf_op jit(solution)/shard_map/ppermute | solution.py:52
  14.8 0.5 copy-start.11
  14.8 0.5 copy-start.13
  17.9 4.7 %collective-permute-start.1 = (bf16[2,16,1536]{2,1,0:T(8,128)(2,1)S(1)}, bf16[2,16,1536]{2,1,0:T(8,128)(2,1)S(1)}, u32[]{:S(2)}, u32[]{:S(2)}) collective-permute-start(bf16[2,16,1536]{2,1,0:T(8,128)(2,1)S(1)} %maximum_select_fusion.1), channel_id=1, source_target_pairs={{0,2},{1,3},{2,0},{3,1},{4,6},{5,7},{6,4},{7,5},{8,10},{9,11},{10,... | collective-permute-start | bytes 294920 | tf_op jit(solution)/shard_map/ppermute | solution.py:52
  22.6 1.8 %copy-start.5 = (bf16[4,16,1536]{2,1,0:T(8,128)(2,1)}, bf16[4,16,1536]{2,1,0:T(8,128)(2,1)S(1)}, u32[]{:S(2)}) copy-start(bf16[4,16,1536]{2,1,0:T(8,128)(2,1)S(1)} %maximum_select_fusion) | copy-start | bytes 589828
  25.5 0.9 copy-start.7
  28.8 6.0 %collective-permute-start.2 = (f32[2,16,1536]{2,1,0:T(8,128)}, f32[2,16,1536]{2,1,0:T(8,128)}, u32[]{:S(2)}, u32[]{:S(2)}) collective-permute-start(f32[2,16,1536]{2,1,0:T(8,128)} %dynamic-slice_bitcast_fusion.1), channel_id=1, source_target_pairs={{0,1},{1,0},{2,3},{3,2},{4,5},{5,4},{6,7},{7,6},{8,9},{9,8},{10,11... | collective-permute-start | bytes 589832 | tf_op jit(solution)/shard_map/ppermute | solution.py:69
  35.7 0.7 copy-start.6
  36.4 4.7 %collective-permute-start.3 = (f32[1,16,1536]{2,1,0:T(8,128)S(1)}, f32[1,16,1536]{2,1,0:T(8,128)S(1)}, u32[]{:S(2)}, u32[]{:S(2)}) collective-permute-start(f32[1,16,1536]{2,1,0:T(8,128)S(1)} %constant_dynamic-slice_fusion.1), channel_id=1, source_target_pairs={{0,2},{1,3},{2,0},{3,1},{4,6},{5,7},{6,4},{7,5},{8,10},{9,11},{10,... | collective-permute-start | bytes 294920 | tf_op jit(solution)/shard_map/ppermute | solution.py:69
  42.0 7.4 %copy-start.4 = (bf16[1600,384]{1,0:T(8,128)(2,1)S(1)}, bf16[1600,384]{1,0:T(8,128)(2,1)}, u32[]{:S(2)}) copy-start(bf16[1600,384]{1,0:T(8,128)(2,1)} %param.8) | copy-start | bytes 3686404
  42.1 7.4 %copy-start.18 = (f32[1536]{0:T(1024)S(1)}, f32[1536]{0:T(1024)}, u32[]{:S(2)}) copy-start(f32[1536]{0:T(1024)} %param.10) | copy-start | bytes 18436
  56.6 8.5 %copy-start.14 = (s32[64]{0:T(128)S(1)}, s32[64]{0:T(128)}, u32[]{:S(2)}) copy-start(s32[64]{0:T(128)} %copy-done.13) | copy-start | bytes 772
  56.6 8.6 %copy-start.12 = (s32[64]{0:T(128)S(1)}, s32[64]{0:T(128)}, u32[]{:S(2)}) copy-start(s32[64]{0:T(128)} %copy-done.11) | copy-start | bytes 772
  56.6 3.3 %collective-permute-start.4 = (f32[4,1,200,384]{3,2,0,1:T(8,128)}, f32[4,1,200,384]{3,2,0,1:T(8,128)}, u32[]{:S(2)}, u32[]{:S(2)}) collective-permute-start(f32[4,1,200,384]{3,2,0,1:T(8,128)} %fusion.21), channel_id=1, source_target_pairs={{0,4},{4,0},{8,12},{12,8},{16,20},{20,16},{24,28},{28,24},{1,5},{5... | collective-permute-start | bytes 3686408 | tf_op jit(solution)/shard_map/ppermute | solution.py:69
  56.6 10.0 %copy-start.8 = (bf16[64,64]{1,0:T(8,128)(2,1)S(1)}, bf16[64,64]{1,0:T(8,128)(2,1)}, u32[]{:S(2)}) copy-start(bf16[64,64]{1,0:T(8,128)(2,1)} %copy-done.7) | copy-start | bytes 24580
  61.6 1.1 copy-start.2
  63.5 19.1 %collective-permute-start.5 = (f32[2,1,200,384]{3,2,1,0:T(8,128)}, f32[2,1,200,384]{3,2,1,0:T(8,128)}, u32[]{:S(2)}, u32[]{:S(2)}) collective-permute-start(f32[2,1,200,384]{3,2,1,0:T(8,128)} %dynamic-slice_bitcast_fusion), channel_id=1, source_target_pairs={{0,8},{4,12},{8,0},{12,4},{16,24},{20,28},{24,16},{28,20},{1,9},{5... | collective-permute-start | bytes 1843208 | tf_op jit(solution)/shard_map/ppermute | solution.py:69
  67.6 21.7 %all-to-all-start = ((bf16[8,64,322]{2,1,0:T(8,128)(2,1)}), bf16[8,64,322]{2,1,0:T(8,128)(2,1)}, u32[]{:S(2)}, u32[]{:S(2)}) async-start(bf16[8,64,322]{2,1,0:T(8,128)(2,1)} %pad_maximum_fusion), calls=%async_computation | async-start | bytes 786432 | tf_op jit(solution)/shard_map/all_to_all | solution.py:147
  84.0 0.8 copy-start.3
  85.5 15.7 %collective-permute-start.6 = (f32[1,1,200,384]{3,2,1,0:T(8,128)}, f32[1,1,200,384]{3,2,1,0:T(8,128)}, u32[]{:S(2)}, u32[]{:S(2)}) collective-permute-start(f32[1,1,200,384]{3,2,1,0:T(8,128)} %constant_dynamic-slice_fusion), channel_id=1, source_target_pairs={{0,16},{4,20},{8,24},{12,28},{16,0},{20,4},{24,8},{28,12},{1,17},{... | collective-permute-start | bytes 921608 | tf_op jit(solution)/shard_map/ppermute | solution.py:69
  103.1 7.4 %collective-permute-start.7 = (f32[200,384]{1,0:T(8,128)}, f32[200,384]{1,0:T(8,128)}, u32[]{:S(2)}, u32[]{:S(2)}) collective-permute-start(f32[200,384]{1,0:T(8,128)} %add_bitcast_fusion), channel_id=1, source_target_pairs={{0,1},{1,0},{2,3},{3,2},{4,5},{5,4},{6,7},{7,6},{8,9},{9,8},{10,11... | collective-permute-start | bytes 921608 | tf_op jit(solution)/shard_map/ppermute | solution.py:80
  111.6 6.9 %collective-permute-start.8 = (f32[200,384]{1,0:T(8,128)S(1)}, f32[200,384]{1,0:T(8,128)S(1)}, u32[]{:S(2)}, u32[]{:S(2)}) collective-permute-start(f32[200,384]{1,0:T(8,128)S(1)} %add.291), channel_id=1, source_target_pairs={{0,2},{1,3},{2,0},{3,1},{4,6},{5,7},{6,4},{7,5},{8,10},{9,11},{10,... | collective-permute-start | bytes 921608 | tf_op jit(solution)/shard_map/ppermute | solution.py:80

commit v12 on v11

--- a/solution.py
+++ b/solution.py
@@ -83,6 +83,17 @@
     return cur
 
 
+def direct_scatter(x, name):
+    size = lax.axis_size(name)
+    idx = lax.axis_index(name)
+    blocks = x.reshape((size, x.shape[0] // size) + x.shape[1:])
+    total = lax.dynamic_index_in_dim(blocks, idx, 0, keepdims=False)
+    for k in range(1, size):
+        give = lax.dynamic_index_in_dim(blocks, jnp.bitwise_xor(idx, k), 0, keepdims=False)
+        total = total + lax.ppermute(give, name, [(i, i ^ k) for i in range(size)])
+    return total
+
+
 def shards(features, head_weight, gain, shift, node_weights, subtree_map, node_ids):
     rows = features.shape[0]
     images_here = rows // P_SIZE
@@ -128,7 +139,10 @@
     neg_coef = neg_coef.astype(jnp.bfloat16)
     table = block_table(pos_coef, pos_here, neg_coef, neg_here, blocks).astype(jnp.bfloat16)
     grad_part = jnp.dot(table, node_weights, preferred_element_type=jnp.float32)
-    (emb_grad,) = halving_scatter([grad_part], "leaf")
+    if lax.axis_size("leaf") <= 4:
+        emb_grad = direct_scatter(grad_part, "leaf")
+    else:
+        (emb_grad,) = halving_scatter([grad_part], "leaf")
 
     col_width = width // n_dp
     column_chunks = grouped.reshape(group, n_dp, col_width).transpose(1, 0, 2)

time: 122 us -> 117 us (0.959)
  waiting for transfers between devices: 40.1 us -> 34 us
  starting transfers between devices: 17.9 us -> 20.5 us
    ppermute x5 -> x3, waiting for transfers between devices: 33.2 us -> 25 us  [halving_scatter(): got = lax.ppermute(tuple(give), name, partners(size, bit))]
    ppermute x0 -> x3, starting transfers between devices: none -> 3.49 us  [direct_scatter(): total = total + lax.ppermute(give, name, [(i, i ^ k) for i in range(size)])]
    ppermute x0 -> x3, waiting for transfers between devices: none -> 2.86 us  [direct_scatter(): total = total + lax.ppermute(give, name, [(i, i ^ k) for i in range(size)])]
    ppermute x5 -> x3, starting transfers between devices: 7.1 us -> 5.38 us  [halving_scatter(): got = lax.ppermute(tuple(give), name, partners(size, bit))]
    add x3 -> x2, other arithmetic: 4.03 us -> 3.08 us  [halving_scatter(): cur = [k + g for k, g in zip(keep, got)]]
  transfers between devices with their start and end apart: 10 -> 11, of which waited for: 8 -> 9; matrix products, arithmetic and copies ran while one was open for 15% -> 16% of each run, Pallas kernels for 0% -> 0%
where the time goes in v12:
time: 117 us; the launch traced here: 116 us
  waiting for transfers between devices  34 us (29%)
  matrix products  27.7 us (24%)
  starting transfers between devices  20.5 us (18%)
  local copies, waits for them, and re-layouts  16.5 us (14%)
  other arithmetic  15.7 us (13%)
  between operations  1.18 us (1%)
    ppermute x3, waiting for transfers between devices, halving_scatter(): got = lax.ppermute(tuple(give), name, partners(size, bit))  25 us
    dot_general x1, matrix products, shards(): jnp.dot(jnp.concatenate([select.T.astype(jnp.bfloat16)] * 3, axis=1), jnp...  8.21 us
    dot_general x1, matrix products, shards(): jnp.dot(select, active, precision=HIGHEST, preferred_element_type=jnp.flo...  5.63 us
    unnamed x44, local copies, waits for them, and re-layouts  5.53 us
    ppermute x3, starting transfers between devices, halving_scatter(): got = lax.ppermute(tuple(give), name, partners(size, bit))  5.38 us
    ppermute x2, starting transfers between devices, doubling_gather(): other = lax.ppermute(cur, name, partners(size, bit))  4.59 us
    dot_general x1, matrix products, shards(): jnp.dot(features, head_weight, preferred_element_type=jnp.float32)  4.5 us
    dot_general x1, matrix products, shards(): lax.dot_general(lin_grad, features, (((0,), (0,)), ((), ())), preferred_e...  4.48 us
  transfers between devices with their start and end apart: 11, of which 9 were waited for; matrix products, arithmetic and copies ran while one was open for 16% of the time, Pallas kernels for 0%

profile of v12, /device:TPU:0, one launch (start us, length us, event | category | flops | bytes accessed | tf_op | source)
XLA Modules:
  0.0 115.6 jit_solution(14542885022448979518)
XLA Ops:
  0.7 4.5 %fusion.82 = f32[1600,1536]{1,0:T(8,128)S(1)} fusion(bf16[1600,384]{1,0:T(8,128)(2,1)} %param.8, bf16[384,1536]{1,0:T(8,128)(2,1)} %param.9), kind=kOutput, calls=%fused_computation.192 | convolution fusion | flops 1887436800 | bytes 12238848 | tf_op jit(solution)/shard_map/dot_general | solution.py:111
  5.3 5.6 %fusion.15 = bf16[1,16,1536]{2,1,0:T(8,128)(2,1)S(1)} fusion(f32[1600,1536]{1,0:T(8,128)S(1)} %fusion.82, f32[1536]{0:T(1024)S(1)} %copy-done.16, f32[1536]{0:T(1024)S(1)} %copy-done.17, s32[1600]{0:T(1024)S(1)} %add_select_fusion.7), kind=kOutput, calls=%fused_computation.21 | convolution fusion | flops 486679552 | bytes 9898240 | tf_op jit(solution)/shard_map/dot_general | solution.py:115
  10.9 3.0 %collective-permute-start = (bf16[1,16,1536]{2,1,0:T(8,128)(2,1)S(1)}, bf16[1,16,1536]{2,1,0:T(8,128)(2,1)S(1)}, u32[]{:S(2)}, u32[]{:S(2)}) collective-permute-start(bf16[1,16,1536]{2,1,0:T(8,128)(2,1)S(1)} %fusion.15), channel_id=1, source_target_pairs={{0,1},{1,0},{2,3},{3,2},{4,5},{5,4},{6,7},{7,6},{8,9},{9,8},{10,11... | collective-permute-start | bytes 147464 | tf_op jit(solution)/shard_map/ppermute | solution.py:52
  15.7 1.1 fusion.19
  17.9 1.6 %collective-permute-start.1 = (bf16[2,16,1536]{2,1,0:T(8,128)(2,1)S(1)}, bf16[2,16,1536]{2,1,0:T(8,128)(2,1)S(1)}, u32[]{:S(2)}, u32[]{:S(2)}) collective-permute-start(bf16[2,16,1536]{2,1,0:T(8,128)(2,1)S(1)} %maximum_select_fusion.1), channel_id=1, source_target_pairs={{0,2},{1,3},{2,0},{3,1},{4,6},{5,7},{6,4},{7,5},{8,10},{9,11},{10,... | collective-permute-start | bytes 294920 | tf_op jit(solution)/shard_map/ppermute | solution.py:52
  20.0 2.5 %collective-permute-done.1 = bf16[2,16,1536]{2,1,0:T(8,128)(2,1)S(1)} collective-permute-done((bf16[2,16,1536]{2,1,0:T(8,128)(2,1)S(1)}, bf16[2,16,1536]{2,1,0:T(8,128)(2,1)S(1)}, u32[]{:S(2)}, u32[]{:S(2)}) %collective-permute-start.1) | collective-permute-done | bytes 98336 | tf_op jit(solution)/shard_map/ppermute | solution.py:52
  22.6 1.8 %select_reduce_fusion = (f32[64,64]{1,0:T(8,128)S(1)}, f32[64,64]{1,0:T(8,128)S(1)}) fusion(pred[64,16]{0,1:T(8,128)(4,1)S(1)} %iota_compare_fusion.8, pred[64,16]{0,1:T(8,128)(4,1)S(1)} %iota_compare_fusion.9, bf16[64,1536,1]{1,0,2:T(8,128)(2,1)S(1)} %bitcast.85, bf16[16,64,1536]{2,1,0:T(8,128)(2,1)S(1)} %bitcast.73), kind=kOutput, calls=%fused_computation.35 | convolution fusion | flops 201580544 | bytes 3377152 | tf_op jit(solution)/shard_map/dot_general | solution.py:131
  26.4 1.7 %fusion.7 = f32[4,16,1536]{2,1,0:T(8,128)S(1)} fusion(bf16[1024,1536]{1,0:T(8,128)(2,1)S(1)} %copy-done, bf16[4,16,1024]{2,1,0:T(8,128)(2,1)} %tile.13, bf16[4,16,1024]{2,1,0:T(8,128)(2,1)} %tile.15, s32[4,16]{1,0:T(4,128)} %get-tuple-element.31, s32[4,16]{1,0:T(4,128)} %get-tuple-element.30, s32[1024]{0:T(1024)} %add_select_fusion.8), kind=kOutput, calls=%fused_computation.15 | convolution fusion | flops 201654272 | bytes 3805696 | tf_op jit(solution)/shard_map/dot_general | solution.py:141
  28.8 1.5 %collective-permute-start.4 = (f32[16,1536]{1,0:T(8,128)}, f32[16,1536]{1,0:T(8,128)}, u32[]{:S(2)}, u32[]{:S(2)}) collective-permute-start(f32[16,1536]{1,0:T(8,128)} %get-tuple-element.17), channel_id=1, source_target_pairs={{0,3},{1,2},{2,1},{3,0},{4,7},{5,6},{6,5},{7,4},{8,11},{9,10},{10,... | collective-permute-start | bytes 294920 | tf_op jit(solution)/shard_map/ppermute | solution.py:93
  30.4 1.9 %collective-permute-start.2 = (f32[16,1536]{1,0:T(8,128)}, f32[16,1536]{1,0:T(8,128)}, u32[]{:S(2)}, u32[]{:S(2)}) collective-permute-start(f32[16,1536]{1,0:T(8,128)} %get-tuple-element.16), channel_id=1, source_target_pairs={{0,1},{1,0},{2,3},{3,2},{4,5},{5,4},{6,7},{7,6},{8,9},{9,8},{10,11... | collective-permute-start | bytes 294920 | tf_op jit(solution)/shard_map/ppermute | solution.py:93
  32.9 1.8 %collective-permute-done.4 = f32[16,1536]{1,0:T(8,128)} collective-permute-done((f32[16,1536]{1,0:T(8,128)}, f32[16,1536]{1,0:T(8,128)}, u32[]{:S(2)}, u32[]{:S(2)}) %collective-permute-start.4) | collective-permute-done | bytes 98336 | tf_op jit(solution)/shard_map/ppermute | solution.py:93
  36.9 8.2 %multiply_reduce_fusion = (f32[1536]{0:T(1024)S(1)}, f32[1536]{0:T(1024)S(1)}, f32[1600,1536]{1,0:T(8,128)S(1)}) fusion(f32[1600,1536]{1,0:T(8,128)} %copy-done.1, f32[1536]{0:T(1024)} %param.11, f32[1536]{0:T(1024)} %param.10, bf16[16,1536]{1,0:T(8,128)(2,1)S(1)} %get-tuple-element.24, bf16[16,1536]{1,0:T(8,128)(2,1)S(1)} %get-tuple-element.23, ...), kind=kOutput, calls=%fused_computation.1 | convolution fusion | flops 268778496 | bytes 19884032 | tf_op jit(solution)/shard_map/dot_general | solution.py:173
  45.1 4.5 %fusion.2 = f32[1536,384]{1,0:T(8,128)} fusion(bf16[1600,384]{1,0:T(8,128)(2,1)S(1)} %copy-done.4, f32[1600,1536]{1,0:T(8,128)S(1)} %get-tuple-element.29, f32[1536]{0:T(1024)S(1)} %copy-done.18), kind=kOutput, calls=%fused_computation.8 | convolution fusion | flops 1892352000 | bytes 13424640 | tf_op jit(solution)/shard_map/dot_general | solution.py:180
  49.8 2.4 %fusion.21 = f32[4,1,200,384]{3,2,0,1:T(8,128)} fusion(s32[]{:T(128)S(6)} %select_n.412, f32[4,2,1,192,384]{4,3,1,0,2:T(8,128)} %bitcast.74, f32[4,2,1,8,384]{4,3,1,0,2:T(8,128)S(1)} %bitcast.83), kind=kLoop, calls=%fused_computation.28 | loop fusion | flops 307200 | bytes 3686404 | tf_op jit(solution)/shard_map/jit(dynamic_index_in_dim)/squeeze | solution.py:68
  52.2 3.3 %collective-permute-done.5 = f32[4,1,200,384]{3,2,0,1:T(8,128)} collective-permute-done((f32[4,1,200,384]{3,2,0,1:T(8,128)}, f32[4,1,200,384]{3,2,0,1:T(8,128)}, u32[]{:S(2)}, u32[]{:S(2)}) %collective-permute-start.5) | collective-permute-done | bytes 1228832 | tf_op jit(solution)/shard_map/ppermute | solution.py:69
  55.5 1.8 %fusion.24 = f32[4,1,200,384]{3,2,0,1:T(8,128)S(1)} fusion(f32[4,1,200,384]{3,2,0,1:T(8,128)} %collective-permute-done.5, s32[]{:T(128)S(6)} %select_n.411, f32[4,2,1,192,384]{4,3,1,0,2:T(8,128)} %bitcast.75, f32[4,2,1,8,384]{4,3,1,0,2:T(8,128)S(1)} %bitcast.84), kind=kLoop, calls=%fused_computation.31 | loop fusion | flops 614400 | bytes 4915204 | tf_op jit(solution)/shard_map/add | solution.py:70
  59.2 1.6 %collective-permute-start.6 = (f32[2,1,200,384]{3,2,1,0:T(8,128)}, f32[2,1,200,384]{3,2,1,0:T(8,128)}, u32[]{:S(2)}, u32[]{:S(2)}) collective-permute-start(f32[2,1,200,384]{3,2,1,0:T(8,128)} %dynamic-slice_bitcast_fusion), channel_id=1, source_target_pairs={{0,8},{4,12},{8,0},{12,4},{16,24},{20,28},{24,16},{28,20},{1,9},{5... | collective-permute-start | bytes 1843208 | tf_op jit(solution)/shard_map/ppermute | solution.py:69
  61.0 1.2 %select_n.422 = bf16[64,8,192]{2,1,0:T(8,128)(2,1)S(1)} reshape(bf16[4,16,1536]{2,1,0:T(8,128)(2,1)} %copy-done.5) | data formatting | bytes 393216 | tf_op jit(solution)/shard_map/jit(_where)/select_n | solution.py:54
  63.3 4.1 %all-to-all-start = ((bf16[8,64,322]{2,1,0:T(8,128)(2,1)}), bf16[8,64,322]{2,1,0:T(8,128)(2,1)}, u32[]{:S(2)}, u32[]{:S(2)}) async-start(bf16[8,64,322]{2,1,0:T(8,128)(2,1)} %pad_maximum_fusion), calls=%async_computation | async-start | bytes 786432 | tf_op jit(solution)/shard_map/all_to_all | solution.py:161
  67.4 10.9 %collective-permute-done.6 = f32[2,1,200,384]{3,2,1,0:T(8,128)} collective-permute-done((f32[2,1,200,384]{3,2,1,0:T(8,128)}, f32[2,1,200,384]{3,2,1,0:T(8,128)}, u32[]{:S(2)}, u32[]{:S(2)}) %collective-permute-start.6) | collective-permute-done | bytes 614432 | tf_op jit(solution)/shard_map/ppermute | solution.py:69
  78.3 1.3 %bitcast_add_fusion = f32[2,1,200,384]{3,2,1,0:T(8,128)S(1)} fusion(f32[2,1,200,384]{3,2,1,0:T(8,128)} %collective-permute-done.6, f32[2,2,1,200,384]{4,3,1,0,2:T(8,128)} %bitcast.77, s32[]{:T(128)S(6)} %select_n.415), kind=kLoop, calls=%fused_computation.33 | loop fusion | flops 153600 | bytes 1843204 | tf_op jit(solution)/shard_map/add | solution.py:70
  81.2 3.8 %collective-permute-start.7 = (f32[1,1,200,384]{3,2,1,0:T(8,128)}, f32[1,1,200,384]{3,2,1,0:T(8,128)}, u32[]{:S(2)}, u32[]{:S(2)}) collective-permute-start(f32[1,1,200,384]{3,2,1,0:T(8,128)} %constant_dynamic-slice_fusion), channel_id=1, source_target_pairs={{0,16},{4,20},{8,24},{12,28},{16,0},{20,4},{24,8},{28,12},{1,17},{... | collective-permute-start | bytes 921608 | tf_op jit(solution)/shard_map/ppermute | solution.py:69
  85.0 1.1 slice.74
  86.1 10.8 %collective-permute-done.7 = f32[1,1,200,384]{3,2,1,0:T(8,128)} collective-permute-done((f32[1,1,200,384]{3,2,1,0:T(8,128)}, f32[1,1,200,384]{3,2,1,0:T(8,128)}, u32[]{:S(2)}, u32[]{:S(2)}) %collective-permute-start.7) | collective-permute-done | bytes 307232 | tf_op jit(solution)/shard_map/ppermute | solution.py:69
  96.9 1.8 %add_bitcast_fusion = f32[200,384]{1,0:T(8,128)} fusion(f32[1,1,200,384]{3,2,1,0:T(8,128)} %collective-permute-done.7, f32[2,1,200,384]{3,2,1,0:T(8,128)} %copy-done.3, s32[]{:T(128)S(6)} %select_n.419), kind=kLoop, calls=%fused_computation.41 | loop fusion | flops 76800 | bytes 921604 | tf_op jit(solution)/shard_map/squeeze;reshape | solution.py:197
  98.7 1.4 %collective-permute-start.8 = (f32[200,384]{1,0:T(8,128)}, f32[200,384]{1,0:T(8,128)}, u32[]{:S(2)}, u32[]{:S(2)}) collective-permute-start(f32[200,384]{1,0:T(8,128)} %add_bitcast_fusion), channel_id=1, source_target_pairs={{0,1},{1,0},{2,3},{3,2},{4,5},{5,4},{6,7},{7,6},{8,9},{9,8},{10,11... | collective-permute-start | bytes 921608 | tf_op jit(solution)/shard_map/ppermute | solution.py:80
  102.0 1.1 copy.62
  105.0 1.2 %collective-permute-done.8 = f32[200,384]{1,0:T(8,128)} collective-permute-done((f32[200,384]{1,0:T(8,128)}, f32[200,384]{1,0:T(8,128)}, u32[]{:S(2)}, u32[]{:S(2)}) %collective-permute-start.8) | collective-permute-done | bytes 307232 | tf_op jit(solution)/shard_map/ppermute | solution.py:80
  106.2 1.1 add.290
  107.3 1.5 %collective-permute-start.9 = (f32[200,384]{1,0:T(8,128)S(1)}, f32[200,384]{1,0:T(8,128)S(1)}, u32[]{:S(2)}, u32[]{:S(2)}) collective-permute-start(f32[200,384]{1,0:T(8,128)S(1)} %add.290), channel_id=1, source_target_pairs={{0,2},{1,3},{2,0},{3,1},{4,6},{5,7},{6,4},{7,5},{8,10},{9,11},{10,... | collective-permute-start | bytes 921608 | tf_op jit(solution)/shard_map/ppermute | solution.py:80
  110.3 1.4 %fusion.83 = f32[1024,192]{0,1:T(8,128)} fusion(bf16[512,1024]{0,1:T(8,128)(2,1)S(1)} %bitcast.78, bf16[512,192]{1,0:T(8,128)(2,1)S(1)} %bitcast.82), kind=kOutput, calls=%fused_computation.193 | convolution fusion | flops 201326592 | bytes 2031616 | tf_op jit(solution)/shard_map/dot_general | solution.py:169
  111.7 2.5 %collective-permute-done.9 = f32[200,384]{1,0:T(8,128)S(1)} collective-permute-done((f32[200,384]{1,0:T(8,128)S(1)}, f32[200,384]{1,0:T(8,128)S(1)}, u32[]{:S(2)}, u32[]{:S(2)}) %collective-permute-start.9) | collective-permute-done | bytes 307232 | tf_op jit(solution)/shard_map/ppermute | solution.py:80
  (108 shorter events, 20.6 us)
Async XLA Ops:
  0.6 21.9 %copy-start = (bf16[1024,1536]{1,0:T(8,128)(2,1)S(1)}, bf16[1024,1536]{1,0:T(8,128)(2,1)}, u32[]{:S(2)}) copy-start(bf16[1024,1536]{1,0:T(8,128)(2,1)} %param.12) | copy-start | bytes 9437188
  0.7 4.5 %copy-start.8 = (s32[1600]{0:T(1024)}, s32[1600]{0:T(1024)S(1)}, u32[]{:S(2)}) copy-start(s32[1600]{0:T(1024)S(1)} %add_select_fusion.7) | copy-start | bytes 19204
  0.7 4.5 %copy-start.16 = (f32[1536]{0:T(1024)S(1)}, f32[1536]{0:T(1024)}, u32[]{:S(2)}) copy-start(f32[1536]{0:T(1024)} %param.11) | copy-start | bytes 18436
  0.7 4.5 %copy-start.17 = (f32[1536]{0:T(1024)S(1)}, f32[1536]{0:T(1024)}, u32[]{:S(2)}) copy-start(f32[1536]{0:T(1024)} %param.10) | copy-start | bytes 18436
  5.2 5.7 %copy-start.1 = (f32[1600,1536]{1,0:T(8,128)}, f32[1600,1536]{1,0:T(8,128)S(1)}, u32[]{:S(2)}) copy-start(f32[1600,1536]{1,0:T(8,128)S(1)} %fusion.82) | copy-start | bytes 29491204
  5.2 8.7 %copy-start.10 = (s32[64,64]{1,0:T(8,128)S(1)}, s32[64,64]{1,0:T(8,128)}, u32[]{:S(2)}) copy-start(s32[64,64]{1,0:T(8,128)} %param.14) | copy-start | bytes 49156
  5.3 9.4 %copy-start.15 = (s32[64]{0:T(128)S(1)}, s32[64]{0:T(128)}, u32[]{:S(2)}) copy-start(s32[64]{0:T(128)} %param.13) | copy-start | bytes 772
  10.9 6.9 %collective-permute-start = (bf16[1,16,1536]{2,1,0:T(8,128)(2,1)S(1)}, bf16[1,16,1536]{2,1,0:T(8,128)(2,1)S(1)}, u32[]{:S(2)}, u32[]{:S(2)}) collective-permute-start(bf16[1,16,1536]{2,1,0:T(8,128)(2,1)S(1)} %fusion.15), channel_id=1, source_target_pairs={{0,1},{1,0},{2,3},{3,2},{4,5},{5,4},{6,7},{7,6},{8,9},{9,8},{10,11... | collective-permute-start | bytes 147464 | tf_op jit(solution)/shard_map/ppermute | solution.py:52
  14.8 0.5 copy-start.11
  14.8 0.5 copy-start.13
  17.9 4.7 %collective-permute-start.1 = (bf16[2,16,1536]{2,1,0:T(8,128)(2,1)S(1)}, bf16[2,16,1536]{2,1,0:T(8,128)(2,1)S(1)}, u32[]{:S(2)}, u32[]{:S(2)}) collective-permute-start(bf16[2,16,1536]{2,1,0:T(8,128)(2,1)S(1)} %maximum_select_fusion.1), channel_id=1, source_target_pairs={{0,2},{1,3},{2,0},{3,1},{4,6},{5,7},{6,4},{7,5},{8,10},{9,11},{10,... | collective-permute-start | bytes 294920 | tf_op jit(solution)/shard_map/ppermute | solution.py:52
  22.6 1.8 %copy-start.5 = (bf16[4,16,1536]{2,1,0:T(8,128)(2,1)}, bf16[4,16,1536]{2,1,0:T(8,128)(2,1)S(1)}, u32[]{:S(2)}) copy-start(bf16[4,16,1536]{2,1,0:T(8,128)(2,1)S(1)} %maximum_select_fusion) | copy-start | bytes 589828
  25.5 0.9 copy-start.6
  26.4 5.9 %copy-start.9 = (s32[1600]{0:T(1024)S(1)}, s32[1600]{0:T(1024)}, u32[]{:S(2)}) copy-start(s32[1600]{0:T(1024)} %copy-done.8) | copy-start | bytes 19204
  28.8 5.9 %collective-permute-start.4 = (f32[16,1536]{1,0:T(8,128)}, f32[16,1536]{1,0:T(8,128)}, u32[]{:S(2)}, u32[]{:S(2)}) collective-permute-start(f32[16,1536]{1,0:T(8,128)} %get-tuple-element.17), channel_id=1, source_target_pairs={{0,3},{1,2},{2,1},{3,0},{4,7},{5,6},{6,5},{7,4},{8,11},{9,10},{10,... | collective-permute-start | bytes 294920 | tf_op jit(solution)/shard_map/ppermute | solution.py:93
  30.3 5.4 %collective-permute-start.3 = (f32[16,1536]{1,0:T(8,128)}, f32[16,1536]{1,0:T(8,128)}, u32[]{:S(2)}, u32[]{:S(2)}) collective-permute-start(f32[16,1536]{1,0:T(8,128)} %get-tuple-element.18), channel_id=1, source_target_pairs={{0,2},{1,3},{2,0},{3,1},{4,6},{5,7},{6,4},{7,5},{8,10},{9,11},{10,... | collective-permute-start | bytes 294920 | tf_op jit(solution)/shard_map/ppermute | solution.py:93
  30.4 5.4 %collective-permute-start.2 = (f32[16,1536]{1,0:T(8,128)}, f32[16,1536]{1,0:T(8,128)}, u32[]{:S(2)}, u32[]{:S(2)}) collective-permute-start(f32[16,1536]{1,0:T(8,128)} %get-tuple-element.16), channel_id=1, source_target_pairs={{0,1},{1,0},{2,3},{3,2},{4,5},{5,4},{6,7},{7,6},{8,9},{9,8},{10,11... | collective-permute-start | bytes 294920 | tf_op jit(solution)/shard_map/ppermute | solution.py:93
  36.8 8.2 %copy-start.4 = (bf16[1600,384]{1,0:T(8,128)(2,1)S(1)}, bf16[1600,384]{1,0:T(8,128)(2,1)}, u32[]{:S(2)}) copy-start(bf16[1600,384]{1,0:T(8,128)(2,1)} %param.8) | copy-start | bytes 3686404
  36.8 8.2 %copy-start.18 = (f32[1536]{0:T(1024)S(1)}, f32[1536]{0:T(1024)}, u32[]{:S(2)}) copy-start(f32[1536]{0:T(1024)} %param.10) | copy-start | bytes 18436
  52.2 8.5 %copy-start.14 = (s32[64]{0:T(128)S(1)}, s32[64]{0:T(128)}, u32[]{:S(2)}) copy-start(s32[64]{0:T(128)} %copy-done.13) | copy-start | bytes 772
  52.2 8.6 %copy-start.12 = (s32[64]{0:T(128)S(1)}, s32[64]{0:T(128)}, u32[]{:S(2)}) copy-start(s32[64]{0:T(128)} %copy-done.11) | copy-start | bytes 772
  52.2 3.3 %collective-permute-start.5 = (f32[4,1,200,384]{3,2,0,1:T(8,128)}, f32[4,1,200,384]{3,2,0,1:T(8,128)}, u32[]{:S(2)}, u32[]{:S(2)}) collective-permute-start(f32[4,1,200,384]{3,2,0,1:T(8,128)} %fusion.21), channel_id=1, source_target_pairs={{0,4},{4,0},{8,12},{12,8},{16,20},{20,16},{24,28},{28,24},{1,5},{5... | collective-permute-start | bytes 3686408 | tf_op jit(solution)/shard_map/ppermute | solution.py:69
  52.2 10.0 %copy-start.7 = (bf16[64,64]{1,0:T(8,128)(2,1)S(1)}, bf16[64,64]{1,0:T(8,128)(2,1)}, u32[]{:S(2)}) copy-start(bf16[64,64]{1,0:T(8,128)(2,1)} %copy-done.6) | copy-start | bytes 24580
  57.3 1.0 copy-start.2
  59.2 19.1 %collective-permute-start.6 = (f32[2,1,200,384]{3,2,1,0:T(8,128)}, f32[2,1,200,384]{3,2,1,0:T(8,128)}, u32[]{:S(2)}, u32[]{:S(2)}) collective-permute-start(f32[2,1,200,384]{3,2,1,0:T(8,128)} %dynamic-slice_bitcast_fusion), channel_id=1, source_target_pairs={{0,8},{4,12},{8,0},{12,4},{16,24},{20,28},{24,16},{28,20},{1,9},{5... | collective-permute-start | bytes 1843208 | tf_op jit(solution)/shard_map/ppermute | solution.py:69
  63.3 21.7 %all-to-all-start = ((bf16[8,64,322]{2,1,0:T(8,128)(2,1)}), bf16[8,64,322]{2,1,0:T(8,128)(2,1)}, u32[]{:S(2)}, u32[]{:S(2)}) async-start(bf16[8,64,322]{2,1,0:T(8,128)(2,1)} %pad_maximum_fusion), calls=%async_computation | async-start | bytes 786432 | tf_op jit(solution)/shard_map/all_to_all | solution.py:161
  79.6 0.8 copy-start.3
  81.2 15.7 %collective-permute-start.7 = (f32[1,1,200,384]{3,2,1,0:T(8,128)}, f32[1,1,200,384]{3,2,1,0:T(8,128)}, u32[]{:S(2)}, u32[]{:S(2)}) collective-permute-start(f32[1,1,200,384]{3,2,1,0:T(8,128)} %constant_dynamic-slice_fusion), channel_id=1, source_target_pairs={{0,16},{4,20},{8,24},{12,28},{16,0},{20,4},{24,8},{28,12},{1,17},{... | collective-permute-start | bytes 921608 | tf_op jit(solution)/shard_map/ppermute | solution.py:69
  98.7 7.5 %collective-permute-start.8 = (f32[200,384]{1,0:T(8,128)}, f32[200,384]{1,0:T(8,128)}, u32[]{:S(2)}, u32[]{:S(2)}) collective-permute-start(f32[200,384]{1,0:T(8,128)} %add_bitcast_fusion), channel_id=1, source_target_pairs={{0,1},{1,0},{2,3},{3,2},{4,5},{5,4},{6,7},{7,6},{8,9},{9,8},{10,11... | collective-permute-start | bytes 921608 | tf_op jit(solution)/shard_map/ppermute | solution.py:80
  107.3 6.9 %collective-permute-start.9 = (f32[200,384]{1,0:T(8,128)S(1)}, f32[200,384]{1,0:T(8,128)S(1)}, u32[]{:S(2)}, u32[]{:S(2)}) collective-permute-start(f32[200,384]{1,0:T(8,128)S(1)} %add.290), channel_id=1, source_target_pairs={{0,2},{1,3},{2,0},{3,1},{4,6},{5,7},{6,4},{7,5},{8,10},{9,11},{10,... | collective-permute-start | bytes 921608 | tf_op jit(solution)/shard_map/ppermute | solution.py:80

commit v13 on v12

--- a/solution.py
+++ b/solution.py
@@ -91,6 +91,18 @@
     for k in range(1, size):
         give = lax.dynamic_index_in_dim(blocks, jnp.bitwise_xor(idx, k), 0, keepdims=False)
         total = total + lax.ppermute(give, name, [(i, i ^ k) for i in range(size)])
+    return total
+
+
+def direct_sum(x, name):
+    size = lax.axis_size(name)
+    idx = lax.axis_index(name)
+    got = [x] + [lax.ppermute(x, name, [(i, i ^ k) for i in range(size)]) for k in range(1, size)]
+    stacked = jnp.stack(got)
+    order = jnp.bitwise_xor(jnp.arange(size, dtype=jnp.int32), idx)
+    total = lax.dynamic_index_in_dim(stacked, order[0], 0, keepdims=False)
+    for j in range(1, size):
+        total = total + lax.dynamic_index_in_dim(stacked, order[j], 0, keepdims=False)
     return total
 
 
@@ -194,7 +206,10 @@
         [head_term.reshape(n_dp, chunk, e_size), side_rows.reshape(n_dp, pad_rows, e_size)], axis=1
     )
     (part,) = halving_scatter([stacked], "dp")
-    (total,) = butterfly_sum([part[0]], "leaf")
+    if lax.axis_size("leaf") <= 4:
+        total = direct_sum(part[0], "leaf")
+    else:
+        (total,) = butterfly_sum([part[0]], "leaf")
     side_flat = total[chunk:].reshape(-1)
     side_sum = jnp.stack([side_flat[:chunk], side_flat[chunk : 2 * chunk]], axis=1)
     return (total[:chunk].T, side_sum[:, 0], side_sum[:, 1], node_grad)

time: 117 us -> 121 us (1.034)
  between operations: 1.18 us -> 8.93 us
  waiting for transfers between devices: 34 us -> 30.8 us
  starting transfers between devices: 20.5 us -> 19.1 us
    ppermute x3, waiting for transfers between devices: 25 us -> 9.11 us  [halving_scatter(): got = lax.ppermute(tuple(give), name, partners(size, bit))]
    all_to_all x1, waiting for transfers between devices: 0.01 us -> 8.26 us  [shards(): recv = lax.all_to_all(send, 'dp', split_axis=0, concat_axis=0, tiled=True)]
    ppermute x2 -> x3, waiting for transfers between devices: 3.66 us -> 8.01 us  [direct_sum(): lax.ppermute(x, name, [(i, i ^ k) for i in range(size)])]
    ppermute x3, starting transfers between devices: 5.38 us -> 3.41 us  [halving_scatter(): got = lax.ppermute(tuple(give), name, partners(size, bit))]
    ppermute x2 -> x3, starting transfers between devices: 2.94 us -> 3.55 us  [direct_sum(): lax.ppermute(x, name, [(i, i ^ k) for i in range(size)])]
  transfers between devices with their start and end apart: 11 -> 12, of which waited for: 9 -> 9; matrix products, arithmetic and copies ran while one was open for 16% -> 15% of each run, Pallas kernels for 0% -> 0%
where the time goes in v13:
time: 121 us; the launch traced here: 119 us
  waiting for transfers between devices  30.8 us (25%)
  matrix products  27.7 us (23%)
  starting transfers between devices  19.1 us (16%)
  local copies, waits for them, and re-layouts  17.1 us (14%)
  other arithmetic  15.5 us (13%)
  between operations  8.93 us (7%)
    ppermute x3, waiting for transfers between devices, halving_scatter(): got = lax.ppermute(tuple(give), name, partners(size, bit))  9.11 us
    all_to_all x1, waiting for transfers between devices, shards(): recv = lax.all_to_all(send, 'dp', split_axis=0, concat_axis=0, tiled=True)  8.26 us
    dot_general x1, matrix products, shards(): jnp.dot(jnp.concatenate([select.T.astype(jnp.bfloat16)] * 3, axis=1), jnp...  8.15 us
    ppermute x3, waiting for transfers between devices, direct_sum(): lax.ppermute(x, name, [(i, i ^ k) for i in range(size)])  8.01 us
    dot_general x1, matrix products, shards(): jnp.dot(select, active, precision=HIGHEST, preferred_element_type=jnp.flo...  5.63 us
    unnamed x44, local copies, waits for them, and re-layouts  5.55 us
    ppermute x2, starting transfers between devices, doubling_gather(): other = lax.ppermute(cur, name, partners(size, bit))  4.59 us
    dot_general x1, matrix products, shards(): jnp.dot(features, head_weight, preferred_element_type=jnp.float32)  4.5 us
  transfers between devices with their start and end apart: 12, of which 9 were waited for; matrix products, arithmetic and copies ran while one was open for 15% of the time, Pallas kernels for 0%

profile of v13, /device:TPU:0, one launch (start us, length us, event | category | flops | bytes accessed | tf_op | source)
XLA Modules:
  0.0 119.1 jit_solution(4122151447063607505)
XLA Ops:
  0.7 4.5 %fusion.85 = f32[1600,1536]{1,0:T(8,128)S(1)} fusion(bf16[1600,384]{1,0:T(8,128)(2,1)} %param.8, bf16[384,1536]{1,0:T(8,128)(2,1)} %param.9), kind=kOutput, calls=%fused_computation.198 | convolution fusion | flops 1887436800 | bytes 12238848 | tf_op jit(solution)/shard_map/dot_general | solution.py:123
  5.3 5.6 %fusion.15 = bf16[1,16,1536]{2,1,0:T(8,128)(2,1)S(1)} fusion(f32[1600,1536]{1,0:T(8,128)S(1)} %fusion.85, f32[1536]{0:T(1024)S(1)} %copy-done.16, f32[1536]{0:T(1024)S(1)} %copy-done.17, s32[1600]{0:T(1024)S(1)} %add_select_fusion.7), kind=kOutput, calls=%fused_computation.21 | convolution fusion | flops 486679552 | bytes 9898240 | tf_op jit(solution)/shard_map/dot_general | solution.py:127
  10.9 3.0 %collective-permute-start = (bf16[1,16,1536]{2,1,0:T(8,128)(2,1)S(1)}, bf16[1,16,1536]{2,1,0:T(8,128)(2,1)S(1)}, u32[]{:S(2)}, u32[]{:S(2)}) collective-permute-start(bf16[1,16,1536]{2,1,0:T(8,128)(2,1)S(1)} %fusion.15), channel_id=1, source_target_pairs={{0,1},{1,0},{2,3},{3,2},{4,5},{5,4},{6,7},{7,6},{8,9},{9,8},{10,11... | collective-permute-start | bytes 147464 | tf_op jit(solution)/shard_map/ppermute | solution.py:52
  15.7 1.1 fusion.19
  17.9 1.6 %collective-permute-start.1 = (bf16[2,16,1536]{2,1,0:T(8,128)(2,1)S(1)}, bf16[2,16,1536]{2,1,0:T(8,128)(2,1)S(1)}, u32[]{:S(2)}, u32[]{:S(2)}) collective-permute-start(bf16[2,16,1536]{2,1,0:T(8,128)(2,1)S(1)} %maximum_select_fusion.1), channel_id=1, source_target_pairs={{0,2},{1,3},{2,0},{3,1},{4,6},{5,7},{6,4},{7,5},{8,10},{9,11},{10,... | collective-permute-start | bytes 294920 | tf_op jit(solution)/shard_map/ppermute | solution.py:52
  20.1 2.5 %collective-permute-done.1 = bf16[2,16,1536]{2,1,0:T(8,128)(2,1)S(1)} collective-permute-done((bf16[2,16,1536]{2,1,0:T(8,128)(2,1)S(1)}, bf16[2,16,1536]{2,1,0:T(8,128)(2,1)S(1)}, u32[]{:S(2)}, u32[]{:S(2)}) %collective-permute-start.1) | collective-permute-done | bytes 98336 | tf_op jit(solution)/shard_map/ppermute | solution.py:52
  22.6 1.8 %select_reduce_fusion = (f32[64,64]{1,0:T(8,128)S(1)}, f32[64,64]{1,0:T(8,128)S(1)}) fusion(pred[64,16]{0,1:T(8,128)(4,1)S(1)} %iota_compare_fusion.8, pred[64,16]{0,1:T(8,128)(4,1)S(1)} %iota_compare_fusion.9, bf16[64,1536,1]{1,0,2:T(8,128)(2,1)S(1)} %bitcast.96, bf16[16,64,1536]{2,1,0:T(8,128)(2,1)S(1)} %bitcast.84), kind=kOutput, calls=%fused_computation.36 | convolution fusion | flops 201580544 | bytes 3377152 | tf_op jit(solution)/shard_map/dot_general | solution.py:143
  26.4 1.7 %fusion.7 = f32[4,16,1536]{2,1,0:T(8,128)S(1)} fusion(bf16[1024,1536]{1,0:T(8,128)(2,1)S(1)} %copy-done, bf16[4,16,1024]{2,1,0:T(8,128)(2,1)} %tile.13, bf16[4,16,1024]{2,1,0:T(8,128)(2,1)} %tile.15, s32[4,16]{1,0:T(4,128)} %get-tuple-element.37, s32[4,16]{1,0:T(4,128)} %get-tuple-element.36, s32[1024]{0:T(1024)} %add_select_fusion.8), kind=kOutput, calls=%fused_computation.15 | convolution fusion | flops 201654272 | bytes 3805696 | tf_op jit(solution)/shard_map/dot_general | solution.py:153
  28.8 1.5 %collective-permute-start.4 = (f32[16,1536]{1,0:T(8,128)}, f32[16,1536]{1,0:T(8,128)}, u32[]{:S(2)}, u32[]{:S(2)}) collective-permute-start(f32[16,1536]{1,0:T(8,128)} %get-tuple-element.19), channel_id=1, source_target_pairs={{0,3},{1,2},{2,1},{3,0},{4,7},{5,6},{6,5},{7,4},{8,11},{9,10},{10,... | collective-permute-start | bytes 294920 | tf_op jit(solution)/shard_map/ppermute | solution.py:93
  30.4 1.9 %collective-permute-start.2 = (f32[16,1536]{1,0:T(8,128)}, f32[16,1536]{1,0:T(8,128)}, u32[]{:S(2)}, u32[]{:S(2)}) collective-permute-start(f32[16,1536]{1,0:T(8,128)} %get-tuple-element.18), channel_id=1, source_target_pairs={{0,1},{1,0},{2,3},{3,2},{4,5},{5,4},{6,7},{7,6},{8,9},{9,8},{10,11... | collective-permute-start | bytes 294920 | tf_op jit(solution)/shard_map/ppermute | solution.py:93
  33.0 1.8 %collective-permute-done.4 = f32[16,1536]{1,0:T(8,128)} collective-permute-done((f32[16,1536]{1,0:T(8,128)}, f32[16,1536]{1,0:T(8,128)}, u32[]{:S(2)}, u32[]{:S(2)}) %collective-permute-start.4) | collective-permute-done | bytes 98336 | tf_op jit(solution)/shard_map/ppermute | solution.py:93
  35.8 1.0 reduce-precision_convert_fusion.1
  36.9 8.1 %multiply_reduce_fusion = (f32[1536]{0:T(1024)S(1)}, f32[1536]{0:T(1024)S(1)}, f32[1600,1536]{1,0:T(8,128)S(1)}) fusion(f32[1600,1536]{1,0:T(8,128)} %copy-done.1, f32[1536]{0:T(1024)} %param.11, f32[1536]{0:T(1024)} %param.10, bf16[16,1536]{1,0:T(8,128)(2,1)S(1)} %get-tuple-element.26, bf16[16,1536]{1,0:T(8,128)(2,1)S(1)} %get-tuple-element.25, ...), kind=kOutput, calls=%fused_computation.1 | convolution fusion | flops 268778496 | bytes 19884032 | tf_op jit(solution)/shard_map/dot_general | solution.py:185
  45.1 4.5 %fusion.2 = f32[1536,384]{1,0:T(8,128)} fusion(bf16[1600,384]{1,0:T(8,128)(2,1)S(1)} %copy-done.4, f32[1600,1536]{1,0:T(8,128)S(1)} %get-tuple-element.35, f32[1536]{0:T(1024)S(1)} %copy-done.18), kind=kOutput, calls=%fused_computation.8 | convolution fusion | flops 1892352000 | bytes 13424640 | tf_op jit(solution)/shard_map/dot_general | solution.py:192
  49.8 2.4 %fusion.21 = f32[4,1,200,384]{3,2,0,1:T(8,128)} fusion(s32[]{:T(128)S(6)} %select_n.425, f32[4,2,1,192,384]{4,3,1,0,2:T(8,128)} %bitcast.85, f32[4,2,1,8,384]{4,3,1,0,2:T(8,128)S(1)} %bitcast.94), kind=kLoop, calls=%fused_computation.28 | loop fusion | flops 307200 | bytes 3686404 | tf_op jit(solution)/shard_map/jit(dynamic_index_in_dim)/squeeze | solution.py:68
  53.1 1.2 select_n.439
  55.5 1.8 %fusion.24 = f32[4,1,200,384]{3,2,0,1:T(8,128)S(1)} fusion(f32[4,1,200,384]{3,2,0,1:T(8,128)} %collective-permute-done.5, s32[]{:T(128)S(6)} %select_n.424, f32[4,2,1,192,384]{4,3,1,0,2:T(8,128)} %bitcast.86, f32[4,2,1,8,384]{4,3,1,0,2:T(8,128)S(1)} %bitcast.95), kind=kLoop, calls=%fused_computation.31 | loop fusion | flops 614400 | bytes 4915204 | tf_op jit(solution)/shard_map/add | solution.py:70
  57.3 1.1 copy-done.2
  59.2 1.6 %collective-permute-start.6 = (f32[2,1,200,384]{3,2,1,0:T(8,128)}, f32[2,1,200,384]{3,2,1,0:T(8,128)}, u32[]{:S(2)}, u32[]{:S(2)}) collective-permute-start(f32[2,1,200,384]{3,2,1,0:T(8,128)} %dynamic-slice_bitcast_fusion), channel_id=1, source_target_pairs={{0,8},{4,12},{8,0},{12,4},{16,24},{20,28},{24,16},{28,20},{1,9},{5... | collective-permute-start | bytes 1843208 | tf_op jit(solution)/shard_map/ppermute | solution.py:69
  61.7 4.1 %all-to-all-start = ((bf16[8,64,322]{2,1,0:T(8,128)(2,1)}), bf16[8,64,322]{2,1,0:T(8,128)(2,1)}, u32[]{:S(2)}, u32[]{:S(2)}) async-start(bf16[8,64,322]{2,1,0:T(8,128)(2,1)} %pad_maximum_fusion.1), calls=%async_computation | async-start | bytes 786432 | tf_op jit(solution)/shard_map/all_to_all | solution.py:173
  74.2 8.3 %all-to-all-done = bf16[8,64,322]{2,1,0:T(8,128)(2,1)} async-done(((bf16[8,64,322]{2,1,0:T(8,128)(2,1)}), bf16[8,64,322]{2,1,0:T(8,128)(2,1)}, u32[]{:S(2)}, u32[]{:S(2)}) %all-to-all-start) | async-done | bytes 329760 | tf_op jit(solution)/shard_map/all_to_all | solution.py:173
  82.4 1.1 slice.95
  83.5 1.3 %bitcast_add_fusion = f32[2,1,200,384]{3,2,1,0:T(8,128)S(1)} fusion(f32[2,1,200,384]{3,2,1,0:T(8,128)} %collective-permute-done.6, f32[2,2,1,200,384]{4,3,1,0,2:T(8,128)} %bitcast.88, s32[]{:T(128)S(6)} %select_n.428), kind=kLoop, calls=%fused_computation.34 | loop fusion | flops 153600 | bytes 1843204 | tf_op jit(solution)/shard_map/add | solution.py:70
  86.4 1.8 %collective-permute-start.7 = (f32[1,1,200,384]{3,2,1,0:T(8,128)}, f32[1,1,200,384]{3,2,1,0:T(8,128)}, u32[]{:S(2)}, u32[]{:S(2)}) collective-permute-start(f32[1,1,200,384]{3,2,1,0:T(8,128)} %constant_dynamic-slice_fusion), channel_id=1, source_target_pairs={{0,16},{4,20},{8,24},{12,28},{16,0},{20,4},{24,8},{28,12},{1,17},{... | collective-permute-start | bytes 921608 | tf_op jit(solution)/shard_map/ppermute | solution.py:69
  89.1 1.1 copy.63
  90.2 1.1 copy.62
  93.1 8.8 %collective-permute-done.7 = f32[1,1,200,384]{3,2,1,0:T(8,128)} collective-permute-done((f32[1,1,200,384]{3,2,1,0:T(8,128)}, f32[1,1,200,384]{3,2,1,0:T(8,128)}, u32[]{:S(2)}, u32[]{:S(2)}) %collective-permute-start.7) | collective-permute-done | bytes 307232 | tf_op jit(solution)/shard_map/ppermute | solution.py:69
  101.9 1.1 fusion.44
  103.0 2.5 %collective-permute-start.10 = (f32[200,384]{1,0:T(8,128)S(1)}, f32[200,384]{1,0:T(8,128)S(1)}, u32[]{:S(2)}, u32[]{:S(2)}) collective-permute-start(f32[200,384]{1,0:T(8,128)S(1)} %get-tuple-element.17), channel_id=1, source_target_pairs={{0,3},{1,2},{2,1},{3,0},{4,7},{5,6},{6,5},{7,4},{8,11},{9,10},{10,... | collective-permute-start | bytes 921608 | tf_op jit(solution)/shard_map/ppermute | solution.py:100
  108.1 1.4 %fusion.86 = f32[1024,192]{0,1:T(8,128)} fusion(bf16[512,1024]{0,1:T(8,128)(2,1)S(1)} %bitcast.89, bf16[512,192]{1,0:T(8,128)(2,1)S(1)} %bitcast.93), kind=kOutput, calls=%fused_computation.199 | convolution fusion | flops 201326592 | bytes 2031616 | tf_op jit(solution)/shard_map/dot_general | solution.py:181
  109.5 4.7 %collective-permute-done.10 = f32[200,384]{1,0:T(8,128)S(1)} collective-permute-done((f32[200,384]{1,0:T(8,128)S(1)}, f32[200,384]{1,0:T(8,128)S(1)}, u32[]{:S(2)}, u32[]{:S(2)}) %collective-permute-start.10) | collective-permute-done | bytes 307232 | tf_op jit(solution)/shard_map/ppermute | solution.py:100
  114.2 3.3 %collective-permute-done.9 = f32[200,384]{1,0:T(8,128)S(1)} collective-permute-done((f32[200,384]{1,0:T(8,128)S(1)}, f32[200,384]{1,0:T(8,128)S(1)}, u32[]{:S(2)}, u32[]{:S(2)}) %collective-permute-start.9) | collective-permute-done | bytes 307232 | tf_op jit(solution)/shard_map/ppermute | solution.py:100
  (112 shorter events, 21.1 us)
Async XLA Ops:
  0.6 22.0 %copy-start = (bf16[1024,1536]{1,0:T(8,128)(2,1)S(1)}, bf16[1024,1536]{1,0:T(8,128)(2,1)}, u32[]{:S(2)}) copy-start(bf16[1024,1536]{1,0:T(8,128)(2,1)} %param.12) | copy-start | bytes 9437188
  0.7 4.5 %copy-start.8 = (s32[1600]{0:T(1024)}, s32[1600]{0:T(1024)S(1)}, u32[]{:S(2)}) copy-start(s32[1600]{0:T(1024)S(1)} %add_select_fusion.7) | copy-start | bytes 19204
  0.7 4.5 %copy-start.16 = (f32[1536]{0:T(1024)S(1)}, f32[1536]{0:T(1024)}, u32[]{:S(2)}) copy-start(f32[1536]{0:T(1024)} %param.11) | copy-start | bytes 18436
  0.7 4.5 %copy-start.17 = (f32[1536]{0:T(1024)S(1)}, f32[1536]{0:T(1024)}, u32[]{:S(2)}) copy-start(f32[1536]{0:T(1024)} %param.10) | copy-start | bytes 18436
  5.2 5.7 %copy-start.1 = (f32[1600,1536]{1,0:T(8,128)}, f32[1600,1536]{1,0:T(8,128)S(1)}, u32[]{:S(2)}) copy-start(f32[1600,1536]{1,0:T(8,128)S(1)} %fusion.85) | copy-start | bytes 29491204
  5.2 8.7 %copy-start.10 = (s32[64,64]{1,0:T(8,128)S(1)}, s32[64,64]{1,0:T(8,128)}, u32[]{:S(2)}) copy-start(s32[64,64]{1,0:T(8,128)} %param.14) | copy-start | bytes 49156
  5.3 9.4 %copy-start.15 = (s32[64]{0:T(128)S(1)}, s32[64]{0:T(128)}, u32[]{:S(2)}) copy-start(s32[64]{0:T(128)} %param.13) | copy-start | bytes 772
  10.9 7.0 %collective-permute-start = (bf16[1,16,1536]{2,1,0:T(8,128)(2,1)S(1)}, bf16[1,16,1536]{2,1,0:T(8,128)(2,1)S(1)}, u32[]{:S(2)}, u32[]{:S(2)}) collective-permute-start(bf16[1,16,1536]{2,1,0:T(8,128)(2,1)S(1)} %fusion.15), channel_id=1, source_target_pairs={{0,1},{1,0},{2,3},{3,2},{4,5},{5,4},{6,7},{7,6},{8,9},{9,8},{10,11... | collective-permute-start | bytes 147464 | tf_op jit(solution)/shard_map/ppermute | solution.py:52
  14.8 0.5 copy-start.11
  14.8 0.5 copy-start.13
  17.9 4.7 %collective-permute-start.1 = (bf16[2,16,1536]{2,1,0:T(8,128)(2,1)S(1)}, bf16[2,16,1536]{2,1,0:T(8,128)(2,1)S(1)}, u32[]{:S(2)}, u32[]{:S(2)}) collective-permute-start(bf16[2,16,1536]{2,1,0:T(8,128)(2,1)S(1)} %maximum_select_fusion.1), channel_id=1, source_target_pairs={{0,2},{1,3},{2,0},{3,1},{4,6},{5,7},{6,4},{7,5},{8,10},{9,11},{10,... | collective-permute-start | bytes 294920 | tf_op jit(solution)/shard_map/ppermute | solution.py:52
  22.6 1.8 %copy-start.5 = (bf16[4,16,1536]{2,1,0:T(8,128)(2,1)}, bf16[4,16,1536]{2,1,0:T(8,128)(2,1)S(1)}, u32[]{:S(2)}) copy-start(bf16[4,16,1536]{2,1,0:T(8,128)(2,1)S(1)} %maximum_select_fusion) | copy-start | bytes 589828
  25.5 0.9 copy-start.6
  26.4 5.9 %copy-start.9 = (s32[1600]{0:T(1024)S(1)}, s32[1600]{0:T(1024)}, u32[]{:S(2)}) copy-start(s32[1600]{0:T(1024)} %copy-done.8) | copy-start | bytes 19204
  28.8 5.9 %collective-permute-start.4 = (f32[16,1536]{1,0:T(8,128)}, f32[16,1536]{1,0:T(8,128)}, u32[]{:S(2)}, u32[]{:S(2)}) collective-permute-start(f32[16,1536]{1,0:T(8,128)} %get-tuple-element.19), channel_id=1, source_target_pairs={{0,3},{1,2},{2,1},{3,0},{4,7},{5,6},{6,5},{7,4},{8,11},{9,10},{10,... | collective-permute-start | bytes 294920 | tf_op jit(solution)/shard_map/ppermute | solution.py:93
  30.3 5.4 %collective-permute-start.3 = (f32[16,1536]{1,0:T(8,128)}, f32[16,1536]{1,0:T(8,128)}, u32[]{:S(2)}, u32[]{:S(2)}) collective-permute-start(f32[16,1536]{1,0:T(8,128)} %get-tuple-element.20), channel_id=1, source_target_pairs={{0,2},{1,3},{2,0},{3,1},{4,6},{5,7},{6,4},{7,5},{8,10},{9,11},{10,... | collective-permute-start | bytes 294920 | tf_op jit(solution)/shard_map/ppermute | solution.py:93
  30.4 5.4 %collective-permute-start.2 = (f32[16,1536]{1,0:T(8,128)}, f32[16,1536]{1,0:T(8,128)}, u32[]{:S(2)}, u32[]{:S(2)}) collective-permute-start(f32[16,1536]{1,0:T(8,128)} %get-tuple-element.18), channel_id=1, source_target_pairs={{0,1},{1,0},{2,3},{3,2},{4,5},{5,4},{6,7},{7,6},{8,9},{9,8},{10,11... | collective-permute-start | bytes 294920 | tf_op jit(solution)/shard_map/ppermute | solution.py:93
  36.9 8.2 %copy-start.4 = (bf16[1600,384]{1,0:T(8,128)(2,1)S(1)}, bf16[1600,384]{1,0:T(8,128)(2,1)}, u32[]{:S(2)}) copy-start(bf16[1600,384]{1,0:T(8,128)(2,1)} %param.8) | copy-start | bytes 3686404
  36.9 8.2 %copy-start.18 = (f32[1536]{0:T(1024)S(1)}, f32[1536]{0:T(1024)}, u32[]{:S(2)}) copy-start(f32[1536]{0:T(1024)} %param.10) | copy-start | bytes 18436
  49.6 2.7 %copy-start.14 = (s32[64]{0:T(128)S(1)}, s32[64]{0:T(128)}, u32[]{:S(2)}) copy-start(s32[64]{0:T(128)} %copy-done.13) | copy-start | bytes 772
  49.6 2.8 %copy-start.12 = (s32[64]{0:T(128)S(1)}, s32[64]{0:T(128)}, u32[]{:S(2)}) copy-start(s32[64]{0:T(128)} %copy-done.11) | copy-start | bytes 772
  49.6 4.8 %copy-start.7 = (bf16[64,64]{1,0:T(8,128)(2,1)S(1)}, bf16[64,64]{1,0:T(8,128)(2,1)}, u32[]{:S(2)}) copy-start(bf16[64,64]{1,0:T(8,128)(2,1)} %copy-done.6) | copy-start | bytes 24580
  52.2 3.3 %collective-permute-start.5 = (f32[4,1,200,384]{3,2,0,1:T(8,128)}, f32[4,1,200,384]{3,2,0,1:T(8,128)}, u32[]{:S(2)}, u32[]{:S(2)}) collective-permute-start(f32[4,1,200,384]{3,2,0,1:T(8,128)} %fusion.21), channel_id=1, source_target_pairs={{0,4},{4,0},{8,12},{12,8},{16,20},{20,16},{24,28},{28,24},{1,5},{5... | collective-permute-start | bytes 3686408 | tf_op jit(solution)/shard_map/ppermute | solution.py:69
  57.3 1.1 copy-start.2
  59.2 24.3 %collective-permute-start.6 = (f32[2,1,200,384]{3,2,1,0:T(8,128)}, f32[2,1,200,384]{3,2,1,0:T(8,128)}, u32[]{:S(2)}, u32[]{:S(2)}) collective-permute-start(f32[2,1,200,384]{3,2,1,0:T(8,128)} %dynamic-slice_bitcast_fusion), channel_id=1, source_target_pairs={{0,8},{4,12},{8,0},{12,4},{16,24},{20,28},{24,16},{28,20},{1,9},{5... | collective-permute-start | bytes 1843208 | tf_op jit(solution)/shard_map/ppermute | solution.py:69
  61.7 20.7 %all-to-all-start = ((bf16[8,64,322]{2,1,0:T(8,128)(2,1)}), bf16[8,64,322]{2,1,0:T(8,128)(2,1)}, u32[]{:S(2)}, u32[]{:S(2)}) async-start(bf16[8,64,322]{2,1,0:T(8,128)(2,1)} %pad_maximum_fusion.1), calls=%async_computation | async-start | bytes 786432 | tf_op jit(solution)/shard_map/all_to_all | solution.py:173
  84.9 0.8 copy-start.3
  86.4 15.4 %collective-permute-start.7 = (f32[1,1,200,384]{3,2,1,0:T(8,128)}, f32[1,1,200,384]{3,2,1,0:T(8,128)}, u32[]{:S(2)}, u32[]{:S(2)}) collective-permute-start(f32[1,1,200,384]{3,2,1,0:T(8,128)} %constant_dynamic-slice_fusion), channel_id=1, source_target_pairs={{0,16},{4,20},{8,24},{12,28},{16,0},{20,4},{24,8},{28,12},{1,17},{... | collective-permute-start | bytes 921608 | tf_op jit(solution)/shard_map/ppermute | solution.py:69
  103.0 11.2 %collective-permute-start.10 = (f32[200,384]{1,0:T(8,128)S(1)}, f32[200,384]{1,0:T(8,128)S(1)}, u32[]{:S(2)}, u32[]{:S(2)}) collective-permute-start(f32[200,384]{1,0:T(8,128)S(1)} %get-tuple-element.17), channel_id=1, source_target_pairs={{0,3},{1,2},{2,1},{3,0},{4,7},{5,6},{6,5},{7,4},{8,11},{9,10},{10,... | collective-permute-start | bytes 921608 | tf_op jit(solution)/shard_map/ppermute | solution.py:100
  105.4 12.0 %collective-permute-start.9 = (f32[200,384]{1,0:T(8,128)S(1)}, f32[200,384]{1,0:T(8,128)S(1)}, u32[]{:S(2)}, u32[]{:S(2)}) collective-permute-start(f32[200,384]{1,0:T(8,128)S(1)} %get-tuple-element.17), channel_id=1, source_target_pairs={{0,2},{1,3},{2,0},{3,1},{4,6},{5,7},{6,4},{7,5},{8,10},{9,11},{10,... | collective-permute-start | bytes 921608 | tf_op jit(solution)/shard_map/ppermute | solution.py:100
  105.9 11.6 %collective-permute-start.8 = (f32[200,384]{1,0:T(8,128)S(1)}, f32[200,384]{1,0:T(8,128)S(1)}, u32[]{:S(2)}, u32[]{:S(2)}) collective-permute-start(f32[200,384]{1,0:T(8,128)S(1)} %get-tuple-element.17), channel_id=1, source_target_pairs={{0,1},{1,0},{2,3},{3,2},{4,5},{5,4},{6,7},{7,6},{8,9},{9,8},{10,11... | collective-permute-start | bytes 921608 | tf_op jit(solution)/shard_map/ppermute | solution.py:100

commit v14 on v12

--- a/solution.py
+++ b/solution.py
@@ -112,7 +112,13 @@
     shifted = gain * linear_scores + shift
     sig = jax.nn.sigmoid(shifted)
     active = shifted * sig
-    image_sum = jnp.dot(select, active, precision=HIGHEST, preferred_element_type=jnp.float32)
+    active_hi = lax.reduce_precision(active, exponent_bits=8, mantissa_bits=7)
+    pieces = jnp.concatenate(
+        [active_hi.astype(jnp.bfloat16), (active - active_hi).astype(jnp.bfloat16)], axis=0
+    )
+    image_sum = jnp.dot(
+        jnp.concatenate([select.astype(jnp.bfloat16)] * 2, axis=1), pieces, preferred_element_type=jnp.float32
+    )
     embedded = (image_sum / P_SIZE).astype(jnp.bfloat16)
     grouped = doubling_gather(embedded, "leaf")
     group = grouped.shape[0]

time: 117 us -> 118 us (level)
    dot_general x1, matrix products: 5.63 us -> 1.59 us  [shards(): jnp.dot(jnp.concatenate([select.astype(jnp.bfloat16)] * 2, axis=1), piece...]
    dot_general x1, matrix products: 4.5 us -> 8.43 us  [shards(): jnp.dot(features, head_weight, preferred_element_type=jnp.float32)]
    unnamed x44 -> x36, local copies, waits for them, and re-layouts: 5.53 us -> 6.11 us
where the time goes in v14:
time: 118 us; the launch traced here: 116 us
  waiting for transfers between devices  33.2 us (28%)
  matrix products  27.5 us (23%)
  starting transfers between devices  20.4 us (17%)
  local copies, waits for them, and re-layouts  17.1 us (14%)
  other arithmetic  16.5 us (14%)
    ppermute x3, waiting for transfers between devices, halving_scatter(): got = lax.ppermute(tuple(give), name, partners(size, bit))  25 us
    dot_general x1, matrix products, shards(): jnp.dot(features, head_weight, preferred_element_type=jnp.float32)  8.43 us
    dot_general x1, matrix products, shards(): jnp.dot(jnp.concatenate([select.T.astype(jnp.bfloat16)] * 3, axis=1), jnp...  8.15 us
    unnamed x36, local copies, waits for them, and re-layouts  6.11 us
    ppermute x3, starting transfers between devices, halving_scatter(): got = lax.ppermute(tuple(give), name, partners(size, bit))  5.37 us
    ppermute x2, starting transfers between devices, doubling_gather(): other = lax.ppermute(cur, name, partners(size, bit))  4.54 us
    dot_general x1, matrix products, shards(): lax.dot_general(lin_grad, features, (((0,), (0,)), ((), ())), preferred_e...  4.49 us
    all_to_all x1, starting transfers between devices, shards(): recv = lax.all_to_all(send, 'dp', split_axis=0, concat_axis=0, tiled=True)  4.09 us
  transfers between devices with their start and end apart: 11, of which 9 were waited for; matrix products, arithmetic and copies ran while one was open for 16% of the time, Pallas kernels for 0%

profile of v14, /device:TPU:0, one launch (start us, length us, event | category | flops | bytes accessed | tf_op | source)
XLA Modules:
  0.0 115.9 jit_solution(14966466120780780981)
XLA Ops:
  1.3 8.4 %reduce-precision_convert_fusion = (bf16[1600,1536]{1,0:T(8,128)(2,1)S(1)}, bf16[1600,1536]{1,0:T(8,128)(2,1)S(1)}, f32[1600,1536]{1,0:T(8,128)}) fusion(f32[1536]{0:T(1024)} %param.11, f32[1536]{0:T(1024)} %param.10, bf16[1600,384]{1,0:T(8,128)(2,1)} %param.8, bf16[384,1536]{1,0:T(8,128)(2,1)} %param.9), kind=kOutput, calls=%fused_computation.2 | convolution fusion | flops 1912012800 | bytes 22081536 | tf_op jit(solution)/shard_map/dot_general | solution.py:111
  9.7 1.6 %fusion.16 = bf16[1,16,1536]{2,1,0:T(8,128)(2,1)S(1)} fusion(bf16[1600,1536]{1,0:T(8,128)(2,1)S(1)} %get-tuple-element.17, bf16[1600,1536]{1,0:T(8,128)(2,1)S(1)} %get-tuple-element.16, bf16[16,1600]{1,0:T(8,128)(2,1)S(1)} %convert_convert_fusion), kind=kOutput, calls=%fused_computation.24 | convolution fusion | flops 177201152 | bytes 9930752 | tf_op jit(solution)/shard_map/dot_general | solution.py:119
  11.3 3.0 %collective-permute-start = (bf16[1,16,1536]{2,1,0:T(8,128)(2,1)S(1)}, bf16[1,16,1536]{2,1,0:T(8,128)(2,1)S(1)}, u32[]{:S(2)}, u32[]{:S(2)}) collective-permute-start(bf16[1,16,1536]{2,1,0:T(8,128)(2,1)S(1)} %fusion.16), channel_id=1, source_target_pairs={{0,1},{1,0},{2,3},{3,2},{4,5},{5,4},{6,7},{7,6},{8,9},{9,8},{10,11... | collective-permute-start | bytes 147464 | tf_op jit(solution)/shard_map/ppermute | solution.py:52
  16.0 1.1 fusion.20
  18.2 1.6 %collective-permute-start.1 = (bf16[2,16,1536]{2,1,0:T(8,128)(2,1)S(1)}, bf16[2,16,1536]{2,1,0:T(8,128)(2,1)S(1)}, u32[]{:S(2)}, u32[]{:S(2)}) collective-permute-start(bf16[2,16,1536]{2,1,0:T(8,128)(2,1)S(1)} %maximum_select_fusion.1), channel_id=1, source_target_pairs={{0,2},{1,3},{2,0},{3,1},{4,6},{5,7},{6,4},{7,5},{8,10},{9,11},{10,... | collective-permute-start | bytes 294920 | tf_op jit(solution)/shard_map/ppermute | solution.py:52
  20.4 2.5 %collective-permute-done.1 = bf16[2,16,1536]{2,1,0:T(8,128)(2,1)S(1)} collective-permute-done((bf16[2,16,1536]{2,1,0:T(8,128)(2,1)S(1)}, bf16[2,16,1536]{2,1,0:T(8,128)(2,1)S(1)}, u32[]{:S(2)}, u32[]{:S(2)}) %collective-permute-start.1) | collective-permute-done | bytes 98336 | tf_op jit(solution)/shard_map/ppermute | solution.py:52
  22.9 1.8 %select_reduce_fusion = (f32[64,64]{1,0:T(8,128)S(1)}, f32[64,64]{1,0:T(8,128)S(1)}) fusion(pred[64,16]{0,1:T(8,128)(4,1)S(1)} %iota_compare_fusion.7, pred[64,16]{0,1:T(8,128)(4,1)S(1)} %iota_compare_fusion.8, bf16[64,1536,1]{1,0,2:T(8,128)(2,1)S(1)} %bitcast.85, bf16[16,64,1536]{2,1,0:T(8,128)(2,1)S(1)} %bitcast.73), kind=kOutput, calls=%fused_computation.38 | convolution fusion | flops 201580544 | bytes 3377152 | tf_op jit(solution)/shard_map/dot_general | solution.py:137
  26.7 1.7 %fusion.8 = f32[4,16,1536]{2,1,0:T(8,128)S(1)} fusion(bf16[1024,1536]{1,0:T(8,128)(2,1)S(1)} %copy-done, bf16[4,16,1024]{2,1,0:T(8,128)(2,1)} %tile.13, bf16[4,16,1024]{2,1,0:T(8,128)(2,1)} %tile.15, s32[4,16]{1,0:T(4,128)} %get-tuple-element.34, s32[4,16]{1,0:T(4,128)} %get-tuple-element.33, s32[1024]{0:T(1024)} %add_select_fusion.8), kind=kOutput, calls=%fused_computation.18 | convolution fusion | flops 201654272 | bytes 3805696 | tf_op jit(solution)/shard_map/dot_general | solution.py:147
  29.1 1.5 %collective-permute-start.4 = (f32[16,1536]{1,0:T(8,128)}, f32[16,1536]{1,0:T(8,128)}, u32[]{:S(2)}, u32[]{:S(2)}) collective-permute-start(f32[16,1536]{1,0:T(8,128)} %get-tuple-element.19), channel_id=1, source_target_pairs={{0,3},{1,2},{2,1},{3,0},{4,7},{5,6},{6,5},{7,4},{8,11},{9,10},{10,... | collective-permute-start | bytes 294920 | tf_op jit(solution)/shard_map/ppermute | solution.py:93
  30.7 1.9 %collective-permute-start.2 = (f32[16,1536]{1,0:T(8,128)}, f32[16,1536]{1,0:T(8,128)}, u32[]{:S(2)}, u32[]{:S(2)}) collective-permute-start(f32[16,1536]{1,0:T(8,128)} %get-tuple-element.18), channel_id=1, source_target_pairs={{0,1},{1,0},{2,3},{3,2},{4,5},{5,4},{6,7},{7,6},{8,9},{9,8},{10,11... | collective-permute-start | bytes 294920 | tf_op jit(solution)/shard_map/ppermute | solution.py:93
  32.6 1.3 %convert_convert_fusion.1 = bf16[1600,16]{0,1:T(8,128)(2,1)} fusion(s32[1600]{0:T(1024)} %copy-done.6), kind=kLoop, calls=%fused_computation.72 | loop fusion | flops 76800 | bytes 57600 | tf_op jit(solution)/shard_map/convert_element_type | solution.py:180
  37.2 8.1 %multiply_reduce_fusion = (f32[1536]{0:T(1024)S(1)}, f32[1536]{0:T(1024)S(1)}, f32[1600,1536]{1,0:T(8,128)S(1)}) fusion(f32[1600,1536]{1,0:T(8,128)} %get-tuple-element.31, f32[1536]{0:T(1024)} %param.11, f32[1536]{0:T(1024)} %param.10, bf16[16,1536]{1,0:T(8,128)(2,1)S(1)} %get-tuple-element.26, bf16[16,1536]{1,0:T(8,128)(2,1)S(1)} %get-tuple-element.25, ...), kind=kOutput, calls=%fused_computation.8 | convolution fusion | flops 268778496 | bytes 19884032 | tf_op jit(solution)/shard_map/dot_general | solution.py:179
  45.4 4.5 %fusion.6 = f32[1536,384]{1,0:T(8,128)} fusion(bf16[1600,384]{1,0:T(8,128)(2,1)S(1)} %copy-done.13, f32[1600,1536]{1,0:T(8,128)S(1)} %get-tuple-element.32, f32[1536]{0:T(1024)S(1)} %copy-done.14), kind=kOutput, calls=%fused_computation.14 | convolution fusion | flops 1892352000 | bytes 13424640 | tf_op jit(solution)/shard_map/dot_general | solution.py:186
  50.1 2.4 %fusion.22 = f32[4,1,200,384]{3,2,0,1:T(8,128)} fusion(s32[]{:T(128)S(6)} %select_n.414, f32[4,2,1,192,384]{4,3,1,0,2:T(8,128)} %bitcast.74, f32[4,2,1,8,384]{4,3,1,0,2:T(8,128)S(1)} %bitcast.83), kind=kLoop, calls=%fused_computation.31 | loop fusion | flops 307200 | bytes 3686404 | tf_op jit(solution)/shard_map/jit(dynamic_index_in_dim)/squeeze | solution.py:68
  52.6 3.3 %collective-permute-done.5 = f32[4,1,200,384]{3,2,0,1:T(8,128)} collective-permute-done((f32[4,1,200,384]{3,2,0,1:T(8,128)}, f32[4,1,200,384]{3,2,0,1:T(8,128)}, u32[]{:S(2)}, u32[]{:S(2)}) %collective-permute-start.5) | collective-permute-done | bytes 1228832 | tf_op jit(solution)/shard_map/ppermute | solution.py:69
  55.8 1.8 %fusion.25 = f32[4,1,200,384]{3,2,0,1:T(8,128)S(1)} fusion(f32[4,1,200,384]{3,2,0,1:T(8,128)} %collective-permute-done.5, s32[]{:T(128)S(6)} %select_n.413, f32[4,2,1,192,384]{4,3,1,0,2:T(8,128)} %bitcast.75, f32[4,2,1,8,384]{4,3,1,0,2:T(8,128)S(1)} %bitcast.84), kind=kLoop, calls=%fused_computation.34 | loop fusion | flops 614400 | bytes 4915204 | tf_op jit(solution)/shard_map/add | solution.py:70
  59.5 1.6 %collective-permute-start.6 = (f32[2,1,200,384]{3,2,1,0:T(8,128)}, f32[2,1,200,384]{3,2,1,0:T(8,128)}, u32[]{:S(2)}, u32[]{:S(2)}) collective-permute-start(f32[2,1,200,384]{3,2,1,0:T(8,128)} %dynamic-slice_bitcast_fusion), channel_id=1, source_target_pairs={{0,8},{4,12},{8,0},{12,4},{16,24},{20,28},{24,16},{28,20},{1,9},{5... | collective-permute-start | bytes 1843208 | tf_op jit(solution)/shard_map/ppermute | solution.py:69
  61.4 1.2 %select_n.424 = bf16[64,8,192]{2,1,0:T(8,128)(2,1)S(1)} reshape(bf16[4,16,1536]{2,1,0:T(8,128)(2,1)} %copy-done.3) | data formatting | bytes 393216 | tf_op jit(solution)/shard_map/jit(_where)/select_n | solution.py:54
  63.6 4.1 %all-to-all-start = ((bf16[8,64,322]{2,1,0:T(8,128)(2,1)}), bf16[8,64,322]{2,1,0:T(8,128)(2,1)}, u32[]{:S(2)}, u32[]{:S(2)}) async-start(bf16[8,64,322]{2,1,0:T(8,128)(2,1)} %pad_maximum_fusion), calls=%async_computation | async-start | bytes 786432 | tf_op jit(solution)/shard_map/all_to_all | solution.py:167
  67.7 10.9 %collective-permute-done.6 = f32[2,1,200,384]{3,2,1,0:T(8,128)} collective-permute-done((f32[2,1,200,384]{3,2,1,0:T(8,128)}, f32[2,1,200,384]{3,2,1,0:T(8,128)}, u32[]{:S(2)}, u32[]{:S(2)}) %collective-permute-start.6) | collective-permute-done | bytes 614432 | tf_op jit(solution)/shard_map/ppermute | solution.py:69
  78.6 1.3 %bitcast_add_fusion = f32[2,1,200,384]{3,2,1,0:T(8,128)S(1)} fusion(f32[2,1,200,384]{3,2,1,0:T(8,128)} %collective-permute-done.6, f32[2,2,1,200,384]{4,3,1,0,2:T(8,128)} %bitcast.77, s32[]{:T(128)S(6)} %select_n.417), kind=kLoop, calls=%fused_computation.36 | loop fusion | flops 153600 | bytes 1843204 | tf_op jit(solution)/shard_map/add | solution.py:70
  81.5 3.8 %collective-permute-start.7 = (f32[1,1,200,384]{3,2,1,0:T(8,128)}, f32[1,1,200,384]{3,2,1,0:T(8,128)}, u32[]{:S(2)}, u32[]{:S(2)}) collective-permute-start(f32[1,1,200,384]{3,2,1,0:T(8,128)} %constant_dynamic-slice_fusion), channel_id=1, source_target_pairs={{0,16},{4,20},{8,24},{12,28},{16,0},{20,4},{24,8},{28,12},{1,17},{... | collective-permute-start | bytes 921608 | tf_op jit(solution)/shard_map/ppermute | solution.py:69
  85.3 1.1 slice.74
  86.4 10.8 %collective-permute-done.7 = f32[1,1,200,384]{3,2,1,0:T(8,128)} collective-permute-done((f32[1,1,200,384]{3,2,1,0:T(8,128)}, f32[1,1,200,384]{3,2,1,0:T(8,128)}, u32[]{:S(2)}, u32[]{:S(2)}) %collective-permute-start.7) | collective-permute-done | bytes 307232 | tf_op jit(solution)/shard_map/ppermute | solution.py:69
  97.2 1.8 %add_bitcast_fusion = f32[200,384]{1,0:T(8,128)} fusion(f32[1,1,200,384]{3,2,1,0:T(8,128)} %collective-permute-done.7, f32[2,1,200,384]{3,2,1,0:T(8,128)} %copy-done.2, s32[]{:T(128)S(6)} %select_n.421), kind=kLoop, calls=%fused_computation.44 | loop fusion | flops 76800 | bytes 921604 | tf_op jit(solution)/shard_map/squeeze;reshape | solution.py:203
  99.1 1.4 %collective-permute-start.8 = (f32[200,384]{1,0:T(8,128)}, f32[200,384]{1,0:T(8,128)}, u32[]{:S(2)}, u32[]{:S(2)}) collective-permute-start(f32[200,384]{1,0:T(8,128)} %add_bitcast_fusion), channel_id=1, source_target_pairs={{0,1},{1,0},{2,3},{3,2},{4,5},{5,4},{6,7},{7,6},{8,9},{9,8},{10,11... | collective-permute-start | bytes 921608 | tf_op jit(solution)/shard_map/ppermute | solution.py:80
  102.4 1.1 copy.62
  105.3 1.2 %collective-permute-done.8 = f32[200,384]{1,0:T(8,128)} collective-permute-done((f32[200,384]{1,0:T(8,128)}, f32[200,384]{1,0:T(8,128)}, u32[]{:S(2)}, u32[]{:S(2)}) %collective-permute-start.8) | collective-permute-done | bytes 307232 | tf_op jit(solution)/shard_map/ppermute | solution.py:80
  106.5 1.1 add.290
  107.6 1.5 %collective-permute-start.9 = (f32[200,384]{1,0:T(8,128)S(1)}, f32[200,384]{1,0:T(8,128)S(1)}, u32[]{:S(2)}, u32[]{:S(2)}) collective-permute-start(f32[200,384]{1,0:T(8,128)S(1)} %add.290), channel_id=1, source_target_pairs={{0,2},{1,3},{2,0},{3,1},{4,6},{5,7},{6,4},{7,5},{8,10},{9,11},{10,... | collective-permute-start | bytes 921608 | tf_op jit(solution)/shard_map/ppermute | solution.py:80
  110.7 1.4 %fusion.85 = f32[1024,192]{0,1:T(8,128)} fusion(bf16[512,1024]{0,1:T(8,128)(2,1)S(1)} %bitcast.78, bf16[512,192]{1,0:T(8,128)(2,1)S(1)} %bitcast.82), kind=kOutput, calls=%fused_computation.198 | convolution fusion | flops 201326592 | bytes 2031616 | tf_op jit(solution)/shard_map/dot_general | solution.py:175
  112.1 2.5 %collective-permute-done.9 = f32[200,384]{1,0:T(8,128)S(1)} collective-permute-done((f32[200,384]{1,0:T(8,128)S(1)}, f32[200,384]{1,0:T(8,128)S(1)}, u32[]{:S(2)}, u32[]{:S(2)}) %collective-permute-start.9) | collective-permute-done | bytes 307232 | tf_op jit(solution)/shard_map/ppermute | solution.py:80
  (101 shorter events, 21.7 us)
Async XLA Ops:
  0.6 22.3 %copy-start = (bf16[1024,1536]{1,0:T(8,128)(2,1)S(1)}, bf16[1024,1536]{1,0:T(8,128)(2,1)}, u32[]{:S(2)}) copy-start(bf16[1024,1536]{1,0:T(8,128)(2,1)} %param.12) | copy-start | bytes 9437188
  0.7 0.6 copy-start.6
  9.7 4.6 %copy-start.7 = (s32[64,64]{1,0:T(8,128)S(1)}, s32[64,64]{1,0:T(8,128)}, u32[]{:S(2)}) copy-start(s32[64,64]{1,0:T(8,128)} %param.14) | copy-start | bytes 49156
  9.7 5.3 %copy-start.12 = (s32[64]{0:T(128)S(1)}, s32[64]{0:T(128)}, u32[]{:S(2)}) copy-start(s32[64]{0:T(128)} %param.13) | copy-start | bytes 772
  11.3 6.9 %collective-permute-start = (bf16[1,16,1536]{2,1,0:T(8,128)(2,1)S(1)}, bf16[1,16,1536]{2,1,0:T(8,128)(2,1)S(1)}, u32[]{:S(2)}, u32[]{:S(2)}) collective-permute-start(bf16[1,16,1536]{2,1,0:T(8,128)(2,1)S(1)} %fusion.16), channel_id=1, source_target_pairs={{0,1},{1,0},{2,3},{3,2},{4,5},{5,4},{6,7},{7,6},{8,9},{9,8},{10,11... | collective-permute-start | bytes 147464 | tf_op jit(solution)/shard_map/ppermute | solution.py:52
  15.1 0.5 copy-start.8
  15.1 0.5 copy-start.10
  18.2 4.7 %collective-permute-start.1 = (bf16[2,16,1536]{2,1,0:T(8,128)(2,1)S(1)}, bf16[2,16,1536]{2,1,0:T(8,128)(2,1)S(1)}, u32[]{:S(2)}, u32[]{:S(2)}) collective-permute-start(bf16[2,16,1536]{2,1,0:T(8,128)(2,1)S(1)} %maximum_select_fusion.1), channel_id=1, source_target_pairs={{0,2},{1,3},{2,0},{3,1},{4,6},{5,7},{6,4},{7,5},{8,10},{9,11},{10,... | collective-permute-start | bytes 294920 | tf_op jit(solution)/shard_map/ppermute | solution.py:52
  22.9 1.8 %copy-start.3 = (bf16[4,16,1536]{2,1,0:T(8,128)(2,1)}, bf16[4,16,1536]{2,1,0:T(8,128)(2,1)S(1)}, u32[]{:S(2)}) copy-start(bf16[4,16,1536]{2,1,0:T(8,128)(2,1)S(1)} %maximum_select_fusion) | copy-start | bytes 589828
  25.8 0.9 copy-start.4
  29.1 5.9 %collective-permute-start.4 = (f32[16,1536]{1,0:T(8,128)}, f32[16,1536]{1,0:T(8,128)}, u32[]{:S(2)}, u32[]{:S(2)}) collective-permute-start(f32[16,1536]{1,0:T(8,128)} %get-tuple-element.19), channel_id=1, source_target_pairs={{0,3},{1,2},{2,1},{3,0},{4,7},{5,6},{6,5},{7,4},{8,11},{9,10},{10,... | collective-permute-start | bytes 294920 | tf_op jit(solution)/shard_map/ppermute | solution.py:93
  30.6 5.4 %collective-permute-start.3 = (f32[16,1536]{1,0:T(8,128)}, f32[16,1536]{1,0:T(8,128)}, u32[]{:S(2)}, u32[]{:S(2)}) collective-permute-start(f32[16,1536]{1,0:T(8,128)} %get-tuple-element.20), channel_id=1, source_target_pairs={{0,2},{1,3},{2,0},{3,1},{4,6},{5,7},{6,4},{7,5},{8,10},{9,11},{10,... | collective-permute-start | bytes 294920 | tf_op jit(solution)/shard_map/ppermute | solution.py:93
  30.7 5.4 %collective-permute-start.2 = (f32[16,1536]{1,0:T(8,128)}, f32[16,1536]{1,0:T(8,128)}, u32[]{:S(2)}, u32[]{:S(2)}) collective-permute-start(f32[16,1536]{1,0:T(8,128)} %get-tuple-element.18), channel_id=1, source_target_pairs={{0,1},{1,0},{2,3},{3,2},{4,5},{5,4},{6,7},{7,6},{8,9},{9,8},{10,11... | collective-permute-start | bytes 294920 | tf_op jit(solution)/shard_map/ppermute | solution.py:93
  37.2 8.2 %copy-start.13 = (bf16[1600,384]{1,0:T(8,128)(2,1)S(1)}, bf16[1600,384]{1,0:T(8,128)(2,1)}, u32[]{:S(2)}) copy-start(bf16[1600,384]{1,0:T(8,128)(2,1)} %param.8) | copy-start | bytes 3686404
  37.2 8.2 %copy-start.14 = (f32[1536]{0:T(1024)S(1)}, f32[1536]{0:T(1024)}, u32[]{:S(2)}) copy-start(f32[1536]{0:T(1024)} %param.10) | copy-start | bytes 18436
  50.1 11.0 %copy-start.11 = (s32[64]{0:T(128)S(1)}, s32[64]{0:T(128)}, u32[]{:S(2)}) copy-start(s32[64]{0:T(128)} %copy-done.10) | copy-start | bytes 772
  50.1 11.1 %copy-start.9 = (s32[64]{0:T(128)S(1)}, s32[64]{0:T(128)}, u32[]{:S(2)}) copy-start(s32[64]{0:T(128)} %copy-done.8) | copy-start | bytes 772
  50.1 12.5 %copy-start.5 = (bf16[64,64]{1,0:T(8,128)(2,1)S(1)}, bf16[64,64]{1,0:T(8,128)(2,1)}, u32[]{:S(2)}) copy-start(bf16[64,64]{1,0:T(8,128)(2,1)} %copy-done.4) | copy-start | bytes 24580
  52.6 3.3 %collective-permute-start.5 = (f32[4,1,200,384]{3,2,0,1:T(8,128)}, f32[4,1,200,384]{3,2,0,1:T(8,128)}, u32[]{:S(2)}, u32[]{:S(2)}) collective-permute-start(f32[4,1,200,384]{3,2,0,1:T(8,128)} %fusion.22), channel_id=1, source_target_pairs={{0,4},{4,0},{8,12},{12,8},{16,20},{20,16},{24,28},{28,24},{1,5},{5... | collective-permute-start | bytes 3686408 | tf_op jit(solution)/shard_map/ppermute | solution.py:69
  57.6 1.1 copy-start.1
  59.5 19.1 %collective-permute-start.6 = (f32[2,1,200,384]{3,2,1,0:T(8,128)}, f32[2,1,200,384]{3,2,1,0:T(8,128)}, u32[]{:S(2)}, u32[]{:S(2)}) collective-permute-start(f32[2,1,200,384]{3,2,1,0:T(8,128)} %dynamic-slice_bitcast_fusion), channel_id=1, source_target_pairs={{0,8},{4,12},{8,0},{12,4},{16,24},{20,28},{24,16},{28,20},{1,9},{5... | collective-permute-start | bytes 1843208 | tf_op jit(solution)/shard_map/ppermute | solution.py:69
  63.6 21.7 %all-to-all-start = ((bf16[8,64,322]{2,1,0:T(8,128)(2,1)}), bf16[8,64,322]{2,1,0:T(8,128)(2,1)}, u32[]{:S(2)}, u32[]{:S(2)}) async-start(bf16[8,64,322]{2,1,0:T(8,128)(2,1)} %pad_maximum_fusion), calls=%async_computation | async-start | bytes 786432 | tf_op jit(solution)/shard_map/all_to_all | solution.py:167
  80.0 0.8 copy-start.2
  81.5 15.7 %collective-permute-start.7 = (f32[1,1,200,384]{3,2,1,0:T(8,128)}, f32[1,1,200,384]{3,2,1,0:T(8,128)}, u32[]{:S(2)}, u32[]{:S(2)}) collective-permute-start(f32[1,1,200,384]{3,2,1,0:T(8,128)} %constant_dynamic-slice_fusion), channel_id=1, source_target_pairs={{0,16},{4,20},{8,24},{12,28},{16,0},{20,4},{24,8},{28,12},{1,17},{... | collective-permute-start | bytes 921608 | tf_op jit(solution)/shard_map/ppermute | solution.py:69
  99.1 7.4 %collective-permute-start.8 = (f32[200,384]{1,0:T(8,128)}, f32[200,384]{1,0:T(8,128)}, u32[]{:S(2)}, u32[]{:S(2)}) collective-permute-start(f32[200,384]{1,0:T(8,128)} %add_bitcast_fusion), channel_id=1, source_target_pairs={{0,1},{1,0},{2,3},{3,2},{4,5},{5,4},{6,7},{7,6},{8,9},{9,8},{10,11... | collective-permute-start | bytes 921608 | tf_op jit(solution)/shard_map/ppermute | solution.py:80
  107.6 6.9 %collective-permute-start.9 = (f32[200,384]{1,0:T(8,128)S(1)}, f32[200,384]{1,0:T(8,128)S(1)}, u32[]{:S(2)}, u32[]{:S(2)}) collective-permute-start(f32[200,384]{1,0:T(8,128)S(1)} %add.290), channel_id=1, source_target_pairs={{0,2},{1,3},{2,0},{3,1},{4,6},{5,7},{6,4},{7,5},{8,10},{9,11},{10,... | collective-permute-start | bytes 921608 | tf_op jit(solution)/shard_map/ppermute | solution.py:80

commit v15 on v12

--- a/solution.py
+++ b/solution.py
@@ -158,6 +158,31 @@
     send = jnp.concatenate(
         [column_chunks, jnp.broadcast_to(compact[None], (n_dp,) + compact.shape)], axis=2
     )
+    spread = jnp.dot(
+        jnp.concatenate([select.T.astype(jnp.bfloat16)] * 3, axis=1),
+        jnp.concatenate(split3(emb_grad / P_SIZE), axis=0),
+        preferred_element_type=jnp.float32,
+    )
+    pixel_gradient = spread * (sig * (1.0 + shifted * (1.0 - sig)))
+    lin_grad = (pixel_gradient * gain).astype(jnp.bfloat16)
+    head_term = lax.dot_general(
+        lin_grad, features, (((0,), (0,)), ((), ())), preferred_element_type=jnp.float32
+    )
+    gain_term = jnp.sum(pixel_gradient * linear_scores, axis=0)
+    shift_term = jnp.sum(pixel_gradient, axis=0)
+    e_size = head_term.shape[1]
+    chunk = width // n_dp
+    extra = -(-2 * chunk // e_size)
+    pad_rows = -(-extra // 8) * 8
+    side_rows = jnp.concatenate(
+        [gain_term.reshape(n_dp, chunk), shift_term.reshape(n_dp, chunk)], axis=1
+    )
+    side_rows = jnp.pad(side_rows, ((0, 0), (0, pad_rows * e_size - 2 * chunk)))
+    stacked = jnp.concatenate(
+        [head_term.reshape(n_dp, chunk, e_size), side_rows.reshape(n_dp, pad_rows, e_size)], axis=1
+    )
+    (part,) = halving_scatter([stacked], "dp")
+    send, part = lax.optimization_barrier((send, part))
     recv = lax.all_to_all(send, "dp", split_axis=0, concat_axis=0, tiled=True)
     columns = recv[:, :, :col_width].reshape(n_dp * group, col_width)
     info = recv[:, :, col_width:].reshape(n_dp * group, compact.shape[1])
@@ -170,30 +195,6 @@
         all_table, columns, (((0,), (0,)), ((), ())), preferred_element_type=jnp.float32
     )
 
-    spread = jnp.dot(
-        jnp.concatenate([select.T.astype(jnp.bfloat16)] * 3, axis=1),
-        jnp.concatenate(split3(emb_grad / P_SIZE), axis=0),
-        preferred_element_type=jnp.float32,
-    )
-    pixel_gradient = spread * (sig * (1.0 + shifted * (1.0 - sig)))
-    lin_grad = (pixel_gradient * gain).astype(jnp.bfloat16)
-    head_term = lax.dot_general(
-        lin_grad, features, (((0,), (0,)), ((), ())), preferred_element_type=jnp.float32
-    )
-    gain_term = jnp.sum(pixel_gradient * linear_scores, axis=0)
-    shift_term = jnp.sum(pixel_gradient, axis=0)
-    e_size = head_term.shape[1]
-    chunk = width // n_dp
-    extra = -(-2 * chunk // e_size)
-    pad_rows = -(-extra // 8) * 8
-    side_rows = jnp.concatenate(
-        [gain_term.reshape(n_dp, chunk), shift_term.reshape(n_dp, chunk)], axis=1
-    )
-    side_rows = jnp.pad(side_rows, ((0, 0), (0, pad_rows * e_size - 2 * chunk)))
-    stacked = jnp.concatenate(
-        [head_term.reshape(n_dp, chunk, e_size), side_rows.reshape(n_dp, pad_rows, e_size)], axis=1
-    )
-    (part,) = halving_scatter([stacked], "dp")
     (total,) = butterfly_sum([part[0]], "leaf")
     side_flat = total[chunk:].reshape(-1)
     side_sum = jnp.stack([side_flat[:chunk], side_flat[chunk : 2 * chunk]], axis=1)

time: 117 us -> 132 us (1.13)
  waiting for transfers between devices: 34 us -> 44.1 us
  matrix products: 27.7 us -> 31.9 us
  local copies, waits for them, and re-layouts: 16.5 us -> 18.2 us
  starting transfers between devices: 20.5 us -> 19 us
  other arithmetic: 15.7 us -> 17.1 us
    ppermute x2, waiting for transfers between devices: 3.66 us -> 8.38 us  [butterfly_sum(): got = lax.ppermute(cur, name, partners(size, bit))]
    ppermute x3, waiting for transfers between devices: 25 us -> 29 us  [halving_scatter(): got = lax.ppermute(tuple(give), name, partners(size, bit))]
    unnamed x44, local copies, waits for them, and re-layouts: 5.53 us -> 9.1 us
    dot_general x1, matrix products: 8.21 us -> 10.8 us  [shards(): jnp.dot(jnp.concatenate([select.T.astype(jnp.bfloat16)] * 3, axis=1), jnp...]
    reshape x0 -> x1, other arithmetic: none -> 1.83 us  [halving_scatter(): return [c.reshape(c.shape[1:]) for c in cur]]
    another operation x1 -> x0, other arithmetic: 1.8 us -> none  [shards(): total, = butterfly_sum([part[0]], 'leaf')]
    add x2, other arithmetic: 1.13 us -> 2.83 us  [butterfly_sum(): cur = tuple((c + g for c, g in zip(cur, got)))]
    dot_general x1, matrix products: 4.48 us -> 6 us  [shards(): lax.dot_general(lin_grad, features, (((0,), (0,)), ((), ())), preferred_e...]
  transfers between devices with their start and end apart: 11 -> 11, of which waited for: 9 -> 9; matrix products, arithmetic and copies ran while one was open for 16% -> 14% of each run, Pallas kernels for 0% -> 0%
where the time goes in v15:
time: 132 us; the launch traced here: 131 us
  waiting for transfers between devices  44.1 us (33%)
  matrix products  31.9 us (24%)
  starting transfers between devices  19 us (14%)
  local copies, waits for them, and re-layouts  18.2 us (14%)
  other arithmetic  17.1 us (13%)
    ppermute x3, waiting for transfers between devices, halving_scatter(): got = lax.ppermute(tuple(give), name, partners(size, bit))  29 us
    dot_general x1, matrix products, shards(): jnp.dot(jnp.concatenate([select.T.astype(jnp.bfloat16)] * 3, axis=1), jnp...  10.8 us
    unnamed x44, local copies, waits for them, and re-layouts  9.1 us
    ppermute x2, waiting for transfers between devices, butterfly_sum(): got = lax.ppermute(cur, name, partners(size, bit))  8.38 us
    dot_general x1, matrix products, shards(): lax.dot_general(lin_grad, features, (((0,), (0,)), ((), ())), preferred_e...  6 us
    dot_general x1, matrix products, shards(): jnp.dot(select, active, precision=HIGHEST, preferred_element_type=jnp.flo...  5.63 us
    all_to_all x1, starting transfers between devices, shards(): recv = lax.all_to_all(send, 'dp', split_axis=0, concat_axis=0, tiled=True)  4.76 us
    ppermute x2, starting transfers between devices, doubling_gather(): other = lax.ppermute(cur, name, partners(size, bit))  4.59 us
  transfers between devices with their start and end apart: 11, of which 9 were waited for; matrix products, arithmetic and copies ran while one was open for 14% of the time, Pallas kernels for 0%

profile of v15, /device:TPU:0, one launch (start us, length us, event | category | flops | bytes accessed | tf_op | source)
XLA Modules:
  0.0 131.4 jit_solution(4929130194522168067)
XLA Ops:
  0.7 4.5 %fusion.82 = f32[1600,1536]{1,0:T(8,128)S(1)} fusion(bf16[1600,384]{1,0:T(8,128)(2,1)} %param.8, bf16[384,1536]{1,0:T(8,128)(2,1)} %param.9), kind=kOutput, calls=%fused_computation.193 | convolution fusion | flops 1887436800 | bytes 12238848 | tf_op jit(solution)/shard_map/dot_general | solution.py:111
  5.3 5.6 %fusion.15 = bf16[1,16,1536]{2,1,0:T(8,128)(2,1)S(1)} fusion(f32[1600,1536]{1,0:T(8,128)S(1)} %fusion.82, f32[1536]{0:T(1024)S(1)} %copy-done.16, f32[1536]{0:T(1024)S(1)} %copy-done.17, s32[1600]{0:T(1024)S(1)} %add_select_fusion.7), kind=kOutput, calls=%fused_computation.21 | convolution fusion | flops 486679552 | bytes 9898240 | tf_op jit(solution)/shard_map/dot_general | solution.py:115
  10.9 3.0 %collective-permute-start = (bf16[1,16,1536]{2,1,0:T(8,128)(2,1)S(1)}, bf16[1,16,1536]{2,1,0:T(8,128)(2,1)S(1)}, u32[]{:S(2)}, u32[]{:S(2)}) collective-permute-start(bf16[1,16,1536]{2,1,0:T(8,128)(2,1)S(1)} %fusion.15), channel_id=1, source_target_pairs={{0,1},{1,0},{2,3},{3,2},{4,5},{5,4},{6,7},{7,6},{8,9},{9,8},{10,11... | collective-permute-start | bytes 147464 | tf_op jit(solution)/shard_map/ppermute | solution.py:52
  15.7 1.1 fusion.19
  17.9 1.6 %collective-permute-start.1 = (bf16[2,16,1536]{2,1,0:T(8,128)(2,1)S(1)}, bf16[2,16,1536]{2,1,0:T(8,128)(2,1)S(1)}, u32[]{:S(2)}, u32[]{:S(2)}) collective-permute-start(bf16[2,16,1536]{2,1,0:T(8,128)(2,1)S(1)} %maximum_select_fusion.1), channel_id=1, source_target_pairs={{0,2},{1,3},{2,0},{3,1},{4,6},{5,7},{6,4},{7,5},{8,10},{9,11},{10,... | collective-permute-start | bytes 294920 | tf_op jit(solution)/shard_map/ppermute | solution.py:52
  20.1 2.5 %collective-permute-done.1 = bf16[2,16,1536]{2,1,0:T(8,128)(2,1)S(1)} collective-permute-done((bf16[2,16,1536]{2,1,0:T(8,128)(2,1)S(1)}, bf16[2,16,1536]{2,1,0:T(8,128)(2,1)S(1)}, u32[]{:S(2)}, u32[]{:S(2)}) %collective-permute-start.1) | collective-permute-done | bytes 98336 | tf_op jit(solution)/shard_map/ppermute | solution.py:52
  22.6 1.8 %select_reduce_fusion.1 = (f32[64,64]{1,0:T(8,128)S(1)}, f32[64,64]{1,0:T(8,128)S(1)}) fusion(pred[64,16]{0,1:T(8,128)(4,1)S(1)} %iota_compare_fusion.9, pred[64,16]{0,1:T(8,128)(4,1)S(1)} %iota_compare_fusion.8, bf16[64,1536,1]{1,0,2:T(8,128)(2,1)S(1)} %bitcast.88, bf16[16,64,1536]{2,1,0:T(8,128)(2,1)S(1)} %bitcast.75), kind=kOutput, calls=%fused_computation.36 | convolution fusion | flops 201580544 | bytes 3377152 | tf_op jit(solution)/shard_map/dot_general | solution.py:131
  26.4 1.7 %fusion.7 = f32[4,16,1536]{2,1,0:T(8,128)S(1)} fusion(bf16[1024,1536]{1,0:T(8,128)(2,1)S(1)} %copy-done, bf16[4,16,1024]{2,1,0:T(8,128)(2,1)} %tile.13, bf16[4,16,1024]{2,1,0:T(8,128)(2,1)} %tile.15, s32[4,16]{1,0:T(4,128)} %get-tuple-element.35, s32[4,16]{1,0:T(4,128)} %get-tuple-element.34, s32[1024]{0:T(1024)} %add_select_fusion.8), kind=kOutput, calls=%fused_computation.15 | convolution fusion | flops 201654272 | bytes 3805696 | tf_op jit(solution)/shard_map/dot_general | solution.py:141
  29.0 1.9 %collective-permute-start.3 = (f32[16,1536]{1,0:T(8,128)}, f32[16,1536]{1,0:T(8,128)}, u32[]{:S(2)}, u32[]{:S(2)}) collective-permute-start(f32[16,1536]{1,0:T(8,128)} %get-tuple-element.22), channel_id=1, source_target_pairs={{0,2},{1,3},{2,0},{3,1},{4,6},{5,7},{6,4},{7,5},{8,10},{9,11},{10,... | collective-permute-start | bytes 294920 | tf_op jit(solution)/shard_map/ppermute | solution.py:93
  30.9 1.4 %collective-permute-start.4 = (f32[16,1536]{1,0:T(8,128)}, f32[16,1536]{1,0:T(8,128)}, u32[]{:S(2)}, u32[]{:S(2)}) collective-permute-start(f32[16,1536]{1,0:T(8,128)} %get-tuple-element.21), channel_id=1, source_target_pairs={{0,3},{1,2},{2,1},{3,0},{4,7},{5,6},{6,5},{7,4},{8,11},{9,10},{10,... | collective-permute-start | bytes 294920 | tf_op jit(solution)/shard_map/ppermute | solution.py:93
  34.6 2.1 %collective-permute-done.4 = f32[16,1536]{1,0:T(8,128)} collective-permute-done((f32[16,1536]{1,0:T(8,128)}, f32[16,1536]{1,0:T(8,128)}, u32[]{:S(2)}, u32[]{:S(2)}) %collective-permute-start.4) | collective-permute-done | bytes 98336 | tf_op jit(solution)/shard_map/ppermute | solution.py:93
  37.8 10.8 %multiply_reduce_fusion = (f32[1536]{0:T(1024)S(1)}, f32[1536]{0:T(1024)S(1)}, f32[1600,1536]{1,0:T(8,128)}) fusion(f32[1600,1536]{1,0:T(8,128)} %copy-done.1, f32[1536]{0:T(1024)} %param.11, f32[1536]{0:T(1024)} %param.10, bf16[16,1536]{1,0:T(8,128)(2,1)S(1)} %get-tuple-element.28, bf16[16,1536]{1,0:T(8,128)(2,1)S(1)} %get-tuple-element.27, ...), kind=kOutput, calls=%fused_computation.1 | convolution fusion | flops 268778496 | bytes 19884032 | tf_op jit(solution)/shard_map/dot_general | solution.py:161
  48.9 6.0 %fusion.2 = f32[1536,384]{1,0:T(8,128)S(1)} fusion(bf16[1600,384]{1,0:T(8,128)(2,1)} %param.8, f32[1600,1536]{1,0:T(8,128)} %get-tuple-element.33, f32[1536]{0:T(1024)S(1)} %copy-done.18), kind=kOutput, calls=%fused_computation.8 | convolution fusion | flops 1892352000 | bytes 13424640 | tf_op jit(solution)/shard_map/dot_general | solution.py:168
  54.9 1.4 %copy-done.2 = f32[1536,384]{1,0:T(8,128)} copy-done((f32[1536,384]{1,0:T(8,128)}, f32[1536,384]{1,0:T(8,128)S(1)}, u32[]{:S(2)}) %copy-start.2) | copy-done | bytes 2359320
  56.3 1.1 fusion.21
  57.4 3.3 %collective-permute-done.5 = f32[4,1,200,384]{3,2,0,1:T(8,128)} collective-permute-done((f32[4,1,200,384]{3,2,0,1:T(8,128)}, f32[4,1,200,384]{3,2,0,1:T(8,128)}, u32[]{:S(2)}, u32[]{:S(2)}) %collective-permute-start.5) | collective-permute-done | bytes 1228832 | tf_op jit(solution)/shard_map/ppermute | solution.py:69
  60.7 1.8 %fusion.24 = f32[4,1,200,384]{3,2,0,1:T(8,128)S(1)} fusion(f32[4,1,200,384]{3,2,0,1:T(8,128)} %collective-permute-done.5, s32[]{:T(128)S(6)} %select_n.418, f32[4,2,1,192,384]{4,3,1,0,2:T(8,128)} %bitcast.77, f32[4,2,1,8,384]{4,3,1,0,2:T(8,128)S(1)} %bitcast.87), kind=kLoop, calls=%fused_computation.31 | loop fusion | flops 614400 | bytes 4915204 | tf_op jit(solution)/shard_map/add | solution.py:70
  64.4 1.6 %collective-permute-start.6 = (f32[2,1,200,384]{3,2,1,0:T(8,128)}, f32[2,1,200,384]{3,2,1,0:T(8,128)}, u32[]{:S(2)}, u32[]{:S(2)}) collective-permute-start(f32[2,1,200,384]{3,2,1,0:T(8,128)} %dynamic-slice_bitcast_fusion), channel_id=1, source_target_pairs={{0,8},{4,12},{8,0},{12,4},{16,24},{20,28},{24,16},{28,20},{1,9},{5... | collective-permute-start | bytes 1843208 | tf_op jit(solution)/shard_map/ppermute | solution.py:69
  66.2 14.4 %collective-permute-done.6 = f32[2,1,200,384]{3,2,1,0:T(8,128)} collective-permute-done((f32[2,1,200,384]{3,2,1,0:T(8,128)}, f32[2,1,200,384]{3,2,1,0:T(8,128)}, u32[]{:S(2)}, u32[]{:S(2)}) %collective-permute-start.6) | collective-permute-done | bytes 614432 | tf_op jit(solution)/shard_map/ppermute | solution.py:69
  80.6 1.3 %bitcast_add_fusion = f32[2,1,200,384]{3,2,1,0:T(8,128)S(1)} fusion(f32[2,1,200,384]{3,2,1,0:T(8,128)} %collective-permute-done.6, f32[2,2,1,200,384]{4,3,1,0,2:T(8,128)} %bitcast.79, s32[]{:T(128)S(6)} %select_n.422), kind=kLoop, calls=%fused_computation.33 | loop fusion | flops 153600 | bytes 1843204 | tf_op jit(solution)/shard_map/add | solution.py:70
  83.5 2.6 %collective-permute-start.7 = (f32[1,1,200,384]{3,2,1,0:T(8,128)}, f32[1,1,200,384]{3,2,1,0:T(8,128)}, u32[]{:S(2)}, u32[]{:S(2)}) collective-permute-start(f32[1,1,200,384]{3,2,1,0:T(8,128)} %constant_dynamic-slice_fusion), channel_id=1, source_target_pairs={{0,16},{4,20},{8,24},{12,28},{16,0},{20,4},{24,8},{28,12},{1,17},{... | collective-permute-start | bytes 921608 | tf_op jit(solution)/shard_map/ppermute | solution.py:69
  86.2 1.2 select_n.379
  88.4 11.3 %collective-permute-done.7 = f32[1,1,200,384]{3,2,1,0:T(8,128)} collective-permute-done((f32[1,1,200,384]{3,2,1,0:T(8,128)}, f32[1,1,200,384]{3,2,1,0:T(8,128)}, u32[]{:S(2)}, u32[]{:S(2)}) %collective-permute-start.7) | collective-permute-done | bytes 307232 | tf_op jit(solution)/shard_map/ppermute | solution.py:69
  99.8 1.8 %add_bitcast_fusion = f32[1,200,384]{2,1,0:T(8,128)} fusion(f32[1,1,200,384]{3,2,1,0:T(8,128)} %collective-permute-done.7, f32[2,1,200,384]{3,2,1,0:T(8,128)} %copy-done.4, s32[]{:T(128)S(6)} %select_n.426), kind=kLoop, calls=%fused_computation.41 | loop fusion | flops 76800 | bytes 921604 | tf_op jit(solution)/shard_map/reshape | solution.py:72
  101.6 4.8 %all-to-all-start = ((bf16[8,64,322]{2,1,0:T(8,128)(2,1)}), bf16[8,64,322]{2,1,0:T(8,128)(2,1)S(1)}, u32[]{:S(2)}, u32[]{:S(2)}) async-start(bf16[8,64,322]{2,1,0:T(8,128)(2,1)} %pad_maximum_fusion), calls=%async_computation | async-start | bytes 786432 | tf_op jit(solution)/shard_map/all_to_all | solution.py:186
  106.4 1.5 %collective-permute-start.8 = (f32[200,384]{1,0:T(8,128)}, f32[200,384]{1,0:T(8,128)S(1)}, u32[]{:S(2)}, u32[]{:S(2)}) collective-permute-start(f32[200,384]{1,0:T(8,128)} %bitcast.83), channel_id=1, source_target_pairs={{0,1},{1,0},{2,3},{3,2},{4,5},{5,4},{6,7},{7,6},{8,9},{9,8},{10,11... | collective-permute-start | bytes 921608 | tf_op jit(solution)/shard_map/ppermute | solution.py:80
  107.9 8.4 %collective-permute-done.8 = f32[200,384]{1,0:T(8,128)S(1)} collective-permute-done((f32[200,384]{1,0:T(8,128)}, f32[200,384]{1,0:T(8,128)S(1)}, u32[]{:S(2)}, u32[]{:S(2)}) %collective-permute-start.8) | collective-permute-done | bytes 307232 | tf_op jit(solution)/shard_map/ppermute | solution.py:80
  116.3 1.7 %bitcast_add_fusion.2 = f32[200,384]{1,0:T(8,128)} fusion(f32[200,384]{1,0:T(8,128)S(1)} %collective-permute-done.8, f32[1,200,384]{2,1,0:T(8,128)} %add_bitcast_fusion), kind=kLoop, calls=%fused_computation.188 | loop fusion | flops 76800 | bytes 921600 | tf_op jit(solution)/shard_map/add | solution.py:81
  122.8 1.6 %copy.58 = bf16[512,64]{0,1:T(8,128)(2,1)} copy(bf16[512,64]{1,0:T(8,128)(2,1)} %get-tuple-element.23) | data formatting | bytes 131072
  124.5 1.6 %copy.60 = bf16[512,64]{0,1:T(8,128)(2,1)} copy(bf16[512,64]{1,0:T(8,128)(2,1)} %get-tuple-element.24) | data formatting | bytes 131072
  126.1 1.4 %fusion.25 = bf16[512,16,64]{0,2,1:T(8,128)(2,1)S(1)} fusion(s32[512]{0:T(512)S(1)} %bitcast.91, s32[512]{0:T(512)S(1)} %bitcast.90, s32[16,64]{1,0:T(8,128)S(1)} %add_select_fusion.5, bf16[512,64]{0,1:T(8,128)(2,1)} %copy.60, bf16[512,64]{0,1:T(8,128)(2,1)} %copy.58), kind=kLoop, calls=%fused_computation.32 | loop fusion | flops 2621440 | bytes 1187840 | tf_op jit(solution)/shard_map/add | solution.py:18
  127.5 1.4 %fusion.83 = f32[1024,192]{0,1:T(8,128)} fusion(bf16[512,1024]{0,1:T(8,128)(2,1)S(1)} %bitcast.80, bf16[512,192]{1,0:T(8,128)(2,1)S(1)} %bitcast.85), kind=kOutput, calls=%fused_computation.194 | convolution fusion | flops 201326592 | bytes 2031616 | tf_op jit(solution)/shard_map/dot_general | solution.py:194
  (108 shorter events, 21.8 us)
Async XLA Ops:
  0.6 22.0 %copy-start = (bf16[1024,1536]{1,0:T(8,128)(2,1)S(1)}, bf16[1024,1536]{1,0:T(8,128)(2,1)}, u32[]{:S(2)}) copy-start(bf16[1024,1536]{1,0:T(8,128)(2,1)} %param.12) | copy-start | bytes 9437188
  0.7 4.5 %copy-start.8 = (s32[1600]{0:T(1024)}, s32[1600]{0:T(1024)S(1)}, u32[]{:S(2)}) copy-start(s32[1600]{0:T(1024)S(1)} %add_select_fusion.7) | copy-start | bytes 19204
  0.7 4.5 %copy-start.16 = (f32[1536]{0:T(1024)S(1)}, f32[1536]{0:T(1024)}, u32[]{:S(2)}) copy-start(f32[1536]{0:T(1024)} %param.11) | copy-start | bytes 18436
  0.7 4.5 %copy-start.17 = (f32[1536]{0:T(1024)S(1)}, f32[1536]{0:T(1024)}, u32[]{:S(2)}) copy-start(f32[1536]{0:T(1024)} %param.10) | copy-start | bytes 18436
  5.2 5.7 %copy-start.1 = (f32[1600,1536]{1,0:T(8,128)}, f32[1600,1536]{1,0:T(8,128)S(1)}, u32[]{:S(2)}) copy-start(f32[1600,1536]{1,0:T(8,128)S(1)} %fusion.82) | copy-start | bytes 29491204
  5.2 8.7 %copy-start.10 = (s32[64,64]{1,0:T(8,128)S(1)}, s32[64,64]{1,0:T(8,128)}, u32[]{:S(2)}) copy-start(s32[64,64]{1,0:T(8,128)} %param.14) | copy-start | bytes 49156
  5.3 9.4 %copy-start.15 = (s32[64]{0:T(128)S(1)}, s32[64]{0:T(128)}, u32[]{:S(2)}) copy-start(s32[64]{0:T(128)} %param.13) | copy-start | bytes 772
  10.9 7.0 %collective-permute-start = (bf16[1,16,1536]{2,1,0:T(8,128)(2,1)S(1)}, bf16[1,16,1536]{2,1,0:T(8,128)(2,1)S(1)}, u32[]{:S(2)}, u32[]{:S(2)}) collective-permute-start(bf16[1,16,1536]{2,1,0:T(8,128)(2,1)S(1)} %fusion.15), channel_id=1, source_target_pairs={{0,1},{1,0},{2,3},{3,2},{4,5},{5,4},{6,7},{7,6},{8,9},{9,8},{10,11... | collective-permute-start | bytes 147464 | tf_op jit(solution)/shard_map/ppermute | solution.py:52
  14.8 0.5 copy-start.11
  14.8 0.5 copy-start.13
  17.9 4.7 %collective-permute-start.1 = (bf16[2,16,1536]{2,1,0:T(8,128)(2,1)S(1)}, bf16[2,16,1536]{2,1,0:T(8,128)(2,1)S(1)}, u32[]{:S(2)}, u32[]{:S(2)}) collective-permute-start(bf16[2,16,1536]{2,1,0:T(8,128)(2,1)S(1)} %maximum_select_fusion.1), channel_id=1, source_target_pairs={{0,2},{1,3},{2,0},{3,1},{4,6},{5,7},{6,4},{7,5},{8,10},{9,11},{10,... | collective-permute-start | bytes 294920 | tf_op jit(solution)/shard_map/ppermute | solution.py:52
  22.6 1.8 %copy-start.5 = (bf16[4,16,1536]{2,1,0:T(8,128)(2,1)}, bf16[4,16,1536]{2,1,0:T(8,128)(2,1)S(1)}, u32[]{:S(2)}) copy-start(bf16[4,16,1536]{2,1,0:T(8,128)(2,1)S(1)} %maximum_select_fusion) | copy-start | bytes 589828
  25.5 0.9 copy-start.6
  26.4 5.9 %copy-start.9 = (s32[1600]{0:T(1024)S(1)}, s32[1600]{0:T(1024)}, u32[]{:S(2)}) copy-start(s32[1600]{0:T(1024)} %copy-done.8) | copy-start | bytes 19204
  28.8 4.9 %collective-permute-start.2 = (f32[16,1536]{1,0:T(8,128)}, f32[16,1536]{1,0:T(8,128)}, u32[]{:S(2)}, u32[]{:S(2)}) collective-permute-start(f32[16,1536]{1,0:T(8,128)} %get-tuple-element.20), channel_id=1, source_target_pairs={{0,1},{1,0},{2,3},{3,2},{4,5},{5,4},{6,7},{7,6},{8,9},{9,8},{10,11... | collective-permute-start | bytes 294920 | tf_op jit(solution)/shard_map/ppermute | solution.py:93
  29.0 5.7 %collective-permute-start.3 = (f32[16,1536]{1,0:T(8,128)}, f32[16,1536]{1,0:T(8,128)}, u32[]{:S(2)}, u32[]{:S(2)}) collective-permute-start(f32[16,1536]{1,0:T(8,128)} %get-tuple-element.22), channel_id=1, source_target_pairs={{0,2},{1,3},{2,0},{3,1},{4,6},{5,7},{6,4},{7,5},{8,10},{9,11},{10,... | collective-permute-start | bytes 294920 | tf_op jit(solution)/shard_map/ppermute | solution.py:93
  30.9 5.8 %collective-permute-start.4 = (f32[16,1536]{1,0:T(8,128)}, f32[16,1536]{1,0:T(8,128)}, u32[]{:S(2)}, u32[]{:S(2)}) collective-permute-start(f32[16,1536]{1,0:T(8,128)} %get-tuple-element.21), channel_id=1, source_target_pairs={{0,3},{1,2},{2,1},{3,0},{4,7},{5,6},{6,5},{7,4},{8,11},{9,10},{10,... | collective-permute-start | bytes 294920 | tf_op jit(solution)/shard_map/ppermute | solution.py:93
  37.8 11.1 %copy-start.18 = (f32[1536]{0:T(1024)S(1)}, f32[1536]{0:T(1024)}, u32[]{:S(2)}) copy-start(f32[1536]{0:T(1024)} %param.10) | copy-start | bytes 18436
  54.9 1.4 %copy-start.2 = (f32[1536,384]{1,0:T(8,128)}, f32[1536,384]{1,0:T(8,128)S(1)}, u32[]{:S(2)}) copy-start(f32[1536,384]{1,0:T(8,128)S(1)} %fusion.2) | copy-start | bytes 7077892
  57.4 8.5 %copy-start.14 = (s32[64]{0:T(128)S(1)}, s32[64]{0:T(128)}, u32[]{:S(2)}) copy-start(s32[64]{0:T(128)} %copy-done.13) | copy-start | bytes 772
  57.4 8.6 %copy-start.12 = (s32[64]{0:T(128)S(1)}, s32[64]{0:T(128)}, u32[]{:S(2)}) copy-start(s32[64]{0:T(128)} %copy-done.11) | copy-start | bytes 772
  57.4 3.3 %collective-permute-start.5 = (f32[4,1,200,384]{3,2,0,1:T(8,128)}, f32[4,1,200,384]{3,2,0,1:T(8,128)}, u32[]{:S(2)}, u32[]{:S(2)}) collective-permute-start(f32[4,1,200,384]{3,2,0,1:T(8,128)} %fusion.21), channel_id=1, source_target_pairs={{0,4},{4,0},{8,12},{12,8},{16,20},{20,16},{24,28},{28,24},{1,5},{5... | collective-permute-start | bytes 3686408 | tf_op jit(solution)/shard_map/ppermute | solution.py:69
  62.5 1.0 copy-start.3
  62.5 24.9 %copy-start.7 = (bf16[64,64]{1,0:T(8,128)(2,1)S(1)}, bf16[64,64]{1,0:T(8,128)(2,1)}, u32[]{:S(2)}) copy-start(bf16[64,64]{1,0:T(8,128)(2,1)} %copy-done.6) | copy-start | bytes 24580
  64.4 16.2 %collective-permute-start.6 = (f32[2,1,200,384]{3,2,1,0:T(8,128)}, f32[2,1,200,384]{3,2,1,0:T(8,128)}, u32[]{:S(2)}, u32[]{:S(2)}) collective-permute-start(f32[2,1,200,384]{3,2,1,0:T(8,128)} %dynamic-slice_bitcast_fusion), channel_id=1, source_target_pairs={{0,8},{4,12},{8,0},{12,4},{16,24},{20,28},{24,16},{28,20},{1,9},{5... | collective-permute-start | bytes 1843208 | tf_op jit(solution)/shard_map/ppermute | solution.py:69
  81.9 0.8 copy-start.4
  83.5 16.3 %collective-permute-start.7 = (f32[1,1,200,384]{3,2,1,0:T(8,128)}, f32[1,1,200,384]{3,2,1,0:T(8,128)}, u32[]{:S(2)}, u32[]{:S(2)}) collective-permute-start(f32[1,1,200,384]{3,2,1,0:T(8,128)} %constant_dynamic-slice_fusion), channel_id=1, source_target_pairs={{0,16},{4,20},{8,24},{12,28},{16,0},{20,4},{24,8},{28,12},{1,17},{... | collective-permute-start | bytes 921608 | tf_op jit(solution)/shard_map/ppermute | solution.py:69
  101.6 17.3 %all-to-all-start = ((bf16[8,64,322]{2,1,0:T(8,128)(2,1)}), bf16[8,64,322]{2,1,0:T(8,128)(2,1)S(1)}, u32[]{:S(2)}, u32[]{:S(2)}) async-start(bf16[8,64,322]{2,1,0:T(8,128)(2,1)} %pad_maximum_fusion), calls=%async_computation | async-start | bytes 786432 | tf_op jit(solution)/shard_map/all_to_all | solution.py:186
  106.4 9.9 %collective-permute-start.8 = (f32[200,384]{1,0:T(8,128)}, f32[200,384]{1,0:T(8,128)S(1)}, u32[]{:S(2)}, u32[]{:S(2)}) collective-permute-start(f32[200,384]{1,0:T(8,128)} %bitcast.83), channel_id=1, source_target_pairs={{0,1},{1,0},{2,3},{3,2},{4,5},{5,4},{6,7},{7,6},{8,9},{9,8},{10,11... | collective-permute-start | bytes 921608 | tf_op jit(solution)/shard_map/ppermute | solution.py:80
  118.0 10.9 %collective-permute-start.9 = (f32[200,384]{1,0:T(8,128)}, f32[200,384]{1,0:T(8,128)}, u32[]{:S(2)}, u32[]{:S(2)}) collective-permute-start(f32[200,384]{1,0:T(8,128)} %bitcast_add_fusion.2), channel_id=1, source_target_pairs={{0,2},{1,3},{2,0},{3,1},{4,6},{5,7},{6,4},{7,5},{8,10},{9,11},{10,... | collective-permute-start | bytes 921608 | tf_op jit(solution)/shard_map/ppermute | solution.py:80

commit v16 on v12

--- a/solution.py
+++ b/solution.py
@@ -83,6 +83,18 @@
     return cur
 
 
+def crossed_sum(x, name, split):
+    size = lax.axis_size(name)
+    bits = []
+    while (1 << len(bits)) < size:
+        bits.append(len(bits))
+    first, second = x[:split], x[split:]
+    for low, high in zip(bits, bits[::-1]):
+        first = first + lax.ppermute(first, name, partners(size, low))
+        second = second + lax.ppermute(second, name, partners(size, high))
+    return jnp.concatenate([first, second], axis=0)
+
+
 def direct_scatter(x, name):
     size = lax.axis_size(name)
     idx = lax.axis_index(name)
@@ -194,7 +206,7 @@
         [head_term.reshape(n_dp, chunk, e_size), side_rows.reshape(n_dp, pad_rows, e_size)], axis=1
     )
     (part,) = halving_scatter([stacked], "dp")
-    (total,) = butterfly_sum([part[0]], "leaf")
+    total = crossed_sum(part[0], "leaf", (chunk + pad_rows) // 16 * 8)
     side_flat = total[chunk:].reshape(-1)
     side_sum = jnp.stack([side_flat[:chunk], side_flat[chunk : 2 * chunk]], axis=1)
     return (total[:chunk].T, side_sum[:, 0], side_sum[:, 1], node_grad)

time: 117 us -> 119 us (1.017)
  starting transfers between devices: 20.5 us -> 22.9 us
    ppermute x3, waiting for transfers between devices: 25 us -> 16.8 us  [halving_scatter(): got = lax.ppermute(tuple(give), name, partners(size, bit))]
    all_to_all x1, waiting for transfers between devices: 0.01 us -> 6.96 us  [shards(): recv = lax.all_to_all(send, 'dp', split_axis=0, concat_axis=0, tiled=True)]
    ppermute x2 -> x4, starting transfers between devices: 2.94 us -> 6.16 us  [the longest x2 3.15 us: crossed_sum(): second = second + lax.ppermute(second, name, partners(size, high))]
    unnamed x44 -> x46, local copies, waits for them, and re-layouts: 5.53 us -> 8.35 us
    another operation x1 -> x0, other arithmetic: 1.8 us -> none  [shards(): total, = butterfly_sum([part[0]], 'leaf')]
    ppermute x3, starting transfers between devices: 5.38 us -> 3.65 us  [halving_scatter(): got = lax.ppermute(tuple(give), name, partners(size, bit))]
    ppermute x2 -> x4, waiting for transfers between devices: 3.66 us -> 5.12 us  [the longest x2 3.47 us: crossed_sum(): first = first + lax.ppermute(first, name, partners(size, low))]
    add x2 -> x3, other arithmetic: 3.08 us -> 4.18 us  [halving_scatter(): cur = [k + g for k, g in zip(keep, got)]]
  transfers between devices with their start and end apart: 11 -> 13, of which waited for: 9 -> 10; matrix products, arithmetic and copies ran while one was open for 16% -> 17% of each run, Pallas kernels for 0% -> 0%
where the time goes in v16:
time: 119 us; the launch traced here: 118 us
  waiting for transfers between devices  34.2 us (29%)
  matrix products  27.7 us (23%)
  starting transfers between devices  22.9 us (19%)
  local copies, waits for them, and re-layouts  16.7 us (14%)
  other arithmetic  15.6 us (13%)
    ppermute x3, waiting for transfers between devices, halving_scatter(): got = lax.ppermute(tuple(give), name, partners(size, bit))  16.8 us
    unnamed x46, local copies, waits for them, and re-layouts  8.35 us
    dot_general x1, matrix products, shards(): jnp.dot(jnp.concatenate([select.T.astype(jnp.bfloat16)] * 3, axis=1), jnp...  8.15 us
    all_to_all x1, waiting for transfers between devices, shards(): recv = lax.all_to_all(send, 'dp', split_axis=0, concat_axis=0, tiled=True)  6.96 us
    dot_general x1, matrix products, shards(): jnp.dot(select, active, precision=HIGHEST, preferred_element_type=jnp.flo...  5.63 us
    all_to_all x1, starting transfers between devices, shards(): recv = lax.all_to_all(send, 'dp', split_axis=0, concat_axis=0, tiled=True)  5 us
    ppermute x2, starting transfers between devices, doubling_gather(): other = lax.ppermute(cur, name, partners(size, bit))  4.58 us
    dot_general x1, matrix products, shards(): jnp.dot(features, head_weight, preferred_element_type=jnp.float32)  4.5 us
  transfers between devices with their start and end apart: 13, of which 10 were waited for; matrix products, arithmetic and copies ran while one was open for 17% of the time, Pallas kernels for 0%

profile of v16, /device:TPU:0, one launch (start us, length us, event | category | flops | bytes accessed | tf_op | source)
XLA Modules:
  0.0 118.2 jit_solution(6299585743131180959)
XLA Ops:
  0.7 4.5 %fusion.85 = f32[1600,1536]{1,0:T(8,128)S(1)} fusion(bf16[1600,384]{1,0:T(8,128)(2,1)} %param.8, bf16[384,1536]{1,0:T(8,128)(2,1)} %param.9), kind=kOutput, calls=%fused_computation.197 | convolution fusion | flops 1887436800 | bytes 12238848 | tf_op jit(solution)/shard_map/dot_general | solution.py:123
  5.3 5.6 %fusion.15 = bf16[1,16,1536]{2,1,0:T(8,128)(2,1)S(1)} fusion(f32[1600,1536]{1,0:T(8,128)S(1)} %fusion.85, f32[1536]{0:T(1024)S(1)} %copy-done.17, f32[1536]{0:T(1024)S(1)} %copy-done.18, s32[1600]{0:T(1024)S(1)} %add_select_fusion.7), kind=kOutput, calls=%fused_computation.21 | convolution fusion | flops 486679552 | bytes 9898240 | tf_op jit(solution)/shard_map/dot_general | solution.py:127
  10.9 3.0 %collective-permute-start = (bf16[1,16,1536]{2,1,0:T(8,128)(2,1)S(1)}, bf16[1,16,1536]{2,1,0:T(8,128)(2,1)S(1)}, u32[]{:S(2)}, u32[]{:S(2)}) collective-permute-start(bf16[1,16,1536]{2,1,0:T(8,128)(2,1)S(1)} %fusion.15), channel_id=1, source_target_pairs={{0,1},{1,0},{2,3},{3,2},{4,5},{5,4},{6,7},{7,6},{8,9},{9,8},{10,11... | collective-permute-start | bytes 147464 | tf_op jit(solution)/shard_map/ppermute | solution.py:52
  17.9 1.6 %collective-permute-start.1 = (bf16[2,16,1536]{2,1,0:T(8,128)(2,1)S(1)}, bf16[2,16,1536]{2,1,0:T(8,128)(2,1)S(1)}, u32[]{:S(2)}, u32[]{:S(2)}) collective-permute-start(bf16[2,16,1536]{2,1,0:T(8,128)(2,1)S(1)} %maximum_select_fusion.1), channel_id=1, source_target_pairs={{0,2},{1,3},{2,0},{3,1},{4,6},{5,7},{6,4},{7,5},{8,10},{9,11},{10,... | collective-permute-start | bytes 294920 | tf_op jit(solution)/shard_map/ppermute | solution.py:52
  20.1 2.5 %collective-permute-done.1 = bf16[2,16,1536]{2,1,0:T(8,128)(2,1)S(1)} collective-permute-done((bf16[2,16,1536]{2,1,0:T(8,128)(2,1)S(1)}, bf16[2,16,1536]{2,1,0:T(8,128)(2,1)S(1)}, u32[]{:S(2)}, u32[]{:S(2)}) %collective-permute-start.1) | collective-permute-done | bytes 98336 | tf_op jit(solution)/shard_map/ppermute | solution.py:52
  22.6 1.8 %select_reduce_fusion = (f32[64,64]{1,0:T(8,128)S(1)}, f32[64,64]{1,0:T(8,128)S(1)}) fusion(pred[64,16]{0,1:T(8,128)(4,1)S(1)} %iota_compare_fusion.8, pred[64,16]{0,1:T(8,128)(4,1)S(1)} %iota_compare_fusion.9, bf16[64,1536,1]{1,0,2:T(8,128)(2,1)S(1)} %bitcast.91, bf16[16,64,1536]{2,1,0:T(8,128)(2,1)S(1)} %bitcast.79), kind=kOutput, calls=%fused_computation.35 | convolution fusion | flops 201580544 | bytes 3377152 | tf_op jit(solution)/shard_map/dot_general | solution.py:143
  26.4 1.7 %fusion.7 = f32[4,16,1536]{2,1,0:T(8,128)S(1)} fusion(bf16[1024,1536]{1,0:T(8,128)(2,1)S(1)} %copy-done, bf16[4,16,1024]{2,1,0:T(8,128)(2,1)} %tile.13, bf16[4,16,1024]{2,1,0:T(8,128)(2,1)} %tile.15, s32[4,16]{1,0:T(4,128)} %get-tuple-element.31, s32[4,16]{1,0:T(4,128)} %get-tuple-element.30, s32[1024]{0:T(1024)} %add_select_fusion.8), kind=kOutput, calls=%fused_computation.15 | convolution fusion | flops 201654272 | bytes 3805696 | tf_op jit(solution)/shard_map/dot_general | solution.py:153
  28.8 1.5 %collective-permute-start.4 = (f32[16,1536]{1,0:T(8,128)}, f32[16,1536]{1,0:T(8,128)}, u32[]{:S(2)}, u32[]{:S(2)}) collective-permute-start(f32[16,1536]{1,0:T(8,128)} %get-tuple-element.17), channel_id=1, source_target_pairs={{0,3},{1,2},{2,1},{3,0},{4,7},{5,6},{6,5},{7,4},{8,11},{9,10},{10,... | collective-permute-start | bytes 294920 | tf_op jit(solution)/shard_map/ppermute | solution.py:105
  30.4 1.9 %collective-permute-start.2 = (f32[16,1536]{1,0:T(8,128)}, f32[16,1536]{1,0:T(8,128)}, u32[]{:S(2)}, u32[]{:S(2)}) collective-permute-start(f32[16,1536]{1,0:T(8,128)} %get-tuple-element.16), channel_id=1, source_target_pairs={{0,1},{1,0},{2,3},{3,2},{4,5},{5,4},{6,7},{7,6},{8,9},{9,8},{10,11... | collective-permute-start | bytes 294920 | tf_op jit(solution)/shard_map/ppermute | solution.py:105
  32.9 1.8 %collective-permute-done.4 = f32[16,1536]{1,0:T(8,128)} collective-permute-done((f32[16,1536]{1,0:T(8,128)}, f32[16,1536]{1,0:T(8,128)}, u32[]{:S(2)}, u32[]{:S(2)}) %collective-permute-start.4) | collective-permute-done | bytes 98336 | tf_op jit(solution)/shard_map/ppermute | solution.py:105
  36.9 8.1 %multiply_reduce_fusion = (f32[1536]{0:T(1024)S(1)}, f32[1536]{0:T(1024)S(1)}, f32[1600,1536]{1,0:T(8,128)S(1)}) fusion(f32[1600,1536]{1,0:T(8,128)} %copy-done.1, f32[1536]{0:T(1024)} %param.11, f32[1536]{0:T(1024)} %param.10, bf16[16,1536]{1,0:T(8,128)(2,1)S(1)} %get-tuple-element.24, bf16[16,1536]{1,0:T(8,128)(2,1)S(1)} %get-tuple-element.23, ...), kind=kOutput, calls=%fused_computation.1 | convolution fusion | flops 268778496 | bytes 19884032 | tf_op jit(solution)/shard_map/dot_general | solution.py:185
  45.1 4.5 %fusion.2 = f32[1536,384]{1,0:T(8,128)} fusion(bf16[1600,384]{1,0:T(8,128)(2,1)S(1)} %copy-done.4, f32[1600,1536]{1,0:T(8,128)S(1)} %get-tuple-element.29, f32[1536]{0:T(1024)S(1)} %copy-done.19), kind=kOutput, calls=%fused_computation.8 | convolution fusion | flops 1892352000 | bytes 13424640 | tf_op jit(solution)/shard_map/dot_general | solution.py:192
  50.4 2.4 %fusion.21 = f32[4,1,200,384]{3,2,0,1:T(8,128)} fusion(s32[]{:T(128)S(6)} %select_n.412, f32[4,2,1,192,384]{4,3,1,0,2:T(8,128)} %bitcast.80, f32[4,2,1,8,384]{4,3,1,0,2:T(8,128)S(1)} %bitcast.89), kind=kLoop, calls=%fused_computation.28 | loop fusion | flops 307200 | bytes 3686404 | tf_op jit(solution)/shard_map/jit(dynamic_index_in_dim)/squeeze | solution.py:68
  53.1 1.2 select_n.422
  55.4 5.0 %all-to-all-start = ((bf16[8,64,322]{2,1,0:T(8,128)(2,1)}), bf16[8,64,322]{2,1,0:T(8,128)(2,1)S(1)}, u32[]{:S(2)}, u32[]{:S(2)}) async-start(bf16[8,64,322]{2,1,0:T(8,128)(2,1)} %pad_maximum_fusion), calls=%async_computation | async-start | bytes 786432 | tf_op jit(solution)/shard_map/all_to_all | solution.py:173
  60.4 1.8 %fusion.24 = f32[4,1,200,384]{3,2,0,1:T(8,128)S(1)} fusion(f32[4,1,200,384]{3,2,0,1:T(8,128)} %collective-permute-done.5, s32[]{:T(128)S(6)} %select_n.411, f32[4,2,1,192,384]{4,3,1,0,2:T(8,128)} %bitcast.81, f32[4,2,1,8,384]{4,3,1,0,2:T(8,128)} %bitcast.90), kind=kLoop, calls=%fused_computation.31 | loop fusion | flops 614400 | bytes 4915204 | tf_op jit(solution)/shard_map/add | solution.py:70
  64.1 2.0 %collective-permute-start.6 = (f32[2,1,200,384]{3,2,1,0:T(8,128)}, f32[2,1,200,384]{3,2,1,0:T(8,128)}, u32[]{:S(2)}, u32[]{:S(2)}) collective-permute-start(f32[2,1,200,384]{3,2,1,0:T(8,128)} %dynamic-slice_bitcast_fusion), channel_id=1, source_target_pairs={{0,8},{4,12},{8,0},{12,4},{16,24},{20,28},{24,16},{28,20},{1,9},{5... | collective-permute-start | bytes 1843208 | tf_op jit(solution)/shard_map/ppermute | solution.py:69
  66.1 7.0 %all-to-all-done = bf16[8,64,322]{2,1,0:T(8,128)(2,1)S(1)} async-done(((bf16[8,64,322]{2,1,0:T(8,128)(2,1)}), bf16[8,64,322]{2,1,0:T(8,128)(2,1)S(1)}, u32[]{:S(2)}, u32[]{:S(2)}) %all-to-all-start) | async-done | bytes 329760 | tf_op jit(solution)/shard_map/all_to_all | solution.py:173
  74.1 10.0 %collective-permute-done.6 = f32[2,1,200,384]{3,2,1,0:T(8,128)} collective-permute-done((f32[2,1,200,384]{3,2,1,0:T(8,128)}, f32[2,1,200,384]{3,2,1,0:T(8,128)}, u32[]{:S(2)}, u32[]{:S(2)}) %collective-permute-start.6) | collective-permute-done | bytes 614432 | tf_op jit(solution)/shard_map/ppermute | solution.py:69
  84.1 1.3 %bitcast_add_fusion = f32[2,1,200,384]{3,2,1,0:T(8,128)S(1)} fusion(f32[2,1,200,384]{3,2,1,0:T(8,128)} %collective-permute-done.6, f32[2,2,1,200,384]{4,3,1,0,2:T(8,128)} %bitcast.83, s32[]{:T(128)S(6)} %select_n.415), kind=kLoop, calls=%fused_computation.33 | loop fusion | flops 153600 | bytes 1843204 | tf_op jit(solution)/shard_map/add | solution.py:70
  86.9 1.6 %collective-permute-start.7 = (f32[1,1,200,384]{3,2,1,0:T(8,128)}, f32[1,1,200,384]{3,2,1,0:T(8,128)}, u32[]{:S(2)}, u32[]{:S(2)}) collective-permute-start(f32[1,1,200,384]{3,2,1,0:T(8,128)} %constant_dynamic-slice_fusion), channel_id=1, source_target_pairs={{0,16},{4,20},{8,24},{12,28},{16,0},{20,4},{24,8},{28,12},{1,17},{... | collective-permute-start | bytes 921608 | tf_op jit(solution)/shard_map/ppermute | solution.py:69
  91.5 1.6 %copy.60 = bf16[512,64]{0,1:T(8,128)(2,1)} copy(bf16[512,64]{1,0:T(8,128)(2,1)} %get-tuple-element.20) | data formatting | bytes 131072
  93.1 1.6 %copy.58 = bf16[512,64]{0,1:T(8,128)(2,1)} copy(bf16[512,64]{1,0:T(8,128)(2,1)} %get-tuple-element.19) | data formatting | bytes 131072
  94.7 1.4 %fusion.25 = bf16[512,16,64]{0,2,1:T(8,128)(2,1)S(1)} fusion(s32[512]{0:T(512)S(1)} %bitcast.93, s32[512]{0:T(512)S(1)} %bitcast.94, s32[16,64]{1,0:T(8,128)S(1)} %add_select_fusion.5, bf16[512,64]{0,1:T(8,128)(2,1)} %copy.60, bf16[512,64]{0,1:T(8,128)(2,1)} %copy.58), kind=kLoop, calls=%fused_computation.32 | loop fusion | flops 2621440 | bytes 1187840 | tf_op jit(solution)/shard_map/add | solution.py:18
  96.2 6.8 %collective-permute-done.7 = f32[1,1,200,384]{3,2,1,0:T(8,128)} collective-permute-done((f32[1,1,200,384]{3,2,1,0:T(8,128)}, f32[1,1,200,384]{3,2,1,0:T(8,128)}, u32[]{:S(2)}, u32[]{:S(2)}) %collective-permute-start.7) | collective-permute-done | bytes 307232 | tf_op jit(solution)/shard_map/ppermute | solution.py:69
  104.1 1.5 %collective-permute-start.8 = (f32[96,384]{1,0:T(8,128)S(1)}, f32[96,384]{1,0:T(8,128)S(1)}, u32[]{:S(2)}, u32[]{:S(2)}) collective-permute-start(f32[96,384]{1,0:T(8,128)S(1)} %slice_bitcast_fusion.1), channel_id=1, source_target_pairs={{0,1},{1,0},{2,3},{3,2},{4,5},{5,4},{6,7},{7,6},{8,9},{9,8},{10,11... | collective-permute-start | bytes 442376 | tf_op jit(solution)/shard_map/ppermute | solution.py:93
  105.6 1.6 %collective-permute-start.10 = (f32[104,384]{1,0:T(8,128)S(1)}, f32[104,384]{1,0:T(8,128)S(1)}, u32[]{:S(2)}, u32[]{:S(2)}) collective-permute-start(f32[104,384]{1,0:T(8,128)S(1)} %slice_bitcast_fusion), channel_id=1, source_target_pairs={{0,2},{1,3},{2,0},{3,1},{4,6},{5,7},{6,4},{7,5},{8,10},{9,11},{10,... | collective-permute-start | bytes 479240 | tf_op jit(solution)/shard_map/ppermute | solution.py:94
  107.2 2.8 %collective-permute-done.8 = f32[96,384]{1,0:T(8,128)S(1)} collective-permute-done((f32[96,384]{1,0:T(8,128)S(1)}, f32[96,384]{1,0:T(8,128)S(1)}, u32[]{:S(2)}, u32[]{:S(2)}) %collective-permute-start.8) | collective-permute-done | bytes 147488 | tf_op jit(solution)/shard_map/ppermute | solution.py:93
  110.0 1.5 %collective-permute-start.9 = (f32[96,384]{1,0:T(8,128)S(1)}, f32[96,384]{1,0:T(8,128)S(1)}, u32[]{:S(2)}, u32[]{:S(2)}) collective-permute-start(f32[96,384]{1,0:T(8,128)S(1)} %fusion.80), channel_id=1, source_target_pairs={{0,2},{1,3},{2,0},{3,1},{4,6},{5,7},{6,4},{7,5},{8,10},{9,11},{10,... | collective-permute-start | bytes 442376 | tf_op jit(solution)/shard_map/ppermute | solution.py:93
  111.5 1.6 %collective-permute-start.11 = (f32[104,384]{1,0:T(8,128)S(1)}, f32[104,384]{1,0:T(8,128)S(1)}, u32[]{:S(2)}, u32[]{:S(2)}) collective-permute-start(f32[104,384]{1,0:T(8,128)S(1)} %fusion.81), channel_id=1, source_target_pairs={{0,1},{1,0},{2,3},{3,2},{4,5},{5,4},{6,7},{7,6},{8,9},{9,8},{10,11... | collective-permute-start | bytes 479240 | tf_op jit(solution)/shard_map/ppermute | solution.py:94
  113.1 1.4 %fusion.86 = f32[1024,192]{0,1:T(8,128)} fusion(bf16[512,1024]{0,1:T(8,128)(2,1)S(1)} %bitcast.84, bf16[512,192]{1,0:T(8,128)(2,1)S(1)} %bitcast.88), kind=kOutput, calls=%fused_computation.198 | convolution fusion | flops 201326592 | bytes 2031616 | tf_op jit(solution)/shard_map/dot_general | solution.py:181
  115.2 1.7 %collective-permute-done.11 = f32[104,384]{1,0:T(8,128)S(1)} collective-permute-done((f32[104,384]{1,0:T(8,128)S(1)}, f32[104,384]{1,0:T(8,128)S(1)}, u32[]{:S(2)}, u32[]{:S(2)}) %collective-permute-start.11) | collective-permute-done | bytes 159776 | tf_op jit(solution)/shard_map/ppermute | solution.py:94
  (118 shorter events, 22.9 us)
Async XLA Ops:
  0.6 22.0 %copy-start = (bf16[1024,1536]{1,0:T(8,128)(2,1)S(1)}, bf16[1024,1536]{1,0:T(8,128)(2,1)}, u32[]{:S(2)}) copy-start(bf16[1024,1536]{1,0:T(8,128)(2,1)} %param.12) | copy-start | bytes 9437188
  0.7 4.5 %copy-start.9 = (s32[1600]{0:T(1024)}, s32[1600]{0:T(1024)S(1)}, u32[]{:S(2)}) copy-start(s32[1600]{0:T(1024)S(1)} %add_select_fusion.7) | copy-start | bytes 19204
  0.7 4.5 %copy-start.17 = (f32[1536]{0:T(1024)S(1)}, f32[1536]{0:T(1024)}, u32[]{:S(2)}) copy-start(f32[1536]{0:T(1024)} %param.11) | copy-start | bytes 18436
  0.7 4.5 %copy-start.18 = (f32[1536]{0:T(1024)S(1)}, f32[1536]{0:T(1024)}, u32[]{:S(2)}) copy-start(f32[1536]{0:T(1024)} %param.10) | copy-start | bytes 18436
  5.2 5.7 %copy-start.1 = (f32[1600,1536]{1,0:T(8,128)}, f32[1600,1536]{1,0:T(8,128)S(1)}, u32[]{:S(2)}) copy-start(f32[1600,1536]{1,0:T(8,128)S(1)} %fusion.85) | copy-start | bytes 29491204
  5.2 8.7 %copy-start.11 = (s32[64,64]{1,0:T(8,128)S(1)}, s32[64,64]{1,0:T(8,128)}, u32[]{:S(2)}) copy-start(s32[64,64]{1,0:T(8,128)} %param.14) | copy-start | bytes 49156
  5.3 9.4 %copy-start.16 = (s32[64]{0:T(128)S(1)}, s32[64]{0:T(128)}, u32[]{:S(2)}) copy-start(s32[64]{0:T(128)} %param.13) | copy-start | bytes 772
  10.9 6.9 %collective-permute-start = (bf16[1,16,1536]{2,1,0:T(8,128)(2,1)S(1)}, bf16[1,16,1536]{2,1,0:T(8,128)(2,1)S(1)}, u32[]{:S(2)}, u32[]{:S(2)}) collective-permute-start(bf16[1,16,1536]{2,1,0:T(8,128)(2,1)S(1)} %fusion.15), channel_id=1, source_target_pairs={{0,1},{1,0},{2,3},{3,2},{4,5},{5,4},{6,7},{7,6},{8,9},{9,8},{10,11... | collective-permute-start | bytes 147464 | tf_op jit(solution)/shard_map/ppermute | solution.py:52
  14.8 0.5 copy-start.14
  17.9 4.7 %collective-permute-start.1 = (bf16[2,16,1536]{2,1,0:T(8,128)(2,1)S(1)}, bf16[2,16,1536]{2,1,0:T(8,128)(2,1)S(1)}, u32[]{:S(2)}, u32[]{:S(2)}) collective-permute-start(bf16[2,16,1536]{2,1,0:T(8,128)(2,1)S(1)} %maximum_select_fusion.1), channel_id=1, source_target_pairs={{0,2},{1,3},{2,0},{3,1},{4,6},{5,7},{6,4},{7,5},{8,10},{9,11},{10,... | collective-permute-start | bytes 294920 | tf_op jit(solution)/shard_map/ppermute | solution.py:52
  22.6 1.8 %copy-start.6 = (bf16[4,16,1536]{2,1,0:T(8,128)(2,1)}, bf16[4,16,1536]{2,1,0:T(8,128)(2,1)S(1)}, u32[]{:S(2)}) copy-start(bf16[4,16,1536]{2,1,0:T(8,128)(2,1)S(1)} %maximum_select_fusion) | copy-start | bytes 589828
  25.5 0.9 copy-start.7
  26.4 5.9 %copy-start.10 = (s32[1600]{0:T(1024)S(1)}, s32[1600]{0:T(1024)}, u32[]{:S(2)}) copy-start(s32[1600]{0:T(1024)} %copy-done.9) | copy-start | bytes 19204
  28.8 5.9 %collective-permute-start.4 = (f32[16,1536]{1,0:T(8,128)}, f32[16,1536]{1,0:T(8,128)}, u32[]{:S(2)}, u32[]{:S(2)}) collective-permute-start(f32[16,1536]{1,0:T(8,128)} %get-tuple-element.17), channel_id=1, source_target_pairs={{0,3},{1,2},{2,1},{3,0},{4,7},{5,6},{6,5},{7,4},{8,11},{9,10},{10,... | collective-permute-start | bytes 294920 | tf_op jit(solution)/shard_map/ppermute | solution.py:105
  30.3 5.4 %collective-permute-start.3 = (f32[16,1536]{1,0:T(8,128)}, f32[16,1536]{1,0:T(8,128)}, u32[]{:S(2)}, u32[]{:S(2)}) collective-permute-start(f32[16,1536]{1,0:T(8,128)} %get-tuple-element.18), channel_id=1, source_target_pairs={{0,2},{1,3},{2,0},{3,1},{4,6},{5,7},{6,4},{7,5},{8,10},{9,11},{10,... | collective-permute-start | bytes 294920 | tf_op jit(solution)/shard_map/ppermute | solution.py:105
  30.4 5.4 %collective-permute-start.2 = (f32[16,1536]{1,0:T(8,128)}, f32[16,1536]{1,0:T(8,128)}, u32[]{:S(2)}, u32[]{:S(2)}) collective-permute-start(f32[16,1536]{1,0:T(8,128)} %get-tuple-element.16), channel_id=1, source_target_pairs={{0,1},{1,0},{2,3},{3,2},{4,5},{5,4},{6,7},{7,6},{8,9},{9,8},{10,11... | collective-permute-start | bytes 294920 | tf_op jit(solution)/shard_map/ppermute | solution.py:105
  36.9 8.2 %copy-start.4 = (bf16[1600,384]{1,0:T(8,128)(2,1)S(1)}, bf16[1600,384]{1,0:T(8,128)(2,1)}, u32[]{:S(2)}) copy-start(bf16[1600,384]{1,0:T(8,128)(2,1)} %param.8) | copy-start | bytes 3686404
  36.9 8.2 %copy-start.19 = (f32[1536]{0:T(1024)S(1)}, f32[1536]{0:T(1024)}, u32[]{:S(2)}) copy-start(f32[1536]{0:T(1024)} %param.10) | copy-start | bytes 18436
  49.6 3.3 %copy-start.15 = (s32[64]{0:T(128)S(1)}, s32[64]{0:T(128)}, u32[]{:S(2)}) copy-start(s32[64]{0:T(128)} %copy-done.14) | copy-start | bytes 772
  49.6 3.4 %copy-start.13 = (s32[64]{0:T(128)S(1)}, s32[64]{0:T(128)}, u32[]{:S(2)}) copy-start(s32[64]{0:T(128)} %copy-done.12) | copy-start | bytes 772
  49.6 4.8 %copy-start.8 = (bf16[64,64]{1,0:T(8,128)(2,1)S(1)}, bf16[64,64]{1,0:T(8,128)(2,1)}, u32[]{:S(2)}) copy-start(bf16[64,64]{1,0:T(8,128)(2,1)} %copy-done.7) | copy-start | bytes 24580
  49.8 0.6 copy-start.5
  52.9 7.5 %collective-permute-start.5 = (f32[4,1,200,384]{3,2,0,1:T(8,128)}, f32[4,1,200,384]{3,2,0,1:T(8,128)}, u32[]{:S(2)}, u32[]{:S(2)}) collective-permute-start(f32[4,1,200,384]{3,2,0,1:T(8,128)} %fusion.21), channel_id=1, source_target_pairs={{0,4},{4,0},{8,12},{12,8},{16,20},{20,16},{24,28},{28,24},{1,5},{5... | collective-permute-start | bytes 3686408 | tf_op jit(solution)/shard_map/ppermute | solution.py:69
  55.4 17.7 %all-to-all-start = ((bf16[8,64,322]{2,1,0:T(8,128)(2,1)}), bf16[8,64,322]{2,1,0:T(8,128)(2,1)S(1)}, u32[]{:S(2)}, u32[]{:S(2)}) async-start(bf16[8,64,322]{2,1,0:T(8,128)(2,1)} %pad_maximum_fusion), calls=%async_computation | async-start | bytes 786432 | tf_op jit(solution)/shard_map/all_to_all | solution.py:173
  62.2 1.1 copy-start.2
  64.1 20.0 %collective-permute-start.6 = (f32[2,1,200,384]{3,2,1,0:T(8,128)}, f32[2,1,200,384]{3,2,1,0:T(8,128)}, u32[]{:S(2)}, u32[]{:S(2)}) collective-permute-start(f32[2,1,200,384]{3,2,1,0:T(8,128)} %dynamic-slice_bitcast_fusion), channel_id=1, source_target_pairs={{0,8},{4,12},{8,0},{12,4},{16,24},{20,28},{24,16},{28,20},{1,9},{5... | collective-permute-start | bytes 1843208 | tf_op jit(solution)/shard_map/ppermute | solution.py:69
  85.4 0.8 copy-start.3
  86.9 16.0 %collective-permute-start.7 = (f32[1,1,200,384]{3,2,1,0:T(8,128)}, f32[1,1,200,384]{3,2,1,0:T(8,128)}, u32[]{:S(2)}, u32[]{:S(2)}) collective-permute-start(f32[1,1,200,384]{3,2,1,0:T(8,128)} %constant_dynamic-slice_fusion), channel_id=1, source_target_pairs={{0,16},{4,20},{8,24},{12,28},{16,0},{20,4},{24,8},{28,12},{1,17},{... | collective-permute-start | bytes 921608 | tf_op jit(solution)/shard_map/ppermute | solution.py:69
  104.1 5.8 %collective-permute-start.8 = (f32[96,384]{1,0:T(8,128)S(1)}, f32[96,384]{1,0:T(8,128)S(1)}, u32[]{:S(2)}, u32[]{:S(2)}) collective-permute-start(f32[96,384]{1,0:T(8,128)S(1)} %slice_bitcast_fusion.1), channel_id=1, source_target_pairs={{0,1},{1,0},{2,3},{3,2},{4,5},{5,4},{6,7},{7,6},{8,9},{9,8},{10,11... | collective-permute-start | bytes 442376 | tf_op jit(solution)/shard_map/ppermute | solution.py:93
  105.6 5.9 %collective-permute-start.10 = (f32[104,384]{1,0:T(8,128)S(1)}, f32[104,384]{1,0:T(8,128)S(1)}, u32[]{:S(2)}, u32[]{:S(2)}) collective-permute-start(f32[104,384]{1,0:T(8,128)S(1)} %slice_bitcast_fusion), channel_id=1, source_target_pairs={{0,2},{1,3},{2,0},{3,1},{4,6},{5,7},{6,4},{7,5},{8,10},{9,11},{10,... | collective-permute-start | bytes 479240 | tf_op jit(solution)/shard_map/ppermute | solution.py:94
  110.0 5.2 %collective-permute-start.9 = (f32[96,384]{1,0:T(8,128)S(1)}, f32[96,384]{1,0:T(8,128)S(1)}, u32[]{:S(2)}, u32[]{:S(2)}) collective-permute-start(f32[96,384]{1,0:T(8,128)S(1)} %fusion.80), channel_id=1, source_target_pairs={{0,2},{1,3},{2,0},{3,1},{4,6},{5,7},{6,4},{7,5},{8,10},{9,11},{10,... | collective-permute-start | bytes 442376 | tf_op jit(solution)/shard_map/ppermute | solution.py:93
  111.5 5.3 %collective-permute-start.11 = (f32[104,384]{1,0:T(8,128)S(1)}, f32[104,384]{1,0:T(8,128)S(1)}, u32[]{:S(2)}, u32[]{:S(2)}) collective-permute-start(f32[104,384]{1,0:T(8,128)S(1)} %fusion.81), channel_id=1, source_target_pairs={{0,1},{1,0},{2,3},{3,2},{4,5},{5,4},{6,7},{7,6},{8,9},{9,8},{10,11... | collective-permute-start | bytes 479240 | tf_op jit(solution)/shard_map/ppermute | solution.py:94
  (1 other events, 0.5 us)

commit v17 on v12

--- a/solution.py
+++ b/solution.py
@@ -158,7 +158,14 @@
     send = jnp.concatenate(
         [column_chunks, jnp.broadcast_to(compact[None], (n_dp,) + compact.shape)], axis=2
     )
-    recv = lax.all_to_all(send, "dp", split_axis=0, concat_axis=0, tiled=True)
+    per_dest = send.shape[1] * send.shape[2]
+    if per_dest % 128 == 0:
+        flat = lax.all_to_all(
+            send.reshape(n_dp, per_dest // 128, 128), "dp", split_axis=0, concat_axis=0, tiled=True
+        )
+        recv = flat.reshape(send.shape)
+    else:
+        recv = lax.all_to_all(send, "dp", split_axis=0, concat_axis=0, tiled=True)
     columns = recv[:, :, :col_width].reshape(n_dp * group, col_width)
     info = recv[:, :, col_width:].reshape(n_dp * group, compact.shape[1])
     all_pos = info[:, :SUB_SIZE]

time: 117 us -> 118 us (level)
  waiting for transfers between devices: 34 us -> 30.4 us
  local copies, waits for them, and re-layouts: 16.5 us -> 20 us
    reshape x0 -> x2, local copies, waits for them, and re-layouts: none -> 3.17 us  [the longest x1 1.68 us: shards(): recv = flat.reshape(send.shape)]
    ppermute x3, waiting for transfers between devices: 25 us -> 22.5 us  [halving_scatter(): got = lax.ppermute(tuple(give), name, partners(size, bit))]
    slice x0 -> x1, local copies, waits for them, and re-layouts: none -> 1.66 us  [shards(): all_neg = info[:, SUB_SIZE:2 * SUB_SIZE]]
    unnamed x44 -> x42, local copies, waits for them, and re-layouts: 5.53 us -> 4.46 us
  transfers between devices with their start and end apart: 11 -> 11, of which waited for: 9 -> 8; matrix products, arithmetic and copies ran while one was open for 16% -> 19% of each run, Pallas kernels for 0% -> 0%
where the time goes in v17:
time: 118 us; the launch traced here: 116 us
  waiting for transfers between devices  30.4 us (26%)
  matrix products  27.9 us (24%)
  starting transfers between devices  20.1 us (17%)
  local copies, waits for them, and re-layouts  20 us (17%)
  other arithmetic  15.9 us (13%)
    ppermute x3, waiting for transfers between devices, halving_scatter(): got = lax.ppermute(tuple(give), name, partners(size, bit))  22.5 us
    dot_general x1, matrix products, shards(): jnp.dot(jnp.concatenate([select.T.astype(jnp.bfloat16)] * 3, axis=1), jnp...  8.42 us
    dot_general x1, matrix products, shards(): jnp.dot(select, active, precision=HIGHEST, preferred_element_type=jnp.flo...  5.63 us
    ppermute x3, starting transfers between devices, halving_scatter(): got = lax.ppermute(tuple(give), name, partners(size, bit))  5.12 us
    ppermute x2, starting transfers between devices, doubling_gather(): other = lax.ppermute(cur, name, partners(size, bit))  4.58 us
    dot_general x1, matrix products, shards(): lax.dot_general(lin_grad, features, (((0,), (0,)), ((), ())), preferred_e...  4.51 us
    dot_general x1, matrix products, shards(): jnp.dot(features, head_weight, preferred_element_type=jnp.float32)  4.5 us
    unnamed x42, local copies, waits for them, and re-layouts  4.46 us
  transfers between devices with their start and end apart: 11, of which 8 were waited for; matrix products, arithmetic and copies ran while one was open for 19% of the time, Pallas kernels for 0%

profile of v17, /device:TPU:0, one launch (start us, length us, event | category | flops | bytes accessed | tf_op | source)
XLA Modules:
  0.0 115.5 jit_solution(3703794232933330778)
XLA Ops:
  0.7 4.5 %fusion.82 = f32[1600,1536]{1,0:T(8,128)S(1)} fusion(bf16[1600,384]{1,0:T(8,128)(2,1)} %param.8, bf16[384,1536]{1,0:T(8,128)(2,1)} %param.9), kind=kOutput, calls=%fused_computation.192 | convolution fusion | flops 1887436800 | bytes 12238848 | tf_op jit(solution)/shard_map/dot_general | solution.py:111
  5.3 5.6 %fusion.15 = bf16[1,16,1536]{2,1,0:T(8,128)(2,1)S(1)} fusion(f32[1600,1536]{1,0:T(8,128)S(1)} %fusion.82, f32[1536]{0:T(1024)S(1)} %copy-done.16, f32[1536]{0:T(1024)S(1)} %copy-done.17, s32[1600]{0:T(1024)S(1)} %add_select_fusion.7), kind=kOutput, calls=%fused_computation.21 | convolution fusion | flops 486679552 | bytes 9898240 | tf_op jit(solution)/shard_map/dot_general | solution.py:115
  10.9 3.0 %collective-permute-start = (bf16[1,16,1536]{2,1,0:T(8,128)(2,1)S(1)}, bf16[1,16,1536]{2,1,0:T(8,128)(2,1)S(1)}, u32[]{:S(2)}, u32[]{:S(2)}) collective-permute-start(bf16[1,16,1536]{2,1,0:T(8,128)(2,1)S(1)} %fusion.15), channel_id=1, source_target_pairs={{0,1},{1,0},{2,3},{3,2},{4,5},{5,4},{6,7},{7,6},{8,9},{9,8},{10,11... | collective-permute-start | bytes 147464 | tf_op jit(solution)/shard_map/ppermute | solution.py:52
  15.7 1.1 fusion.19
  17.9 1.6 %collective-permute-start.1 = (bf16[2,16,1536]{2,1,0:T(8,128)(2,1)S(1)}, bf16[2,16,1536]{2,1,0:T(8,128)(2,1)S(1)}, u32[]{:S(2)}, u32[]{:S(2)}) collective-permute-start(bf16[2,16,1536]{2,1,0:T(8,128)(2,1)S(1)} %maximum_select_fusion.1), channel_id=1, source_target_pairs={{0,2},{1,3},{2,0},{3,1},{4,6},{5,7},{6,4},{7,5},{8,10},{9,11},{10,... | collective-permute-start | bytes 294920 | tf_op jit(solution)/shard_map/ppermute | solution.py:52
  20.1 2.5 %collective-permute-done.1 = bf16[2,16,1536]{2,1,0:T(8,128)(2,1)S(1)} collective-permute-done((bf16[2,16,1536]{2,1,0:T(8,128)(2,1)S(1)}, bf16[2,16,1536]{2,1,0:T(8,128)(2,1)S(1)}, u32[]{:S(2)}, u32[]{:S(2)}) %collective-permute-start.1) | collective-permute-done | bytes 98336 | tf_op jit(solution)/shard_map/ppermute | solution.py:52
  22.6 1.8 %select_reduce_fusion = (f32[64,64]{1,0:T(8,128)S(1)}, f32[64,64]{1,0:T(8,128)S(1)}) fusion(pred[64,16]{0,1:T(8,128)(4,1)S(1)} %iota_compare_fusion.8, pred[64,16]{0,1:T(8,128)(4,1)S(1)} %iota_compare_fusion.9, bf16[64,1536,1]{1,0,2:T(8,128)(2,1)S(1)} %bitcast.85, bf16[16,64,1536]{2,1,0:T(8,128)(2,1)S(1)} %bitcast.73), kind=kOutput, calls=%fused_computation.35 | convolution fusion | flops 201580544 | bytes 3377152 | tf_op jit(solution)/shard_map/dot_general | solution.py:131
  26.4 1.7 %fusion.7 = f32[4,16,1536]{2,1,0:T(8,128)S(1)} fusion(bf16[1024,1536]{1,0:T(8,128)(2,1)S(1)} %copy-done, bf16[4,16,1024]{2,1,0:T(8,128)(2,1)} %tile.13, bf16[4,16,1024]{2,1,0:T(8,128)(2,1)} %tile.15, s32[4,16]{1,0:T(4,128)} %get-tuple-element.31, s32[4,16]{1,0:T(4,128)} %get-tuple-element.30, s32[1024]{0:T(1024)} %add_select_fusion.8), kind=kOutput, calls=%fused_computation.15 | convolution fusion | flops 201654272 | bytes 3805696 | tf_op jit(solution)/shard_map/dot_general | solution.py:141
  28.8 1.5 %collective-permute-start.4 = (f32[16,1536]{1,0:T(8,128)}, f32[16,1536]{1,0:T(8,128)}, u32[]{:S(2)}, u32[]{:S(2)}) collective-permute-start(f32[16,1536]{1,0:T(8,128)} %get-tuple-element.17), channel_id=1, source_target_pairs={{0,3},{1,2},{2,1},{3,0},{4,7},{5,6},{6,5},{7,4},{8,11},{9,10},{10,... | collective-permute-start | bytes 294920 | tf_op jit(solution)/shard_map/ppermute | solution.py:93
  30.4 1.9 %collective-permute-start.2 = (f32[16,1536]{1,0:T(8,128)}, f32[16,1536]{1,0:T(8,128)}, u32[]{:S(2)}, u32[]{:S(2)}) collective-permute-start(f32[16,1536]{1,0:T(8,128)} %get-tuple-element.16), channel_id=1, source_target_pairs={{0,1},{1,0},{2,3},{3,2},{4,5},{5,4},{6,7},{7,6},{8,9},{9,8},{10,11... | collective-permute-start | bytes 294920 | tf_op jit(solution)/shard_map/ppermute | solution.py:93
  32.9 1.8 %collective-permute-done.4 = f32[16,1536]{1,0:T(8,128)} collective-permute-done((f32[16,1536]{1,0:T(8,128)}, f32[16,1536]{1,0:T(8,128)}, u32[]{:S(2)}, u32[]{:S(2)}) %collective-permute-start.4) | collective-permute-done | bytes 98336 | tf_op jit(solution)/shard_map/ppermute | solution.py:93
  36.9 8.4 %multiply_reduce_fusion = (f32[1536]{0:T(1024)S(1)}, f32[1536]{0:T(1024)S(1)}, f32[1600,1536]{1,0:T(8,128)S(1)}) fusion(f32[1600,1536]{1,0:T(8,128)} %copy-done.1, f32[1536]{0:T(1024)} %param.11, f32[1536]{0:T(1024)} %param.10, bf16[16,1536]{1,0:T(8,128)(2,1)S(1)} %get-tuple-element.24, bf16[16,1536]{1,0:T(8,128)(2,1)S(1)} %get-tuple-element.23, ...), kind=kOutput, calls=%fused_computation.1 | convolution fusion | flops 268778496 | bytes 19884032 | tf_op jit(solution)/shard_map/dot_general | solution.py:180
  45.3 4.5 %fusion.2 = f32[1536,384]{1,0:T(8,128)} fusion(bf16[1600,384]{1,0:T(8,128)(2,1)S(1)} %copy-done.4, f32[1600,1536]{1,0:T(8,128)S(1)} %get-tuple-element.29, f32[1536]{0:T(1024)S(1)} %copy-done.18), kind=kOutput, calls=%fused_computation.8 | convolution fusion | flops 1892352000 | bytes 13424640 | tf_op jit(solution)/shard_map/dot_general | solution.py:187
  50.1 2.4 %fusion.21 = f32[4,1,200,384]{3,2,0,1:T(8,128)} fusion(s32[]{:T(128)S(6)} %select_n.412, f32[4,2,1,192,384]{4,3,1,0,2:T(8,128)} %bitcast.74, f32[4,2,1,8,384]{4,3,1,0,2:T(8,128)S(1)} %bitcast.83), kind=kLoop, calls=%fused_computation.28 | loop fusion | flops 307200 | bytes 3686404 | tf_op jit(solution)/shard_map/jit(dynamic_index_in_dim)/squeeze | solution.py:68
  52.5 3.3 %collective-permute-done.5 = f32[4,1,200,384]{3,2,0,1:T(8,128)} collective-permute-done((f32[4,1,200,384]{3,2,0,1:T(8,128)}, f32[4,1,200,384]{3,2,0,1:T(8,128)}, u32[]{:S(2)}, u32[]{:S(2)}) %collective-permute-start.5) | collective-permute-done | bytes 1228832 | tf_op jit(solution)/shard_map/ppermute | solution.py:69
  55.8 1.8 %fusion.24 = f32[4,1,200,384]{3,2,0,1:T(8,128)S(1)} fusion(f32[4,1,200,384]{3,2,0,1:T(8,128)} %collective-permute-done.5, s32[]{:T(128)S(6)} %select_n.411, f32[4,2,1,192,384]{4,3,1,0,2:T(8,128)} %bitcast.75, f32[4,2,1,8,384]{4,3,1,0,2:T(8,128)S(1)} %bitcast.84), kind=kLoop, calls=%fused_computation.31 | loop fusion | flops 614400 | bytes 4915204 | tf_op jit(solution)/shard_map/add | solution.py:70
  59.4 1.6 %collective-permute-start.6 = (f32[2,1,200,384]{3,2,1,0:T(8,128)}, f32[2,1,200,384]{3,2,1,0:T(8,128)}, u32[]{:S(2)}, u32[]{:S(2)}) collective-permute-start(f32[2,1,200,384]{3,2,1,0:T(8,128)} %dynamic-slice_bitcast_fusion), channel_id=1, source_target_pairs={{0,8},{4,12},{8,0},{12,4},{16,24},{20,28},{24,16},{28,20},{1,9},{5... | collective-permute-start | bytes 1843208 | tf_op jit(solution)/shard_map/ppermute | solution.py:69
  61.3 1.2 %select_n.422 = bf16[64,8,192]{2,1,0:T(8,128)(2,1)S(1)} reshape(bf16[4,16,1536]{2,1,0:T(8,128)(2,1)} %copy-done.5) | data formatting | bytes 393216 | tf_op jit(solution)/shard_map/jit(_where)/select_n | solution.py:54
  62.8 1.5 %reshape.606 = bf16[8,161,128]{2,1,0:T(8,128)(2,1)} reshape(bf16[8,64,322]{2,1,0:T(8,128)(2,1)S(1)} %pad_maximum_fusion) | data formatting | bytes 659456 | tf_op jit(solution)/shard_map/reshape | solution.py:164
  64.3 3.9 %all-to-all-start = ((bf16[8,161,128]{2,1,0:T(8,128)(2,1)}), bf16[8,161,128]{2,1,0:T(8,128)(2,1)S(1)}, u32[]{:S(2)}, u32[]{:S(2)}) async-start(bf16[8,161,128]{2,1,0:T(8,128)(2,1)} %reshape.606), calls=%async_computation | async-start | bytes 688128 | tf_op jit(solution)/shard_map/all_to_all | solution.py:163
  68.2 10.1 %collective-permute-done.6 = f32[2,1,200,384]{3,2,1,0:T(8,128)} collective-permute-done((f32[2,1,200,384]{3,2,1,0:T(8,128)}, f32[2,1,200,384]{3,2,1,0:T(8,128)}, u32[]{:S(2)}, u32[]{:S(2)}) %collective-permute-start.6) | collective-permute-done | bytes 614432 | tf_op jit(solution)/shard_map/ppermute | solution.py:69
  78.3 1.3 %bitcast_add_fusion = f32[2,1,200,384]{3,2,1,0:T(8,128)S(1)} fusion(f32[2,1,200,384]{3,2,1,0:T(8,128)} %collective-permute-done.6, f32[2,2,1,200,384]{4,3,1,0,2:T(8,128)} %bitcast.77, s32[]{:T(128)S(6)} %select_n.415), kind=kLoop, calls=%fused_computation.33 | loop fusion | flops 153600 | bytes 1843204 | tf_op jit(solution)/shard_map/add | solution.py:70
  81.2 3.5 %collective-permute-start.7 = (f32[1,1,200,384]{3,2,1,0:T(8,128)}, f32[1,1,200,384]{3,2,1,0:T(8,128)}, u32[]{:S(2)}, u32[]{:S(2)}) collective-permute-start(f32[1,1,200,384]{3,2,1,0:T(8,128)} %constant_dynamic-slice_fusion), channel_id=1, source_target_pairs={{0,16},{4,20},{8,24},{12,28},{16,0},{20,4},{24,8},{28,12},{1,17},{... | collective-permute-start | bytes 921608 | tf_op jit(solution)/shard_map/ppermute | solution.py:69
  84.7 1.7 %reshape.607 = bf16[8,64,322]{2,1,0:T(8,128)(2,1)} reshape(bf16[8,161,128]{2,1,0:T(8,128)(2,1)S(1)} %all-to-all-done) | data formatting | bytes 659456 | tf_op jit(solution)/shard_map/reshape | solution.py:166
  87.5 9.2 %collective-permute-done.7 = f32[1,1,200,384]{3,2,1,0:T(8,128)} collective-permute-done((f32[1,1,200,384]{3,2,1,0:T(8,128)}, f32[1,1,200,384]{3,2,1,0:T(8,128)}, u32[]{:S(2)}, u32[]{:S(2)}) %collective-permute-start.7) | collective-permute-done | bytes 307232 | tf_op jit(solution)/shard_map/ppermute | solution.py:69
  96.7 1.8 %add_bitcast_fusion = f32[200,384]{1,0:T(8,128)} fusion(f32[1,1,200,384]{3,2,1,0:T(8,128)} %collective-permute-done.7, f32[2,1,200,384]{3,2,1,0:T(8,128)} %copy-done.3, s32[]{:T(128)S(6)} %select_n.419), kind=kLoop, calls=%fused_computation.41 | loop fusion | flops 76800 | bytes 921604 | tf_op jit(solution)/shard_map/squeeze;reshape | solution.py:204
  98.5 1.4 %collective-permute-start.8 = (f32[200,384]{1,0:T(8,128)}, f32[200,384]{1,0:T(8,128)}, u32[]{:S(2)}, u32[]{:S(2)}) collective-permute-start(f32[200,384]{1,0:T(8,128)} %add_bitcast_fusion), channel_id=1, source_target_pairs={{0,1},{1,0},{2,3},{3,2},{4,5},{5,4},{6,7},{7,6},{8,9},{9,8},{10,11... | collective-permute-start | bytes 921608 | tf_op jit(solution)/shard_map/ppermute | solution.py:80
  103.7 1.7 %copy.64 = bf16[512,64]{0,1:T(8,128)(2,1)} copy(bf16[512,64]{1,0:T(8,128)(2,1)} %get-tuple-element.20) | data formatting | bytes 131072 | tf_op jit(solution)/shard_map/slice | solution.py:172
  107.2 1.6 %collective-permute-start.9 = (f32[200,384]{1,0:T(8,128)S(1)}, f32[200,384]{1,0:T(8,128)S(1)}, u32[]{:S(2)}, u32[]{:S(2)}) collective-permute-start(f32[200,384]{1,0:T(8,128)S(1)} %add.290), channel_id=1, source_target_pairs={{0,2},{1,3},{2,0},{3,1},{4,6},{5,7},{6,4},{7,5},{8,10},{9,11},{10,... | collective-permute-start | bytes 921608 | tf_op jit(solution)/shard_map/ppermute | solution.py:80
  108.7 1.4 %fusion.25 = bf16[512,16,64]{0,2,1:T(8,128)(2,1)S(1)} fusion(s32[512]{0:T(512)S(1)} %bitcast.87, s32[512]{0:T(512)S(1)} %bitcast.88, s32[16,64]{1,0:T(8,128)S(1)} %add_select_fusion.5, bf16[512,64]{0,1:T(8,128)(2,1)} %copy.64, bf16[512,64]{0,1:T(8,128)(2,1)} %copy.62), kind=kLoop, calls=%fused_computation.32 | loop fusion | flops 2621440 | bytes 1187840 | tf_op jit(solution)/shard_map/add | solution.py:18
  110.2 1.4 %fusion.83 = f32[1024,192]{0,1:T(8,128)} fusion(bf16[512,1024]{0,1:T(8,128)(2,1)S(1)} %bitcast.78, bf16[512,192]{1,0:T(8,128)(2,1)S(1)} %bitcast.81), kind=kOutput, calls=%fused_computation.193 | convolution fusion | flops 201326592 | bytes 2031616 | tf_op jit(solution)/shard_map/dot_general | solution.py:176
  111.6 2.5 %collective-permute-done.9 = f32[200,384]{1,0:T(8,128)S(1)} collective-permute-done((f32[200,384]{1,0:T(8,128)S(1)}, f32[200,384]{1,0:T(8,128)S(1)}, u32[]{:S(2)}, u32[]{:S(2)}) %collective-permute-start.9) | collective-permute-done | bytes 307232 | tf_op jit(solution)/shard_map/ppermute | solution.py:80
  (111 shorter events, 21.2 us)
Async XLA Ops:
  0.6 22.0 %copy-start = (bf16[1024,1536]{1,0:T(8,128)(2,1)S(1)}, bf16[1024,1536]{1,0:T(8,128)(2,1)}, u32[]{:S(2)}) copy-start(bf16[1024,1536]{1,0:T(8,128)(2,1)} %param.12) | copy-start | bytes 9437188
  0.7 4.5 %copy-start.8 = (s32[1600]{0:T(1024)}, s32[1600]{0:T(1024)S(1)}, u32[]{:S(2)}) copy-start(s32[1600]{0:T(1024)S(1)} %add_select_fusion.7) | copy-start | bytes 19204
  0.7 4.5 %copy-start.16 = (f32[1536]{0:T(1024)S(1)}, f32[1536]{0:T(1024)}, u32[]{:S(2)}) copy-start(f32[1536]{0:T(1024)} %param.11) | copy-start | bytes 18436
  0.7 4.5 %copy-start.17 = (f32[1536]{0:T(1024)S(1)}, f32[1536]{0:T(1024)}, u32[]{:S(2)}) copy-start(f32[1536]{0:T(1024)} %param.10) | copy-start | bytes 18436
  5.2 5.7 %copy-start.1 = (f32[1600,1536]{1,0:T(8,128)}, f32[1600,1536]{1,0:T(8,128)S(1)}, u32[]{:S(2)}) copy-start(f32[1600,1536]{1,0:T(8,128)S(1)} %fusion.82) | copy-start | bytes 29491204
  5.2 8.7 %copy-start.10 = (s32[64,64]{1,0:T(8,128)S(1)}, s32[64,64]{1,0:T(8,128)}, u32[]{:S(2)}) copy-start(s32[64,64]{1,0:T(8,128)} %param.14) | copy-start | bytes 49156
  5.3 9.4 %copy-start.15 = (s32[64]{0:T(128)S(1)}, s32[64]{0:T(128)}, u32[]{:S(2)}) copy-start(s32[64]{0:T(128)} %param.13) | copy-start | bytes 772
  10.9 6.9 %collective-permute-start = (bf16[1,16,1536]{2,1,0:T(8,128)(2,1)S(1)}, bf16[1,16,1536]{2,1,0:T(8,128)(2,1)S(1)}, u32[]{:S(2)}, u32[]{:S(2)}) collective-permute-start(bf16[1,16,1536]{2,1,0:T(8,128)(2,1)S(1)} %fusion.15), channel_id=1, source_target_pairs={{0,1},{1,0},{2,3},{3,2},{4,5},{5,4},{6,7},{7,6},{8,9},{9,8},{10,11... | collective-permute-start | bytes 147464 | tf_op jit(solution)/shard_map/ppermute | solution.py:52
  14.8 0.5 copy-start.11
  14.8 0.5 copy-start.13
  17.9 4.7 %collective-permute-start.1 = (bf16[2,16,1536]{2,1,0:T(8,128)(2,1)S(1)}, bf16[2,16,1536]{2,1,0:T(8,128)(2,1)S(1)}, u32[]{:S(2)}, u32[]{:S(2)}) collective-permute-start(bf16[2,16,1536]{2,1,0:T(8,128)(2,1)S(1)} %maximum_select_fusion.1), channel_id=1, source_target_pairs={{0,2},{1,3},{2,0},{3,1},{4,6},{5,7},{6,4},{7,5},{8,10},{9,11},{10,... | collective-permute-start | bytes 294920 | tf_op jit(solution)/shard_map/ppermute | solution.py:52
  22.6 1.8 %copy-start.5 = (bf16[4,16,1536]{2,1,0:T(8,128)(2,1)}, bf16[4,16,1536]{2,1,0:T(8,128)(2,1)S(1)}, u32[]{:S(2)}) copy-start(bf16[4,16,1536]{2,1,0:T(8,128)(2,1)S(1)} %maximum_select_fusion) | copy-start | bytes 589828
  25.5 0.9 copy-start.6
  26.4 5.9 %copy-start.9 = (s32[1600]{0:T(1024)S(1)}, s32[1600]{0:T(1024)}, u32[]{:S(2)}) copy-start(s32[1600]{0:T(1024)} %copy-done.8) | copy-start | bytes 19204
  28.8 5.9 %collective-permute-start.4 = (f32[16,1536]{1,0:T(8,128)}, f32[16,1536]{1,0:T(8,128)}, u32[]{:S(2)}, u32[]{:S(2)}) collective-permute-start(f32[16,1536]{1,0:T(8,128)} %get-tuple-element.17), channel_id=1, source_target_pairs={{0,3},{1,2},{2,1},{3,0},{4,7},{5,6},{6,5},{7,4},{8,11},{9,10},{10,... | collective-permute-start | bytes 294920 | tf_op jit(solution)/shard_map/ppermute | solution.py:93
  30.3 5.4 %collective-permute-start.3 = (f32[16,1536]{1,0:T(8,128)}, f32[16,1536]{1,0:T(8,128)}, u32[]{:S(2)}, u32[]{:S(2)}) collective-permute-start(f32[16,1536]{1,0:T(8,128)} %get-tuple-element.18), channel_id=1, source_target_pairs={{0,2},{1,3},{2,0},{3,1},{4,6},{5,7},{6,4},{7,5},{8,10},{9,11},{10,... | collective-permute-start | bytes 294920 | tf_op jit(solution)/shard_map/ppermute | solution.py:93
  30.4 5.4 %collective-permute-start.2 = (f32[16,1536]{1,0:T(8,128)}, f32[16,1536]{1,0:T(8,128)}, u32[]{:S(2)}, u32[]{:S(2)}) collective-permute-start(f32[16,1536]{1,0:T(8,128)} %get-tuple-element.16), channel_id=1, source_target_pairs={{0,1},{1,0},{2,3},{3,2},{4,5},{5,4},{6,7},{7,6},{8,9},{9,8},{10,11... | collective-permute-start | bytes 294920 | tf_op jit(solution)/shard_map/ppermute | solution.py:93
  36.8 8.5 %copy-start.4 = (bf16[1600,384]{1,0:T(8,128)(2,1)S(1)}, bf16[1600,384]{1,0:T(8,128)(2,1)}, u32[]{:S(2)}) copy-start(bf16[1600,384]{1,0:T(8,128)(2,1)} %param.8) | copy-start | bytes 3686404
  36.9 8.5 %copy-start.18 = (f32[1536]{0:T(1024)S(1)}, f32[1536]{0:T(1024)}, u32[]{:S(2)}) copy-start(f32[1536]{0:T(1024)} %param.10) | copy-start | bytes 18436
  52.5 8.5 %copy-start.14 = (s32[64]{0:T(128)S(1)}, s32[64]{0:T(128)}, u32[]{:S(2)}) copy-start(s32[64]{0:T(128)} %copy-done.13) | copy-start | bytes 772
  52.5 8.6 %copy-start.12 = (s32[64]{0:T(128)S(1)}, s32[64]{0:T(128)}, u32[]{:S(2)}) copy-start(s32[64]{0:T(128)} %copy-done.11) | copy-start | bytes 772
  52.5 3.3 %collective-permute-start.5 = (f32[4,1,200,384]{3,2,0,1:T(8,128)}, f32[4,1,200,384]{3,2,0,1:T(8,128)}, u32[]{:S(2)}, u32[]{:S(2)}) collective-permute-start(f32[4,1,200,384]{3,2,0,1:T(8,128)} %fusion.21), channel_id=1, source_target_pairs={{0,4},{4,0},{8,12},{12,8},{16,20},{20,16},{24,28},{28,24},{1,5},{5... | collective-permute-start | bytes 3686408 | tf_op jit(solution)/shard_map/ppermute | solution.py:69
  52.5 10.0 %copy-start.7 = (bf16[64,64]{1,0:T(8,128)(2,1)S(1)}, bf16[64,64]{1,0:T(8,128)(2,1)}, u32[]{:S(2)}) copy-start(bf16[64,64]{1,0:T(8,128)(2,1)} %copy-done.6) | copy-start | bytes 24580
  57.5 1.1 copy-start.2
  59.4 18.9 %collective-permute-start.6 = (f32[2,1,200,384]{3,2,1,0:T(8,128)}, f32[2,1,200,384]{3,2,1,0:T(8,128)}, u32[]{:S(2)}, u32[]{:S(2)}) collective-permute-start(f32[2,1,200,384]{3,2,1,0:T(8,128)} %dynamic-slice_bitcast_fusion), channel_id=1, source_target_pairs={{0,8},{4,12},{8,0},{12,4},{16,24},{20,28},{24,16},{28,20},{1,9},{5... | collective-permute-start | bytes 1843208 | tf_op jit(solution)/shard_map/ppermute | solution.py:69
  64.3 20.4 %all-to-all-start = ((bf16[8,161,128]{2,1,0:T(8,128)(2,1)}), bf16[8,161,128]{2,1,0:T(8,128)(2,1)S(1)}, u32[]{:S(2)}, u32[]{:S(2)}) async-start(bf16[8,161,128]{2,1,0:T(8,128)(2,1)} %reshape.606), calls=%async_computation | async-start | bytes 688128 | tf_op jit(solution)/shard_map/all_to_all | solution.py:163
  79.6 0.8 copy-start.3
  81.2 15.5 %collective-permute-start.7 = (f32[1,1,200,384]{3,2,1,0:T(8,128)}, f32[1,1,200,384]{3,2,1,0:T(8,128)}, u32[]{:S(2)}, u32[]{:S(2)}) collective-permute-start(f32[1,1,200,384]{3,2,1,0:T(8,128)} %constant_dynamic-slice_fusion), channel_id=1, source_target_pairs={{0,16},{4,20},{8,24},{12,28},{16,0},{20,4},{24,8},{28,12},{1,17},{... | collective-permute-start | bytes 921608 | tf_op jit(solution)/shard_map/ppermute | solution.py:69
  98.5 7.6 %collective-permute-start.8 = (f32[200,384]{1,0:T(8,128)}, f32[200,384]{1,0:T(8,128)}, u32[]{:S(2)}, u32[]{:S(2)}) collective-permute-start(f32[200,384]{1,0:T(8,128)} %add_bitcast_fusion), channel_id=1, source_target_pairs={{0,1},{1,0},{2,3},{3,2},{4,5},{5,4},{6,7},{7,6},{8,9},{9,8},{10,11... | collective-permute-start | bytes 921608 | tf_op jit(solution)/shard_map/ppermute | solution.py:80
  103.7 6.5 %slice-start = ((bf16[8,64,322]{2,1,0:T(8,128)(2,1)}), bf16[8,64,192]{2,1,0:T(8,128)(2,1)S(1)}, s32[]{:S(2)}) async-start(bf16[8,64,322]{2,1,0:T(8,128)(2,1)} %reshape.607), calls=%async_computation.1 | async-start | bytes 524288 | tf_op jit(solution)/shard_map/slice | solution.py:169
  107.2 6.9 %collective-permute-start.9 = (f32[200,384]{1,0:T(8,128)S(1)}, f32[200,384]{1,0:T(8,128)S(1)}, u32[]{:S(2)}, u32[]{:S(2)}) collective-permute-start(f32[200,384]{1,0:T(8,128)S(1)} %add.290), channel_id=1, source_target_pairs={{0,2},{1,3},{2,0},{3,1},{4,6},{5,7},{6,4},{7,5},{8,10},{9,11},{10,... | collective-permute-start | bytes 921608 | tf_op jit(solution)/shard_map/ppermute | solution.py:80

commit v18 on v12

--- a/solution.py
+++ b/solution.py
@@ -190,10 +190,29 @@
         [gain_term.reshape(n_dp, chunk), shift_term.reshape(n_dp, chunk)], axis=1
     )
     side_rows = jnp.pad(side_rows, ((0, 0), (0, pad_rows * e_size - 2 * chunk)))
-    stacked = jnp.concatenate(
-        [head_term.reshape(n_dp, chunk, e_size), side_rows.reshape(n_dp, pad_rows, e_size)], axis=1
-    )
-    (part,) = halving_scatter([stacked], "dp")
+    dp_idx = lax.axis_index("dp")
+    mine = dp_idx % 2
+    head_pairs = head_term.reshape(n_dp // 2, 2, chunk, e_size)
+    side_pairs = side_rows.reshape(n_dp // 2, 2, pad_rows, e_size)
+
+    def half(which):
+        return jnp.concatenate(
+            [
+                lax.dynamic_index_in_dim(head_pairs, which, axis=1, keepdims=False),
+                lax.dynamic_index_in_dim(side_pairs, which, axis=1, keepdims=False),
+            ],
+            axis=1,
+        )
+
+    part = half(mine) + lax.ppermute(half(1 - mine), "dp", partners(n_dp, 0))
+    bit = 1
+    while (1 << bit) < n_dp:
+        pairs = part.reshape((part.shape[0] // 2, 2) + part.shape[1:])
+        own = (dp_idx // (1 << bit)) % 2
+        keep = lax.dynamic_index_in_dim(pairs, own, axis=1, keepdims=False)
+        give = lax.dynamic_index_in_dim(pairs, 1 - own, axis=1, keepdims=False)
+        part = keep + lax.ppermute(give, "dp", partners(n_dp, bit))
+        bit += 1
     (total,) = butterfly_sum([part[0]], "leaf")
     side_flat = total[chunk:].reshape(-1)
     side_sum = jnp.stack([side_flat[:chunk], side_flat[chunk : 2 * chunk]], axis=1)

time: 117 us -> 121 us (1.034)
  matrix products: 27.7 us -> 32.1 us
  other arithmetic: 15.7 us -> 14.4 us
    dot_general x1, matrix products: 8.21 us -> 11.1 us  [shards(): jnp.dot(jnp.concatenate([select.T.astype(jnp.bfloat16)] * 3, axis=1), jnp...]
    another operation x1 -> x0, other arithmetic: 1.8 us -> none  [shards(): total, = butterfly_sum([part[0]], 'leaf')]
    dot_general x1, matrix products: 4.48 us -> 6.01 us  [shards(): lax.dot_general(lin_grad, features, (((0,), (0,)), ((), ())), preferred_e...]
    squeeze x2 -> x4, local copies, waits for them, and re-layouts: 1.59 us -> 2.79 us  [the longest x2 1.6 us: shards(): give = lax.dynamic_index_in_dim(pairs, 1 - own, axis=1, keepdims=False)]
    unnamed x44 -> x42, local copies, waits for them, and re-layouts: 5.53 us -> 5.52 us
  transfers between devices with their start and end apart: 11 -> 11, of which waited for: 9 -> 9; matrix products, arithmetic and copies ran while one was open for 16% -> 15% of each run, Pallas kernels for 0% -> 0%
where the time goes in v18:
time: 121 us; the launch traced here: 120 us
  waiting for transfers between devices  33.9 us (28%)
  matrix products  32.1 us (27%)
  starting transfers between devices  20.5 us (17%)
  local copies, waits for them, and re-layouts  17.7 us (15%)
  other arithmetic  14.4 us (12%)
    ppermute x2, waiting for transfers between devices, shards(): part = keep + lax.ppermute(give, 'dp', partners(n_dp, bit))  21.7 us
    dot_general x1, matrix products, shards(): jnp.dot(jnp.concatenate([select.T.astype(jnp.bfloat16)] * 3, axis=1), jnp...  11.1 us
    dot_general x1, matrix products, shards(): lax.dot_general(lin_grad, features, (((0,), (0,)), ((), ())), preferred_e...  6.01 us
    dot_general x1, matrix products, shards(): jnp.dot(select, active, precision=HIGHEST, preferred_element_type=jnp.flo...  5.63 us
    unnamed x42, local copies, waits for them, and re-layouts  5.52 us
    ppermute x2, starting transfers between devices, shards(): part = keep + lax.ppermute(give, 'dp', partners(n_dp, bit))  5.37 us
    ppermute x2, starting transfers between devices, doubling_gather(): other = lax.ppermute(cur, name, partners(size, bit))  4.59 us
    dot_general x1, matrix products, shards(): jnp.dot(features, head_weight, preferred_element_type=jnp.float32)  4.5 us
  transfers between devices with their start and end apart: 11, of which 9 were waited for; matrix products, arithmetic and copies ran while one was open for 15% of the time, Pallas kernels for 0%

profile of v18, /device:TPU:0, one launch (start us, length us, event | category | flops | bytes accessed | tf_op | source)
XLA Modules:
  0.0 119.9 jit_solution(3498506683108996012)
XLA Ops:
  0.7 4.5 %fusion.77 = f32[1600,1536]{1,0:T(8,128)S(1)} fusion(bf16[1600,384]{1,0:T(8,128)(2,1)} %param.8, bf16[384,1536]{1,0:T(8,128)(2,1)} %param.9), kind=kOutput, calls=%fused_computation.189 | convolution fusion | flops 1887436800 | bytes 12238848 | tf_op jit(solution)/shard_map/dot_general | solution.py:111
  5.3 5.6 %fusion.15 = bf16[1,16,1536]{2,1,0:T(8,128)(2,1)S(1)} fusion(f32[1600,1536]{1,0:T(8,128)S(1)} %fusion.77, f32[1536]{0:T(1024)S(1)} %copy-done.15, f32[1536]{0:T(1024)S(1)} %copy-done.16, s32[1600]{0:T(1024)S(1)} %add_select_fusion.7), kind=kOutput, calls=%fused_computation.17 | convolution fusion | flops 486679552 | bytes 9898240 | tf_op jit(solution)/shard_map/dot_general | solution.py:115
  10.9 3.0 %collective-permute-start = (bf16[1,16,1536]{2,1,0:T(8,128)(2,1)S(1)}, bf16[1,16,1536]{2,1,0:T(8,128)(2,1)S(1)}, u32[]{:S(2)}, u32[]{:S(2)}) collective-permute-start(bf16[1,16,1536]{2,1,0:T(8,128)(2,1)S(1)} %fusion.15), channel_id=1, source_target_pairs={{0,1},{1,0},{2,3},{3,2},{4,5},{5,4},{6,7},{7,6},{8,9},{9,8},{10,11... | collective-permute-start | bytes 147464 | tf_op jit(solution)/shard_map/ppermute | solution.py:52
  15.7 1.1 fusion.19
  17.9 1.6 %collective-permute-start.1 = (bf16[2,16,1536]{2,1,0:T(8,128)(2,1)S(1)}, bf16[2,16,1536]{2,1,0:T(8,128)(2,1)S(1)}, u32[]{:S(2)}, u32[]{:S(2)}) collective-permute-start(bf16[2,16,1536]{2,1,0:T(8,128)(2,1)S(1)} %maximum_select_fusion.1), channel_id=1, source_target_pairs={{0,2},{1,3},{2,0},{3,1},{4,6},{5,7},{6,4},{7,5},{8,10},{9,11},{10,... | collective-permute-start | bytes 294920 | tf_op jit(solution)/shard_map/ppermute | solution.py:52
  20.1 2.5 %collective-permute-done.1 = bf16[2,16,1536]{2,1,0:T(8,128)(2,1)S(1)} collective-permute-done((bf16[2,16,1536]{2,1,0:T(8,128)(2,1)S(1)}, bf16[2,16,1536]{2,1,0:T(8,128)(2,1)S(1)}, u32[]{:S(2)}, u32[]{:S(2)}) %collective-permute-start.1) | collective-permute-done | bytes 98336 | tf_op jit(solution)/shard_map/ppermute | solution.py:52
  22.6 1.8 %select_reduce_fusion = (f32[64,64]{1,0:T(8,128)S(1)}, f32[64,64]{1,0:T(8,128)S(1)}) fusion(pred[64,16]{0,1:T(8,128)(4,1)S(1)} %iota_compare_fusion.8, pred[64,16]{0,1:T(8,128)(4,1)S(1)} %iota_compare_fusion.9, bf16[64,1536,1]{1,0,2:T(8,128)(2,1)S(1)} %bitcast.83, bf16[16,64,1536]{2,1,0:T(8,128)(2,1)S(1)} %bitcast.74), kind=kOutput, calls=%fused_computation.30 | convolution fusion | flops 201580544 | bytes 3377152 | tf_op jit(solution)/shard_map/dot_general | solution.py:131
  26.4 1.7 %fusion.7 = f32[4,16,1536]{2,1,0:T(8,128)S(1)} fusion(bf16[1024,1536]{1,0:T(8,128)(2,1)S(1)} %copy-done, bf16[4,16,1024]{2,1,0:T(8,128)(2,1)} %tile.13, bf16[4,16,1024]{2,1,0:T(8,128)(2,1)} %tile.15, s32[4,16]{1,0:T(4,128)} %get-tuple-element.35, s32[4,16]{1,0:T(4,128)} %get-tuple-element.34, s32[1024]{0:T(1024)} %add_select_fusion.8), kind=kOutput, calls=%fused_computation.13 | convolution fusion | flops 201654272 | bytes 3805696 | tf_op jit(solution)/shard_map/dot_general | solution.py:141
  28.8 1.5 %collective-permute-start.4 = (f32[16,1536]{1,0:T(8,128)}, f32[16,1536]{1,0:T(8,128)}, u32[]{:S(2)}, u32[]{:S(2)}) collective-permute-start(f32[16,1536]{1,0:T(8,128)} %get-tuple-element.19), channel_id=1, source_target_pairs={{0,3},{1,2},{2,1},{3,0},{4,7},{5,6},{6,5},{7,4},{8,11},{9,10},{10,... | collective-permute-start | bytes 294920 | tf_op jit(solution)/shard_map/ppermute | solution.py:93
  30.4 1.9 %collective-permute-start.2 = (f32[16,1536]{1,0:T(8,128)}, f32[16,1536]{1,0:T(8,128)}, u32[]{:S(2)}, u32[]{:S(2)}) collective-permute-start(f32[16,1536]{1,0:T(8,128)} %get-tuple-element.18), channel_id=1, source_target_pairs={{0,1},{1,0},{2,3},{3,2},{4,5},{5,4},{6,7},{7,6},{8,9},{9,8},{10,11... | collective-permute-start | bytes 294920 | tf_op jit(solution)/shard_map/ppermute | solution.py:93
  33.0 1.8 %collective-permute-done.4 = f32[16,1536]{1,0:T(8,128)} collective-permute-done((f32[16,1536]{1,0:T(8,128)}, f32[16,1536]{1,0:T(8,128)}, u32[]{:S(2)}, u32[]{:S(2)}) %collective-permute-start.4) | collective-permute-done | bytes 98336 | tf_op jit(solution)/shard_map/ppermute | solution.py:93
  36.9 11.1 %multiply_reduce_fusion = (f32[1536]{0:T(1024)S(1)}, f32[1536]{0:T(1024)S(1)}, f32[1600,1536]{1,0:T(8,128)}) fusion(f32[1600,1536]{1,0:T(8,128)} %copy-done.1, f32[1536]{0:T(1024)} %param.11, f32[1536]{0:T(1024)} %param.10, bf16[16,1536]{1,0:T(8,128)(2,1)S(1)} %get-tuple-element.28, bf16[16,1536]{1,0:T(8,128)(2,1)S(1)} %get-tuple-element.27, ...), kind=kOutput, calls=%fused_computation.1 | convolution fusion | flops 268778496 | bytes 19884032 | tf_op jit(solution)/shard_map/dot_general | solution.py:173
  48.2 6.0 %fusion.2 = f32[1536,384]{1,0:T(8,128)S(1)} fusion(bf16[1600,384]{1,0:T(8,128)(2,1)} %param.8, f32[1600,1536]{1,0:T(8,128)} %get-tuple-element.33, f32[1536]{0:T(1024)S(1)} %copy-done.17), kind=kOutput, calls=%fused_computation.8 | convolution fusion | flops 1892352000 | bytes 13424640 | tf_op jit(solution)/shard_map/dot_general | solution.py:180
  54.3 1.2 dynamic-slice_bitcast_fusion.1
  55.5 1.1 pad_maximum_fusion
  56.6 3.3 %collective-permute-done.5 = f32[4,200,384]{2,1,0:T(8,128)} collective-permute-done((f32[4,200,384]{2,1,0:T(8,128)}, f32[4,200,384]{2,1,0:T(8,128)}, u32[]{:S(2)}, u32[]{:S(2)}) %collective-permute-start.5) | collective-permute-done | bytes 1228832 | tf_op jit(solution)/shard_map/ppermute | solution.py:207
  59.8 1.8 %maximum_add_fusion = f32[4,200,384]{2,1,0:T(8,128)S(1)} fusion(f32[4,200,384]{2,1,0:T(8,128)} %collective-permute-done.5, f32[4,8,384]{2,1,0:T(8,128)S(1)} %get-tuple-element.25, f32[4,192,384]{2,1,0:T(8,128)} %get-tuple-element.16), kind=kLoop, calls=%fused_computation.23 | loop fusion | flops 614400 | bytes 3686400 | tf_op jit(solution)/shard_map/add | solution.py:207
  63.5 1.6 %collective-permute-start.6 = (f32[2,200,384]{2,1,0:T(8,128)}, f32[2,200,384]{2,1,0:T(8,128)}, u32[]{:S(2)}, u32[]{:S(2)}) collective-permute-start(f32[2,200,384]{2,1,0:T(8,128)} %dynamic-slice_bitcast_fusion.2), channel_id=1, source_target_pairs={{0,8},{4,12},{8,0},{12,4},{16,24},{20,28},{24,16},{28,20},{1,9},{5... | collective-permute-start | bytes 1843208 | tf_op jit(solution)/shard_map/ppermute | solution.py:214
  65.3 1.2 select_n.424
  67.6 4.1 %all-to-all-start = ((bf16[8,64,322]{2,1,0:T(8,128)(2,1)}), bf16[8,64,322]{2,1,0:T(8,128)(2,1)}, u32[]{:S(2)}, u32[]{:S(2)}) async-start(bf16[8,64,322]{2,1,0:T(8,128)(2,1)} %pad_maximum_fusion.1), calls=%async_computation | async-start | bytes 786432 | tf_op jit(solution)/shard_map/all_to_all | solution.py:161
  71.7 10.9 %collective-permute-done.6 = f32[2,200,384]{2,1,0:T(8,128)} collective-permute-done((f32[2,200,384]{2,1,0:T(8,128)}, f32[2,200,384]{2,1,0:T(8,128)}, u32[]{:S(2)}, u32[]{:S(2)}) %collective-permute-start.6) | collective-permute-done | bytes 614432 | tf_op jit(solution)/shard_map/ppermute | solution.py:214
  82.6 1.3 %bitcast_add_fusion = f32[2,200,384]{2,1,0:T(8,128)S(1)} fusion(f32[2,200,384]{2,1,0:T(8,128)} %collective-permute-done.6, f32[2,2,200,384]{3,2,1,0:T(8,128)} %bitcast.76, s32[]{:T(128)S(6)} %select_n.417), kind=kLoop, calls=%fused_computation.28 | loop fusion | flops 153600 | bytes 1843204 | tf_op jit(solution)/shard_map/add | solution.py:214
  85.5 3.8 %collective-permute-start.7 = (f32[1,200,384]{2,1,0:T(8,128)}, f32[1,200,384]{2,1,0:T(8,128)}, u32[]{:S(2)}, u32[]{:S(2)}) collective-permute-start(f32[1,200,384]{2,1,0:T(8,128)} %constant_dynamic-slice_fusion), channel_id=1, source_target_pairs={{0,16},{4,20},{8,24},{12,28},{16,0},{20,4},{24,8},{28,12},{1,17},{... | collective-permute-start | bytes 921608 | tf_op jit(solution)/shard_map/ppermute | solution.py:214
  89.3 1.1 slice.74
  90.4 10.8 %collective-permute-done.7 = f32[1,200,384]{2,1,0:T(8,128)} collective-permute-done((f32[1,200,384]{2,1,0:T(8,128)}, f32[1,200,384]{2,1,0:T(8,128)}, u32[]{:S(2)}, u32[]{:S(2)}) %collective-permute-start.7) | collective-permute-done | bytes 307232 | tf_op jit(solution)/shard_map/ppermute | solution.py:214
  101.2 1.8 %add_bitcast_fusion = f32[200,384]{1,0:T(8,128)} fusion(f32[1,200,384]{2,1,0:T(8,128)} %collective-permute-done.7, f32[2,200,384]{2,1,0:T(8,128)} %copy-done.3, s32[]{:T(128)S(6)} %select_n.421), kind=kLoop, calls=%fused_computation.36 | loop fusion | flops 76800 | bytes 921604 | tf_op jit(solution)/shard_map/squeeze | solution.py:216
  103.0 1.4 %collective-permute-start.8 = (f32[200,384]{1,0:T(8,128)}, f32[200,384]{1,0:T(8,128)}, u32[]{:S(2)}, u32[]{:S(2)}) collective-permute-start(f32[200,384]{1,0:T(8,128)} %add_bitcast_fusion), channel_id=1, source_target_pairs={{0,1},{1,0},{2,3},{3,2},{4,5},{5,4},{6,7},{7,6},{8,9},{9,8},{10,11... | collective-permute-start | bytes 921608 | tf_op jit(solution)/shard_map/ppermute | solution.py:80
  109.3 1.1 collective-permute-done.8
  110.4 1.1 add.292
  111.5 1.6 %collective-permute-start.9 = (f32[200,384]{1,0:T(8,128)S(1)}, f32[200,384]{1,0:T(8,128)S(1)}, u32[]{:S(2)}, u32[]{:S(2)}) collective-permute-start(f32[200,384]{1,0:T(8,128)S(1)} %add.292), channel_id=1, source_target_pairs={{0,2},{1,3},{2,0},{3,1},{4,6},{5,7},{6,4},{7,5},{8,10},{9,11},{10,... | collective-permute-start | bytes 921608 | tf_op jit(solution)/shard_map/ppermute | solution.py:80
  114.6 1.4 %fusion.78 = f32[1024,192]{0,1:T(8,128)} fusion(bf16[512,1024]{0,1:T(8,128)(2,1)S(1)} %bitcast.77, bf16[512,192]{1,0:T(8,128)(2,1)S(1)} %bitcast.82), kind=kOutput, calls=%fused_computation.190 | convolution fusion | flops 201326592 | bytes 2031616 | tf_op jit(solution)/shard_map/dot_general | solution.py:169
  116.0 2.4 %collective-permute-done.9 = f32[200,384]{1,0:T(8,128)S(1)} collective-permute-done((f32[200,384]{1,0:T(8,128)S(1)}, f32[200,384]{1,0:T(8,128)S(1)}, u32[]{:S(2)}, u32[]{:S(2)}) %collective-permute-start.9) | collective-permute-done | bytes 307232 | tf_op jit(solution)/shard_map/ppermute | solution.py:80
  (108 shorter events, 21.7 us)
Async XLA Ops:
  0.6 22.0 %copy-start = (bf16[1024,1536]{1,0:T(8,128)(2,1)S(1)}, bf16[1024,1536]{1,0:T(8,128)(2,1)}, u32[]{:S(2)}) copy-start(bf16[1024,1536]{1,0:T(8,128)(2,1)} %param.12) | copy-start | bytes 9437188
  0.7 4.5 %copy-start.7 = (s32[1600]{0:T(1024)}, s32[1600]{0:T(1024)S(1)}, u32[]{:S(2)}) copy-start(s32[1600]{0:T(1024)S(1)} %add_select_fusion.7) | copy-start | bytes 19204
  0.7 4.5 %copy-start.15 = (f32[1536]{0:T(1024)S(1)}, f32[1536]{0:T(1024)}, u32[]{:S(2)}) copy-start(f32[1536]{0:T(1024)} %param.11) | copy-start | bytes 18436
  0.7 4.5 %copy-start.16 = (f32[1536]{0:T(1024)S(1)}, f32[1536]{0:T(1024)}, u32[]{:S(2)}) copy-start(f32[1536]{0:T(1024)} %param.10) | copy-start | bytes 18436
  5.2 5.7 %copy-start.1 = (f32[1600,1536]{1,0:T(8,128)}, f32[1600,1536]{1,0:T(8,128)S(1)}, u32[]{:S(2)}) copy-start(f32[1600,1536]{1,0:T(8,128)S(1)} %fusion.77) | copy-start | bytes 29491204
  5.2 8.7 %copy-start.9 = (s32[64,64]{1,0:T(8,128)S(1)}, s32[64,64]{1,0:T(8,128)}, u32[]{:S(2)}) copy-start(s32[64,64]{1,0:T(8,128)} %param.14) | copy-start | bytes 49156
  5.3 9.4 %copy-start.14 = (s32[64]{0:T(128)S(1)}, s32[64]{0:T(128)}, u32[]{:S(2)}) copy-start(s32[64]{0:T(128)} %param.13) | copy-start | bytes 772
  10.9 7.0 %collective-permute-start = (bf16[1,16,1536]{2,1,0:T(8,128)(2,1)S(1)}, bf16[1,16,1536]{2,1,0:T(8,128)(2,1)S(1)}, u32[]{:S(2)}, u32[]{:S(2)}) collective-permute-start(bf16[1,16,1536]{2,1,0:T(8,128)(2,1)S(1)} %fusion.15), channel_id=1, source_target_pairs={{0,1},{1,0},{2,3},{3,2},{4,5},{5,4},{6,7},{7,6},{8,9},{9,8},{10,11... | collective-permute-start | bytes 147464 | tf_op jit(solution)/shard_map/ppermute | solution.py:52
  14.8 0.5 copy-start.10
  14.8 0.5 copy-start.12
  17.9 4.7 %collective-permute-start.1 = (bf16[2,16,1536]{2,1,0:T(8,128)(2,1)S(1)}, bf16[2,16,1536]{2,1,0:T(8,128)(2,1)S(1)}, u32[]{:S(2)}, u32[]{:S(2)}) collective-permute-start(bf16[2,16,1536]{2,1,0:T(8,128)(2,1)S(1)} %maximum_select_fusion.1), channel_id=1, source_target_pairs={{0,2},{1,3},{2,0},{3,1},{4,6},{5,7},{6,4},{7,5},{8,10},{9,11},{10,... | collective-permute-start | bytes 294920 | tf_op jit(solution)/shard_map/ppermute | solution.py:52
  22.6 1.8 %copy-start.4 = (bf16[4,16,1536]{2,1,0:T(8,128)(2,1)}, bf16[4,16,1536]{2,1,0:T(8,128)(2,1)S(1)}, u32[]{:S(2)}) copy-start(bf16[4,16,1536]{2,1,0:T(8,128)(2,1)S(1)} %maximum_select_fusion) | copy-start | bytes 589828
  25.5 0.9 copy-start.5
  26.4 5.9 %copy-start.8 = (s32[1600]{0:T(1024)S(1)}, s32[1600]{0:T(1024)}, u32[]{:S(2)}) copy-start(s32[1600]{0:T(1024)} %copy-done.7) | copy-start | bytes 19204
  28.8 5.9 %collective-permute-start.4 = (f32[16,1536]{1,0:T(8,128)}, f32[16,1536]{1,0:T(8,128)}, u32[]{:S(2)}, u32[]{:S(2)}) collective-permute-start(f32[16,1536]{1,0:T(8,128)} %get-tuple-element.19), channel_id=1, source_target_pairs={{0,3},{1,2},{2,1},{3,0},{4,7},{5,6},{6,5},{7,4},{8,11},{9,10},{10,... | collective-permute-start | bytes 294920 | tf_op jit(solution)/shard_map/ppermute | solution.py:93
  30.3 5.4 %collective-permute-start.3 = (f32[16,1536]{1,0:T(8,128)}, f32[16,1536]{1,0:T(8,128)}, u32[]{:S(2)}, u32[]{:S(2)}) collective-permute-start(f32[16,1536]{1,0:T(8,128)} %get-tuple-element.20), channel_id=1, source_target_pairs={{0,2},{1,3},{2,0},{3,1},{4,6},{5,7},{6,4},{7,5},{8,10},{9,11},{10,... | collective-permute-start | bytes 294920 | tf_op jit(solution)/shard_map/ppermute | solution.py:93
  30.4 5.4 %collective-permute-start.2 = (f32[16,1536]{1,0:T(8,128)}, f32[16,1536]{1,0:T(8,128)}, u32[]{:S(2)}, u32[]{:S(2)}) collective-permute-start(f32[16,1536]{1,0:T(8,128)} %get-tuple-element.18), channel_id=1, source_target_pairs={{0,1},{1,0},{2,3},{3,2},{4,5},{5,4},{6,7},{7,6},{8,9},{9,8},{10,11... | collective-permute-start | bytes 294920 | tf_op jit(solution)/shard_map/ppermute | solution.py:93
  36.9 11.4 %copy-start.17 = (f32[1536]{0:T(1024)S(1)}, f32[1536]{0:T(1024)}, u32[]{:S(2)}) copy-start(f32[1536]{0:T(1024)} %param.10) | copy-start | bytes 18436
  55.4 9.6 %copy-start.13 = (s32[64]{0:T(128)S(1)}, s32[64]{0:T(128)}, u32[]{:S(2)}) copy-start(s32[64]{0:T(128)} %copy-done.12) | copy-start | bytes 772
  55.4 9.7 %copy-start.11 = (s32[64]{0:T(128)S(1)}, s32[64]{0:T(128)}, u32[]{:S(2)}) copy-start(s32[64]{0:T(128)} %copy-done.10) | copy-start | bytes 772
  56.6 10.0 %copy-start.6 = (bf16[64,64]{1,0:T(8,128)(2,1)S(1)}, bf16[64,64]{1,0:T(8,128)(2,1)}, u32[]{:S(2)}) copy-start(bf16[64,64]{1,0:T(8,128)(2,1)} %copy-done.5) | copy-start | bytes 24580
  56.6 3.3 %collective-permute-start.5 = (f32[4,200,384]{2,1,0:T(8,128)}, f32[4,200,384]{2,1,0:T(8,128)}, u32[]{:S(2)}, u32[]{:S(2)}) collective-permute-start(f32[4,200,384]{2,1,0:T(8,128)} %pad_maximum_fusion), channel_id=1, source_target_pairs={{0,4},{4,0},{8,12},{12,8},{16,20},{20,16},{24,28},{28,24},{1,5},{5... | collective-permute-start | bytes 3686408 | tf_op jit(solution)/shard_map/ppermute | solution.py:207
  61.6 1.0 copy-start.2
  63.5 19.1 %collective-permute-start.6 = (f32[2,200,384]{2,1,0:T(8,128)}, f32[2,200,384]{2,1,0:T(8,128)}, u32[]{:S(2)}, u32[]{:S(2)}) collective-permute-start(f32[2,200,384]{2,1,0:T(8,128)} %dynamic-slice_bitcast_fusion.2), channel_id=1, source_target_pairs={{0,8},{4,12},{8,0},{12,4},{16,24},{20,28},{24,16},{28,20},{1,9},{5... | collective-permute-start | bytes 1843208 | tf_op jit(solution)/shard_map/ppermute | solution.py:214
  67.6 21.7 %all-to-all-start = ((bf16[8,64,322]{2,1,0:T(8,128)(2,1)}), bf16[8,64,322]{2,1,0:T(8,128)(2,1)}, u32[]{:S(2)}, u32[]{:S(2)}) async-start(bf16[8,64,322]{2,1,0:T(8,128)(2,1)} %pad_maximum_fusion.1), calls=%async_computation | async-start | bytes 786432 | tf_op jit(solution)/shard_map/all_to_all | solution.py:161
  83.9 0.8 copy-start.3
  85.5 15.7 %collective-permute-start.7 = (f32[1,200,384]{2,1,0:T(8,128)}, f32[1,200,384]{2,1,0:T(8,128)}, u32[]{:S(2)}, u32[]{:S(2)}) collective-permute-start(f32[1,200,384]{2,1,0:T(8,128)} %constant_dynamic-slice_fusion), channel_id=1, source_target_pairs={{0,16},{4,20},{8,24},{12,28},{16,0},{20,4},{24,8},{28,12},{1,17},{... | collective-permute-start | bytes 921608 | tf_op jit(solution)/shard_map/ppermute | solution.py:214
  103.0 7.4 %collective-permute-start.8 = (f32[200,384]{1,0:T(8,128)}, f32[200,384]{1,0:T(8,128)}, u32[]{:S(2)}, u32[]{:S(2)}) collective-permute-start(f32[200,384]{1,0:T(8,128)} %add_bitcast_fusion), channel_id=1, source_target_pairs={{0,1},{1,0},{2,3},{3,2},{4,5},{5,4},{6,7},{7,6},{8,9},{9,8},{10,11... | collective-permute-start | bytes 921608 | tf_op jit(solution)/shard_map/ppermute | solution.py:80
  111.5 6.9 %collective-permute-start.9 = (f32[200,384]{1,0:T(8,128)S(1)}, f32[200,384]{1,0:T(8,128)S(1)}, u32[]{:S(2)}, u32[]{:S(2)}) collective-permute-start(f32[200,384]{1,0:T(8,128)S(1)} %add.292), channel_id=1, source_target_pairs={{0,2},{1,3},{2,0},{3,1},{4,6},{5,7},{6,4},{7,5},{8,10},{9,11},{10,... | collective-permute-start | bytes 921608 | tf_op jit(solution)/shard_map/ppermute | solution.py:80

commit v19 on v12

--- a/solution.py
+++ b/solution.py
@@ -114,7 +114,7 @@
     active = shifted * sig
     image_sum = jnp.dot(select, active, precision=HIGHEST, preferred_element_type=jnp.float32)
     embedded = (image_sum / P_SIZE).astype(jnp.bfloat16)
-    grouped = doubling_gather(embedded, "leaf")
+    grouped = lax.all_gather(embedded, "leaf", axis=0, tiled=True)
     group = grouped.shape[0]
 
     valid = node_ids >= 0

time: 117 us -> 135 us (1.15)
  blocking collectives: 0 us -> 10.4 us
  local copies, waits for them, and re-layouts: 16.5 us -> 26.2 us
  starting transfers between devices: 20.5 us -> 14.2 us
  other arithmetic: 15.7 us -> 20.4 us
    all_gather x0 -> x1, blocking collectives: none -> 10.4 us  [shards(): grouped = lax.all_gather(embedded, 'leaf', axis=0, tiled=True)]
    ppermute x2 -> x0, starting transfers between devices: 4.59 us -> none  [doubling_gather(): other = lax.ppermute(cur, name, partners(size, bit))]
    reshape x0 -> x3, local copies, waits for them, and re-layouts: none -> 3.8 us  [the longest x2 1.92 us: shards(): column_chunks = grouped.reshape(group, n_dp, col_width).transpose(1, 0, 2)]
    ppermute x2 -> x0, waiting for transfers between devices: 2.52 us -> none  [doubling_gather(): other = lax.ppermute(cur, name, partners(size, bit))]
    ppermute x2, starting transfers between devices: 2.94 us -> 1.2 us  [butterfly_sum(): got = lax.ppermute(cur, name, partners(size, bit))]
    ppermute x2, waiting for transfers between devices: 3.66 us -> 5.33 us  [butterfly_sum(): got = lax.ppermute(cur, name, partners(size, bit))]
    another operation x2, local copies, waits for them, and re-layouts: 0.89 us -> 2.54 us  [block_table(): neg_wide = jnp.tile(neg_vec, (1, blocks))]
    reduce_sum x0 -> x1, other arithmetic: none -> 1.45 us  [pick_block(): return jnp.sum(jnp.where(hit, split, 0.0), axis=1)]
  transfers between devices with their start and end apart: 11 -> 9, of which waited for: 9 -> 8; matrix products, arithmetic and copies ran while one was open for 16% -> 11% of each run, Pallas kernels for 0% -> 0%
where the time goes in v19:
time: 135 us; the launch traced here: 133 us
  waiting for transfers between devices  33.3 us (25%)
  matrix products  27.4 us (20%)
  local copies, waits for them, and re-layouts  26.2 us (19%)
  other arithmetic  20.4 us (15%)
  starting transfers between devices  14.2 us (11%)
  blocking collectives  10.4 us (8%)
    ppermute x3, waiting for transfers between devices, halving_scatter(): got = lax.ppermute(tuple(give), name, partners(size, bit))  24.2 us
    all_gather x1, blocking collectives, shards(): grouped = lax.all_gather(embedded, 'leaf', axis=0, tiled=True)  10.4 us
    dot_general x1, matrix products, shards(): jnp.dot(jnp.concatenate([select.T.astype(jnp.bfloat16)] * 3, axis=1), jnp...  8.13 us
    unnamed x32, local copies, waits for them, and re-layouts  6.89 us
    dot_general x1, matrix products, shards(): jnp.dot(select, active, precision=HIGHEST, preferred_element_type=jnp.flo...  5.65 us
    ppermute x3, starting transfers between devices, halving_scatter(): got = lax.ppermute(tuple(give), name, partners(size, bit))  5.39 us
    ppermute x2, waiting for transfers between devices, butterfly_sum(): got = lax.ppermute(cur, name, partners(size, bit))  5.33 us
    dot_general x1, matrix products, shards(): lax.dot_general(lin_grad, features, (((0,), (0,)), ((), ())), preferred_e...  4.5 us
  transfers between devices with their start and end apart: 9, of which 8 were waited for; matrix products, arithmetic and copies ran while one was open for 11% of the time, Pallas kernels for 0%

profile of v19, /device:TPU:0, one launch (start us, length us, event | category | flops | bytes accessed | tf_op | source)
XLA Modules:
  0.0 132.9 jit_solution(12750127630156628032)
XLA Ops:
  5.6 4.4 %fusion.79 = f32[1600,1536]{1,0:T(8,128)S(1)} fusion(bf16[1600,384]{1,0:T(8,128)(2,1)} %param.8, bf16[384,1536]{1,0:T(8,128)(2,1)} %param.9), kind=kOutput, calls=%fused_computation.189 | convolution fusion | flops 1887436800 | bytes 12238848 | tf_op jit(solution)/shard_map/dot_general | solution.py:111
  10.0 5.6 %fusion.12 = bf16[16,1536]{1,0:T(8,128)(2,1)S(1)} fusion(f32[1600,1536]{1,0:T(8,128)S(1)} %fusion.79, f32[1536]{0:T(1024)S(1)} %copy-done.9, f32[1536]{0:T(1024)S(1)} %copy-done.11, s32[1600]{0:T(1024)S(1)} %add_select_fusion.7), kind=kOutput, calls=%fused_computation.20 | convolution fusion | flops 486679552 | bytes 9898240 | tf_op jit(solution)/shard_map/dot_general | solution.py:115
  15.7 10.4 %all_gather.3 = bf16[64,1536]{1,0:T(8,128)(2,1)S(1)} all-gather(bf16[16,1536]{1,0:T(8,128)(2,1)S(1)} %fusion.12), channel_id=1, replica_groups=mesh['dp'=8,'leaf'=4] {'leaf'}, dimensions={0}, use_global_device_ids=true | all-gather | bytes 245760 | tf_op jit(solution)/shard_map/all_gather | solution.py:117
  26.0 1.8 %fusion.80 = f32[64,1024]{1,0:T(8,128)} fusion(bf16[64,1536]{1,0:T(8,128)(2,1)S(1)} %all_gather.3, bf16[1024,1536]{1,0:T(8,128)(2,1)S(1)} %copy-done), kind=kOutput, calls=%fused_computation.190 | convolution fusion | flops 201326592 | bytes 3604480 | tf_op jit(solution)/shard_map/dot_general | solution.py:131
  27.8 1.9 %reshape.583 = f32[64,16,64]{2,1,0:T(8,128)} reshape(f32[64,1024]{1,0:T(8,128)} %fusion.80) | data formatting | bytes 524288 | tf_op jit(solution)/shard_map/reshape | solution.py:23
  30.4 1.5 %select_reduce_fusion = (f32[64,64]{1,0:T(8,128)S(1)}, f32[64,64]{1,0:T(8,128)S(1)}) fusion(f32[64,16,64]{2,1,0:T(8,128)} %reshape.583, pred[64,16]{1,0:T(8,128)(4,1)S(1)} %iota_compare_fusion.6, pred[64,16]{1,0:T(8,128)(4,1)S(1)} %iota_compare_fusion.8), kind=kLoop, calls=%fused_computation.34 | loop fusion | flops 253952 | bytes 296960 | tf_op jit(solution)/shard_map/reduce_sum | solution.py:25
  32.7 1.1 tile.13
  33.8 1.4 %copy.44 = s32[64,48]{1,0:T(8,128)} copy(s32[64,48]{0,1:T(8,128)} %add_select_fusion.4) | data formatting | bytes 24576 | tf_op jit(solution)/shard_map/jit(remainder)/select_n | solution.py:30
  36.0 2.3 %fusion.16 = pred[64,64]{1,0:T(8,128)(4,1)S(1)} fusion(s32[64,48]{1,0:T(8,128)} %copy.44, pred[64,48]{1,0:T(8,128)(4,1)} %copy.45), kind=kLoop, calls=%fused_computation.25 | loop fusion | flops 585728 | bytes 19456 | tf_op jit(solution)/shard_map/reduce_or | solution.py:31
  39.7 1.8 %tile.15 = bf16[4,16,1024]{2,1,0:T(8,128)(2,1)} reshape(bf16[64,16,64]{2,1,0:T(8,128)(2,1)} %tile.14) | data formatting | bytes 262144 | tf_op jit(solution)/shard_map/tile | solution.py:15
  42.2 1.6 %fusion.7 = f32[4,16,1536]{2,1,0:T(8,128)S(1)} fusion(bf16[1024,1536]{1,0:T(8,128)(2,1)S(1)} %copy-done, bf16[4,16,1024]{2,1,0:T(8,128)(2,1)S(1)} %tile.13, bf16[4,16,1024]{2,1,0:T(8,128)(2,1)} %tile.15, s32[4,16]{1,0:T(4,128)S(1)} %get-tuple-element.31, s32[4,16]{1,0:T(4,128)S(1)} %get-tuple-element.30, s32[1024]{0:T(1024)S(1)} %add_select_fusion.8), kind=kOutput, calls=%fused_computation.15 | convolution fusion | flops 201654272 | bytes 3805696 | tf_op jit(solution)/shard_map/dot_general | solution.py:141
  45.3 1.5 %collective-permute-start.2 = (f32[16,1536]{1,0:T(8,128)}, f32[16,1536]{1,0:T(8,128)S(1)}, u32[]{:S(2)}, u32[]{:S(2)}) collective-permute-start(f32[16,1536]{1,0:T(8,128)} %get-tuple-element.17), channel_id=1, source_target_pairs={{0,3},{1,2},{2,1},{3,0},{4,7},{5,6},{6,5},{7,4},{8,11},{9,10},{10,... | collective-permute-start | bytes 294920 | tf_op jit(solution)/shard_map/ppermute | solution.py:93
  46.8 1.5 %collective-permute-start.1 = (f32[16,1536]{1,0:T(8,128)}, f32[16,1536]{1,0:T(8,128)}, u32[]{:S(2)}, u32[]{:S(2)}) collective-permute-start(f32[16,1536]{1,0:T(8,128)} %get-tuple-element.18), channel_id=1, source_target_pairs={{0,2},{1,3},{2,0},{3,1},{4,6},{5,7},{6,4},{7,5},{8,10},{9,11},{10,... | collective-permute-start | bytes 294920 | tf_op jit(solution)/shard_map/ppermute | solution.py:93
  49.4 1.7 %collective-permute-done.2 = f32[16,1536]{1,0:T(8,128)S(1)} collective-permute-done((f32[16,1536]{1,0:T(8,128)}, f32[16,1536]{1,0:T(8,128)S(1)}, u32[]{:S(2)}, u32[]{:S(2)}) %collective-permute-start.2) | collective-permute-done | bytes 98336 | tf_op jit(solution)/shard_map/ppermute | solution.py:93
  51.1 1.1 collective-permute-done.1
  54.3 8.1 %multiply_reduce_fusion = (f32[1536]{0:T(1024)S(1)}, f32[1536]{0:T(1024)S(1)}, f32[1600,1536]{1,0:T(8,128)S(1)}) fusion(f32[1600,1536]{1,0:T(8,128)} %copy-done.1, f32[1536]{0:T(1024)S(1)} %copy-done.10, f32[1536]{0:T(1024)S(1)} %copy-done.12, bf16[16,1536]{1,0:T(8,128)(2,1)S(1)} %get-tuple-element.24, bf16[16,1536]{1,0:T(8,128)(2,1)S(1)} %get-tuple-element.23, ...), kind=kOutput, calls=%fused_computation.1 | convolution fusion | flops 268778496 | bytes 19884032 | tf_op jit(solution)/shard_map/dot_general | solution.py:173
  62.4 4.5 %fusion.2 = f32[1536,384]{1,0:T(8,128)} fusion(bf16[1600,384]{1,0:T(8,128)(2,1)S(1)} %copy-done.5, f32[1600,1536]{1,0:T(8,128)S(1)} %get-tuple-element.29, f32[1536]{0:T(1024)S(1)} %copy-done.12), kind=kOutput, calls=%fused_computation.8 | convolution fusion | flops 1892352000 | bytes 13424640 | tf_op jit(solution)/shard_map/dot_general | solution.py:180
  67.2 2.4 %fusion.18 = f32[4,1,200,384]{3,2,0,1:T(8,128)} fusion(s32[]{:T(128)S(6)} %select_n.362, f32[4,2,1,192,384]{4,3,1,0,2:T(8,128)} %bitcast.67, f32[4,2,1,8,384]{4,3,1,0,2:T(8,128)S(1)} %bitcast.76), kind=kLoop, calls=%fused_computation.27 | loop fusion | flops 307200 | bytes 3686404 | tf_op jit(solution)/shard_map/jit(dynamic_index_in_dim)/squeeze | solution.py:68
  69.6 3.3 %collective-permute-done.3 = f32[4,1,200,384]{3,2,0,1:T(8,128)} collective-permute-done((f32[4,1,200,384]{3,2,0,1:T(8,128)}, f32[4,1,200,384]{3,2,0,1:T(8,128)}, u32[]{:S(2)}, u32[]{:S(2)}) %collective-permute-start.3) | collective-permute-done | bytes 1228832 | tf_op jit(solution)/shard_map/ppermute | solution.py:69
  72.8 1.8 %fusion.21 = f32[4,1,200,384]{3,2,0,1:T(8,128)S(1)} fusion(f32[4,1,200,384]{3,2,0,1:T(8,128)} %collective-permute-done.3, s32[]{:T(128)S(6)} %select_n.361, f32[4,2,1,192,384]{4,3,1,0,2:T(8,128)} %bitcast.68, f32[4,2,1,8,384]{4,3,1,0,2:T(8,128)S(1)} %bitcast.77), kind=kLoop, calls=%fused_computation.30 | loop fusion | flops 614400 | bytes 4915204 | tf_op jit(solution)/shard_map/add | solution.py:70
  76.5 1.6 %collective-permute-start.4 = (f32[2,1,200,384]{3,2,1,0:T(8,128)}, f32[2,1,200,384]{3,2,1,0:T(8,128)}, u32[]{:S(2)}, u32[]{:S(2)}) collective-permute-start(f32[2,1,200,384]{3,2,1,0:T(8,128)} %dynamic-slice_bitcast_fusion), channel_id=1, source_target_pairs={{0,8},{4,12},{8,0},{12,4},{16,24},{20,28},{24,16},{28,20},{1,9},{5... | collective-permute-start | bytes 1843208 | tf_op jit(solution)/shard_map/ppermute | solution.py:69
  81.3 4.1 %all-to-all-start = ((bf16[8,64,322]{2,1,0:T(8,128)(2,1)}), bf16[8,64,322]{2,1,0:T(8,128)(2,1)}, u32[]{:S(2)}, u32[]{:S(2)}) async-start(bf16[8,64,322]{2,1,0:T(8,128)(2,1)} %pad_maximum_fusion), calls=%async_computation | async-start | bytes 786432 | tf_op jit(solution)/shard_map/all_to_all | solution.py:161
  85.5 10.2 %collective-permute-done.4 = f32[2,1,200,384]{3,2,1,0:T(8,128)} collective-permute-done((f32[2,1,200,384]{3,2,1,0:T(8,128)}, f32[2,1,200,384]{3,2,1,0:T(8,128)}, u32[]{:S(2)}, u32[]{:S(2)}) %collective-permute-start.4) | collective-permute-done | bytes 614432 | tf_op jit(solution)/shard_map/ppermute | solution.py:69
  95.7 1.3 bitcast_add_fusion
  98.6 3.8 %collective-permute-start.5 = (f32[1,1,200,384]{3,2,1,0:T(8,128)}, f32[1,1,200,384]{3,2,1,0:T(8,128)}, u32[]{:S(2)}, u32[]{:S(2)}) collective-permute-start(f32[1,1,200,384]{3,2,1,0:T(8,128)} %constant_dynamic-slice_fusion), channel_id=1, source_target_pairs={{0,16},{4,20},{8,24},{12,28},{16,0},{20,4},{24,8},{28,12},{1,17},{... | collective-permute-start | bytes 921608 | tf_op jit(solution)/shard_map/ppermute | solution.py:69
  102.4 1.1 slice.74
  103.5 10.8 %collective-permute-done.5 = f32[1,1,200,384]{3,2,1,0:T(8,128)} collective-permute-done((f32[1,1,200,384]{3,2,1,0:T(8,128)}, f32[1,1,200,384]{3,2,1,0:T(8,128)}, u32[]{:S(2)}, u32[]{:S(2)}) %collective-permute-start.5) | collective-permute-done | bytes 307232 | tf_op jit(solution)/shard_map/ppermute | solution.py:69
  114.3 1.8 %add_bitcast_fusion = f32[200,384]{1,0:T(8,128)} fusion(f32[1,1,200,384]{3,2,1,0:T(8,128)} %collective-permute-done.5, f32[2,1,200,384]{3,2,1,0:T(8,128)} %copy-done.3, s32[]{:T(128)S(6)} %select_n.369), kind=kLoop, calls=%fused_computation.40 | loop fusion | flops 76800 | bytes 921604 | tf_op jit(solution)/shard_map/squeeze;reshape | solution.py:197
  121.5 2.0 %collective-permute-done.6 = f32[200,384]{1,0:T(8,128)} collective-permute-done((f32[200,384]{1,0:T(8,128)}, f32[200,384]{1,0:T(8,128)}, u32[]{:S(2)}, u32[]{:S(2)}) %collective-permute-start.6) | collective-permute-done | bytes 307232 | tf_op jit(solution)/shard_map/ppermute | solution.py:80
  123.5 1.1 add.280
  126.8 1.4 %fusion.81 = f32[1024,192]{0,1:T(8,128)} fusion(bf16[512,1024]{0,1:T(8,128)(2,1)S(1)} %bitcast.71, bf16[512,192]{1,0:T(8,128)(2,1)S(1)} %bitcast.75), kind=kOutput, calls=%fused_computation.191 | convolution fusion | flops 201326592 | bytes 2031616 | tf_op jit(solution)/shard_map/dot_general | solution.py:169
  128.2 3.3 %collective-permute-done.7 = f32[200,384]{1,0:T(8,128)S(1)} collective-permute-done((f32[200,384]{1,0:T(8,128)S(1)}, f32[200,384]{1,0:T(8,128)S(1)}, u32[]{:S(2)}, u32[]{:S(2)}) %collective-permute-start.7) | collective-permute-done | bytes 307232 | tf_op jit(solution)/shard_map/ppermute | solution.py:80
  (95 shorter events, 29.9 us)
Async XLA Ops:
  0.6 25.4 %copy-start = (bf16[1024,1536]{1,0:T(8,128)(2,1)S(1)}, bf16[1024,1536]{1,0:T(8,128)(2,1)}, u32[]{:S(2)}) copy-start(bf16[1024,1536]{1,0:T(8,128)(2,1)} %param.12) | copy-start | bytes 9437188
  1.7 8.2 %copy-start.6 = (pred[64,64]{0,1:T(8,128)(4,1)}, pred[64,64]{0,1:T(8,128)(4,1)S(1)}, u32[]{:S(2)}) copy-start(pred[64,64]{0,1:T(8,128)(4,1)S(1)} %broadcast_compare_fusion) | copy-start | bytes 12292
  3.7 6.3 %copy-start.7 = (s32[64]{0:T(128)}, s32[64]{0:T(128)S(1)}, u32[]{:S(2)}) copy-start(s32[64]{0:T(128)S(1)} %get-tuple-element.9) | copy-start | bytes 772
  5.6 4.4 %copy-start.9 = (f32[1536]{0:T(1024)S(1)}, f32[1536]{0:T(1024)}, u32[]{:S(2)}) copy-start(f32[1536]{0:T(1024)} %param.11) | copy-start | bytes 18436
  5.6 4.4 %copy-start.11 = (f32[1536]{0:T(1024)S(1)}, f32[1536]{0:T(1024)}, u32[]{:S(2)}) copy-start(f32[1536]{0:T(1024)} %param.10) | copy-start | bytes 18436
  10.0 5.7 %copy-start.1 = (f32[1600,1536]{1,0:T(8,128)}, f32[1600,1536]{1,0:T(8,128)S(1)}, u32[]{:S(2)}) copy-start(f32[1600,1536]{1,0:T(8,128)S(1)} %fusion.79) | copy-start | bytes 29491204
  15.6 14.3 %slice-start = ((pred[64,64]{0,1:T(8,128)(4,1)}), pred[64,16]{0,1:T(8,128)(4,1)S(1)}, s32[]{:S(2)}) async-start(pred[64,64]{0,1:T(8,128)(4,1)} %copy-done.6), calls=%async_computation.1 | async-start | bytes 4096 | tf_op jit(solution)/shard_map/slice | solution.py:128
  15.7 19.6 %slice-start.1 = ((pred[64,64]{0,1:T(8,128)(4,1)}), pred[64,48]{0,1:T(8,128)(4,1)S(1)}, s32[]{:S(2)}) async-start(pred[64,64]{0,1:T(8,128)(4,1)} %copy-done.6), calls=%async_computation.2 | async-start | bytes 12288 | tf_op jit(solution)/shard_map/slice | solution.py:129
  42.2 12.0 %copy-start.10 = (f32[1536]{0:T(1024)S(1)}, f32[1536]{0:T(1024)}, u32[]{:S(2)}) copy-start(f32[1536]{0:T(1024)} %param.11) | copy-start | bytes 18436
  42.2 12.0 %copy-start.12 = (f32[1536]{0:T(1024)S(1)}, f32[1536]{0:T(1024)}, u32[]{:S(2)}) copy-start(f32[1536]{0:T(1024)} %param.10) | copy-start | bytes 18436
  43.9 0.8 copy-start.4
  45.3 5.8 %collective-permute-start.2 = (f32[16,1536]{1,0:T(8,128)}, f32[16,1536]{1,0:T(8,128)S(1)}, u32[]{:S(2)}, u32[]{:S(2)}) collective-permute-start(f32[16,1536]{1,0:T(8,128)} %get-tuple-element.17), channel_id=1, source_target_pairs={{0,3},{1,2},{2,1},{3,0},{4,7},{5,6},{6,5},{7,4},{8,11},{9,10},{10,... | collective-permute-start | bytes 294920 | tf_op jit(solution)/shard_map/ppermute | solution.py:93
  46.8 5.4 %collective-permute-start.1 = (f32[16,1536]{1,0:T(8,128)}, f32[16,1536]{1,0:T(8,128)}, u32[]{:S(2)}, u32[]{:S(2)}) collective-permute-start(f32[16,1536]{1,0:T(8,128)} %get-tuple-element.18), channel_id=1, source_target_pairs={{0,2},{1,3},{2,0},{3,1},{4,6},{5,7},{6,4},{7,5},{8,10},{9,11},{10,... | collective-permute-start | bytes 294920 | tf_op jit(solution)/shard_map/ppermute | solution.py:93
  48.3 4.9 %collective-permute-start = (f32[16,1536]{1,0:T(8,128)}, f32[16,1536]{1,0:T(8,128)}, u32[]{:S(2)}, u32[]{:S(2)}) collective-permute-start(f32[16,1536]{1,0:T(8,128)} %get-tuple-element.16), channel_id=1, source_target_pairs={{0,1},{1,0},{2,3},{3,2},{4,5},{5,4},{6,7},{7,6},{8,9},{9,8},{10,11... | collective-permute-start | bytes 294920 | tf_op jit(solution)/shard_map/ppermute | solution.py:93
  54.3 8.1 %copy-start.5 = (bf16[1600,384]{1,0:T(8,128)(2,1)S(1)}, bf16[1600,384]{1,0:T(8,128)(2,1)}, u32[]{:S(2)}) copy-start(bf16[1600,384]{1,0:T(8,128)(2,1)} %param.8) | copy-start | bytes 3686404
  69.6 3.3 %collective-permute-start.3 = (f32[4,1,200,384]{3,2,0,1:T(8,128)}, f32[4,1,200,384]{3,2,0,1:T(8,128)}, u32[]{:S(2)}, u32[]{:S(2)}) collective-permute-start(f32[4,1,200,384]{3,2,0,1:T(8,128)} %fusion.18), channel_id=1, source_target_pairs={{0,4},{4,0},{8,12},{12,8},{16,20},{20,16},{24,28},{28,24},{1,5},{5... | collective-permute-start | bytes 3686408 | tf_op jit(solution)/shard_map/ppermute | solution.py:69
  69.6 9.5 %copy-start.8 = (s32[64]{0:T(128)S(1)}, s32[64]{0:T(128)}, u32[]{:S(2)}) copy-start(s32[64]{0:T(128)} %copy-done.7) | copy-start | bytes 772
  74.6 1.1 copy-start.2
  76.5 19.1 %collective-permute-start.4 = (f32[2,1,200,384]{3,2,1,0:T(8,128)}, f32[2,1,200,384]{3,2,1,0:T(8,128)}, u32[]{:S(2)}, u32[]{:S(2)}) collective-permute-start(f32[2,1,200,384]{3,2,1,0:T(8,128)} %dynamic-slice_bitcast_fusion), channel_id=1, source_target_pairs={{0,8},{4,12},{8,0},{12,4},{16,24},{20,28},{24,16},{28,20},{1,9},{5... | collective-permute-start | bytes 1843208 | tf_op jit(solution)/shard_map/ppermute | solution.py:69
  81.3 21.0 %all-to-all-start = ((bf16[8,64,322]{2,1,0:T(8,128)(2,1)}), bf16[8,64,322]{2,1,0:T(8,128)(2,1)}, u32[]{:S(2)}, u32[]{:S(2)}) async-start(bf16[8,64,322]{2,1,0:T(8,128)(2,1)} %pad_maximum_fusion), calls=%async_computation | async-start | bytes 786432 | tf_op jit(solution)/shard_map/all_to_all | solution.py:161
  97.0 0.8 copy-start.3
  98.6 15.7 %collective-permute-start.5 = (f32[1,1,200,384]{3,2,1,0:T(8,128)}, f32[1,1,200,384]{3,2,1,0:T(8,128)}, u32[]{:S(2)}, u32[]{:S(2)}) collective-permute-start(f32[1,1,200,384]{3,2,1,0:T(8,128)} %constant_dynamic-slice_fusion), channel_id=1, source_target_pairs={{0,16},{4,20},{8,24},{12,28},{16,0},{20,4},{24,8},{28,12},{1,17},{... | collective-permute-start | bytes 921608 | tf_op jit(solution)/shard_map/ppermute | solution.py:69
  116.1 7.4 %collective-permute-start.6 = (f32[200,384]{1,0:T(8,128)}, f32[200,384]{1,0:T(8,128)}, u32[]{:S(2)}, u32[]{:S(2)}) collective-permute-start(f32[200,384]{1,0:T(8,128)} %add_bitcast_fusion), channel_id=1, source_target_pairs={{0,1},{1,0},{2,3},{3,2},{4,5},{5,4},{6,7},{7,6},{8,9},{9,8},{10,11... | collective-permute-start | bytes 921608 | tf_op jit(solution)/shard_map/ppermute | solution.py:80
  124.6 6.9 %collective-permute-start.7 = (f32[200,384]{1,0:T(8,128)S(1)}, f32[200,384]{1,0:T(8,128)S(1)}, u32[]{:S(2)}, u32[]{:S(2)}) collective-permute-start(f32[200,384]{1,0:T(8,128)S(1)} %add.280), channel_id=1, source_target_pairs={{0,2},{1,3},{2,0},{3,1},{4,6},{5,7},{6,4},{7,5},{8,10},{9,11},{10,... | collective-permute-start | bytes 921608 | tf_op jit(solution)/shard_map/ppermute | solution.py:80

commit v20 on v19

--- a/solution.py
+++ b/solution.py
@@ -94,6 +94,20 @@
     return total
 
 
+def direct_gather(x, name):
+    size = lax.axis_size(name)
+    idx = lax.axis_index(name)
+    got = [x] + [lax.ppermute(x, name, [(i, i ^ k) for i in range(size)]) for k in range(1, size)]
+    placed = []
+    for j in range(size):
+        source = jnp.bitwise_xor(idx, j)
+        block = got[0]
+        for k in range(1, size):
+            block = jnp.where(source == k, got[k], block)
+        placed.append(block)
+    return jnp.concatenate(placed, axis=0)
+
+
 def shards(features, head_weight, gain, shift, node_weights, subtree_map, node_ids):
     rows = features.shape[0]
     images_here = rows // P_SIZE
@@ -114,7 +128,10 @@
     active = shifted * sig
     image_sum = jnp.dot(select, active, precision=HIGHEST, preferred_element_type=jnp.float32)
     embedded = (image_sum / P_SIZE).astype(jnp.bfloat16)
-    grouped = lax.all_gather(embedded, "leaf", axis=0, tiled=True)
+    if lax.axis_size("leaf") <= 4:
+        grouped = direct_gather(embedded, "leaf")
+    else:
+        grouped = doubling_gather(embedded, "leaf")
     group = grouped.shape[0]
 
     valid = node_ids >= 0

time: 135 us -> 118 us (0.87)
  blocking collectives: 10.4 us -> 0 us
  local copies, waits for them, and re-layouts: 26.2 us -> 17.9 us
  starting transfers between devices: 14.2 us -> 19.9 us
  waiting for transfers between devices: 33.3 us -> 31.3 us
    all_gather x1 -> x0, blocking collectives: 10.4 us -> none  [shards(): grouped = lax.all_gather(embedded, 'leaf', axis=0, tiled=True)]
    ppermute x0 -> x3, starting transfers between devices: none -> 4.59 us  [direct_gather(): lax.ppermute(x, name, [(i, i ^ k) for i in range(size)])]
    another operation x2, local copies, waits for them, and re-layouts: 2.54 us -> 0.9 us  [block_table(): neg_wide = jnp.tile(neg_vec, (1, blocks))]
    select_n x2, local copies, waits for them, and re-layouts: 1.52 us -> 0.16 us  [lane_mask(): hit = ((ids % SUB_SIZE)[:, :, None] == column) & valid[:, :, None]]
    unnamed x32 -> x58, local copies, waits for them, and re-layouts: 6.89 us -> 5.96 us
  transfers between devices with their start and end apart: 9 -> 12, of which waited for: 8 -> 8; matrix products, arithmetic and copies ran while one was open for 11% -> 17% of each run, Pallas kernels for 0% -> 0%
where the time goes in v20:
time: 118 us; the launch traced here: 117 us
  waiting for transfers between devices  31.3 us (27%)
  matrix products  27.1 us (23%)
  starting transfers between devices  19.9 us (17%)
  other arithmetic  19.3 us (16%)
  local copies, waits for them, and re-layouts  17.9 us (15%)
    ppermute x3, waiting for transfers between devices, halving_scatter(): got = lax.ppermute(tuple(give), name, partners(size, bit))  22.9 us
    dot_general x1, matrix products, shards(): jnp.dot(jnp.concatenate([select.T.astype(jnp.bfloat16)] * 3, axis=1), jnp...  8.31 us
    unnamed x58, local copies, waits for them, and re-layouts  5.96 us
    dot_general x1, matrix products, shards(): jnp.dot(select, active, precision=HIGHEST, preferred_element_type=jnp.flo...  5.63 us
    ppermute x3, starting transfers between devices, halving_scatter(): got = lax.ppermute(tuple(give), name, partners(size, bit))  5.37 us
    ppermute x3, starting transfers between devices, direct_gather(): lax.ppermute(x, name, [(i, i ^ k) for i in range(size)])  4.59 us
    dot_general x1, matrix products, shards(): jnp.dot(features, head_weight, preferred_element_type=jnp.float32)  4.5 us
    dot_general x1, matrix products, shards(): lax.dot_general(lin_grad, features, (((0,), (0,)), ((), ())), preferred_e...  4.49 us
  transfers between devices with their start and end apart: 12, of which 8 were waited for; matrix products, arithmetic and copies ran while one was open for 17% of the time, Pallas kernels for 0%

profile of v20, /device:TPU:0, one launch (start us, length us, event | category | flops | bytes accessed | tf_op | source)
XLA Modules:
  0.0 116.7 jit_solution(193902716755071374)
XLA Ops:
  0.7 4.5 %fusion.80 = f32[1600,1536]{1,0:T(8,128)S(1)} fusion(bf16[1600,384]{1,0:T(8,128)(2,1)} %param.8, bf16[384,1536]{1,0:T(8,128)(2,1)} %param.9), kind=kOutput, calls=%fused_computation.195 | convolution fusion | flops 1887436800 | bytes 12238848 | tf_op jit(solution)/shard_map/dot_general | solution.py:125
  5.3 5.6 %fusion.12 = bf16[16,1536]{1,0:T(8,128)(2,1)S(1)} fusion(f32[1600,1536]{1,0:T(8,128)S(1)} %fusion.80, f32[1536]{0:T(1024)S(1)} %copy-done.23, f32[1536]{0:T(1024)S(1)} %copy-done.24, s32[1600]{0:T(1024)S(1)} %add_select_fusion.7), kind=kOutput, calls=%fused_computation.20 | convolution fusion | flops 486679552 | bytes 9898240 | tf_op jit(solution)/shard_map/dot_general | solution.py:129
  10.9 4.0 %collective-permute-start = (bf16[16,1536]{1,0:T(8,128)(2,1)S(1)}, bf16[16,1536]{1,0:T(8,128)(2,1)S(1)}, u32[]{:S(2)}, u32[]{:S(2)}) collective-permute-start(bf16[16,1536]{1,0:T(8,128)(2,1)S(1)} %fusion.12), channel_id=1, source_target_pairs={{0,3},{1,2},{2,1},{3,0},{4,7},{5,6},{6,5},{7,4},{8,11},{9,10},{10,... | collective-permute-start | bytes 147464 | tf_op jit(solution)/shard_map/ppermute | solution.py:100
  17.6 1.1 fusion.16
  20.7 1.1 fusion.76
  22.7 1.4 %select_reduce_fusion = (f32[64,64]{1,0:T(8,128)S(1)}, f32[64,64]{1,0:T(8,128)S(1)}) fusion(f32[64,16,64]{2,1,0:T(8,128)} %reshape.583, pred[64,16]{1,0:T(8,128)(4,1)S(1)} %iota_compare_fusion.6, pred[64,16]{1,0:T(8,128)(4,1)S(1)} %iota_compare_fusion.8), kind=kLoop, calls=%fused_computation.34 | loop fusion | flops 253952 | bytes 296960 | tf_op jit(solution)/shard_map/reduce_sum | solution.py:25
  26.1 1.7 %fusion.7 = f32[4,16,1536]{2,1,0:T(8,128)S(1)} fusion(bf16[1024,1536]{1,0:T(8,128)(2,1)S(1)} %copy-done, bf16[4,16,1024]{2,1,0:T(8,128)(2,1)} %tile.13, bf16[4,16,1024]{2,1,0:T(8,128)(2,1)} %tile.15, s32[4,16]{1,0:T(4,128)} %get-tuple-element.35, s32[4,16]{1,0:T(4,128)} %get-tuple-element.34, s32[1024]{0:T(1024)} %add_select_fusion.8), kind=kOutput, calls=%fused_computation.15 | convolution fusion | flops 201654272 | bytes 3805696 | tf_op jit(solution)/shard_map/dot_general | solution.py:158
  28.5 2.8 %collective-permute-start.5 = (f32[16,1536]{1,0:T(8,128)}, f32[16,1536]{1,0:T(8,128)}, u32[]{:S(2)}, u32[]{:S(2)}) collective-permute-start(f32[16,1536]{1,0:T(8,128)} %get-tuple-element.17), channel_id=1, source_target_pairs={{0,3},{1,2},{2,1},{3,0},{4,7},{5,6},{6,5},{7,4},{8,11},{9,10},{10,... | collective-permute-start | bytes 294920 | tf_op jit(solution)/shard_map/ppermute | solution.py:93
  32.6 1.9 %collective-permute-done.5 = f32[16,1536]{1,0:T(8,128)} collective-permute-done((f32[16,1536]{1,0:T(8,128)}, f32[16,1536]{1,0:T(8,128)}, u32[]{:S(2)}, u32[]{:S(2)}) %collective-permute-start.5) | collective-permute-done | bytes 98336 | tf_op jit(solution)/shard_map/ppermute | solution.py:93
  34.5 1.8 %collective-permute-done.4 = f32[16,1536]{1,0:T(8,128)} collective-permute-done((f32[16,1536]{1,0:T(8,128)}, f32[16,1536]{1,0:T(8,128)}, u32[]{:S(2)}, u32[]{:S(2)}) %collective-permute-start.4) | collective-permute-done | bytes 98336 | tf_op jit(solution)/shard_map/ppermute | solution.py:93
  37.9 8.3 %multiply_reduce_fusion = (f32[1536]{0:T(1024)S(1)}, f32[1536]{0:T(1024)S(1)}, f32[1600,1536]{1,0:T(8,128)S(1)}) fusion(f32[1600,1536]{1,0:T(8,128)} %copy-done.1, f32[1536]{0:T(1024)} %param.11, f32[1536]{0:T(1024)} %param.10, bf16[16,1536]{1,0:T(8,128)(2,1)S(1)} %get-tuple-element.28, bf16[16,1536]{1,0:T(8,128)(2,1)S(1)} %get-tuple-element.27, ...), kind=kOutput, calls=%fused_computation.1 | convolution fusion | flops 268778496 | bytes 19884032 | tf_op jit(solution)/shard_map/dot_general | solution.py:190
  46.2 4.5 %fusion.2 = f32[1536,384]{1,0:T(8,128)} fusion(bf16[1600,384]{1,0:T(8,128)(2,1)S(1)} %copy-done.4, f32[1600,1536]{1,0:T(8,128)S(1)} %get-tuple-element.33, f32[1536]{0:T(1024)S(1)} %copy-done.25), kind=kOutput, calls=%fused_computation.8 | convolution fusion | flops 1892352000 | bytes 13424640 | tf_op jit(solution)/shard_map/dot_general | solution.py:197
  50.9 2.4 %fusion.18 = f32[4,1,200,384]{3,2,0,1:T(8,128)} fusion(s32[]{:T(128)S(6)} %select_n.460, f32[4,2,1,192,384]{4,3,1,0,2:T(8,128)} %bitcast.66, f32[4,2,1,8,384]{4,3,1,0,2:T(8,128)S(1)} %bitcast.75), kind=kLoop, calls=%fused_computation.27 | loop fusion | flops 307200 | bytes 3686404 | tf_op jit(solution)/shard_map/jit(dynamic_index_in_dim)/squeeze | solution.py:68
  53.6 3.0 %collective-permute-done.6 = f32[4,1,200,384]{3,2,0,1:T(8,128)} collective-permute-done((f32[4,1,200,384]{3,2,0,1:T(8,128)}, f32[4,1,200,384]{3,2,0,1:T(8,128)}, u32[]{:S(2)}, u32[]{:S(2)}) %collective-permute-start.6) | collective-permute-done | bytes 1228832 | tf_op jit(solution)/shard_map/ppermute | solution.py:69
  56.6 1.8 %fusion.21 = f32[4,1,200,384]{3,2,0,1:T(8,128)S(1)} fusion(f32[4,1,200,384]{3,2,0,1:T(8,128)} %collective-permute-done.6, s32[]{:T(128)S(6)} %select_n.459, f32[4,2,1,192,384]{4,3,1,0,2:T(8,128)} %bitcast.67, f32[4,2,1,8,384]{4,3,1,0,2:T(8,128)S(1)} %bitcast.76), kind=kLoop, calls=%fused_computation.30 | loop fusion | flops 614400 | bytes 4915204 | tf_op jit(solution)/shard_map/add | solution.py:70
  58.4 1.0 copy-done.2
  60.2 1.6 %collective-permute-start.7 = (f32[2,1,200,384]{3,2,1,0:T(8,128)}, f32[2,1,200,384]{3,2,1,0:T(8,128)}, u32[]{:S(2)}, u32[]{:S(2)}) collective-permute-start(f32[2,1,200,384]{3,2,1,0:T(8,128)} %dynamic-slice_bitcast_fusion), channel_id=1, source_target_pairs={{0,8},{4,12},{8,0},{12,4},{16,24},{20,28},{24,16},{28,20},{1,9},{5... | collective-permute-start | bytes 1843208 | tf_op jit(solution)/shard_map/ppermute | solution.py:69
  63.2 1.2 reshape.588
  66.2 4.1 %all-to-all-start = ((bf16[8,64,322]{2,1,0:T(8,128)(2,1)}), bf16[8,64,322]{2,1,0:T(8,128)(2,1)}, u32[]{:S(2)}, u32[]{:S(2)}) async-start(bf16[8,64,322]{2,1,0:T(8,128)(2,1)} %pad_maximum_fusion), calls=%async_computation | async-start | bytes 786432 | tf_op jit(solution)/shard_map/all_to_all | solution.py:178
  70.3 9.1 %collective-permute-done.7 = f32[2,1,200,384]{3,2,1,0:T(8,128)} collective-permute-done((f32[2,1,200,384]{3,2,1,0:T(8,128)}, f32[2,1,200,384]{3,2,1,0:T(8,128)}, u32[]{:S(2)}, u32[]{:S(2)}) %collective-permute-start.7) | collective-permute-done | bytes 614432 | tf_op jit(solution)/shard_map/ppermute | solution.py:69
  79.4 1.3 %bitcast_add_fusion = f32[2,1,200,384]{3,2,1,0:T(8,128)S(1)} fusion(f32[2,1,200,384]{3,2,1,0:T(8,128)} %collective-permute-done.7, f32[2,2,1,200,384]{4,3,1,0,2:T(8,128)} %bitcast.69, s32[]{:T(128)S(6)} %select_n.463), kind=kLoop, calls=%fused_computation.32 | loop fusion | flops 153600 | bytes 1843204 | tf_op jit(solution)/shard_map/add | solution.py:70
  82.2 3.8 %collective-permute-start.8 = (f32[1,1,200,384]{3,2,1,0:T(8,128)}, f32[1,1,200,384]{3,2,1,0:T(8,128)}, u32[]{:S(2)}, u32[]{:S(2)}) collective-permute-start(f32[1,1,200,384]{3,2,1,0:T(8,128)} %constant_dynamic-slice_fusion), channel_id=1, source_target_pairs={{0,16},{4,20},{8,24},{12,28},{16,0},{20,4},{24,8},{28,12},{1,17},{... | collective-permute-start | bytes 921608 | tf_op jit(solution)/shard_map/ppermute | solution.py:69
  86.1 1.1 slice.74
  87.2 10.8 %collective-permute-done.8 = f32[1,1,200,384]{3,2,1,0:T(8,128)} collective-permute-done((f32[1,1,200,384]{3,2,1,0:T(8,128)}, f32[1,1,200,384]{3,2,1,0:T(8,128)}, u32[]{:S(2)}, u32[]{:S(2)}) %collective-permute-start.8) | collective-permute-done | bytes 307232 | tf_op jit(solution)/shard_map/ppermute | solution.py:69
  98.0 1.8 %add_bitcast_fusion = f32[200,384]{1,0:T(8,128)} fusion(f32[1,1,200,384]{3,2,1,0:T(8,128)} %collective-permute-done.8, f32[2,1,200,384]{3,2,1,0:T(8,128)} %copy-done.3, s32[]{:T(128)S(6)} %select_n.467), kind=kLoop, calls=%fused_computation.40 | loop fusion | flops 76800 | bytes 921604 | tf_op jit(solution)/shard_map/squeeze;reshape | solution.py:214
  101.4 1.1 copy.63
  102.4 1.1 copy.62
  105.4 1.9 %collective-permute-done.9 = f32[200,384]{1,0:T(8,128)} collective-permute-done((f32[200,384]{1,0:T(8,128)}, f32[200,384]{1,0:T(8,128)}, u32[]{:S(2)}, u32[]{:S(2)}) %collective-permute-start.9) | collective-permute-done | bytes 307232 | tf_op jit(solution)/shard_map/ppermute | solution.py:80
  107.2 1.1 add.280
  108.3 1.6 %collective-permute-start.10 = (f32[200,384]{1,0:T(8,128)S(1)}, f32[200,384]{1,0:T(8,128)S(1)}, u32[]{:S(2)}, u32[]{:S(2)}) collective-permute-start(f32[200,384]{1,0:T(8,128)S(1)} %add.280), channel_id=1, source_target_pairs={{0,2},{1,3},{2,0},{3,1},{4,6},{5,7},{6,4},{7,5},{8,10},{9,11},{10,... | collective-permute-start | bytes 921608 | tf_op jit(solution)/shard_map/ppermute | solution.py:80
  111.4 1.4 %fusion.81 = f32[1024,192]{0,1:T(8,128)} fusion(bf16[512,1024]{0,1:T(8,128)(2,1)S(1)} %bitcast.70, bf16[512,192]{1,0:T(8,128)(2,1)S(1)} %bitcast.74), kind=kOutput, calls=%fused_computation.196 | convolution fusion | flops 201326592 | bytes 2031616 | tf_op jit(solution)/shard_map/dot_general | solution.py:186
  112.8 2.4 %collective-permute-done.10 = f32[200,384]{1,0:T(8,128)S(1)} collective-permute-done((f32[200,384]{1,0:T(8,128)S(1)}, f32[200,384]{1,0:T(8,128)S(1)}, u32[]{:S(2)}, u32[]{:S(2)}) %collective-permute-start.10) | collective-permute-done | bytes 307232 | tf_op jit(solution)/shard_map/ppermute | solution.py:80
  (126 shorter events, 23.4 us)
Async XLA Ops:
  0.6 20.0 %copy-start = (bf16[1024,1536]{1,0:T(8,128)(2,1)S(1)}, bf16[1024,1536]{1,0:T(8,128)(2,1)}, u32[]{:S(2)}) copy-start(bf16[1024,1536]{1,0:T(8,128)(2,1)} %param.12) | copy-start | bytes 9437188
  0.7 4.5 %copy-start.15 = (s32[1600]{0:T(1024)}, s32[1600]{0:T(1024)S(1)}, u32[]{:S(2)}) copy-start(s32[1600]{0:T(1024)S(1)} %add_select_fusion.7) | copy-start | bytes 19204
  0.7 4.5 %copy-start.23 = (f32[1536]{0:T(1024)S(1)}, f32[1536]{0:T(1024)}, u32[]{:S(2)}) copy-start(f32[1536]{0:T(1024)} %param.11) | copy-start | bytes 18436
  0.7 4.5 %copy-start.24 = (f32[1536]{0:T(1024)S(1)}, f32[1536]{0:T(1024)}, u32[]{:S(2)}) copy-start(f32[1536]{0:T(1024)} %param.10) | copy-start | bytes 18436
  5.2 5.7 %copy-start.1 = (f32[1600,1536]{1,0:T(8,128)}, f32[1600,1536]{1,0:T(8,128)S(1)}, u32[]{:S(2)}) copy-start(f32[1600,1536]{1,0:T(8,128)S(1)} %fusion.80) | copy-start | bytes 29491204
  5.2 10.3 %copy-start.17 = (s32[64,64]{1,0:T(8,128)S(1)}, s32[64,64]{1,0:T(8,128)}, u32[]{:S(2)}) copy-start(s32[64,64]{1,0:T(8,128)} %param.14) | copy-start | bytes 49156
  5.3 11.0 %copy-start.22 = (s32[64]{0:T(128)S(1)}, s32[64]{0:T(128)}, u32[]{:S(2)}) copy-start(s32[64]{0:T(128)} %param.13) | copy-start | bytes 772
  10.9 9.0 %collective-permute-start = (bf16[16,1536]{1,0:T(8,128)(2,1)S(1)}, bf16[16,1536]{1,0:T(8,128)(2,1)S(1)}, u32[]{:S(2)}, u32[]{:S(2)}) collective-permute-start(bf16[16,1536]{1,0:T(8,128)(2,1)S(1)} %fusion.12), channel_id=1, source_target_pairs={{0,3},{1,2},{2,1},{3,0},{4,7},{5,6},{6,5},{7,4},{8,11},{9,10},{10,... | collective-permute-start | bytes 147464 | tf_op jit(solution)/shard_map/ppermute | solution.py:100
  14.9 5.1 %collective-permute-start.1 = (bf16[16,1536]{1,0:T(8,128)(2,1)S(1)}, bf16[16,1536]{1,0:T(8,128)(2,1)S(1)}, u32[]{:S(2)}, u32[]{:S(2)}) collective-permute-start(bf16[16,1536]{1,0:T(8,128)(2,1)S(1)} %fusion.12), channel_id=1, source_target_pairs={{0,2},{1,3},{2,0},{3,1},{4,6},{5,7},{6,4},{7,5},{8,10},{9,11},{10,... | collective-permute-start | bytes 147464 | tf_op jit(solution)/shard_map/ppermute | solution.py:100
  15.4 4.6 %collective-permute-start.2 = (bf16[16,1536]{1,0:T(8,128)(2,1)S(1)}, bf16[16,1536]{1,0:T(8,128)(2,1)S(1)}, u32[]{:S(2)}, u32[]{:S(2)}) collective-permute-start(bf16[16,1536]{1,0:T(8,128)(2,1)S(1)} %fusion.12), channel_id=1, source_target_pairs={{0,1},{1,0},{2,3},{3,2},{4,5},{5,4},{6,7},{7,6},{8,9},{9,8},{10,11... | collective-permute-start | bytes 147464 | tf_op jit(solution)/shard_map/ppermute | solution.py:100
  25.2 0.9 copy-start.13
  26.1 5.9 %copy-start.16 = (s32[1600]{0:T(1024)S(1)}, s32[1600]{0:T(1024)}, u32[]{:S(2)}) copy-start(s32[1600]{0:T(1024)} %copy-done.15) | copy-start | bytes 19204
  28.5 6.0 %collective-permute-start.5 = (f32[16,1536]{1,0:T(8,128)}, f32[16,1536]{1,0:T(8,128)}, u32[]{:S(2)}, u32[]{:S(2)}) collective-permute-start(f32[16,1536]{1,0:T(8,128)} %get-tuple-element.17), channel_id=1, source_target_pairs={{0,3},{1,2},{2,1},{3,0},{4,7},{5,6},{6,5},{7,4},{8,11},{9,10},{10,... | collective-permute-start | bytes 294920 | tf_op jit(solution)/shard_map/ppermute | solution.py:93
  31.3 4.9 %collective-permute-start.4 = (f32[16,1536]{1,0:T(8,128)}, f32[16,1536]{1,0:T(8,128)}, u32[]{:S(2)}, u32[]{:S(2)}) collective-permute-start(f32[16,1536]{1,0:T(8,128)} %get-tuple-element.18), channel_id=1, source_target_pairs={{0,2},{1,3},{2,0},{3,1},{4,6},{5,7},{6,4},{7,5},{8,10},{9,11},{10,... | collective-permute-start | bytes 294920 | tf_op jit(solution)/shard_map/ppermute | solution.py:93
  31.8 4.9 %collective-permute-start.3 = (f32[16,1536]{1,0:T(8,128)}, f32[16,1536]{1,0:T(8,128)}, u32[]{:S(2)}, u32[]{:S(2)}) collective-permute-start(f32[16,1536]{1,0:T(8,128)} %get-tuple-element.16), channel_id=1, source_target_pairs={{0,1},{1,0},{2,3},{3,2},{4,5},{5,4},{6,7},{7,6},{8,9},{9,8},{10,11... | collective-permute-start | bytes 294920 | tf_op jit(solution)/shard_map/ppermute | solution.py:93
  37.8 8.3 %copy-start.4 = (bf16[1600,384]{1,0:T(8,128)(2,1)S(1)}, bf16[1600,384]{1,0:T(8,128)(2,1)}, u32[]{:S(2)}) copy-start(bf16[1600,384]{1,0:T(8,128)(2,1)} %param.8) | copy-start | bytes 3686404
  37.8 8.3 %copy-start.25 = (f32[1536]{0:T(1024)S(1)}, f32[1536]{0:T(1024)}, u32[]{:S(2)}) copy-start(f32[1536]{0:T(1024)} %param.10) | copy-start | bytes 18436
  50.7 2.6 %copy-start.21 = (s32[64]{0:T(128)S(1)}, s32[64]{0:T(128)}, u32[]{:S(2)}) copy-start(s32[64]{0:T(128)} %copy-done.20) | copy-start | bytes 772
  50.7 2.8 %copy-start.19 = (s32[64]{0:T(128)S(1)}, s32[64]{0:T(128)}, u32[]{:S(2)}) copy-start(s32[64]{0:T(128)} %copy-done.18) | copy-start | bytes 772
  53.3 3.3 %collective-permute-start.6 = (f32[4,1,200,384]{3,2,0,1:T(8,128)}, f32[4,1,200,384]{3,2,0,1:T(8,128)}, u32[]{:S(2)}, u32[]{:S(2)}) collective-permute-start(f32[4,1,200,384]{3,2,0,1:T(8,128)} %fusion.18), channel_id=1, source_target_pairs={{0,4},{4,0},{8,12},{12,8},{16,20},{20,16},{24,28},{28,24},{1,5},{5... | collective-permute-start | bytes 3686408 | tf_op jit(solution)/shard_map/ppermute | solution.py:69
  53.4 9.1 %copy-start.6 = (bf16[16,1536]{1,0:T(8,128)(2,1)S(1)}, bf16[16,1536]{1,0:T(8,128)(2,1)}, u32[]{:S(2)}) copy-start(bf16[16,1536]{1,0:T(8,128)(2,1)} %copy-done.5) | copy-start | bytes 147460
  53.4 9.1 %copy-start.8 = (bf16[16,1536]{1,0:T(8,128)(2,1)S(1)}, bf16[16,1536]{1,0:T(8,128)(2,1)}, u32[]{:S(2)}) copy-start(bf16[16,1536]{1,0:T(8,128)(2,1)} %copy-done.7) | copy-start | bytes 147460
  53.4 9.1 %copy-start.10 = (bf16[16,1536]{1,0:T(8,128)(2,1)S(1)}, bf16[16,1536]{1,0:T(8,128)(2,1)}, u32[]{:S(2)}) copy-start(bf16[16,1536]{1,0:T(8,128)(2,1)} %copy-done.9) | copy-start | bytes 147460
  53.4 9.1 %copy-start.12 = (bf16[16,1536]{1,0:T(8,128)(2,1)S(1)}, bf16[16,1536]{1,0:T(8,128)(2,1)}, u32[]{:S(2)}) copy-start(bf16[16,1536]{1,0:T(8,128)(2,1)} %copy-done.11) | copy-start | bytes 147460
  53.6 10.9 %copy-start.14 = (bf16[64,64]{1,0:T(8,128)(2,1)S(1)}, bf16[64,64]{1,0:T(8,128)(2,1)}, u32[]{:S(2)}) copy-start(bf16[64,64]{1,0:T(8,128)(2,1)} %copy-done.13) | copy-start | bytes 24580
  58.3 1.0 copy-start.2
  60.2 19.1 %collective-permute-start.7 = (f32[2,1,200,384]{3,2,1,0:T(8,128)}, f32[2,1,200,384]{3,2,1,0:T(8,128)}, u32[]{:S(2)}, u32[]{:S(2)}) collective-permute-start(f32[2,1,200,384]{3,2,1,0:T(8,128)} %dynamic-slice_bitcast_fusion), channel_id=1, source_target_pairs={{0,8},{4,12},{8,0},{12,4},{16,24},{20,28},{24,16},{28,20},{1,9},{5... | collective-permute-start | bytes 1843208 | tf_op jit(solution)/shard_map/ppermute | solution.py:69
  66.2 19.9 %all-to-all-start = ((bf16[8,64,322]{2,1,0:T(8,128)(2,1)}), bf16[8,64,322]{2,1,0:T(8,128)(2,1)}, u32[]{:S(2)}, u32[]{:S(2)}) async-start(bf16[8,64,322]{2,1,0:T(8,128)(2,1)} %pad_maximum_fusion), calls=%async_computation | async-start | bytes 786432 | tf_op jit(solution)/shard_map/all_to_all | solution.py:178
  80.7 0.8 copy-start.3
  82.2 15.7 %collective-permute-start.8 = (f32[1,1,200,384]{3,2,1,0:T(8,128)}, f32[1,1,200,384]{3,2,1,0:T(8,128)}, u32[]{:S(2)}, u32[]{:S(2)}) collective-permute-start(f32[1,1,200,384]{3,2,1,0:T(8,128)} %constant_dynamic-slice_fusion), channel_id=1, source_target_pairs={{0,16},{4,20},{8,24},{12,28},{16,0},{20,4},{24,8},{28,12},{1,17},{... | collective-permute-start | bytes 921608 | tf_op jit(solution)/shard_map/ppermute | solution.py:69
  99.8 7.4 %collective-permute-start.9 = (f32[200,384]{1,0:T(8,128)}, f32[200,384]{1,0:T(8,128)}, u32[]{:S(2)}, u32[]{:S(2)}) collective-permute-start(f32[200,384]{1,0:T(8,128)} %add_bitcast_fusion), channel_id=1, source_target_pairs={{0,1},{1,0},{2,3},{3,2},{4,5},{5,4},{6,7},{7,6},{8,9},{9,8},{10,11... | collective-permute-start | bytes 921608 | tf_op jit(solution)/shard_map/ppermute | solution.py:80
  108.3 6.9 %collective-permute-start.10 = (f32[200,384]{1,0:T(8,128)S(1)}, f32[200,384]{1,0:T(8,128)S(1)}, u32[]{:S(2)}, u32[]{:S(2)}) collective-permute-start(f32[200,384]{1,0:T(8,128)S(1)} %add.280), channel_id=1, source_target_pairs={{0,2},{1,3},{2,0},{3,1},{4,6},{5,7},{6,4},{7,5},{8,10},{9,11},{10,... | collective-permute-start | bytes 921608 | tf_op jit(solution)/shard_map/ppermute | solution.py:80
  (6 other events, 3.6 us)
